TPU v7x, 32 devices: a whole 2x2x4 slice. The times are simulated.
32 devices in a mesh: space: 4 (over y, x), scen: 8 (over z, core).
Axes of the slice: x: 2, y: 2, z: 4, core: 2. Of those that a mesh axis runs over, the one named last changes fastest.
Arguments:
- tracers: float32 [8, 2, 20, 32, 512], P('scen', None, None, None, 'space'), may hold values from -6 to 6
- diffusivity: float32 [2, 20, 32, 512], P(None, None, 'scen', 'space'), may hold values from 0.02 to 0.16
- level_count: int32 [32, 512], P(None, 'space'), may hold values from 0 to 20
- shelf_mask: int32 [32, 512], P(None, 'space'), may hold values 0 or 1
- cotangent: float32 [8, 2, 20, 32, 512], P('scen', None, None, None, 'space'), may hold values from -6 to 6
Outputs:
- final_tracers: float32 [8, 2, 20, 32, 512], P('scen', None, None, None, 'space')
- adjoint_tracers: float32 [8, 2, 20, 32, 512], P('scen', None, None, None, 'space')
- kappa_grad: float32 [2, 20, 32, 512], P(None, None, 'scen', 'space')
Inputs may be any that keep to these rules, and one draw needn't show every extreme that they name: `level_count`: wet levels of a column, counted from the surface; 0 marks land.
All inputs are finite; a program needn't handle non-finite values. No bound on the sum of `shelf_mask` on one device may be relied on, other than what follows from the above.
Results may differ from a plain program's by a relative error of at most 0.00002.
Values sent between devices are 32-bit elements; how exact they have to be, the bound alone decides.
No kernel may reach another device: no remote copies, remote signals or barrier semaphores. Data moves between devices by JAX's collectives and lax.ppermute only.
A program may use at most 64 MiB of HBM per device.

v0:
```python
import jax
import jax.numpy as jnp
from jax import lax
from jax.sharding import PartitionSpec as P

STEPS = 2


vertical_rate = 0.1
thaw_rate = 0.3


def with_halo(block, sides, width):
    for axis, dim in sides:
        count = lax.axis_size(axis)
        forward = [(i, i + 1) for i in range(count - 1)]
        forward.append((count - 1, 0))
        backward = [(target, source) for source, target in forward]
        low = lax.ppermute(
            lax.slice_in_dim(block, block.shape[dim] - width, None, axis=dim), axis, forward
        )
        high = lax.ppermute(lax.slice_in_dim(block, 0, width, axis=dim), axis, backward)
        block = jnp.concatenate([low, block, high], axis=dim)
    return block


def from_partner(value, axis, stride):
    return lax.ppermute(value, axis, [(i, i ^ 1 << stride) for i in range(lax.axis_size(axis))])


def with_edges(field_now):
    return with_halo(field_now, (("space", 3),), 1)


def partner_row(top_row):
    exchanged = top_row
    for bit_index in range(lax.axis_size("space").bit_length() - 1):
        exchanged = from_partner(exchanged, "space", bit_index)
    return exchanged[:, :, ::-1]


def sources_of(wetness, shelf_mask):
    below_wet = jnp.concatenate([wetness[1:], jnp.zeros_like(wetness[:1])], axis=0)
    heat_source = thaw_rate * shelf_mask.astype(jnp.float32)[None] * wetness * (1.0 - below_wet)
    return jnp.stack([heat_source, jnp.zeros_like(heat_source)])


def operate_on(tracer_now, coeffs):
    east_coeff, north_coeff, fold_coeff, down_coeff = coeffs
    edged_field = with_edges(tracer_now)
    east_flux = east_coeff * (edged_field[..., 1:] - edged_field[..., :-1])
    across_x = east_flux[..., 1:] - east_flux[..., :-1]
    north_flux = north_coeff * (tracer_now[:, :, 1:] - tracer_now[:, :, :-1])
    top_row = tracer_now[:, :, -1]
    partner = partner_row(top_row)
    fold_flux = fold_coeff * (partner - top_row)
    all_north = jnp.concatenate([north_flux, fold_flux[:, :, None]], axis=2)
    zero_row = jnp.zeros_like(all_north[:, :, :1])
    across_y = all_north - jnp.concatenate([zero_row, all_north[:, :, :-1]], axis=2)
    down_flux = down_coeff * (tracer_now[:, 1:] - tracer_now[:, :-1])
    zero_level = jnp.zeros_like(down_flux[:, :1])
    across_z = jnp.concatenate([down_flux, zero_level], axis=1) - jnp.concatenate(
        [zero_level, down_flux], axis=1
    )
    return (across_x + across_y + across_z, edged_field, partner)


def on_device(tracers, diffusivity, level_count, shelf_mask, cotangent):
    full_kappa = lax.all_gather(diffusivity, "scen", axis=2, tiled=True)
    levels = lax.broadcasted_iota(jnp.int32, (full_kappa.shape[1],) + level_count.shape, 0)
    wetness = (levels < level_count[None]).astype(jnp.float32)
    sources = sources_of(wetness, shelf_mask)
    edged_coeff = with_edges(jnp.stack([wetness, full_kappa[0]]))
    wet_edge = edged_coeff[0]
    kappa_edge = edged_coeff[1]
    east_mask = wet_edge[..., :-1] * wet_edge[..., 1:]
    east_coeff = kappa_edge[..., :-1] * east_mask
    north_kappa = full_kappa[1]
    north_mask = wetness[:, :-1] * wetness[:, 1:]
    north_coeff = north_kappa[:, :-1] * north_mask
    top_wet = wetness[:, -1]
    top_kappa = north_kappa[:, -1]
    partner_coeff = partner_row(jnp.stack([top_wet, top_kappa]))
    fold_mask = top_wet * partner_coeff[0]
    fold_coeff = 0.5 * (top_kappa + partner_coeff[1]) * fold_mask
    down_coeff = vertical_rate * wetness[:-1] * wetness[1:]
    coeffs = (east_coeff, north_coeff, fold_coeff, down_coeff)
    tracer_now = tracers[0]
    stored = []
    for substep in range(STEPS):
        change, edged_field, partner = operate_on(tracer_now, coeffs)
        stored.append((tracer_now, edged_field, partner))
        tracer_now = wetness * (tracer_now + change + sources)
    adjoint = cotangent[0]
    summed = None
    for substep in reversed(range(STEPS)):
        weighted = wetness * adjoint
        change, weighted_edge, weighted_partner = operate_on(weighted, coeffs)
        adjoint = weighted + change
        before, before_edge, before_partner = stored[substep]
        grad_east = jnp.sum(
            east_mask[..., 1:]
            * (before_edge[..., 2:] - before_edge[..., 1:-1])
            * (weighted_edge[..., 1:-1] - weighted_edge[..., 2:]),
            axis=0,
        )
        grad_inner = jnp.sum(
            north_mask
            * (before[:, :, 1:] - before[:, :, :-1])
            * (weighted[:, :, :-1] - weighted[:, :, 1:]),
            axis=0,
        )
        grad_fold = jnp.sum(
            0.5
            * fold_mask
            * (before_partner - before[:, :, -1])
            * (weighted[:, :, -1] - weighted_partner),
            axis=0,
        )
        grad_term = jnp.stack(
            [grad_east, jnp.concatenate([grad_inner, grad_fold[:, None]], axis=1)]
        )
        summed = grad_term if summed is None else summed + grad_term
    kappa_grad = lax.psum_scatter(summed, "scen", scatter_dimension=2, tiled=True)
    return (tracer_now[None], adjoint[None], kappa_grad)


def solution(mesh):
    placed = (
        P("scen", None, None, None, "space"),
        P(None, None, "scen", "space"),
        P(None, "space"),
        P(None, "space"),
        P("scen", None, None, None, "space"),
    )
    return jax.shard_map(
        on_device,
        mesh=mesh,
        in_specs=placed,
        out_specs=(
            P("scen", None, None, None, "space"),
            P("scen", None, None, None, "space"),
            P(None, None, "scen", "space"),
        ),
        check_vma=False,
    )
```

profile of v0, /device:TPU:0, one launch (start us, length us, event | category | flops | bytes accessed | tf_op | source)
XLA Modules:
  0.0 178.3 jit_solution(11726017105144906224)
XLA Ops:
  7.2 0.9 copy.135
  8.1 0.7 fusion.41
  8.9 17.0 %all_gather.3 = f32[2,20,32,128]{3,0,1,2:T(2,128)S(1)} all-gather(f32[2,20,4,128]{3,0,1,2:T(2,128)S(1)} %copy.135), channel_id=1, replica_groups=mesh['space'=4,'scen'=8] {'scen'}, dimensions={2}, use_global_device_ids=true | all-gather | bytes 737280 | tf_op jit(solution)/shard_map/all_gather | solution.py:69
  25.9 1.2 fusion.47
  27.2 1.6 collective-permute-start.4
  29.3 0.7 fusion.48
  30.0 0.9 copy.142
  30.9 1.5 collective-permute-start.2
  33.3 1.0 copy.172
  34.6 0.9 copy.138
  35.5 2.4 %collective-permute-start.1 = (f32[2,20,32,1]{2,0,3,1:T(2,128)}, f32[2,20,32,1]{2,0,3,1:T(2,128)}, u32[]{:S(2)}, u32[]{:S(2)}) collective-permute-start(f32[2,20,32,1]{2,0,3,1:T(2,128)} %copy.138), channel_id=1, source_target_pairs={{8,0},{16,8},{24,16},{0,24},{9,1},{17,9},{25,17},{1,25},{10,2},{18... | collective-permute-start | bytes 15368 | tf_op jit(solution)/shard_map/ppermute | solution.py:22
  37.9 0.9 copy.137
  39.1 0.6 copy-done
  40.2 0.7 bitcast_multiply_fusion
  40.9 1.7 fusion.45
  43.1 1.6 fusion.38
  44.8 1.6 subtract_multiply_fusion.1
  46.5 1.1 copy.149
  47.5 0.9 copy.164
  48.5 2.0 %copy.157 = f32[2,20,32,1]{2,0,3,1:T(2,128)} copy(f32[2,20,32,1]{3,0,1,2:T(2,128)} %get-tuple-element.37) | data formatting | bytes 10240 | tf_op jit(solution)/shard_map/slice | solution.py:20
  50.5 0.9 copy.155
  51.4 2.9 %collective-permute-start.12 = (f32[2,20,32,1]{2,0,3,1:T(2,128)}, f32[2,20,32,1]{2,0,3,1:T(2,128)}, u32[]{:S(2)}, u32[]{:S(2)}) collective-permute-start(f32[2,20,32,1]{2,0,3,1:T(2,128)} %copy.155), channel_id=1, source_target_pairs={{8,0},{16,8},{24,16},{0,24},{9,1},{17,9},{25,17},{1,25},{10,2},{18... | collective-permute-start | bytes 15368 | tf_op jit(solution)/shard_map/ppermute | solution.py:22
  54.3 1.0 copy.139
  55.6 1.9 %copy.140 = f32[2,20,32,1]{3,2,1,0:T(8,128)} copy(f32[2,20,32,1]{2,0,3,1:T(2,128)} %collective-permute-done.1) | data formatting | bytes 10240 | tf_op jit(solution)/shard_map/ppermute | solution.py:22
  57.5 1.7 pad_maximum_fusion.4
  59.2 1.1 slice_multiply_fusion.1
  60.7 2.0 %collective-permute-start.14 = (f32[2,20,128]{2,0,1:T(2,128)S(1)}, f32[2,20,128]{2,0,1:T(2,128)}, u32[]{:S(2)}, u32[]{:S(2)}) collective-permute-start(f32[2,20,128]{2,0,1:T(2,128)S(1)} %slice_bitcast_fusion.3), channel_id=1, source_target_pairs={{0,8},{8,0},{16,24},{24,16},{1,9},{9,1},{17,25},{25,17},{2,10},{10... | collective-permute-start | bytes 61448 | tf_op jit(solution)/shard_map/ppermute | solution.py:28
  63.4 1.2 copy.145
  64.5 1.9 %copy.156 = f32[2,20,32,1]{3,0,1,2:T(2,128)} copy(f32[2,20,32,1]{2,0,3,1:T(2,128)} %collective-permute-done.12) | data formatting | bytes 10240 | tf_op jit(solution)/shard_map/ppermute | solution.py:22
  66.4 1.9 %copy.158 = f32[2,20,32,1]{3,0,1,2:T(2,128)} copy(f32[2,20,32,1]{2,0,3,1:T(2,128)} %collective-permute-done.13) | data formatting | bytes 10240 | tf_op jit(solution)/shard_map/ppermute | solution.py:19
  68.3 1.5 collective-permute-start.5
  69.8 5.6 %fusion.3 = (f32[2,20,32,129]{3,0,1,2:T(2,128)}, f32[2,20,32,129]{3,0,1,2:T(2,128)}) fusion(f32[2,20,32,1]{3,0,1,2:T(2,128)} %copy.156, f32[2,20,32,128]{3,0,1,2:T(2,128)S(1)} %bitcast_multiply_fusion, f32[2,20,32,1]{3,0,1,2:T(2,128)} %copy.158, f32[20,32,129]{2,0,1:T(8,128)S(1)} %copy.141, f32[2,20,32,128]{3,0,1,2:T(2,128)S(1)} %bitcast.82, ...), kind=kLoop, calls=%fused_computation.15 | loop fusion | flops 1320960 | bytes 2982400 | tf_op jit(solution)/shard_map/mul | solution.py:51
  75.5 1.0 copy.163
  76.5 0.6 collective-permute-start.15
  77.0 1.5 collective-permute-start.7
  78.8 1.6 collective-permute-done.15
  81.0 6.4 %fusion.33 = (f32[2,20,32,128]{3,0,1,2:T(2,128)S(1)}, f32[2,20,32,128]{3,0,1,2:T(2,128)S(1)}) fusion(f32[2,19,32,128]{3,0,1,2:T(2,128)} %get-tuple-element.51, f32[2,20,31,128]{3,0,1,2:T(2,128)} %get-tuple-element.53, f32[2,20,1,128]{3,0,1,2:T(2,128)S(1)} %get-tuple-element.61, f32[2,20,32,129]{3,0,1,2:T(2,128)} %get-tuple-element.29, ...), kind=kLoop, calls=%fused_computation.65 | loop fusion | flops 2949120 | bytes 8454144 | tf_op jit(solution)/shard_map/mul | solution.py:97
  87.4 1.7 fusion.44
  89.1 1.8 fusion.46
  90.9 2.0 %collective-permute-start.10 = (f32[2,20,128]{2,0,1:T(2,128)S(1)}, f32[2,20,128]{2,0,1:T(2,128)}, u32[]{:S(2)}, u32[]{:S(2)}) collective-permute-start(f32[2,20,128]{2,0,1:T(2,128)S(1)} %slice_bitcast_fusion.4), channel_id=1, source_target_pairs={{0,8},{8,0},{16,24},{24,16},{1,9},{9,1},{17,25},{25,17},{2,10},{10... | collective-permute-start | bytes 61448 | tf_op jit(solution)/shard_map/ppermute | solution.py:28
  92.9 6.6 %multiply_reduce_fusion = (f32[20,31,128]{2,0,1:T(8,128)}, f32[20,31,128]{2,0,1:T(8,128)}, f32[2,20,31,128]{3,0,1,2:T(2,128)}, f32[2,20,31,128]{3,0,1,2:T(2,128)}) fusion(f32[2,20,32,128]{3,0,1,2:T(2,128)S(1)} %get-tuple-element.49, f32[20,31,128]{2,0,1:T(8,128)S(1)} %copy-done.18, f32[2,20,32,128]{3,0,1,2:T(2,128)S(1)} %bitcast.84, ...), kind=kLoop, calls=%fused_computation.71 | loop fusion | flops 1904640 | bytes 7618560 | tf_op jit(solution)/shard_map/reduce_sum | solution.py:107
  99.5 2.0 %copy.159 = f32[2,20,32,1]{2,0,3,1:T(2,128)} copy(f32[2,20,32,1]{3,0,1,2:T(2,128)} %get-tuple-element.36) | data formatting | bytes 10240 | tf_op jit(solution)/shard_map/slice | solution.py:22
  101.5 2.9 %collective-permute-start.16 = (f32[2,20,32,1]{2,0,3,1:T(2,128)}, f32[2,20,32,1]{2,0,3,1:T(2,128)}, u32[]{:S(2)}, u32[]{:S(2)}) collective-permute-start(f32[2,20,32,1]{2,0,3,1:T(2,128)} %copy.159), channel_id=1, source_target_pairs={{8,0},{16,8},{24,16},{0,24},{9,1},{17,9},{25,17},{1,25},{10,2},{18... | collective-permute-start | bytes 15368 | tf_op jit(solution)/shard_map/ppermute | solution.py:22
  104.4 2.0 %copy.150 = f32[2,20,32,1]{2,0,3,1:T(2,128)} copy(f32[2,20,32,1]{3,0,1,2:T(2,128)} %get-tuple-element.40) | data formatting | bytes 10240 | tf_op jit(solution)/shard_map/slice | solution.py:22
  106.4 2.7 %fusion.37 = (f32[2,19,32,128]{3,0,1,2:T(2,128)}, f32[2,19,32,128]{3,0,1,2:T(2,128)}) fusion(f32[2,20,32,128]{3,0,1,2:T(2,128)S(1)} %get-tuple-element.49, f32[19,32,128]{2,0,1:T(8,128)} %copy-done.5, f32[2,20,32,128]{3,0,1,2:T(2,128)S(1)} %get-tuple-element.50), kind=kLoop, calls=%fused_computation.76 | loop fusion | flops 622592 | bytes 4046848 | tf_op jit(solution)/shard_map/mul | solution.py:60
  109.2 1.4 copy.161
  110.6 2.0 %collective-permute-start.17 = (f32[2,20,32,1]{2,0,3,1:T(2,128)S(1)}, f32[2,20,32,1]{2,0,3,1:T(2,128)}, u32[]{:S(2)}, u32[]{:S(2)}) collective-permute-start(f32[2,20,32,1]{2,0,3,1:T(2,128)S(1)} %copy.161), channel_id=1, source_target_pairs={{0,8},{8,16},{16,24},{24,0},{1,9},{9,17},{17,25},{25,1},{2,10},{10... | collective-permute-start | bytes 15368 | tf_op jit(solution)/shard_map/ppermute | solution.py:19
  112.6 2.0 %copy.152 = f32[2,20,32,1]{2,0,3,1:T(2,128)} copy(f32[2,20,32,1]{3,0,1,2:T(2,128)} %get-tuple-element.39) | data formatting | bytes 10240 | tf_op jit(solution)/shard_map/slice | solution.py:20
  114.6 1.9 %copy.160 = f32[2,20,32,1]{3,0,1,2:T(2,128)} copy(f32[2,20,32,1]{2,0,3,1:T(2,128)} %collective-permute-done.16) | data formatting | bytes 10240 | tf_op jit(solution)/shard_map/ppermute | solution.py:22
  116.5 1.9 %copy.151 = f32[2,20,32,1]{3,0,1,2:T(2,128)} copy(f32[2,20,32,1]{2,0,3,1:T(2,128)} %collective-permute-done.8) | data formatting | bytes 10240 | tf_op jit(solution)/shard_map/ppermute | solution.py:22
  118.4 1.5 collective-permute-start.11
  120.4 8.7 %fusion.36 = (f32[20,32,128]{2,0,1:T(8,128)}, f32[20,32,128]{2,0,1:T(8,128)}) fusion(f32[2,20,32,128]{3,0,1,2:T(2,128)S(1)} %get-tuple-element.49, f32[2,20,32,1]{3,0,1,2:T(2,128)} %copy.160, f32[2,20,32,128]{3,0,1,2:T(2,128)S(1)} %bitcast.85, f32[2,20,32,1]{3,0,1,2:T(2,128)} %copy-done.2, f32[20,32,128]{2,0,1:T(8,128)} %copy.163, ...), kind=kLoop, calls=%fused_computation.68 | loop fusion | flops 2129920 | bytes 3624960 | tf_op jit(solution)/shard_map/reduce_sum | solution.py:101
  129.1 1.9 %copy.162 = f32[2,20,32,1]{3,0,1,2:T(2,128)} copy(f32[2,20,32,1]{2,0,3,1:T(2,128)} %collective-permute-done.17) | data formatting | bytes 10240 | tf_op jit(solution)/shard_map/ppermute | solution.py:19
  131.0 1.9 %copy.153 = f32[2,20,32,1]{3,0,1,2:T(2,128)} copy(f32[2,20,32,1]{2,0,3,1:T(2,128)} %collective-permute-done.9) | data formatting | bytes 10240 | tf_op jit(solution)/shard_map/ppermute | solution.py:19
  133.3 1.1 maximum_bitcast_fusion.1
  134.3 1.0 maximum_bitcast_fusion
  135.5 1.0 copy.165
  137.1 4.8 %fusion.1 = (f32[2,20,32,129]{3,0,1,2:T(2,128)S(1)}, f32[2,20,32,129]{3,0,1,2:T(2,128)S(1)}) fusion(f32[2,20,32,1]{3,0,1,2:T(2,128)S(1)} %copy-done.3, f32[2,20,32,128]{3,0,1,2:T(2,128)S(1)} %get-tuple-element.49, f32[2,20,32,1]{3,0,1,2:T(2,128)} %copy.162, f32[20,32,129]{2,0,1:T(8,128)S(1)} %copy.141, f32[2,20,32,128]{3,0,1,2:T(2,128)S(1)} %get-tuple-element.50, ...), kind=kLoop, calls=%fused_computation.13 | loop fusion | flops 1320960 | bytes 2982400 | tf_op jit(solution)/shard_map/mul | solution.py:51
  141.9 1.4 fusion.34
  143.4 1.0 copy.167
  144.7 1.6 fusion.10
  146.3 1.0 copy.166
  147.3 22.6 %reduce-scatter.2.cloned.1.call-done = f32[2,20,4,128]{3,1,0,2:T(8,128)} async-done(((f32[2,20,32,128]{3,1,0,2:T(8,128)}), f32[2,20,4,128]{3,1,0,2:T(8,128)}) %reduce-scatter.2.cloned.1.call-update) | async-done | bytes 81936 | tf_op jit(solution)/shard_map/reduce_scatter | solution.py:124
  169.9 1.6 copy.168
  (107 shorter events, 7.5 us)
Async XLA Ops:
  7.2 162.7 %reduce-scatter.2.cloned.1.call-start = ((), (), s32[]{:S(2)}) async-start(), calls=%async_computation.1 | async-start | bytes 884736 | tf_op jit(solution)/shard_map/reduce_scatter | solution.py:124
  8.9 19.9 %copy-start.10 = (f32[1,2,20,32,128]{4,3,2,1,0:T(8,128)S(1)}, f32[1,2,20,32,128]{4,3,2,1,0:T(8,128)}, u32[]{:S(2)}) copy-start(f32[1,2,20,32,128]{4,3,2,1,0:T(8,128)} %param.5) | copy-start | bytes 1966084
  27.2 41.1 %collective-permute-start.4 = (f32[2,20,128]{2,0,1:T(2,128)S(1)}, f32[2,20,128]{2,0,1:T(2,128)}, u32[]{:S(2)}, u32[]{:S(2)}) collective-permute-start(f32[2,20,128]{2,0,1:T(2,128)S(1)} %pad_maximum_fusion.6), channel_id=1, source_target_pairs={{0,8},{8,0},{16,24},{24,16},{1,9},{9,1},{17,25},{25,17},{2,10},{10... | collective-permute-start | bytes 61448 | tf_op jit(solution)/shard_map/ppermute | solution.py:28
  30.0 3.3 %copy-start.20 = (s32[32,128]{1,0:T(8,128)S(1)}, s32[32,128]{1,0:T(8,128)}, u32[]{:S(2)}) copy-start(s32[32,128]{1,0:T(8,128)} %param.7) | copy-start | bytes 49156
  30.9 29.8 %collective-permute-start.2 = (f32[2,20,32,1]{2,0,3,1:T(2,128)}, f32[2,20,32,1]{2,0,3,1:T(2,128)S(1)}, u32[]{:S(2)}, u32[]{:S(2)}) collective-permute-start(f32[2,20,32,1]{2,0,3,1:T(2,128)} %copy.142), channel_id=1, source_target_pairs={{8,0},{16,8},{24,16},{0,24},{9,1},{17,9},{25,17},{1,25},{10,2},{18... | collective-permute-start | bytes 15368 | tf_op jit(solution)/shard_map/ppermute | solution.py:22
  32.7 30.5 %collective-permute-start.3 = (f32[2,20,32,1]{2,0,3,1:T(2,128)S(1)}, f32[2,20,32,1]{2,0,3,1:T(2,128)S(1)}, u32[]{:S(2)}, u32[]{:S(2)}) collective-permute-start(f32[2,20,32,1]{2,0,3,1:T(2,128)S(1)} %copy.144), channel_id=1, source_target_pairs={{0,8},{8,16},{16,24},{24,0},{1,9},{9,17},{17,25},{25,1},{2,10},{10... | collective-permute-start | bytes 15368 | tf_op jit(solution)/shard_map/ppermute | solution.py:19
  35.5 19.8 %collective-permute-start.1 = (f32[2,20,32,1]{2,0,3,1:T(2,128)}, f32[2,20,32,1]{2,0,3,1:T(2,128)}, u32[]{:S(2)}, u32[]{:S(2)}) collective-permute-start(f32[2,20,32,1]{2,0,3,1:T(2,128)} %copy.138), channel_id=1, source_target_pairs={{8,0},{16,8},{24,16},{0,24},{9,1},{17,9},{25,17},{1,25},{10,2},{18... | collective-permute-start | bytes 15368 | tf_op jit(solution)/shard_map/ppermute | solution.py:22
  38.8 12.6 %collective-permute-start = (f32[2,20,32,1]{2,0,3,1:T(2,128)}, f32[2,20,32,1]{2,0,3,1:T(2,128)}, u32[]{:S(2)}, u32[]{:S(2)}) collective-permute-start(f32[2,20,32,1]{2,0,3,1:T(2,128)} %copy.137), channel_id=1, source_target_pairs={{0,8},{8,16},{16,24},{24,0},{1,9},{9,17},{17,25},{25,1},{2,10},{10... | collective-permute-start | bytes 15368 | tf_op jit(solution)/shard_map/ppermute | solution.py:19
  39.0 0.7 copy-start
  39.0 1.2 copy-start.9
  40.9 1.8 copy-start.21
  42.9 1.9 %copy-start.6 = (f32[20,31,128]{2,0,1:T(8,128)}, f32[20,31,128]{2,0,1:T(8,128)S(1)}, u32[]{:S(2)}) copy-start(f32[20,31,128]{2,0,1:T(8,128)S(1)} %copy.147) | copy-start | bytes 952324
  43.1 1.7 copy-start.5
  46.4 4.1 %copy-start.11 = (f32[2,20,32,1]{3,0,1,2:T(2,128)S(1)}, f32[2,20,32,1]{3,0,1,2:T(2,128)}, u32[]{:S(2)}) copy-start(f32[2,20,32,1]{3,0,1,2:T(2,128)} %get-tuple-element.38) | copy-start | bytes 15364
  51.4 13.2 %collective-permute-start.12 = (f32[2,20,32,1]{2,0,3,1:T(2,128)}, f32[2,20,32,1]{2,0,3,1:T(2,128)}, u32[]{:S(2)}, u32[]{:S(2)}) collective-permute-start(f32[2,20,32,1]{2,0,3,1:T(2,128)} %copy.155), channel_id=1, source_target_pairs={{8,0},{16,8},{24,16},{0,24},{9,1},{17,9},{25,17},{1,25},{10,2},{18... | collective-permute-start | bytes 15368 | tf_op jit(solution)/shard_map/ppermute | solution.py:22
  55.4 11.1 %collective-permute-start.13 = (f32[2,20,32,1]{2,0,3,1:T(2,128)}, f32[2,20,32,1]{2,0,3,1:T(2,128)}, u32[]{:S(2)}, u32[]{:S(2)}) collective-permute-start(f32[2,20,32,1]{2,0,3,1:T(2,128)} %copy.157), channel_id=1, source_target_pairs={{0,8},{8,16},{16,24},{24,0},{1,9},{9,17},{17,25},{25,1},{2,10},{10... | collective-permute-start | bytes 15368 | tf_op jit(solution)/shard_map/ppermute | solution.py:19
  60.7 15.7 %collective-permute-start.14 = (f32[2,20,128]{2,0,1:T(2,128)S(1)}, f32[2,20,128]{2,0,1:T(2,128)}, u32[]{:S(2)}, u32[]{:S(2)}) collective-permute-start(f32[2,20,128]{2,0,1:T(2,128)S(1)} %slice_bitcast_fusion.3), channel_id=1, source_target_pairs={{0,8},{8,0},{16,24},{24,16},{1,9},{9,1},{17,25},{25,17},{2,10},{10... | collective-permute-start | bytes 61448 | tf_op jit(solution)/shard_map/ppermute | solution.py:28
  63.2 12.1 %copy-start.2 = (f32[2,20,32,1]{3,0,1,2:T(2,128)}, f32[2,20,32,1]{3,0,1,2:T(2,128)S(1)}, u32[]{:S(2)}) copy-start(f32[2,20,32,1]{3,0,1,2:T(2,128)S(1)} %copy.143) | copy-start | bytes 15364
  63.2 13.8 %collective-permute-start.6 = (f32[2,20,128]{2,0,1:T(2,128)S(1)}, f32[2,20,128]{2,0,1:T(2,128)S(1)}, u32[]{:S(2)}, u32[]{:S(2)}) collective-permute-start(f32[2,20,128]{2,0,1:T(2,128)S(1)} %slice_bitcast_fusion.5), channel_id=1, source_target_pairs={{0,8},{8,0},{16,24},{24,16},{1,9},{9,1},{17,25},{25,17},{2,10},{10... | collective-permute-start | bytes 61448 | tf_op jit(solution)/shard_map/ppermute | solution.py:28
  68.3 7.0 %copy-start.19 = (f32[20,32,129]{2,1,0:T(8,128)S(1)}, f32[20,32,129]{2,1,0:T(8,128)}, u32[]{:S(2)}) copy-start(f32[20,32,129]{2,1,0:T(8,128)} %get-tuple-element.24) | copy-start | bytes 990724
  68.3 10.2 %collective-permute-start.5 = (f32[2,20,128]{2,0,1:T(2,128)}, f32[2,20,128]{2,0,1:T(2,128)S(1)}, u32[]{:S(2)}, u32[]{:S(2)}) collective-permute-start(f32[2,20,128]{2,0,1:T(2,128)} %collective-permute-done.4), channel_id=1, source_target_pairs={{0,16},{8,24},{16,0},{24,8},{1,17},{9,25},{17,1},{25,9},{2,18},{10... | collective-permute-start | bytes 61448 | tf_op jit(solution)/shard_map/ppermute | solution.py:28
  76.5 4.0 %collective-permute-start.15 = (f32[2,20,128]{2,0,1:T(2,128)}, f32[2,20,128]{2,0,1:T(2,128)S(1)}, u32[]{:S(2)}, u32[]{:S(2)}) collective-permute-start(f32[2,20,128]{2,0,1:T(2,128)} %collective-permute-done.14), channel_id=1, source_target_pairs={{0,16},{8,24},{16,0},{24,8},{1,17},{9,25},{17,1},{25,9},{2,18},{10... | collective-permute-start | bytes 61448 | tf_op jit(solution)/shard_map/ppermute | solution.py:28
  77.0 3.8 %collective-permute-start.7 = (f32[2,20,128]{2,0,1:T(2,128)S(1)}, f32[2,20,128]{2,0,1:T(2,128)S(1)}, u32[]{:S(2)}, u32[]{:S(2)}) collective-permute-start(f32[2,20,128]{2,0,1:T(2,128)S(1)} %collective-permute-done.6), channel_id=1, source_target_pairs={{0,16},{8,24},{16,0},{24,8},{1,17},{9,25},{17,1},{25,9},{2,18},{10... | collective-permute-start | bytes 61448 | tf_op jit(solution)/shard_map/ppermute | solution.py:28
  89.1 3.8 %copy-start.7 = (f32[20,31,128]{2,0,1:T(8,128)S(1)}, f32[20,31,128]{2,0,1:T(8,128)}, u32[]{:S(2)}) copy-start(f32[20,31,128]{2,0,1:T(8,128)} %copy-done.6) | copy-start | bytes 952324
  89.1 3.8 %copy-start.18 = (f32[20,31,128]{2,0,1:T(8,128)S(1)}, f32[20,31,128]{2,0,1:T(8,128)}, u32[]{:S(2)}) copy-start(f32[20,31,128]{2,0,1:T(8,128)} %copy.164) | copy-start | bytes 952324
  90.9 27.5 %collective-permute-start.10 = (f32[2,20,128]{2,0,1:T(2,128)S(1)}, f32[2,20,128]{2,0,1:T(2,128)}, u32[]{:S(2)}, u32[]{:S(2)}) collective-permute-start(f32[2,20,128]{2,0,1:T(2,128)S(1)} %slice_bitcast_fusion.4), channel_id=1, source_target_pairs={{0,8},{8,0},{16,24},{24,16},{1,9},{9,1},{17,25},{25,17},{2,10},{10... | collective-permute-start | bytes 61448 | tf_op jit(solution)/shard_map/ppermute | solution.py:28
  92.9 27.0 %collective-permute-start.18 = (f32[2,20,128]{2,0,1:T(2,128)S(1)}, f32[2,20,128]{2,0,1:T(2,128)}, u32[]{:S(2)}, u32[]{:S(2)}) collective-permute-start(f32[2,20,128]{2,0,1:T(2,128)S(1)} %slice_bitcast_fusion.2), channel_id=1, source_target_pairs={{0,8},{8,0},{16,24},{24,16},{1,9},{9,1},{17,25},{25,17},{2,10},{10... | collective-permute-start | bytes 61448 | tf_op jit(solution)/shard_map/ppermute | solution.py:28
  101.5 13.1 %collective-permute-start.16 = (f32[2,20,32,1]{2,0,3,1:T(2,128)}, f32[2,20,32,1]{2,0,3,1:T(2,128)}, u32[]{:S(2)}, u32[]{:S(2)}) collective-permute-start(f32[2,20,32,1]{2,0,3,1:T(2,128)} %copy.159), channel_id=1, source_target_pairs={{8,0},{16,8},{24,16},{0,24},{9,1},{17,9},{25,17},{1,25},{10,2},{18... | collective-permute-start | bytes 15368 | tf_op jit(solution)/shard_map/ppermute | solution.py:22
  106.4 10.1 %collective-permute-start.8 = (f32[2,20,32,1]{2,0,3,1:T(2,128)}, f32[2,20,32,1]{2,0,3,1:T(2,128)}, u32[]{:S(2)}, u32[]{:S(2)}) collective-permute-start(f32[2,20,32,1]{2,0,3,1:T(2,128)} %copy.150), channel_id=1, source_target_pairs={{8,0},{16,8},{24,16},{0,24},{9,1},{17,9},{25,17},{1,25},{10,2},{18... | collective-permute-start | bytes 15368 | tf_op jit(solution)/shard_map/ppermute | solution.py:22
  110.6 18.5 %collective-permute-start.17 = (f32[2,20,32,1]{2,0,3,1:T(2,128)S(1)}, f32[2,20,32,1]{2,0,3,1:T(2,128)}, u32[]{:S(2)}, u32[]{:S(2)}) collective-permute-start(f32[2,20,32,1]{2,0,3,1:T(2,128)S(1)} %copy.161), channel_id=1, source_target_pairs={{0,8},{8,16},{16,24},{24,0},{1,9},{9,17},{17,25},{25,1},{2,10},{10... | collective-permute-start | bytes 15368 | tf_op jit(solution)/shard_map/ppermute | solution.py:19
  114.6 16.4 %collective-permute-start.9 = (f32[2,20,32,1]{2,0,3,1:T(2,128)}, f32[2,20,32,1]{2,0,3,1:T(2,128)}, u32[]{:S(2)}, u32[]{:S(2)}) collective-permute-start(f32[2,20,32,1]{2,0,3,1:T(2,128)} %copy.152), channel_id=1, source_target_pairs={{0,8},{8,16},{16,24},{24,0},{1,9},{9,17},{17,25},{25,1},{2,10},{10... | collective-permute-start | bytes 15368 | tf_op jit(solution)/shard_map/ppermute | solution.py:19
  118.4 14.5 %collective-permute-start.11 = (f32[2,20,128]{2,0,1:T(2,128)}, f32[2,20,128]{2,0,1:T(2,128)S(1)}, u32[]{:S(2)}, u32[]{:S(2)}) collective-permute-start(f32[2,20,128]{2,0,1:T(2,128)} %collective-permute-done.10), channel_id=1, source_target_pairs={{0,16},{8,24},{16,0},{24,8},{1,17},{9,25},{17,1},{25,9},{2,18},{10... | collective-permute-start | bytes 61448 | tf_op jit(solution)/shard_map/ppermute | solution.py:28
  119.8 13.1 %collective-permute-start.19 = (f32[2,20,128]{2,0,1:T(2,128)}, f32[2,20,128]{2,0,1:T(2,128)S(1)}, u32[]{:S(2)}, u32[]{:S(2)}) collective-permute-start(f32[2,20,128]{2,0,1:T(2,128)} %collective-permute-done.18), channel_id=1, source_target_pairs={{0,16},{8,24},{16,0},{24,8},{1,17},{9,25},{17,1},{25,9},{2,18},{10... | collective-permute-start | bytes 61448 | tf_op jit(solution)/shard_map/ppermute | solution.py:28
  133.1 2.2 %copy-start.16 = (f32[20,32,128]{2,0,1:T(8,128)S(1)}, f32[20,32,128]{2,0,1:T(8,128)}, u32[]{:S(2)}) copy-start(f32[20,32,128]{2,0,1:T(8,128)} %get-tuple-element.15) | copy-start | bytes 983044
  133.1 2.2 %copy-start.17 = (f32[20,32,128]{2,0,1:T(8,128)S(1)}, f32[20,32,128]{2,0,1:T(8,128)}, u32[]{:S(2)}) copy-start(f32[20,32,128]{2,0,1:T(8,128)} %get-tuple-element.16) | copy-start | bytes 983044
  135.5 1.4 copy-start.3
  135.5 1.6 copy-start.4
  137.1 4.8 %copy-start.13 = (f32[2,20,31,128]{3,0,1,2:T(2,128)S(1)}, f32[2,20,31,128]{3,0,1,2:T(2,128)}, u32[]{:S(2)}) copy-start(f32[2,20,31,128]{3,0,1,2:T(2,128)} %get-tuple-element.34) | copy-start | bytes 1904644
  137.1 4.8 %copy-start.15 = (f32[2,19,32,128]{3,0,1,2:T(2,128)S(1)}, f32[2,19,32,128]{3,0,1,2:T(2,128)}, u32[]{:S(2)}) copy-start(f32[2,19,32,128]{3,0,1,2:T(2,128)} %get-tuple-element.47) | copy-start | bytes 1867780
  141.9 2.4 %copy-start.12 = (f32[2,20,31,128]{3,0,1,2:T(2,128)S(1)}, f32[2,20,31,128]{3,0,1,2:T(2,128)}, u32[]{:S(2)}) copy-start(f32[2,20,31,128]{3,0,1,2:T(2,128)} %get-tuple-element.33) | copy-start | bytes 1904644
  141.9 2.4 %copy-start.14 = (f32[2,19,32,128]{3,0,1,2:T(2,128)S(1)}, f32[2,19,32,128]{3,0,1,2:T(2,128)}, u32[]{:S(2)}) copy-start(f32[2,19,32,128]{3,0,1,2:T(2,128)} %get-tuple-element.48) | copy-start | bytes 1867780
  143.3 1.0 copy-start.1
  143.4 1.4 copy-start.8
Sparse Core Ops, SparseCore 0:
  136.6 33.1 reduce-scatter.1
where the time goes:
time: 180 us; the launch traced here: 178 us
  local copies, waits for them, and re-layouts  50.3 us (28%)
  other arithmetic  48 us (27%)
  waiting for transfers between devices  24.5 us (14%)
  starting transfers between devices  23.9 us (13%)
  blocking collectives  17 us (9%)
  between operations  14.5 us (8%)
    reduce_scatter x1, waiting for transfers between devices, on_device(): lax.psum_scatter(summed, 'scen', scatter_dimension=2, tiled=True)  22.6 us
    all_gather x1, blocking collectives, on_device(): full_kappa = lax.all_gather(diffusivity, 'scen', axis=2, tiled=True)  17 us
    slice x9, local copies, waits for them, and re-layouts, with_halo(): lax.slice_in_dim(block, block.shape[dim] - width, None, axis=dim)  12.6 us
    ppermute x10, starting transfers between devices, from_partner(): lax.ppermute(value, axis, [(i, i ^ 1 << stride) for i in range(lax.axis_s...  11.3 us
    mul x2, other arithmetic, operate_on(): east_flux = east_coeff * (edged_field[..., 1:] - edged_field[..., :-1])  10.4 us
    ppermute x5, starting transfers between devices, with_halo(): lax.ppermute(lax.slice_in_dim(block, 0, width, axis=dim), axis, backward)  9.74 us
    reduce_sum x1, other arithmetic, on_device(): jnp.sum(east_mask[..., 1:] * (before_edge[..., 2:] - before_edge[..., 1:-...  8.7 us
    unnamed x53, local copies, waits for them, and re-layouts  8.08 us
  transfers between devices with their start and end apart: 21, of which 3 were waited for; matrix products, arithmetic and copies ran while one was open for 44% of the time, Pallas kernels for 0%

commit v1 on v0

v1 whole, which is shorter than its diff:
```python
import jax
import jax.numpy as jnp
from jax import lax
from jax.experimental import pallas as pl
from jax.experimental.pallas import tpu as pltpu
from jax.sharding import PartitionSpec as P

STEPS = 2
HALO = 2

vertical_rate = 0.1
thaw_rate = 0.3

INTERPRET = False


def shifted(x, perm):
    return lax.ppermute(x, "space", perm)


def extended(fields, lanes, rows):
    n = lax.axis_size("space")
    count, ny, width = fields.shape
    west = shifted(fields[..., width - HALO:], [(q, (q + 1) % n) for q in range(n)])
    east = shifted(fields[..., :HALO], [(q, (q - 1) % n) for q in range(n)])
    mirrored = fields[:, ny - 1:ny - 3:-1, ::-1]
    ghost = shifted(mirrored, [(q, n - 1 - q) for q in range(n)])
    ghost_east = shifted(mirrored[..., :HALO], [(q, (n - 2 - q) % n) for q in range(n)])
    ghost_west = shifted(mirrored[..., width - HALO:], [(q, (n - q) % n) for q in range(n)])
    gap = lanes - width - 2 * HALO
    top = jnp.concatenate(
        [fields, east, jnp.zeros((count, ny, gap), fields.dtype), west], axis=-1
    )
    folded = jnp.concatenate(
        [ghost, ghost_east, jnp.zeros((count, 2, gap), fields.dtype), ghost_west], axis=-1
    )
    pad = jnp.zeros((count, rows - ny - 2, lanes), fields.dtype)
    return jnp.concatenate([top, folded, pad], axis=1)


def roll(x, shift, axis):
    return pltpu.roll(x, shift % x.shape[axis], axis)


def diffusion_kernel(
    ue_ref, ve_ref, ke_ref, kn_ref, lev_ref, shelf_ref,
    fin_ref, adj_ref, grad_ref,
    wet_ref, ce_ref, cn_ref, cz_ref, src_ref, gem_ref, gnm_ref, u1_ref, a_ref, b_ref,
):
    levels, rows, lanes = wet_ref.shape
    ny, width = fin_ref.shape[2:]
    row = lax.broadcasted_iota(jnp.int32, (rows, lanes), 0)
    lane = lax.broadcasted_iota(jnp.int32, (rows, lanes), 1)
    owned = (row < ny) & (lane < width)
    lev = lev_ref[...]
    shelf = shelf_ref[...]

    def wet_of(k):
        return (lev > k.astype(jnp.float32)).astype(jnp.float32)

    cz_ref[0] = jnp.zeros((rows, lanes), jnp.float32)

    def setup(k, carry):
        w = wet_of(k)
        w_next = jnp.where(k + 1 < levels, wet_of(k + 1), 0.0)
        w_east = roll(w, -1, 1)
        w_north = roll(w, -1, 0)
        ke = ke_ref[k]
        ke_sel = jnp.where(row >= ny, roll(ke, -1, 1), ke)
        east_mask = w * w_east
        ce_ref[k] = ke_sel * east_mask
        kn = kn_ref[k]
        kn_up = roll(kn, -1, 0)
        kn_sel = jnp.where(
            row < ny - 1, kn, jnp.where(row == ny - 1, 0.5 * (kn + kn_up), jnp.where(row == ny, kn_up, 0.0))
        )
        north_mask = w * w_north
        cn_ref[k] = kn_sel * north_mask
        cz_ref[k + 1] = vertical_rate * w * w_next
        src_ref[k] = thaw_rate * shelf * w * (1.0 - w_next)
        wet_ref[k] = w
        gem_ref[k] = jnp.where(owned, east_mask, 0.0)
        gnm_ref[k] = jnp.where(
            owned, jnp.where(row < ny - 1, north_mask, jnp.where(row == ny - 1, 0.5 * north_mask, 0.0)), 0.0
        )
        return carry

    lax.fori_loop(0, levels, setup, 0)

    def operate(x_ref, c, k):
        x = x_ref[c, k]
        above = x_ref[c, jnp.minimum(k + 1, levels - 1)]
        below = x_ref[c, jnp.maximum(k - 1, 0)]
        east = ce_ref[k] * (roll(x, -1, 1) - x)
        north = cn_ref[k] * (roll(x, -1, 0) - x)
        change = (east - roll(east, 1, 1)) + (north - roll(north, 1, 0))
        change = change + (cz_ref[k + 1] * (above - x) - cz_ref[k] * (x - below))
        return x, change

    planes = 2 * levels

    def forward_first(ck, carry):
        c = ck // levels
        k = ck % levels
        x, change = operate(ue_ref, c, k)
        heat = jnp.where(c == 0, 1.0, 0.0)
        u1_ref[c, k] = wet_ref[k] * (x + change + heat * src_ref[k])
        return carry

    lax.fori_loop(0, planes, forward_first, 0)

    def forward_second(ck, carry):
        c = ck // levels
        k = ck % levels
        x, change = operate(u1_ref, c, k)
        heat = jnp.where(c == 0, 1.0, 0.0)
        out = wet_ref[k] * (x + change + heat * src_ref[k])
        fin_ref[c, k] = out[:ny, :width]
        return carry

    lax.fori_loop(0, planes, forward_second, 0)

    def weigh(ck, carry):
        c = ck // levels
        k = ck % levels
        a_ref[c, k] = wet_ref[k] * ve_ref[c, k]
        return carry

    lax.fori_loop(0, planes, weigh, 0)

    def backward_second(ck, carry):
        c = ck // levels
        k = ck % levels
        x, change = operate(a_ref, c, k)
        b_ref[c, k] = wet_ref[k] * (x + change)
        return carry

    lax.fori_loop(0, planes, backward_second, 0)

    def backward_first(ck, carry):
        c = ck // levels
        k = ck % levels
        x, change = operate(b_ref, c, k)
        adj_ref[c, k] = (x + change)[:ny, :width]
        return carry

    lax.fori_loop(0, planes, backward_first, 0)

    def gradient(k, carry):
        gem = gem_ref[k]
        gnm = gnm_ref[k]
        g_east = jnp.zeros((rows, lanes), jnp.float32)
        g_north = jnp.zeros((rows, lanes), jnp.float32)
        for c in range(2):
            for u_ref, v_ref in ((ue_ref, b_ref), (u1_ref, a_ref)):
                u = u_ref[c, k]
                v = v_ref[c, k]
                g_east = g_east + (roll(u, -1, 1) - u) * (v - roll(v, -1, 1))
                g_north = g_north + (roll(u, -1, 0) - u) * (v - roll(v, -1, 0))
        grad_ref[0, k] = (gem * g_east)[:ny, :width]
        grad_ref[1, k] = (gnm * g_north)[:ny, :width]
        return carry

    lax.fori_loop(0, levels, gradient, 0)


def on_device(tracers, diffusivity, level_count, shelf_mask, cotangent):
    _, chans, levels, ny, width = tracers.shape
    lanes = width + 128
    rows = -(-(ny + 2) // 8) * 8
    first = jnp.concatenate(
        [
            tracers[0].reshape(chans * levels, ny, width),
            cotangent[0].reshape(chans * levels, ny, width),
            level_count.astype(jnp.float32)[None],
            shelf_mask.astype(jnp.float32)[None],
        ]
    )
    first_ext = extended(first, lanes, rows)
    full_kappa = lax.all_gather(diffusivity, "scen", axis=2, tiled=True)
    kappa_ext = extended(full_kappa.reshape(2 * levels, ny, width), lanes, rows)
    planes = chans * levels
    ue = first_ext[:planes].reshape(chans, levels, rows, lanes)
    ve = first_ext[planes:2 * planes].reshape(chans, levels, rows, lanes)
    lev = first_ext[2 * planes]
    shelf = first_ext[2 * planes + 1]
    ke = kappa_ext[:levels]
    kn = kappa_ext[levels:]
    field = jax.ShapeDtypeStruct((chans, levels, ny, width), jnp.float32)
    plane = pltpu.VMEM((levels, rows, lanes), jnp.float32)
    planes_c = pltpu.VMEM((chans, levels, rows, lanes), jnp.float32)
    final, adjoint, grad = pl.pallas_call(
        diffusion_kernel,
        out_shape=(field, field, jax.ShapeDtypeStruct((2, levels, ny, width), jnp.float32)),
        scratch_shapes=[
            plane,
            plane,
            plane,
            pltpu.VMEM((levels + 1, rows, lanes), jnp.float32),
            plane,
            plane,
            plane,
            planes_c,
            planes_c,
            planes_c,
        ],
        compiler_params=pltpu.CompilerParams(vmem_limit_bytes=48 * 1024 * 1024),
        interpret=INTERPRET,
    )(ue, ve, ke, kn, lev, shelf)
    kappa_grad = lax.psum_scatter(grad, "scen", scatter_dimension=2, tiled=True)
    return (final[None], adjoint[None], kappa_grad)


def solution(mesh):
    placed = (
        P("scen", None, None, None, "space"),
        P(None, None, "scen", "space"),
        P(None, "space"),
        P(None, "space"),
        P("scen", None, None, None, "space"),
    )
    return jax.shard_map(
        on_device,
        mesh=mesh,
        in_specs=placed,
        out_specs=(
            P("scen", None, None, None, "space"),
            P("scen", None, None, None, "space"),
            P(None, None, "scen", "space"),
        ),
        check_vma=False,
    )
```

time: 180 us -> 170 us (0.944)
  other arithmetic: 48 us -> 6.6 us
  waiting for transfers between devices: 24.5 us -> 58.8 us
  Pallas kernels: 0 us -> 33.7 us
  local copies, waits for them, and re-layouts: 50.3 us -> 20 us
  starting transfers between devices: 23.9 us -> 19.9 us
    unnamed x1 -> x2, waiting for transfers between devices: 0.02 us -> 55.2 us
    pallas_call x0 -> x1, Pallas kernels: none -> 33.7 us  [on_device(): pl.pallas_call(diffusion_kernel, out_shape=(field, field, jax.ShapeDtypeS...]
    mul x12 -> x0, other arithmetic: 24.7 us -> none  [the longest x2 10.4 us: operate_on(): east_flux = east_coeff * (edged_field[..., 1:] - edged_field[..., :-1])]
    reduce_scatter x1 -> x0, waiting for transfers between devices: 22.6 us -> none  [on_device(): lax.psum_scatter(summed, 'scen', scatter_dimension=2, tiled=True)]
    reduce_sum x3 -> x0, other arithmetic: 15.4 us -> none  [the longest x1 8.7 us: on_device(): jnp.sum(east_mask[..., 1:] * (before_edge[..., 2:] - before_edge[..., 1:-...]
    slice x20 -> x14, local copies, waits for them, and re-layouts: 21.9 us -> 7.96 us  [the longest x4 2 us: extended(): east = shifted(fields[..., :HALO], [(q, (q - 1) % n) for q in range(n)])]
    ppermute x10 -> x4, local copies, waits for them, and re-layouts: 15.8 us -> 7.65 us  [shifted(): return lax.ppermute(x, 'space', perm)]
    unnamed x53 -> x15, local copies, waits for them, and re-layouts: 8.08 us -> 2.82 us
  transfers between devices with their start and end apart: 21 -> 11, of which waited for: 3 -> 2; matrix products, arithmetic and copies ran while one was open for 44% -> 11% of each run, Pallas kernels for 0% -> 0%
where the time goes in v1:
time: 170 us; the launch traced here: 169 us
  waiting for transfers between devices  58.8 us (35%)
  Pallas kernels  33.7 us (20%)
  local copies, waits for them, and re-layouts  20 us (12%)
  starting transfers between devices  19.9 us (12%)
  blocking collectives  15.4 us (9%)
  between operations  14.9 us (9%)
  other arithmetic  6.6 us (4%)
    unnamed x2, waiting for transfers between devices  55.2 us
    pallas_call x1, Pallas kernels, on_device(): pl.pallas_call(diffusion_kernel, out_shape=(field, field, jax.ShapeDtypeS...  33.7 us
    ppermute x10, starting transfers between devices, shifted(): return lax.ppermute(x, 'space', perm)  19.8 us
    all_gather x1, blocking collectives, on_device(): full_kappa = lax.all_gather(diffusivity, 'scen', axis=2, tiled=True)  15.4 us
    ppermute x4, local copies, waits for them, and re-layouts, shifted(): return lax.ppermute(x, 'space', perm)  7.65 us
    concatenate x2, other arithmetic, extended(): return jnp.concatenate([top, folded, pad], axis=1)  4.28 us
    ppermute x10, waiting for transfers between devices, shifted(): return lax.ppermute(x, 'space', perm)  3.54 us
  transfers between devices with their start and end apart: 11, of which 2 were waited for; matrix products, arithmetic and copies ran while one was open for 11% of the time, Pallas kernels for 0%

profile of v1, /device:TPU:0, one launch (start us, length us, event | category | flops | bytes accessed | tf_op | source)
XLA Modules:
  0.0 169.2 jit_solution(2917622641626531590)
XLA Ops:
  7.2 0.0 all-reduce.3.cloned.1.call-start
  7.2 0.7 convert_bitcast_fusion
  8.0 1.4 pad_maximum_fusion
  9.3 0.5 fusion.2
  9.8 0.0 copy-start.3
  9.8 0.9 copy.8
  10.7 3.9 %collective-permute-start = (f32[82,32,2]{0,1,2:T(8,128)S(1)}, f32[82,32,2]{0,1,2:T(8,128)S(1)}, u32[]{:S(2)}, u32[]{:S(2)}) collective-permute-start(f32[82,32,2]{0,1,2:T(8,128)S(1)} %copy.8), channel_id=1, source_target_pairs={{0,24},{8,0},{16,8},{24,16},{1,25},{9,1},{17,9},{25,17},{2,26},{10... | collective-permute-start | bytes 62984 | tf_op jit(solution)/shard_map/ppermute | solution.py:18
  14.6 1.5 copy.9
  16.1 0.0 collective-permute-start.1
  16.1 0.0 copy-done.3
  16.2 15.4 %all_gather.3 = f32[2,20,32,128]{3,0,1,2:T(2,128)S(1)} all-gather(f32[2,20,4,128]{3,0,1,2:T(2,128)S(1)} %copy.12), channel_id=1, replica_groups=mesh['space'=4,'scen'=8] {'scen'}, dimensions={2}, use_global_device_ids=true | all-gather | bytes 737280 | tf_op jit(solution)/shard_map/all_gather | solution.py:180
  31.5 0.1 copy.13
  31.7 0.0 copy-start
  31.7 0.0 copy-start.1
  31.7 0.2 fusion.3
  31.9 0.4 copy.14
  32.3 3.0 %collective-permute-start.5 = (f32[40,32,2]{0,1,2:T(8,128)S(1)}, f32[40,32,2]{0,1,2:T(8,128)S(1)}, u32[]{:S(2)}, u32[]{:S(2)}) collective-permute-start(f32[40,32,2]{0,1,2:T(8,128)S(1)} %copy.14), channel_id=1, source_target_pairs={{0,24},{8,0},{16,8},{24,16},{1,25},{9,1},{17,9},{25,17},{2,26},{10... | collective-permute-start | bytes 30728 | tf_op jit(solution)/shard_map/ppermute | solution.py:18
  35.3 0.4 copy.15
  35.7 0.0 collective-permute-start.6
  35.8 0.8 rev.7
  36.6 2.9 %collective-permute-start.7 = (f32[40,2,128]{2,1,0:T(2,128)}, f32[40,2,128]{2,1,0:T(2,128)S(1)}, u32[]{:S(2)}, u32[]{:S(2)}) collective-permute-start(f32[40,2,128]{2,1,0:T(2,128)} %rev.7), channel_id=1, source_target_pairs={{0,24},{8,16},{16,8},{24,0},{1,25},{9,17},{17,9},{25,1},{2,26},{10... | collective-permute-start | bytes 122888 | tf_op jit(solution)/shard_map/ppermute | solution.py:18
  39.5 0.0 copy-done
  39.5 0.0 copy-done.1
  39.5 0.2 pad_maximum_fusion.2
  39.7 0.1 fusion.4
  39.9 1.0 slice.68
  40.8 1.0 slice.70
  41.8 0.4 rev.6
  42.2 0.8 slice.77
  43.0 0.8 slice.79
  43.8 0.1 pad.14.clone
  43.9 0.0 collective-permute-done.5
  43.9 2.4 %collective-permute-start.8 = (f32[40,2,2]{2,1,0:T(2,128)}, f32[40,2,2]{2,1,0:T(2,128)}, u32[]{:S(2)}, u32[]{:S(2)}) collective-permute-start(f32[40,2,2]{2,1,0:T(2,128)} %slice.77), channel_id=1, source_target_pairs={{0,16},{8,8},{16,0},{24,24},{1,17},{9,9},{17,1},{25,25},{2,18},{10... | collective-permute-start | bytes 1928 | tf_op jit(solution)/shard_map/ppermute | solution.py:18
  46.3 0.0 collective-permute-done.6
  46.3 2.1 %collective-permute-start.9 = (f32[40,2,2]{2,1,0:T(2,128)}, f32[40,2,2]{2,1,0:T(2,128)}, u32[]{:S(2)}, u32[]{:S(2)}) collective-permute-start(f32[40,2,2]{2,1,0:T(2,128)} %slice.79), channel_id=1, source_target_pairs={{0,0},{8,24},{16,16},{24,8},{1,1},{9,25},{17,17},{25,9},{2,2},{10,... | collective-permute-start | bytes 1928 | tf_op jit(solution)/shard_map/ppermute | solution.py:18
  48.4 0.1 pad.18.clone
  48.5 0.1 pad.20.clone
  48.5 1.4 copy.16
  49.9 1.4 copy.17
  51.3 0.0 collective-permute-done
  51.4 0.6 copy-done.4
  52.0 3.4 %collective-permute-start.3 = (f32[82,2,2]{2,1,0:T(2,128)}, f32[82,2,2]{2,1,0:T(2,128)}, u32[]{:S(2)}, u32[]{:S(2)}) collective-permute-start(f32[82,2,2]{2,1,0:T(2,128)} %slice.68), channel_id=1, source_target_pairs={{0,16},{8,8},{16,0},{24,24},{1,17},{9,9},{17,1},{25,25},{2,18},{10... | collective-permute-start | bytes 3944 | tf_op jit(solution)/shard_map/ppermute | solution.py:18
  55.4 1.9 %copy.10 = f32[82,32,2]{2,1,0:T(8,128)S(1)} copy(f32[82,32,2]{0,1,2:T(8,128)} %copy-done.4) | data formatting | bytes 41984 | tf_op jit(solution)/shard_map/ppermute | solution.py:18
  57.3 0.0 collective-permute-done.1
  57.3 2.1 %collective-permute-start.4 = (f32[82,2,2]{2,1,0:T(2,128)}, f32[82,2,2]{2,1,0:T(2,128)}, u32[]{:S(2)}, u32[]{:S(2)}) collective-permute-start(f32[82,2,2]{2,1,0:T(2,128)} %slice.70), channel_id=1, source_target_pairs={{0,0},{8,24},{16,16},{24,8},{1,1},{9,25},{17,17},{25,9},{2,2},{10,... | collective-permute-start | bytes 3944 | tf_op jit(solution)/shard_map/ppermute | solution.py:18
  59.5 2.9 %copy.11 = f32[82,32,2]{2,1,0:T(8,128)} copy(f32[82,32,2]{0,1,2:T(8,128)} %collective-permute-done.1) | data formatting | bytes 41984 | tf_op jit(solution)/shard_map/ppermute | solution.py:18
  62.4 0.0 collective-permute-done.8
  62.4 0.0 collective-permute-start.2
  62.4 0.0 collective-permute-done.9
  62.4 0.0 collective-permute-done.7
  62.4 1.7 maximum_maximum_fusion.1
  64.1 0.1 fusion.1
  64.2 0.0 collective-permute-done.3
  64.2 0.0 collective-permute-done.4
  64.2 3.5 %collective-permute-done.2 = f32[82,2,128]{2,1,0:T(2,128)S(1)} collective-permute-done((f32[82,2,128]{2,1,0:T(2,128)S(1)}, f32[82,2,128]{2,1,0:T(2,128)S(1)}, u32[]{:S(2)}, u32[]{:S(2)}) %collective-permute-start.2) | collective-permute-done | bytes 84000 | tf_op jit(solution)/shard_map/ppermute | solution.py:18
  67.7 2.6 %maximum_maximum_fusion = f32[82,40,256]{2,1,0:T(8,128)S(1)} fusion(f32[82,2,2]{2,1,0:T(2,128)} %collective-permute-done.4, f32[82,2,2]{2,1,0:T(2,128)} %collective-permute-done.3, f32[82,2,128]{2,1,0:T(2,128)S(1)} %collective-permute-done.2, f32[82,32,2]{2,1,0:T(8,128)S(1)} %copy-done.2, f32[82,32,2]{2,1,0:T(8,128)S(1)} %copy.10, ...), kind=kLoop, calls=%fused_computation | loop fusion | flops 9236480 | bytes 4912864 | tf_op jit(solution)/shard_map/concatenate | solution.py:38
  70.3 0.2 fusion
  70.6 0.0 copy-start.5
  70.6 33.7 %shard_map.76 = (f32[2,20,32,128]{3,2,1,0:T(8,128)}, f32[2,20,32,128]{3,2,1,0:T(8,128)}, f32[2,20,32,128]{3,2,1,0:T(8,128)}) custom-call(f32[2,20,40,256]{3,2,1,0:T(8,128)S(1)} %bitcast.19, f32[2,20,40,256]{3,2,1,0:T(8,128)S(1)} %bitcast.18, f32[20,40,256]{2,1,0:T(8,128)S(1)} %get-tuple-element.14.ke_ref, f32[20,40,256]{2,1,0:T(8,128)S(1)} %get-tuple-element.13.kn_ref, ...), custom_call_target="tpu_custom_call" | custom-call | tf_op jit(solution)/shard_map/pallas_call | solution.py:192
  104.3 0.0 all-reduce.3.cloned.1.call-update
  104.3 0.0 copy-done.5
  104.3 0.6 dynamic-slice
  105.6 55.2 %all-reduce.3.cloned.1.call-done = f32[2,20,32,128]{3,2,1,0:T(8,128)} async-done(((f32[2,20,32,128]{3,2,1,0:T(8,128)}), f32[2,20,32,128]{3,2,1,0:T(8,128)}) %all-reduce.3.cloned.1.call-update) | async-done | bytes 655376
  160.8 1.6 constant_dynamic-slice_fusion
  (10 shorter events, 0.1 us)
Async XLA Ops:
  7.2 153.6 %all-reduce.3.cloned.1.call-start = ((), (), s32[]{:S(2)}) async-start(), calls=%async_computation | async-start | bytes 1310720
  9.8 6.3 %copy-start.3 = (f32[2,20,4,128]{3,2,1,0:T(4,128)S(1)}, f32[2,20,4,128]{3,2,1,0:T(4,128)}, u32[]{:S(2)}) copy-start(f32[2,20,4,128]{3,2,1,0:T(4,128)} %param.6) | copy-start | bytes 245764
  10.7 40.7 %collective-permute-start = (f32[82,32,2]{0,1,2:T(8,128)S(1)}, f32[82,32,2]{0,1,2:T(8,128)S(1)}, u32[]{:S(2)}, u32[]{:S(2)}) collective-permute-start(f32[82,32,2]{0,1,2:T(8,128)S(1)} %copy.8), channel_id=1, source_target_pairs={{0,24},{8,0},{16,8},{24,16},{1,25},{9,1},{17,9},{25,17},{2,26},{10... | collective-permute-start | bytes 62984 | tf_op jit(solution)/shard_map/ppermute | solution.py:18
  16.1 41.2 %collective-permute-start.1 = (f32[82,32,2]{0,1,2:T(8,128)}, f32[82,32,2]{0,1,2:T(8,128)}, u32[]{:S(2)}, u32[]{:S(2)}) collective-permute-start(f32[82,32,2]{0,1,2:T(8,128)} %copy.9), channel_id=1, source_target_pairs={{0,8},{8,16},{16,24},{24,0},{1,9},{9,17},{17,25},{25,1},{2,10},{10... | collective-permute-start | bytes 62984 | tf_op jit(solution)/shard_map/ppermute | solution.py:18
  31.7 7.9 %copy-start = (f32[1,2,20,32,128]{4,3,2,1,0:T(8,128)S(1)}, f32[1,2,20,32,128]{4,3,2,1,0:T(8,128)}, u32[]{:S(2)}) copy-start(f32[1,2,20,32,128]{4,3,2,1,0:T(8,128)} %param.9) | copy-start | bytes 1966084
  31.7 7.9 %copy-start.1 = (f32[1,2,20,32,128]{4,3,2,1,0:T(8,128)S(1)}, f32[1,2,20,32,128]{4,3,2,1,0:T(8,128)}, u32[]{:S(2)}) copy-start(f32[1,2,20,32,128]{4,3,2,1,0:T(8,128)} %param.5) | copy-start | bytes 1966084
  32.3 11.6 %collective-permute-start.5 = (f32[40,32,2]{0,1,2:T(8,128)S(1)}, f32[40,32,2]{0,1,2:T(8,128)S(1)}, u32[]{:S(2)}, u32[]{:S(2)}) collective-permute-start(f32[40,32,2]{0,1,2:T(8,128)S(1)} %copy.14), channel_id=1, source_target_pairs={{0,24},{8,0},{16,8},{24,16},{1,25},{9,1},{17,9},{25,17},{2,26},{10... | collective-permute-start | bytes 30728 | tf_op jit(solution)/shard_map/ppermute | solution.py:18
  35.7 10.6 %collective-permute-start.6 = (f32[40,32,2]{0,1,2:T(8,128)S(1)}, f32[40,32,2]{0,1,2:T(8,128)S(1)}, u32[]{:S(2)}, u32[]{:S(2)}) collective-permute-start(f32[40,32,2]{0,1,2:T(8,128)S(1)} %copy.15), channel_id=1, source_target_pairs={{0,8},{8,16},{16,24},{24,0},{1,9},{9,17},{17,25},{25,1},{2,10},{10... | collective-permute-start | bytes 30728 | tf_op jit(solution)/shard_map/ppermute | solution.py:18
  36.6 25.8 %collective-permute-start.7 = (f32[40,2,128]{2,1,0:T(2,128)}, f32[40,2,128]{2,1,0:T(2,128)S(1)}, u32[]{:S(2)}, u32[]{:S(2)}) collective-permute-start(f32[40,2,128]{2,1,0:T(2,128)} %rev.7), channel_id=1, source_target_pairs={{0,24},{8,16},{16,8},{24,0},{1,25},{9,17},{17,9},{25,1},{2,26},{10... | collective-permute-start | bytes 122888 | tf_op jit(solution)/shard_map/ppermute | solution.py:18
  43.9 18.5 %collective-permute-start.8 = (f32[40,2,2]{2,1,0:T(2,128)}, f32[40,2,2]{2,1,0:T(2,128)}, u32[]{:S(2)}, u32[]{:S(2)}) collective-permute-start(f32[40,2,2]{2,1,0:T(2,128)} %slice.77), channel_id=1, source_target_pairs={{0,16},{8,8},{16,0},{24,24},{1,17},{9,9},{17,1},{25,25},{2,18},{10... | collective-permute-start | bytes 1928 | tf_op jit(solution)/shard_map/ppermute | solution.py:18
  46.3 16.1 %collective-permute-start.9 = (f32[40,2,2]{2,1,0:T(2,128)}, f32[40,2,2]{2,1,0:T(2,128)}, u32[]{:S(2)}, u32[]{:S(2)}) collective-permute-start(f32[40,2,2]{2,1,0:T(2,128)} %slice.79), channel_id=1, source_target_pairs={{0,0},{8,24},{16,16},{24,8},{1,1},{9,25},{17,17},{25,9},{2,2},{10,... | collective-permute-start | bytes 1928 | tf_op jit(solution)/shard_map/ppermute | solution.py:18
  51.3 0.6 copy-start.4
  52.0 12.3 %collective-permute-start.3 = (f32[82,2,2]{2,1,0:T(2,128)}, f32[82,2,2]{2,1,0:T(2,128)}, u32[]{:S(2)}, u32[]{:S(2)}) collective-permute-start(f32[82,2,2]{2,1,0:T(2,128)} %slice.68), channel_id=1, source_target_pairs={{0,16},{8,8},{16,0},{24,24},{1,17},{9,9},{17,1},{25,25},{2,18},{10... | collective-permute-start | bytes 3944 | tf_op jit(solution)/shard_map/ppermute | solution.py:18
  57.3 6.9 %collective-permute-start.4 = (f32[82,2,2]{2,1,0:T(2,128)}, f32[82,2,2]{2,1,0:T(2,128)}, u32[]{:S(2)}, u32[]{:S(2)}) collective-permute-start(f32[82,2,2]{2,1,0:T(2,128)} %slice.70), channel_id=1, source_target_pairs={{0,0},{8,24},{16,16},{24,8},{1,1},{9,25},{17,17},{25,9},{2,2},{10,... | collective-permute-start | bytes 3944 | tf_op jit(solution)/shard_map/ppermute | solution.py:18
  62.4 5.4 %collective-permute-start.2 = (f32[82,2,128]{2,1,0:T(2,128)S(1)}, f32[82,2,128]{2,1,0:T(2,128)S(1)}, u32[]{:S(2)}, u32[]{:S(2)}) collective-permute-start(f32[82,2,128]{2,1,0:T(2,128)S(1)} %rev.6), channel_id=1, source_target_pairs={{0,24},{8,16},{16,8},{24,0},{1,25},{9,17},{17,9},{25,1},{2,26},{10... | collective-permute-start | bytes 251912 | tf_op jit(solution)/shard_map/ppermute | solution.py:18
  64.1 3.7 %copy-start.2 = (f32[82,32,2]{2,1,0:T(8,128)S(1)}, f32[82,32,2]{2,1,0:T(8,128)}, u32[]{:S(2)}) copy-start(f32[82,32,2]{2,1,0:T(8,128)} %copy.11) | copy-start | bytes 62980
  70.6 33.8 %copy-start.5 = (u32[32]{0:T(128)S(1)}, u32[32]{0:T(128)}, u32[]{:S(2)}) copy-start(u32[32]{0:T(128)} %constant.12) | copy-start | bytes 388
Sparse Core Ops, SparseCore 0:
  104.4 56.2 all-reduce.2

commit v2 on v1

--- a/solution.py
+++ b/solution.py
@@ -42,18 +42,33 @@
     return pltpu.roll(x, shift % x.shape[axis], axis)
 
 
+class Planes:
+    def __init__(self, ref, start, levels):
+        self.ref = ref
+        self.start = start
+        self.levels = levels
+
+    def __getitem__(self, index):
+        c, k = index
+        return self.ref[self.start + c * self.levels + k]
+
+
 def diffusion_kernel(
-    ue_ref, ve_ref, ke_ref, kn_ref, lev_ref, shelf_ref,
+    x_ref,
     fin_ref, adj_ref, grad_ref,
     wet_ref, ce_ref, cn_ref, cz_ref, src_ref, gem_ref, gnm_ref, u1_ref, a_ref, b_ref,
 ):
     levels, rows, lanes = wet_ref.shape
-    ny, width = fin_ref.shape[2:]
+    chans, _, ny, width = fin_ref.shape
     row = lax.broadcasted_iota(jnp.int32, (rows, lanes), 0)
     lane = lax.broadcasted_iota(jnp.int32, (rows, lanes), 1)
     owned = (row < ny) & (lane < width)
-    lev = lev_ref[...]
-    shelf = shelf_ref[...]
+    planes = chans * levels
+    ue_ref = Planes(x_ref, 0, levels)
+    ve_ref = Planes(x_ref, planes, levels)
+    ke_ref = Planes(x_ref, 2 * planes, levels)
+    lev = x_ref[2 * planes + 2 * levels]
+    shelf = x_ref[2 * planes + 2 * levels + 1]
 
     def wet_of(k):
         return (lev > k.astype(jnp.float32)).astype(jnp.float32)
@@ -65,11 +80,11 @@
         w_next = jnp.where(k + 1 < levels, wet_of(k + 1), 0.0)
         w_east = roll(w, -1, 1)
         w_north = roll(w, -1, 0)
-        ke = ke_ref[k]
+        ke = ke_ref[0, k]
         ke_sel = jnp.where(row >= ny, roll(ke, -1, 1), ke)
         east_mask = w * w_east
         ce_ref[k] = ke_sel * east_mask
-        kn = kn_ref[k]
+        kn = ke_ref[1, k]
         kn_up = roll(kn, -1, 0)
         kn_sel = jnp.where(
             row < ny - 1, kn, jnp.where(row == ny - 1, 0.5 * (kn + kn_up), jnp.where(row == ny, kn_up, 0.0))
@@ -97,8 +112,6 @@
         change = change + (cz_ref[k + 1] * (above - x) - cz_ref[k] * (x - below))
         return x, change
 
-    planes = 2 * levels
-
     def forward_first(ck, carry):
         c = ck // levels
         k = ck % levels
@@ -168,24 +181,17 @@
     _, chans, levels, ny, width = tracers.shape
     lanes = width + 128
     rows = -(-(ny + 2) // 8) * 8
-    first = jnp.concatenate(
+    full_kappa = lax.all_gather(diffusivity, "scen", axis=2, tiled=True)
+    fields = jnp.concatenate(
         [
             tracers[0].reshape(chans * levels, ny, width),
             cotangent[0].reshape(chans * levels, ny, width),
+            full_kappa.reshape(2 * levels, ny, width),
             level_count.astype(jnp.float32)[None],
             shelf_mask.astype(jnp.float32)[None],
         ]
     )
-    first_ext = extended(first, lanes, rows)
-    full_kappa = lax.all_gather(diffusivity, "scen", axis=2, tiled=True)
-    kappa_ext = extended(full_kappa.reshape(2 * levels, ny, width), lanes, rows)
-    planes = chans * levels
-    ue = first_ext[:planes].reshape(chans, levels, rows, lanes)
-    ve = first_ext[planes:2 * planes].reshape(chans, levels, rows, lanes)
-    lev = first_ext[2 * planes]
-    shelf = first_ext[2 * planes + 1]
-    ke = kappa_ext[:levels]
-    kn = kappa_ext[levels:]
+    ext = extended(fields, lanes, rows)
     field = jax.ShapeDtypeStruct((chans, levels, ny, width), jnp.float32)
     plane = pltpu.VMEM((levels, rows, lanes), jnp.float32)
     planes_c = pltpu.VMEM((chans, levels, rows, lanes), jnp.float32)
@@ -206,8 +212,11 @@
         ],
         compiler_params=pltpu.CompilerParams(vmem_limit_bytes=48 * 1024 * 1024),
         interpret=INTERPRET,
-    )(ue, ve, ke, kn, lev, shelf)
-    kappa_grad = lax.psum_scatter(grad, "scen", scatter_dimension=2, tiled=True)
+    )(ext)
+    parts = lax.axis_size("scen")
+    split = grad.reshape(2, levels, parts, ny // parts, width)
+    gathered = lax.all_to_all(split, "scen", 2, 2, tiled=True)
+    kappa_grad = gathered.sum(axis=2)
     return (final[None], adjoint[None], kappa_grad)
 
 

time: 170 us -> 105 us (0.62)
  waiting for transfers between devices: 58.8 us -> 0.01 us
  blocking collectives: 15.4 us -> 39.6 us
  between operations: 14.9 us -> 0.78 us
  starting transfers between devices: 19.9 us -> 8.55 us
  local copies, waits for them, and re-layouts: 20 us -> 17.4 us
  other arithmetic: 6.6 us -> 4.07 us
    unnamed x2 -> x0, waiting for transfers between devices: 55.2 us -> none
    all_to_all x0 -> x1, blocking collectives: none -> 22.8 us  [on_device(): gathered = lax.all_to_all(split, 'scen', 2, 2, tiled=True)]
    ppermute x10 -> x5, starting transfers between devices: 19.8 us -> 8.55 us  [shifted(): return lax.ppermute(x, 'space', perm)]
    ppermute x10 -> x5, waiting for transfers between devices: 3.54 us -> 0.01 us  [shifted(): return lax.ppermute(x, 'space', perm)]
    slice x4 -> x2, local copies, waits for them, and re-layouts: 2 us -> 5.26 us  [extended(): east = shifted(fields[..., :HALO], [(q, (q - 1) % n) for q in range(n)])]
    ppermute x4 -> x2, local copies, waits for them, and re-layouts: 7.65 us -> 5.6 us  [shifted(): return lax.ppermute(x, 'space', perm)]
    concatenate x2 -> x1, other arithmetic: 4.28 us -> 3.32 us  [extended(): return jnp.concatenate([top, folded, pad], axis=1)]
  transfers between devices with their start and end apart: 11 -> 5, of which waited for: 2 -> 0; matrix products, arithmetic and copies ran while one was open for 11% -> 14% of each run, Pallas kernels for 0% -> 0%
where the time goes in v2:
time: 105 us; the launch traced here: 104 us
  blocking collectives  39.6 us (38%)
  Pallas kernels  33.7 us (32%)
  local copies, waits for them, and re-layouts  17.4 us (17%)
  starting transfers between devices  8.55 us (8%)
  other arithmetic  4.07 us (4%)
    pallas_call x1, Pallas kernels, on_device(): pl.pallas_call(diffusion_kernel, out_shape=(field, field, jax.ShapeDtypeS...  33.7 us
    all_to_all x1, blocking collectives, on_device(): gathered = lax.all_to_all(split, 'scen', 2, 2, tiled=True)  22.8 us
    all_gather x1, blocking collectives, on_device(): full_kappa = lax.all_gather(diffusivity, 'scen', axis=2, tiled=True)  16.8 us
    ppermute x5, starting transfers between devices, shifted(): return lax.ppermute(x, 'space', perm)  8.55 us
    ppermute x2, local copies, waits for them, and re-layouts, shifted(): return lax.ppermute(x, 'space', perm)  5.6 us
    slice x2, local copies, waits for them, and re-layouts, extended(): east = shifted(fields[..., :HALO], [(q, (q - 1) % n) for q in range(n)])  5.26 us
    concatenate x1, other arithmetic, extended(): return jnp.concatenate([top, folded, pad], axis=1)  3.32 us
    slice x1, local copies, waits for them, and re-layouts, extended(): fields[..., width - HALO:]  2.64 us
  transfers between devices with their start and end apart: 5, of which 0 were waited for; matrix products, arithmetic and copies ran while one was open for 14% of the time, Pallas kernels for 0%

profile of v2, /device:TPU:0, one launch (start us, length us, event | category | flops | bytes accessed | tf_op | source)
XLA Modules:
  0.0 104.1 jit_solution(14555648503831214727)
XLA Ops:
  0.6 0.0 copy-start
  0.6 0.0 copy-start.1
  0.7 1.0 copy.8
  1.7 16.8 %all_gather.3 = f32[2,20,32,128]{3,0,1,2:T(2,128)S(1)} all-gather(f32[2,20,4,128]{3,0,1,2:T(2,128)S(1)} %copy.8), channel_id=1, replica_groups=mesh['space'=4,'scen'=8] {'scen'}, dimensions={2}, use_global_device_ids=true | all-gather | bytes 737280 | tf_op jit(solution)/shard_map/all_gather | solution.py:184
  18.5 0.1 copy.9
  18.6 0.0 copy-start.2
  18.7 0.0 copy-start.3
  18.7 0.0 copy-done
  18.7 0.0 copy-done.1
  18.8 0.5 copy-done.2
  19.4 0.0 copy-done.3
  19.4 0.1 slice.32
  19.5 0.5 rev.3
  19.9 2.5 %collective-permute-start.2 = (f32[122,2,128]{2,1,0:T(2,128)S(1)}, f32[122,2,128]{2,1,0:T(2,128)S(1)}, u32[]{:S(2)}, u32[]{:S(2)}) collective-permute-start(f32[122,2,128]{2,1,0:T(2,128)S(1)} %rev.3), channel_id=1, source_target_pairs={{0,24},{8,16},{16,8},{24,0},{1,25},{9,17},{17,9},{25,1},{2,26},{10... | collective-permute-start | bytes 374792 | tf_op jit(solution)/shard_map/ppermute | solution.py:18
  22.5 2.6 %fusion = (f32[122,32,2]{2,1,0:T(8,128)}, f32[122,32,2]{2,1,0:T(8,128)}) fusion(f32[122,32,128]{2,1,0:T(8,128)S(1)} %bitcast_dynamic-update-slice_fusion), kind=kLoop, calls=%fused_computation.6 | loop fusion | bytes 124928 | tf_op jit(solution)/shard_map/slice | solution.py:25
  25.1 2.6 %copy.11 = f32[122,32,2]{0,1,2:T(8,128)S(1)} copy(f32[122,32,2]{2,1,0:T(8,128)} %get-tuple-element.10) | data formatting | bytes 62464 | tf_op jit(solution)/shard_map/slice | solution.py:24
  27.7 0.6 collective-permute-start.1
  28.3 2.6 %copy.10 = f32[122,32,2]{0,1,2:T(8,128)S(1)} copy(f32[122,32,2]{2,1,0:T(8,128)} %get-tuple-element.9) | data formatting | bytes 62464 | tf_op jit(solution)/shard_map/slice | solution.py:25
  30.9 2.4 %collective-permute-start = (f32[122,32,2]{0,1,2:T(8,128)S(1)}, f32[122,32,2]{0,1,2:T(8,128)S(1)}, u32[]{:S(2)}, u32[]{:S(2)}) collective-permute-start(f32[122,32,2]{0,1,2:T(8,128)S(1)} %copy.10), channel_id=1, source_target_pairs={{0,24},{8,0},{16,8},{24,16},{1,25},{9,1},{17,9},{25,17},{2,26},{10... | collective-permute-start | bytes 93704 | tf_op jit(solution)/shard_map/ppermute | solution.py:18
  33.3 0.2 fusion.1
  33.5 0.5 slice.29
  34.0 0.7 collective-permute-start.4
  34.7 0.5 slice.27
  35.2 2.4 %collective-permute-start.3 = (f32[122,2,2]{2,1,0:T(2,128)S(1)}, f32[122,2,2]{2,1,0:T(2,128)S(1)}, u32[]{:S(2)}, u32[]{:S(2)}) collective-permute-start(f32[122,2,2]{2,1,0:T(2,128)S(1)} %slice.27), channel_id=1, source_target_pairs={{0,16},{8,8},{16,0},{24,24},{1,17},{9,9},{17,1},{25,25},{2,18},{10... | collective-permute-start | bytes 5864 | tf_op jit(solution)/shard_map/ppermute | solution.py:18
  37.6 0.1 pad.8.clone
  37.7 0.1 pad.2.clone
  37.8 0.1 pad.6.clone
  37.9 0.0 collective-permute-done
  37.9 2.8 %copy.12 = f32[122,32,2]{2,1,0:T(8,128)} copy(f32[122,32,2]{0,1,2:T(8,128)S(1)} %collective-permute-done) | data formatting | bytes 62464 | tf_op jit(solution)/shard_map/ppermute | solution.py:18
  40.6 0.0 collective-permute-done.1
  40.6 2.8 %copy.13 = f32[122,32,2]{2,1,0:T(8,128)} copy(f32[122,32,2]{0,1,2:T(8,128)S(1)} %collective-permute-done.1) | data formatting | bytes 62464 | tf_op jit(solution)/shard_map/ppermute | solution.py:18
  43.5 0.0 collective-permute-done.4
  43.5 0.0 collective-permute-done.3
  43.5 0.0 collective-permute-done.2
  43.5 3.3 %maximum_maximum_fusion.x_ref = f32[122,40,256]{2,1,0:T(8,128)S(1)} fusion(f32[122,2,2]{2,1,0:T(2,128)S(1)} %collective-permute-done.4, f32[122,2,2]{2,1,0:T(2,128)S(1)} %collective-permute-done.3, f32[122,2,128]{2,1,0:T(2,128)S(1)} %collective-permute-done.2, f32[122,32,2]{2,1,0:T(8,128)} %copy.13, f32[122,32,2]{2,1,0:T(8,128)} %copy.12, ...), kind=kLoop, calls=%fused_computation | loop fusion | flops 9994240 | bytes 7269344 | tf_op jit(solution)/shard_map/concatenate | solution.py:38
  46.8 33.7 %shard_map.76 = (f32[2,20,32,128]{3,2,1,0:T(8,128)}, f32[2,20,32,128]{3,2,1,0:T(8,128)}, f32[2,20,32,128]{3,2,1,0:T(8,128)S(1)}) custom-call(f32[122,40,256]{2,1,0:T(8,128)S(1)} %maximum_maximum_fusion.x_ref), custom_call_target="tpu_custom_call" | custom-call | tf_op jit(solution)/shard_map/pallas_call | solution.py:198
  80.5 0.1 copy.14
  80.6 22.8 %all_to_all.5 = f32[2,20,8,4,128]{4,3,1,0,2:T(4,128)S(1)} all-to-all(f32[2,20,8,4,128]{4,3,1,0,2:T(4,128)S(1)} %copy.14), channel_id=1, replica_groups=mesh['space'=4,'scen'=8] {'scen'}, dimensions={2} | all-to-all | bytes 1310720 | tf_op jit(solution)/shard_map/all_to_all | solution.py:218
  103.4 0.7 reduce_sum.9
  (8 shorter events, 0.1 us)
Async XLA Ops:
  0.6 18.0 %copy-start = (f32[1,2,20,32,128]{4,3,2,1,0:T(8,128)S(1)}, f32[1,2,20,32,128]{4,3,2,1,0:T(8,128)}, u32[]{:S(2)}) copy-start(f32[1,2,20,32,128]{4,3,2,1,0:T(8,128)} %param.5) | copy-start | bytes 1966084
  0.6 18.1 %copy-start.1 = (f32[1,2,20,32,128]{4,3,2,1,0:T(8,128)S(1)}, f32[1,2,20,32,128]{4,3,2,1,0:T(8,128)}, u32[]{:S(2)}) copy-start(f32[1,2,20,32,128]{4,3,2,1,0:T(8,128)} %param.9) | copy-start | bytes 1966084
  18.6 0.7 copy-start.2
  18.7 0.7 copy-start.3
  19.9 23.5 %collective-permute-start.2 = (f32[122,2,128]{2,1,0:T(2,128)S(1)}, f32[122,2,128]{2,1,0:T(2,128)S(1)}, u32[]{:S(2)}, u32[]{:S(2)}) collective-permute-start(f32[122,2,128]{2,1,0:T(2,128)S(1)} %rev.3), channel_id=1, source_target_pairs={{0,24},{8,16},{16,8},{24,0},{1,25},{9,17},{17,9},{25,1},{2,26},{10... | collective-permute-start | bytes 374792 | tf_op jit(solution)/shard_map/ppermute | solution.py:18
  27.7 12.9 %collective-permute-start.1 = (f32[122,32,2]{0,1,2:T(8,128)S(1)}, f32[122,32,2]{0,1,2:T(8,128)S(1)}, u32[]{:S(2)}, u32[]{:S(2)}) collective-permute-start(f32[122,32,2]{0,1,2:T(8,128)S(1)} %copy.11), channel_id=1, source_target_pairs={{0,8},{8,16},{16,24},{24,0},{1,9},{9,17},{17,25},{25,1},{2,10},{10... | collective-permute-start | bytes 93704 | tf_op jit(solution)/shard_map/ppermute | solution.py:18
  30.9 6.9 %collective-permute-start = (f32[122,32,2]{0,1,2:T(8,128)S(1)}, f32[122,32,2]{0,1,2:T(8,128)S(1)}, u32[]{:S(2)}, u32[]{:S(2)}) collective-permute-start(f32[122,32,2]{0,1,2:T(8,128)S(1)} %copy.10), channel_id=1, source_target_pairs={{0,24},{8,0},{16,8},{24,16},{1,25},{9,1},{17,9},{25,17},{2,26},{10... | collective-permute-start | bytes 93704 | tf_op jit(solution)/shard_map/ppermute | solution.py:18
  34.0 9.4 %collective-permute-start.4 = (f32[122,2,2]{2,1,0:T(2,128)S(1)}, f32[122,2,2]{2,1,0:T(2,128)S(1)}, u32[]{:S(2)}, u32[]{:S(2)}) collective-permute-start(f32[122,2,2]{2,1,0:T(2,128)S(1)} %slice.29), channel_id=1, source_target_pairs={{0,0},{8,24},{16,16},{24,8},{1,1},{9,25},{17,17},{25,9},{2,2},{10,... | collective-permute-start | bytes 5864 | tf_op jit(solution)/shard_map/ppermute | solution.py:18
  35.2 8.3 %collective-permute-start.3 = (f32[122,2,2]{2,1,0:T(2,128)S(1)}, f32[122,2,2]{2,1,0:T(2,128)S(1)}, u32[]{:S(2)}, u32[]{:S(2)}) collective-permute-start(f32[122,2,2]{2,1,0:T(2,128)S(1)} %slice.27), channel_id=1, source_target_pairs={{0,16},{8,8},{16,0},{24,24},{1,17},{9,9},{17,1},{25,25},{2,18},{10... | collective-permute-start | bytes 5864 | tf_op jit(solution)/shard_map/ppermute | solution.py:18

commit v3 on v2

--- a/solution.py
+++ b/solution.py
@@ -18,22 +18,40 @@
     return lax.ppermute(x, "space", perm)
 
 
+def picker(size, positions):
+    where = lax.broadcasted_iota(jnp.int32, (size, len(positions)), 0)
+    slot = lax.broadcasted_iota(jnp.int32, (size, len(positions)), 1)
+    hit = jnp.zeros((size, len(positions)), jnp.bool_)
+    for p, at in enumerate(positions):
+        hit = hit | ((slot == p) & (where == at))
+    return hit.astype(jnp.float32)
+
+
+def contract(a, b, dims):
+    return lax.dot_general(
+        a, b, (dims, ((), ())), precision=lax.Precision.HIGHEST, preferred_element_type=jnp.float32
+    )
+
+
 def extended(fields, lanes, rows):
     n = lax.axis_size("space")
     count, ny, width = fields.shape
-    west = shifted(fields[..., width - HALO:], [(q, (q + 1) % n) for q in range(n)])
-    east = shifted(fields[..., :HALO], [(q, (q - 1) % n) for q in range(n)])
+    spare = lanes - width
+    flat = fields.reshape(count * ny, width)
+    edges = contract(picker(width, [width - 2, width - 1, 0, 1]), flat, ((0,), (1,)))
+    west = shifted(edges[0:2], [(q, (q + 1) % n) for q in range(n)])
+    east = shifted(edges[2:4], [(q, (q - 1) % n) for q in range(n)])
     mirrored = fields[:, ny - 1:ny - 3:-1, ::-1]
     ghost = shifted(mirrored, [(q, n - 1 - q) for q in range(n)])
-    ghost_east = shifted(mirrored[..., :HALO], [(q, (n - 2 - q) % n) for q in range(n)])
-    ghost_west = shifted(mirrored[..., width - HALO:], [(q, (n - q) % n) for q in range(n)])
-    gap = lanes - width - 2 * HALO
-    top = jnp.concatenate(
-        [fields, east, jnp.zeros((count, ny, gap), fields.dtype), west], axis=-1
-    )
-    folded = jnp.concatenate(
-        [ghost, ghost_east, jnp.zeros((count, 2, gap), fields.dtype), ghost_west], axis=-1
-    )
+    top_edges = edges.reshape(4, count, ny)[:, :, ny - 1:ny - 3:-1]
+    ghost_east = shifted(top_edges[1::-1], [(q, (n - 2 - q) % n) for q in range(n)])
+    ghost_west = shifted(top_edges[3:1:-1], [(q, (n - q) % n) for q in range(n)])
+    place = picker(spare, [0, 1, spare - 2, spare - 1]).T
+    side = contract(jnp.concatenate([east, west]), place, ((0,), (0,))).reshape(count, ny, spare)
+    ghost_halo = jnp.concatenate([ghost_east, ghost_west]).reshape(4, count * 2)
+    ghost_side = contract(ghost_halo, place, ((0,), (0,))).reshape(count, 2, spare)
+    top = jnp.concatenate([fields, side], axis=-1)
+    folded = jnp.concatenate([ghost, ghost_side], axis=-1)
     pad = jnp.zeros((count, rows - ny - 2, lanes), fields.dtype)
     return jnp.concatenate([top, folded, pad], axis=1)
 

time: 105 us -> 95.5 us (0.910)
  local copies, waits for them, and re-layouts: 17.4 us -> 3.71 us
  waiting for transfers between devices: 0.01 us -> 4.28 us
  matrix products: 0 us -> 2.96 us
  other arithmetic: 4.07 us -> 1.36 us
    slice x6 -> x2, local copies, waits for them, and re-layouts: 9.08 us -> 0.16 us  [the longest x1 0.12 us: extended(): top_edges[1::-1]]
    ppermute x2 -> x0, local copies, waits for them, and re-layouts: 5.6 us -> none  [shifted(): return lax.ppermute(x, 'space', perm)]
    ppermute x5, waiting for transfers between devices: 0.01 us -> 4.28 us  [shifted(): return lax.ppermute(x, 'space', perm)]
    dot_general x0 -> x3, matrix products: none -> 2.96 us  [contract(): lax.dot_general(a, b, (dims, ((), ())), precision=lax.Precision.HIGHEST,...]
    concatenate x1, other arithmetic: 3.32 us -> 0.49 us  [extended(): return jnp.concatenate([top, folded, pad], axis=1)]
  transfers between devices with their start and end apart: 5 -> 5, of which waited for: 0 -> 1; matrix products, arithmetic and copies ran while one was open for 14% -> 4% of each run, Pallas kernels for 0% -> 0%
where the time goes in v3:
time: 95.5 us; the launch traced here: 95.1 us
  blocking collectives  39.6 us (41%)
  Pallas kernels  33.7 us (35%)
  starting transfers between devices  8.58 us (9%)
  waiting for transfers between devices  4.28 us (4%)
  local copies, waits for them, and re-layouts  3.71 us (4%)
  matrix products  2.96 us (3%)
  other arithmetic  1.36 us (1%)
    pallas_call x1, Pallas kernels, on_device(): pl.pallas_call(diffusion_kernel, out_shape=(field, field, jax.ShapeDtypeS...  33.7 us
    all_to_all x1, blocking collectives, on_device(): gathered = lax.all_to_all(split, 'scen', 2, 2, tiled=True)  22.8 us
    all_gather x1, blocking collectives, on_device(): full_kappa = lax.all_gather(diffusivity, 'scen', axis=2, tiled=True)  16.8 us
    ppermute x5, starting transfers between devices, shifted(): return lax.ppermute(x, 'space', perm)  8.58 us
    ppermute x5, waiting for transfers between devices, shifted(): return lax.ppermute(x, 'space', perm)  4.28 us
    dot_general x3, matrix products, contract(): lax.dot_general(a, b, (dims, ((), ())), precision=lax.Precision.HIGHEST,...  2.96 us
  transfers between devices with their start and end apart: 5, of which 1 were waited for; matrix products, arithmetic and copies ran while one was open for 4% of the time, Pallas kernels for 0%

profile of v3, /device:TPU:0, one launch (start us, length us, event | category | flops | bytes accessed | tf_op | source)
XLA Modules:
  0.0 95.1 jit_solution(11768086890816660344)
XLA Ops:
  0.6 0.0 copy-start
  0.6 0.0 copy-start.1
  0.7 1.0 %copy.20 = f32[2,20,4,128]{3,0,1,2:T(2,128)S(1)} copy(f32[2,20,4,128]{3,2,1,0:T(4,128)} %param.6) | data formatting | bytes 163840 | tf_op args[1]
  1.7 16.8 %all_gather.3 = f32[2,20,32,128]{3,0,1,2:T(2,128)S(1)} all-gather(f32[2,20,4,128]{3,0,1,2:T(2,128)S(1)} %copy.20), channel_id=1, replica_groups=mesh['space'=4,'scen'=8] {'scen'}, dimensions={2}, use_global_device_ids=true | all-gather | bytes 737280 | tf_op jit(solution)/shard_map/all_gather | solution.py:202
  18.6 0.1 copy.21
  18.7 0.0 copy-start.2
  18.7 0.0 copy-start.3
  18.7 0.0 copy-done
  18.8 0.0 copy-done.1
  18.9 0.5 copy-done.2
  19.4 0.0 copy-done.3
  19.4 1.0 %fusion.7 = f32[4,3904]{1,0:T(4,128)S(1)} fusion(f32[3904,128]{1,0:T(8,128)S(1)} %bitcast.19, pred[128]{0:T(512)(128)(4,1)S(1)} %get-tuple-element.13, pred[128]{0:T(512)(128)(4,1)S(1)} %get-tuple-element.14, pred[128]{0:T(512)(128)(4,1)S(1)} %get-tuple-element.15, pred[128]{0:T(512)(128)(4,1)S(1)} %get-tuple-element.16, ...), kind=kOutput, calls=%fused_computation.15 | convolution fusion | flops 23989760 | bytes 2061840 | tf_op jit(solution)/shard_map/dot_general | solution.py:31
  20.5 2.5 %collective-permute-start = (f32[2,3904]{1,0:T(2,128)S(1)}, f32[2,3904]{1,0:T(2,128)S(1)}, u32[]{:S(2)}, u32[]{:S(2)}) collective-permute-start(f32[2,3904]{1,0:T(2,128)S(1)} %get-tuple-element.11), channel_id=1, source_target_pairs={{0,24},{8,0},{16,8},{24,16},{1,25},{9,1},{17,9},{25,17},{2,26},{10... | collective-permute-start | bytes 93704 | tf_op jit(solution)/shard_map/ppermute | solution.py:18
  23.0 0.0 collective-permute-start.1
  23.0 0.1 slice.27
  23.1 0.5 rev.10
  23.6 3.0 %collective-permute-start.2 = (f32[122,2,128]{2,1,0:T(2,128)S(1)}, f32[122,2,128]{2,1,0:T(2,128)S(1)}, u32[]{:S(2)}, u32[]{:S(2)}) collective-permute-start(f32[122,2,128]{2,1,0:T(2,128)S(1)} %rev.10), channel_id=1, source_target_pairs={{0,24},{8,16},{16,8},{24,0},{1,25},{9,17},{17,9},{25,1},{2,26},{10... | collective-permute-start | bytes 374792 | tf_op jit(solution)/shard_map/ppermute | solution.py:18
  26.5 0.1 reshape.29
  26.7 0.1 fusion.24
  26.8 0.2 rev.12
  27.0 0.7 collective-permute-start.4
  27.7 0.2 rev.11
  27.9 2.4 %collective-permute-start.3 = (f32[2,122,2]{2,1,0:T(8,128)S(1)}, f32[2,122,2]{2,1,0:T(8,128)S(1)}, u32[]{:S(2)}, u32[]{:S(2)}) collective-permute-start(f32[2,122,2]{2,1,0:T(8,128)S(1)} %rev.11), channel_id=1, source_target_pairs={{0,16},{8,8},{16,0},{24,24},{1,17},{9,9},{17,1},{25,25},{2,18},{10... | collective-permute-start | bytes 5864 | tf_op jit(solution)/shard_map/ppermute | solution.py:18
  30.3 0.1 and_or_fusion
  30.4 0.1 pad.4.clone
  30.4 0.0 collective-permute-done.4
  30.4 4.3 %collective-permute-done.3 = f32[2,122,2]{2,1,0:T(8,128)S(1)} collective-permute-done((f32[2,122,2]{2,1,0:T(8,128)S(1)}, f32[2,122,2]{2,1,0:T(8,128)S(1)}, u32[]{:S(2)}, u32[]{:S(2)}) %collective-permute-start.3) | collective-permute-done | bytes 1984 | tf_op jit(solution)/shard_map/ppermute | solution.py:18
  34.7 0.2 reshape.33
  34.9 0.1 copy.26
  35.1 0.1 dot_general.16
  35.1 0.2 fusion
  35.3 0.1 copy.24
  35.4 0.0 collective-permute-done
  35.5 0.0 collective-permute-done.1
  35.5 1.7 %fusion.2 = f32[3904,128]{1,0:T(8,128)S(1)} fusion(pred[128,4]{0,1:T(4,128)(4,1)S(1)} %and_or_fusion, f32[2,3904]{1,0:T(2,128)S(1)} %collective-permute-done.1, f32[2,3904]{1,0:T(2,128)S(1)} %collective-permute-done), kind=kOutput, calls=%fused_computation.4 | convolution fusion | flops 24001792 | bytes 2061824 | tf_op jit(solution)/shard_map/dot_general | solution.py:31
  37.2 0.0 collective-permute-done.2
  37.2 0.5 maximum_maximum_fusion.x_ref
  37.7 33.7 %shard_map.76 = (f32[2,20,32,128]{3,2,1,0:T(8,128)}, f32[2,20,32,128]{3,2,1,0:T(8,128)}, f32[2,20,32,128]{3,2,1,0:T(8,128)S(1)}) custom-call(f32[122,40,256]{2,1,0:T(8,128)S(1)} %maximum_maximum_fusion.x_ref), custom_call_target="tpu_custom_call" | custom-call | tf_op jit(solution)/shard_map/pallas_call | solution.py:216
  71.4 0.1 copy.25
  71.5 22.8 %all_to_all.5 = f32[2,20,8,4,128]{4,3,1,0,2:T(4,128)S(1)} all-to-all(f32[2,20,8,4,128]{4,3,1,0,2:T(4,128)S(1)} %copy.25), channel_id=1, replica_groups=mesh['space'=4,'scen'=8] {'scen'}, dimensions={2} | all-to-all | bytes 1310720 | tf_op jit(solution)/shard_map/all_to_all | solution.py:236
  94.3 0.7 reduce_sum.9
  (12 shorter events, 0.2 us)
Async XLA Ops:
  0.6 18.1 %copy-start = (f32[1,2,20,32,128]{4,3,2,1,0:T(8,128)S(1)}, f32[1,2,20,32,128]{4,3,2,1,0:T(8,128)}, u32[]{:S(2)}) copy-start(f32[1,2,20,32,128]{4,3,2,1,0:T(8,128)} %param.5) | copy-start | bytes 1966084
  0.6 18.1 %copy-start.1 = (f32[1,2,20,32,128]{4,3,2,1,0:T(8,128)S(1)}, f32[1,2,20,32,128]{4,3,2,1,0:T(8,128)}, u32[]{:S(2)}) copy-start(f32[1,2,20,32,128]{4,3,2,1,0:T(8,128)} %param.9) | copy-start | bytes 1966084
  18.7 0.7 copy-start.2
  18.7 0.7 copy-start.3
  20.5 15.0 %collective-permute-start = (f32[2,3904]{1,0:T(2,128)S(1)}, f32[2,3904]{1,0:T(2,128)S(1)}, u32[]{:S(2)}, u32[]{:S(2)}) collective-permute-start(f32[2,3904]{1,0:T(2,128)S(1)} %get-tuple-element.11), channel_id=1, source_target_pairs={{0,24},{8,0},{16,8},{24,16},{1,25},{9,1},{17,9},{25,17},{2,26},{10... | collective-permute-start | bytes 93704 | tf_op jit(solution)/shard_map/ppermute | solution.py:18
  23.0 12.5 %collective-permute-start.1 = (f32[2,3904]{1,0:T(2,128)S(1)}, f32[2,3904]{1,0:T(2,128)S(1)}, u32[]{:S(2)}, u32[]{:S(2)}) collective-permute-start(f32[2,3904]{1,0:T(2,128)S(1)} %get-tuple-element.12), channel_id=1, source_target_pairs={{0,8},{8,16},{16,24},{24,0},{1,9},{9,17},{17,25},{25,1},{2,10},{10... | collective-permute-start | bytes 93704 | tf_op jit(solution)/shard_map/ppermute | solution.py:18
  23.6 13.7 %collective-permute-start.2 = (f32[122,2,128]{2,1,0:T(2,128)S(1)}, f32[122,2,128]{2,1,0:T(2,128)S(1)}, u32[]{:S(2)}, u32[]{:S(2)}) collective-permute-start(f32[122,2,128]{2,1,0:T(2,128)S(1)} %rev.10), channel_id=1, source_target_pairs={{0,24},{8,16},{16,8},{24,0},{1,25},{9,17},{17,9},{25,1},{2,26},{10... | collective-permute-start | bytes 374792 | tf_op jit(solution)/shard_map/ppermute | solution.py:18
  27.0 3.5 %collective-permute-start.4 = (f32[2,122,2]{2,1,0:T(8,128)S(1)}, f32[2,122,2]{2,1,0:T(8,128)S(1)}, u32[]{:S(2)}, u32[]{:S(2)}) collective-permute-start(f32[2,122,2]{2,1,0:T(8,128)S(1)} %rev.12), channel_id=1, source_target_pairs={{0,0},{8,24},{16,16},{24,8},{1,1},{9,25},{17,17},{25,9},{2,2},{10,... | collective-permute-start | bytes 5864 | tf_op jit(solution)/shard_map/ppermute | solution.py:18
  27.9 6.9 %collective-permute-start.3 = (f32[2,122,2]{2,1,0:T(8,128)S(1)}, f32[2,122,2]{2,1,0:T(8,128)S(1)}, u32[]{:S(2)}, u32[]{:S(2)}) collective-permute-start(f32[2,122,2]{2,1,0:T(8,128)S(1)} %rev.11), channel_id=1, source_target_pairs={{0,16},{8,8},{16,0},{24,24},{1,17},{9,9},{17,1},{25,25},{2,18},{10... | collective-permute-start | bytes 5864 | tf_op jit(solution)/shard_map/ppermute | solution.py:18

commit v4 on v3

--- a/solution.py
+++ b/solution.py
@@ -231,11 +231,32 @@
         compiler_params=pltpu.CompilerParams(vmem_limit_bytes=48 * 1024 * 1024),
         interpret=INTERPRET,
     )(ext)
+    kappa_grad = summed_over_scen(grad)
+    return (final[None], adjoint[None], kappa_grad)
+
+
+def summed_over_scen(grad):
     parts = lax.axis_size("scen")
-    split = grad.reshape(2, levels, parts, ny // parts, width)
-    gathered = lax.all_to_all(split, "scen", 2, 2, tiled=True)
-    kappa_grad = gathered.sum(axis=2)
-    return (final[None], adjoint[None], kappa_grad)
+    kinds, levels, ny, width = grad.shape
+    if parts % 2:
+        split = grad.reshape(kinds, levels, parts, ny // parts, width)
+        return lax.all_to_all(split, "scen", 2, 2, tiled=True).sum(axis=2)
+    me = lax.axis_index("scen")
+    core = me % 2
+    chip = me // 2
+    chips = parts // 2
+    split = grad.reshape(kinds, levels, chips, 2, ny // parts, width)
+    mine = lax.dynamic_index_in_dim(split, core, axis=3, keepdims=False)
+    other = lax.dynamic_index_in_dim(split, 1 - core, axis=3, keepdims=False)
+    pair = lax.ppermute(other, "scen", [(q, q ^ 1) for q in range(parts)])
+    chip_sum = mine + pair
+    total = lax.dynamic_index_in_dim(chip_sum, chip, axis=2, keepdims=False)
+    for step in range(1, chips):
+        send = lax.dynamic_index_in_dim(chip_sum, (chip + step) % chips, axis=2, keepdims=False)
+        total = total + lax.ppermute(
+            send, "scen", [(q, ((q // 2 + step) % chips) * 2 + q % 2) for q in range(parts)]
+        )
+    return total
 
 
 def solution(mesh):

time: 95.5 us -> 84.6 us (0.89)
  blocking collectives: 39.6 us -> 16.8 us
  waiting for transfers between devices: 4.28 us -> 10.9 us
  starting transfers between devices: 8.58 us -> 12.9 us
  local copies, waits for them, and re-layouts: 3.71 us -> 4.71 us
    all_to_all x1 -> x0, blocking collectives: 22.8 us -> none  [on_device(): gathered = lax.all_to_all(split, 'scen', 2, 2, tiled=True)]
    ppermute x0 -> x4, waiting for transfers between devices: none -> 8.91 us  [the longest x3 7.38 us: summed_over_scen(): lax.ppermute(send, 'scen', [(q, (q // 2 + step) % chips * 2 + q % 2) for...]
    ppermute x0 -> x4, starting transfers between devices: none -> 4.32 us  [the longest x3 4.25 us: summed_over_scen(): lax.ppermute(send, 'scen', [(q, (q // 2 + step) % chips * 2 + q % 2) for...]
    ppermute x5, waiting for transfers between devices: 4.28 us -> 1.94 us  [shifted(): return lax.ppermute(x, 'space', perm)]
    unnamed x12 -> x10, local copies, waits for them, and re-layouts: 1.71 us -> 2.7 us
  transfers between devices with their start and end apart: 5 -> 9, of which waited for: 1 -> 5; matrix products, arithmetic and copies ran while one was open for 4% -> 4% of each run, Pallas kernels for 0% -> 0%
where the time goes in v4:
time: 84.6 us; the launch traced here: 84.2 us
  Pallas kernels  33.7 us (40%)
  blocking collectives  16.8 us (20%)
  starting transfers between devices  12.9 us (15%)
  waiting for transfers between devices  10.9 us (13%)
  local copies, waits for them, and re-layouts  4.71 us (6%)
  matrix products  2.96 us (3%)
  other arithmetic  1.38 us (2%)
  between operations  0.91 us (1%)
    pallas_call x1, Pallas kernels, on_device(): pl.pallas_call(diffusion_kernel, out_shape=(field, field, jax.ShapeDtypeS...  33.7 us
    all_gather x1, blocking collectives, on_device(): full_kappa = lax.all_gather(diffusivity, 'scen', axis=2, tiled=True)  16.8 us
    ppermute x5, starting transfers between devices, shifted(): return lax.ppermute(x, 'space', perm)  8.58 us
    ppermute x3, waiting for transfers between devices, summed_over_scen(): lax.ppermute(send, 'scen', [(q, (q // 2 + step) % chips * 2 + q % 2) for...  7.38 us
    ppermute x3, starting transfers between devices, summed_over_scen(): lax.ppermute(send, 'scen', [(q, (q // 2 + step) % chips * 2 + q % 2) for...  4.25 us
    dot_general x3, matrix products, contract(): lax.dot_general(a, b, (dims, ((), ())), precision=lax.Precision.HIGHEST,...  2.96 us
    unnamed x10, local copies, waits for them, and re-layouts  2.7 us
    ppermute x5, waiting for transfers between devices, shifted(): return lax.ppermute(x, 'space', perm)  1.94 us
  transfers between devices with their start and end apart: 9, of which 5 were waited for; matrix products, arithmetic and copies ran while one was open for 4% of the time, Pallas kernels for 0%

profile of v4, /device:TPU:0, one launch (start us, length us, event | category | flops | bytes accessed | tf_op | source)
XLA Modules:
  0.0 84.2 jit_solution(14553736546399330646)
XLA Ops:
  0.6 0.0 copy-start
  0.7 1.2 %constant_dynamic-update-slice_fusion.2 = f32[122,32,128]{2,1,0:T(8,128)S(1)} fusion(f32[40,32,128]{2,1,0:T(8,128)} %bitcast.43), kind=kLoop, calls=%fused_computation.20 | loop fusion | bytes 1310720
  1.9 0.9 %copy.23 = f32[2,20,4,128]{3,0,1,2:T(2,128)S(1)} copy(f32[2,20,4,128]{3,2,1,0:T(4,128)} %param.6) | data formatting | bytes 163840 | tf_op args[1]
  2.8 16.8 %all_gather.3 = f32[2,20,32,128]{3,0,1,2:T(2,128)S(1)} all-gather(f32[2,20,4,128]{3,0,1,2:T(2,128)S(1)} %copy.23), channel_id=1, replica_groups=mesh['space'=4,'scen'=8] {'scen'}, dimensions={2}, use_global_device_ids=true | all-gather | bytes 737280 | tf_op jit(solution)/shard_map/all_gather | solution.py:202
  19.6 0.0 copy-start.1
  19.6 0.0 copy-start.2
  19.6 0.1 copy.24
  19.8 0.0 copy-done
  19.9 0.5 copy-done.1
  20.4 0.0 copy-done.2
  20.4 1.0 %fusion.9 = f32[4,3904]{1,0:T(4,128)S(1)} fusion(f32[3904,128]{1,0:T(8,128)S(1)} %bitcast.40, pred[128]{0:T(512)(128)(4,1)S(1)} %get-tuple-element.16, pred[128]{0:T(512)(128)(4,1)S(1)} %get-tuple-element.17, pred[128]{0:T(512)(128)(4,1)S(1)} %get-tuple-element.18, pred[128]{0:T(512)(128)(4,1)S(1)} %get-tuple-element.19, ...), kind=kOutput, calls=%fused_computation.23 | convolution fusion | flops 23989760 | bytes 2061840 | tf_op jit(solution)/shard_map/dot_general | solution.py:31
  21.4 0.1 reshape.29
  21.5 0.1 fusion.26
  21.7 0.2 rev.12
  21.9 0.7 collective-permute-start.4
  22.5 0.2 rev.11
  22.7 3.4 %collective-permute-start.3 = (f32[2,122,2]{2,1,0:T(8,128)S(1)}, f32[2,122,2]{2,1,0:T(8,128)S(1)}, u32[]{:S(2)}, u32[]{:S(2)}) collective-permute-start(f32[2,122,2]{2,1,0:T(8,128)S(1)} %rev.11), channel_id=1, source_target_pairs={{0,16},{8,8},{16,0},{24,24},{1,17},{9,9},{17,1},{25,25},{2,18},{10... | collective-permute-start | bytes 5864 | tf_op jit(solution)/shard_map/ppermute | solution.py:18
  26.2 0.1 slice.27
  26.2 0.5 rev.10
  26.7 1.5 %collective-permute-start.2 = (f32[122,2,128]{2,1,0:T(2,128)S(1)}, f32[122,2,128]{2,1,0:T(2,128)S(1)}, u32[]{:S(2)}, u32[]{:S(2)}) collective-permute-start(f32[122,2,128]{2,1,0:T(2,128)S(1)} %rev.10), channel_id=1, source_target_pairs={{0,24},{8,16},{16,8},{24,0},{1,25},{9,17},{17,9},{25,1},{2,26},{10... | collective-permute-start | bytes 374792 | tf_op jit(solution)/shard_map/ppermute | solution.py:18
  28.3 0.6 collective-permute-start.1
  28.9 2.4 %collective-permute-start = (f32[2,3904]{1,0:T(2,128)S(1)}, f32[2,3904]{1,0:T(2,128)S(1)}, u32[]{:S(2)}, u32[]{:S(2)}) collective-permute-start(f32[2,3904]{1,0:T(2,128)S(1)} %get-tuple-element.14), channel_id=1, source_target_pairs={{0,24},{8,0},{16,8},{24,16},{1,25},{9,1},{17,9},{25,17},{2,26},{10... | collective-permute-start | bytes 93704 | tf_op jit(solution)/shard_map/ppermute | solution.py:18
  31.2 0.1 and_or_fusion
  31.3 0.1 pad.4.clone
  31.4 0.0 collective-permute-done.4
  31.4 1.4 %collective-permute-done.3 = f32[2,122,2]{2,1,0:T(8,128)S(1)} collective-permute-done((f32[2,122,2]{2,1,0:T(8,128)S(1)}, f32[2,122,2]{2,1,0:T(8,128)S(1)}, u32[]{:S(2)}, u32[]{:S(2)}) %collective-permute-start.3) | collective-permute-done | bytes 1984 | tf_op jit(solution)/shard_map/ppermute | solution.py:18
  32.8 0.2 reshape.33
  33.0 0.1 copy.30
  33.1 0.1 dot_general.16
  33.2 0.2 fusion
  33.4 0.1 copy.27
  33.5 0.5 collective-permute-done.1
  34.1 0.0 collective-permute-done
  34.1 1.7 %fusion.4 = f32[3904,128]{1,0:T(8,128)S(1)} fusion(pred[128,4]{0,1:T(4,128)(4,1)S(1)} %and_or_fusion, f32[2,3904]{1,0:T(2,128)S(1)} %collective-permute-done.1, f32[2,3904]{1,0:T(2,128)S(1)} %collective-permute-done), kind=kOutput, calls=%fused_computation.12 | convolution fusion | flops 24001792 | bytes 2061824 | tf_op jit(solution)/shard_map/dot_general | solution.py:31
  35.8 0.0 collective-permute-done.2
  35.8 0.5 maximum_maximum_fusion.x_ref
  36.3 33.7 %shard_map.76 = (f32[2,20,32,128]{3,2,1,0:T(8,128)}, f32[2,20,32,128]{3,2,1,0:T(8,128)}, f32[2,20,32,128]{3,2,1,0:T(8,128)S(1)}) custom-call(f32[122,40,256]{2,1,0:T(8,128)S(1)} %maximum_maximum_fusion.x_ref), custom_call_target="tpu_custom_call" | custom-call | tf_op jit(solution)/shard_map/pallas_call | solution.py:216
  70.0 0.1 dynamic-slice_bitcast_fusion
  70.1 0.1 collective-permute-start.5
  70.2 1.5 %collective-permute-done.5 = f32[2,20,4,4,128]{4,3,2,1,0:T(4,128)S(1)} collective-permute-done((f32[2,20,4,4,128]{4,3,2,1,0:T(4,128)S(1)}, f32[2,20,4,4,128]{4,3,2,1,0:T(4,128)S(1)}, u32[]{:S(2)}, u32[]{:S(2)}) %collective-permute-start.5) | collective-permute-done | bytes 327712 | tf_op jit(solution)/shard_map/ppermute | solution.py:251
  71.7 0.1 bitcast_add_fusion
  71.8 0.1 dynamic-slice_bitcast_fusion.3
  71.9 3.6 %collective-permute-start.8 = (f32[2,20,4,128]{3,2,1,0:T(4,128)S(1)}, f32[2,20,4,128]{3,2,1,0:T(4,128)S(1)}, u32[]{:S(2)}, u32[]{:S(2)}) collective-permute-start(f32[2,20,4,128]{3,2,1,0:T(4,128)S(1)} %get-tuple-element.10), channel_id=1, source_target_pairs={{0,6},{1,7},{2,0},{3,1},{4,2},{5,3},{6,4},{7,5},{8,14},{9,15},{10,... | collective-permute-start | bytes 245768 | tf_op jit(solution)/shard_map/ppermute | solution.py:256
  75.5 0.0 collective-permute-start.7
  75.5 0.6 collective-permute-start.6
  76.2 2.2 %collective-permute-done.8 = f32[2,20,4,128]{3,2,1,0:T(4,128)S(1)} collective-permute-done((f32[2,20,4,128]{3,2,1,0:T(4,128)S(1)}, f32[2,20,4,128]{3,2,1,0:T(4,128)S(1)}, u32[]{:S(2)}, u32[]{:S(2)}) %collective-permute-start.8) | collective-permute-done | bytes 81952 | tf_op jit(solution)/shard_map/ppermute | solution.py:256
  78.4 5.2 %collective-permute-done.7 = f32[2,20,4,128]{3,2,1,0:T(4,128)S(1)} collective-permute-done((f32[2,20,4,128]{3,2,1,0:T(4,128)S(1)}, f32[2,20,4,128]{3,2,1,0:T(4,128)S(1)}, u32[]{:S(2)}, u32[]{:S(2)}) %collective-permute-start.7) | collective-permute-done | bytes 81952 | tf_op jit(solution)/shard_map/ppermute | solution.py:256
  83.5 0.0 collective-permute-done.6
  83.5 0.7 fusion.3
  (11 shorter events, 0.2 us)
Async XLA Ops:
  0.6 19.1 %copy-start = (f32[1,2,20,32,128]{4,3,2,1,0:T(8,128)S(1)}, f32[1,2,20,32,128]{4,3,2,1,0:T(8,128)}, u32[]{:S(2)}) copy-start(f32[1,2,20,32,128]{4,3,2,1,0:T(8,128)} %param.9) | copy-start | bytes 1966084
  19.6 0.7 copy-start.1
  19.6 0.7 copy-start.2
  21.9 9.5 %collective-permute-start.4 = (f32[2,122,2]{2,1,0:T(8,128)S(1)}, f32[2,122,2]{2,1,0:T(8,128)S(1)}, u32[]{:S(2)}, u32[]{:S(2)}) collective-permute-start(f32[2,122,2]{2,1,0:T(8,128)S(1)} %rev.12), channel_id=1, source_target_pairs={{0,0},{8,24},{16,16},{24,8},{1,1},{9,25},{17,17},{25,9},{2,2},{10,... | collective-permute-start | bytes 5864 | tf_op jit(solution)/shard_map/ppermute | solution.py:18
  22.7 10.1 %collective-permute-start.3 = (f32[2,122,2]{2,1,0:T(8,128)S(1)}, f32[2,122,2]{2,1,0:T(8,128)S(1)}, u32[]{:S(2)}, u32[]{:S(2)}) collective-permute-start(f32[2,122,2]{2,1,0:T(8,128)S(1)} %rev.11), channel_id=1, source_target_pairs={{0,16},{8,8},{16,0},{24,24},{1,17},{9,9},{17,1},{25,25},{2,18},{10... | collective-permute-start | bytes 5864 | tf_op jit(solution)/shard_map/ppermute | solution.py:18
  26.7 9.1 %collective-permute-start.2 = (f32[122,2,128]{2,1,0:T(2,128)S(1)}, f32[122,2,128]{2,1,0:T(2,128)S(1)}, u32[]{:S(2)}, u32[]{:S(2)}) collective-permute-start(f32[122,2,128]{2,1,0:T(2,128)S(1)} %rev.10), channel_id=1, source_target_pairs={{0,24},{8,16},{16,8},{24,0},{1,25},{9,17},{17,9},{25,1},{2,26},{10... | collective-permute-start | bytes 374792 | tf_op jit(solution)/shard_map/ppermute | solution.py:18
  28.3 5.8 %collective-permute-start.1 = (f32[2,3904]{1,0:T(2,128)S(1)}, f32[2,3904]{1,0:T(2,128)S(1)}, u32[]{:S(2)}, u32[]{:S(2)}) collective-permute-start(f32[2,3904]{1,0:T(2,128)S(1)} %get-tuple-element.15), channel_id=1, source_target_pairs={{0,8},{8,16},{16,24},{24,0},{1,9},{9,17},{17,25},{25,1},{2,10},{10... | collective-permute-start | bytes 93704 | tf_op jit(solution)/shard_map/ppermute | solution.py:18
  28.9 5.2 %collective-permute-start = (f32[2,3904]{1,0:T(2,128)S(1)}, f32[2,3904]{1,0:T(2,128)S(1)}, u32[]{:S(2)}, u32[]{:S(2)}) collective-permute-start(f32[2,3904]{1,0:T(2,128)S(1)} %get-tuple-element.14), channel_id=1, source_target_pairs={{0,24},{8,0},{16,8},{24,16},{1,25},{9,1},{17,9},{25,17},{2,26},{10... | collective-permute-start | bytes 93704 | tf_op jit(solution)/shard_map/ppermute | solution.py:18
  70.1 1.7 %collective-permute-start.5 = (f32[2,20,4,4,128]{4,3,2,1,0:T(4,128)S(1)}, f32[2,20,4,4,128]{4,3,2,1,0:T(4,128)S(1)}, u32[]{:S(2)}, u32[]{:S(2)}) collective-permute-start(f32[2,20,4,4,128]{4,3,2,1,0:T(4,128)S(1)} %dynamic-slice_bitcast_fusion), channel_id=1, source_target_pairs={{0,1},{1,0},{2,3},{3,2},{4,5},{5,4},{6,7},{7,6},{8,9},{9,8},{10,11... | collective-permute-start | bytes 983048 | tf_op jit(solution)/shard_map/ppermute | solution.py:251
  71.9 6.5 %collective-permute-start.8 = (f32[2,20,4,128]{3,2,1,0:T(4,128)S(1)}, f32[2,20,4,128]{3,2,1,0:T(4,128)S(1)}, u32[]{:S(2)}, u32[]{:S(2)}) collective-permute-start(f32[2,20,4,128]{3,2,1,0:T(4,128)S(1)} %get-tuple-element.10), channel_id=1, source_target_pairs={{0,6},{1,7},{2,0},{3,1},{4,2},{5,3},{6,4},{7,5},{8,14},{9,15},{10,... | collective-permute-start | bytes 245768 | tf_op jit(solution)/shard_map/ppermute | solution.py:256
  75.5 8.0 %collective-permute-start.7 = (f32[2,20,4,128]{3,2,1,0:T(4,128)S(1)}, f32[2,20,4,128]{3,2,1,0:T(4,128)S(1)}, u32[]{:S(2)}, u32[]{:S(2)}) collective-permute-start(f32[2,20,4,128]{3,2,1,0:T(4,128)S(1)} %get-tuple-element.11), channel_id=1, source_target_pairs={{0,4},{1,5},{2,6},{3,7},{4,0},{5,1},{6,2},{7,3},{8,12},{9,13},{10,... | collective-permute-start | bytes 245768 | tf_op jit(solution)/shard_map/ppermute | solution.py:256
  75.5 8.0 %collective-permute-start.6 = (f32[2,20,4,128]{3,2,1,0:T(4,128)S(1)}, f32[2,20,4,128]{3,2,1,0:T(4,128)S(1)}, u32[]{:S(2)}, u32[]{:S(2)}) collective-permute-start(f32[2,20,4,128]{3,2,1,0:T(4,128)S(1)} %get-tuple-element.9), channel_id=1, source_target_pairs={{0,2},{1,3},{2,4},{3,5},{4,6},{5,7},{6,0},{7,1},{8,10},{9,11},{10,... | collective-permute-start | bytes 245768 | tf_op jit(solution)/shard_map/ppermute | solution.py:256

commit v5 on v4

--- a/solution.py
+++ b/solution.py
@@ -71,22 +71,14 @@
         return self.ref[self.start + c * self.levels + k]
 
 
-def diffusion_kernel(
-    x_ref,
-    fin_ref, adj_ref, grad_ref,
-    wet_ref, ce_ref, cn_ref, cz_ref, src_ref, gem_ref, gnm_ref, u1_ref, a_ref, b_ref,
-):
+def coefficients(x_ref, wet_ref, ce_ref, cn_ref, cz_ref, src_ref, ny, width, masks=None):
     levels, rows, lanes = wet_ref.shape
-    chans, _, ny, width = fin_ref.shape
     row = lax.broadcasted_iota(jnp.int32, (rows, lanes), 0)
     lane = lax.broadcasted_iota(jnp.int32, (rows, lanes), 1)
     owned = (row < ny) & (lane < width)
-    planes = chans * levels
-    ue_ref = Planes(x_ref, 0, levels)
-    ve_ref = Planes(x_ref, planes, levels)
-    ke_ref = Planes(x_ref, 2 * planes, levels)
-    lev = x_ref[2 * planes + 2 * levels]
-    shelf = x_ref[2 * planes + 2 * levels + 1]
+    ke_ref = Planes(x_ref, 0, levels)
+    lev = x_ref[2 * levels]
+    shelf = x_ref[2 * levels + 1]
 
     def wet_of(k):
         return (lev > k.astype(jnp.float32)).astype(jnp.float32)
@@ -112,10 +104,12 @@
         cz_ref[k + 1] = vertical_rate * w * w_next
         src_ref[k] = thaw_rate * shelf * w * (1.0 - w_next)
         wet_ref[k] = w
-        gem_ref[k] = jnp.where(owned, east_mask, 0.0)
-        gnm_ref[k] = jnp.where(
-            owned, jnp.where(row < ny - 1, north_mask, jnp.where(row == ny - 1, 0.5 * north_mask, 0.0)), 0.0
-        )
+        if masks is not None:
+            gem_ref, gnm_ref = masks
+            gem_ref[k] = jnp.where(owned, east_mask, 0.0)
+            gnm_ref[k] = jnp.where(
+                owned, jnp.where(row < ny - 1, north_mask, jnp.where(row == ny - 1, 0.5 * north_mask, 0.0)), 0.0
+            )
         return carry
 
     lax.fori_loop(0, levels, setup, 0)
@@ -130,6 +124,21 @@
         change = change + (cz_ref[k + 1] * (above - x) - cz_ref[k] * (x - below))
         return x, change
 
+    return operate
+
+
+def gradient_kernel(
+    x_ref, grad_ref, u1_ref, b_ref,
+    wet_ref, ce_ref, cn_ref, cz_ref, src_ref, gem_ref, gnm_ref, a_ref,
+):
+    levels, rows, lanes = wet_ref.shape
+    chans = u1_ref.shape[0]
+    ny, width = grad_ref.shape[2:]
+    operate = coefficients(x_ref, wet_ref, ce_ref, cn_ref, cz_ref, src_ref, ny, width, (gem_ref, gnm_ref))
+    planes = chans * levels
+    ue_ref = Planes(x_ref, 2 * levels + 2, levels)
+    ve_ref = Planes(x_ref, 2 * levels + 2 + planes, levels)
+
     def forward_first(ck, carry):
         c = ck // levels
         k = ck % levels
@@ -140,17 +149,6 @@
 
     lax.fori_loop(0, planes, forward_first, 0)
 
-    def forward_second(ck, carry):
-        c = ck // levels
-        k = ck % levels
-        x, change = operate(u1_ref, c, k)
-        heat = jnp.where(c == 0, 1.0, 0.0)
-        out = wet_ref[k] * (x + change + heat * src_ref[k])
-        fin_ref[c, k] = out[:ny, :width]
-        return carry
-
-    lax.fori_loop(0, planes, forward_second, 0)
-
     def weigh(ck, carry):
         c = ck // levels
         k = ck % levels
@@ -167,22 +165,13 @@
         return carry
 
     lax.fori_loop(0, planes, backward_second, 0)
-
-    def backward_first(ck, carry):
-        c = ck // levels
-        k = ck % levels
-        x, change = operate(b_ref, c, k)
-        adj_ref[c, k] = (x + change)[:ny, :width]
-        return carry
-
-    lax.fori_loop(0, planes, backward_first, 0)
 
     def gradient(k, carry):
         gem = gem_ref[k]
         gnm = gnm_ref[k]
         g_east = jnp.zeros((rows, lanes), jnp.float32)
         g_north = jnp.zeros((rows, lanes), jnp.float32)
-        for c in range(2):
+        for c in range(chans):
             for u_ref, v_ref in ((ue_ref, b_ref), (u1_ref, a_ref)):
                 u = u_ref[c, k]
                 v = v_ref[c, k]
@@ -195,6 +184,36 @@
     lax.fori_loop(0, levels, gradient, 0)
 
 
+def finishing_kernel(
+    x_ref, u1_ref, b_ref, fin_ref, adj_ref,
+    wet_ref, ce_ref, cn_ref, cz_ref, src_ref,
+):
+    levels = wet_ref.shape[0]
+    chans, _, ny, width = fin_ref.shape
+    operate = coefficients(x_ref, wet_ref, ce_ref, cn_ref, cz_ref, src_ref, ny, width)
+    planes = chans * levels
+
+    def forward_second(ck, carry):
+        c = ck // levels
+        k = ck % levels
+        x, change = operate(u1_ref, c, k)
+        heat = jnp.where(c == 0, 1.0, 0.0)
+        out = wet_ref[k] * (x + change + heat * src_ref[k])
+        fin_ref[c, k] = out[:ny, :width]
+        return carry
+
+    lax.fori_loop(0, planes, forward_second, 0)
+
+    def backward_first(ck, carry):
+        c = ck // levels
+        k = ck % levels
+        x, change = operate(b_ref, c, k)
+        adj_ref[c, k] = (x + change)[:ny, :width]
+        return carry
+
+    lax.fori_loop(0, planes, backward_first, 0)
+
+
 def on_device(tracers, diffusivity, level_count, shelf_mask, cotangent):
     _, chans, levels, ny, width = tracers.shape
     lanes = width + 128
@@ -202,35 +221,42 @@
     full_kappa = lax.all_gather(diffusivity, "scen", axis=2, tiled=True)
     fields = jnp.concatenate(
         [
-            tracers[0].reshape(chans * levels, ny, width),
-            cotangent[0].reshape(chans * levels, ny, width),
             full_kappa.reshape(2 * levels, ny, width),
             level_count.astype(jnp.float32)[None],
             shelf_mask.astype(jnp.float32)[None],
+            tracers[0].reshape(chans * levels, ny, width),
+            cotangent[0].reshape(chans * levels, ny, width),
         ]
     )
     ext = extended(fields, lanes, rows)
     field = jax.ShapeDtypeStruct((chans, levels, ny, width), jnp.float32)
+    state = jax.ShapeDtypeStruct((chans, levels, rows, lanes), jnp.float32)
     plane = pltpu.VMEM((levels, rows, lanes), jnp.float32)
     planes_c = pltpu.VMEM((chans, levels, rows, lanes), jnp.float32)
-    final, adjoint, grad = pl.pallas_call(
-        diffusion_kernel,
-        out_shape=(field, field, jax.ShapeDtypeStruct((2, levels, ny, width), jnp.float32)),
-        scratch_shapes=[
-            plane,
-            plane,
-            plane,
-            pltpu.VMEM((levels + 1, rows, lanes), jnp.float32),
-            plane,
-            plane,
-            plane,
-            planes_c,
-            planes_c,
-            planes_c,
-        ],
-        compiler_params=pltpu.CompilerParams(vmem_limit_bytes=48 * 1024 * 1024),
+    heights = pltpu.VMEM((levels + 1, rows, lanes), jnp.float32)
+    params = pltpu.CompilerParams(vmem_limit_bytes=48 * 1024 * 1024)
+    grad, u1, b = pl.pallas_call(
+        gradient_kernel,
+        out_shape=(jax.ShapeDtypeStruct((2, levels, ny, width), jnp.float32), state, state),
+        scratch_shapes=[plane, plane, plane, heights, plane, plane, plane, planes_c],
+        compiler_params=params,
         interpret=INTERPRET,
     )(ext)
+    coeff_planes = 2 * levels + 2
+    final, adjoint = pl.pallas_call(
+        finishing_kernel,
+        out_shape=(field, field),
+        grid=(1,),
+        in_specs=[
+            pl.BlockSpec((coeff_planes, rows, lanes), lambda i: (0, 0, 0)),
+            pl.BlockSpec(state.shape, lambda i: (0, 0, 0, 0)),
+            pl.BlockSpec(state.shape, lambda i: (0, 0, 0, 0)),
+        ],
+        out_specs=[pl.BlockSpec(field.shape, lambda i: (0, 0, 0, 0))] * 2,
+        scratch_shapes=[plane, plane, plane, heights, plane],
+        compiler_params=params,
+        interpret=INTERPRET,
+    )(ext, u1, b)
     kappa_grad = summed_over_scen(grad)
     return (final[None], adjoint[None], kappa_grad)
 

time: 84.6 us -> 90.8 us (1.073)
  the two profiles are of different devices: /device:TPU:0 before, /device:TPU:14 now
where the time goes in v5:
time: 90.8 us; the launch traced here: 90.5 us
  Pallas kernels  39.5 us (44%)
  blocking collectives  15.5 us (17%)
  starting transfers between devices  11.2 us (12%)
  waiting for transfers between devices  7.93 us (9%)
  local copies, waits for them, and re-layouts  6.85 us (8%)
  other arithmetic  5.66 us (6%)
  matrix products  2.96 us (3%)
    pallas_call x1, Pallas kernels, on_device(): pl.pallas_call(gradient_kernel, out_shape=(jax.ShapeDtypeStruct((2, level...  21.9 us
    pallas_call x1, Pallas kernels, on_device(): pl.pallas_call(finishing_kernel, out_shape=(field, field), grid=(1,), in_...  17.6 us
    all_gather x1, blocking collectives, on_device(): full_kappa = lax.all_gather(diffusivity, 'scen', axis=2, tiled=True)  15.5 us
    ppermute x5, starting transfers between devices, shifted(): return lax.ppermute(x, 'space', perm)  6.73 us
    ppermute x5, waiting for transfers between devices, shifted(): return lax.ppermute(x, 'space', perm)  5.96 us
    ppermute x3, starting transfers between devices, summed_over_scen(): lax.ppermute(send, 'scen', [(q, (q // 2 + step) % chips * 2 + q % 2) for...  4.5 us
    unnamed x15, local copies, waits for them, and re-layouts  3.45 us
    dot_general x3, matrix products, contract(): lax.dot_general(a, b, (dims, ((), ())), precision=lax.Precision.HIGHEST,...  2.96 us
  transfers between devices with their start and end apart: 9, of which 2 were waited for; matrix products, arithmetic and copies ran while one was open for 4% of the time, Pallas kernels for 19%

profile of v5, /device:TPU:14, one launch (start us, length us, event | category | flops | bytes accessed | tf_op | source)
XLA Modules:
  0.0 90.5 jit_solution(12602493809310904222)
XLA Ops:
  0.6 0.0 copy-start.4
  0.6 0.0 copy-start.5
  0.7 0.0 copy-start.2
  0.7 1.0 %copy.23 = f32[2,20,4,128]{3,0,1,2:T(2,128)S(1)} copy(f32[2,20,4,128]{3,2,1,0:T(4,128)} %param.6) | data formatting | bytes 163840 | tf_op args[1]
  1.7 15.5 %all_gather.3 = f32[2,20,32,128]{3,0,1,2:T(2,128)S(1)} all-gather(f32[2,20,4,128]{3,0,1,2:T(2,128)S(1)} %copy.23), channel_id=1, replica_groups=mesh['space'=4,'scen'=8] {'scen'}, dimensions={2}, use_global_device_ids=true | all-gather | bytes 737280 | tf_op jit(solution)/shard_map/all_gather | solution.py:221
  17.2 0.0 copy-start.3
  17.2 0.1 copy.24
  17.3 0.0 copy-done.4
  17.4 0.0 copy-done.5
  17.4 0.0 copy-done.2
  17.4 0.8 copy-done.3
  18.3 1.0 %fusion.9 = f32[4,3904]{1,0:T(4,128)S(1)} fusion(f32[3904,128]{1,0:T(8,128)S(1)} %bitcast.40, pred[128]{0:T(512)(128)(4,1)S(1)} %get-tuple-element.20, pred[128]{0:T(512)(128)(4,1)S(1)} %get-tuple-element.21, pred[128]{0:T(512)(128)(4,1)S(1)} %get-tuple-element.22, pred[128]{0:T(512)(128)(4,1)S(1)} %get-tuple-element.23, ...), kind=kOutput, calls=%fused_computation.23 | convolution fusion | flops 23989760 | bytes 2061840 | tf_op jit(solution)/shard_map/dot_general | solution.py:31
  19.4 0.6 collective-permute-start
  19.9 2.4 %collective-permute-start.1 = (f32[2,3904]{1,0:T(2,128)S(1)}, f32[2,3904]{1,0:T(2,128)S(1)}, u32[]{:S(2)}, u32[]{:S(2)}) collective-permute-start(f32[2,3904]{1,0:T(2,128)S(1)} %get-tuple-element.19), channel_id=1, source_target_pairs={{0,8},{8,16},{16,24},{24,0},{1,9},{9,17},{17,25},{25,1},{2,10},{10... | collective-permute-start | bytes 93704 | tf_op jit(solution)/shard_map/ppermute | solution.py:18
  22.3 0.1 reshape.29
  22.5 0.1 fusion.26
  22.6 0.2 rev.11
  22.8 0.7 collective-permute-start.3
  23.5 0.2 rev.12
  23.6 2.4 %collective-permute-start.4 = (f32[2,122,2]{2,1,0:T(8,128)S(1)}, f32[2,122,2]{2,1,0:T(8,128)S(1)}, u32[]{:S(2)}, u32[]{:S(2)}) collective-permute-start(f32[2,122,2]{2,1,0:T(8,128)S(1)} %rev.12), channel_id=1, source_target_pairs={{0,0},{8,24},{16,16},{24,8},{1,1},{9,25},{17,17},{25,9},{2,2},{10,... | collective-permute-start | bytes 5864 | tf_op jit(solution)/shard_map/ppermute | solution.py:18
  26.1 0.1 slice.27
  26.2 0.5 rev.10
  26.6 0.7 collective-permute-start.2
  27.3 0.1 and_or_fusion
  27.4 0.1 pad.4.clone
  27.5 0.0 collective-permute-done.3
  27.5 5.9 %collective-permute-done.4 = f32[2,122,2]{2,1,0:T(8,128)S(1)} collective-permute-done((f32[2,122,2]{2,1,0:T(8,128)S(1)}, f32[2,122,2]{2,1,0:T(8,128)S(1)}, u32[]{:S(2)}, u32[]{:S(2)}) %collective-permute-start.4) | collective-permute-done | bytes 1984 | tf_op jit(solution)/shard_map/ppermute | solution.py:18
  33.4 0.2 reshape.33
  33.6 0.1 copy.30
  33.7 0.1 dot_general.16
  33.8 0.2 fusion
  34.0 0.1 copy.27
  34.1 0.0 collective-permute-done
  34.1 0.0 collective-permute-done.1
  34.2 1.7 %fusion.4 = f32[3904,128]{1,0:T(8,128)S(1)} fusion(pred[128,4]{0,1:T(4,128)(4,1)S(1)} %and_or_fusion, f32[2,3904]{1,0:T(2,128)S(1)} %collective-permute-done.1, f32[2,3904]{1,0:T(2,128)S(1)} %collective-permute-done), kind=kOutput, calls=%fused_computation.12 | convolution fusion | flops 24001792 | bytes 2061824 | tf_op jit(solution)/shard_map/dot_general | solution.py:31
  35.9 0.0 collective-permute-done.2
  35.9 2.7 %maximum_maximum_fusion.x_ref = f32[122,40,256]{2,1,0:T(8,128)} fusion(f32[122,2,128]{2,1,0:T(2,128)S(1)} %copy.27, f32[122,2,128]{2,1,0:T(2,128)S(1)} %collective-permute-done.2, f32[122,32,128]{2,1,0:T(8,128)S(1)} %bitcast.41, f32[122,32,128]{2,1,0:T(8,128)S(1)} %constant_dynamic-update-slice_fusion, f32[40]{0:T(128)S(1)} %pad.4.clone), kind=kLoop, calls=%fused_computation | loop fusion | flops 4997120 | bytes 9244832 | tf_op jit(solution)/shard_map/concatenate | solution.py:56
  38.6 21.9 %shard_map.76 = (f32[2,20,32,128]{3,2,1,0:T(8,128)S(1)}, f32[2,20,40,256]{3,2,1,0:T(8,128)S(1)}, f32[2,20,40,256]{3,2,1,0:T(8,128)S(1)}) custom-call(f32[122,40,256]{2,1,0:T(8,128)} %maximum_maximum_fusion.x_ref), custom_call_target="tpu_custom_call" | custom-call | tf_op jit(solution)/shard_map/pallas_call | solution.py:238
  60.5 0.0 copy-start
  60.5 0.8 copy-done
  61.4 0.8 dynamic-slice_bitcast_fusion
  62.1 0.0 collective-permute-start.5
  62.2 2.0 %collective-permute-done.5 = f32[2,20,4,4,128]{4,3,2,1,0:T(4,128)} collective-permute-done((f32[2,20,4,4,128]{4,3,2,1,0:T(4,128)}, f32[2,20,4,4,128]{4,3,2,1,0:T(4,128)}, u32[]{:S(2)}, u32[]{:S(2)}) %collective-permute-start.5) | collective-permute-done | bytes 327712 | tf_op jit(solution)/shard_map/ppermute | solution.py:277
  64.1 1.2 %bitcast_add_fusion = f32[2,20,4,4,128]{4,3,2,1,0:T(4,128)S(1)} fusion(f32[2,20,4,4,128]{4,3,2,1,0:T(4,128)} %collective-permute-done.5, f32[2,20,4,2,4,128]{5,4,3,2,1,0:T(4,128)} %bitcast.39, s32[]{:T(128)S(6)} %select_n.44), kind=kLoop, calls=%fused_computation.1 | loop fusion | flops 81920 | bytes 983044 | tf_op jit(solution)/shard_map/add | solution.py:278
  65.3 0.0 copy-start.1
  65.3 0.7 copy-done.1
  66.0 0.7 dynamic-slice_bitcast_fusion.3
  66.7 0.0 collective-permute-start.6
  66.7 2.7 %collective-permute-start.7 = (f32[2,20,4,128]{3,2,1,0:T(4,128)S(1)}, f32[2,20,4,128]{3,2,1,0:T(4,128)}, u32[]{:S(2)}, u32[]{:S(2)}) collective-permute-start(f32[2,20,4,128]{3,2,1,0:T(4,128)S(1)} %get-tuple-element.15), channel_id=1, source_target_pairs={{0,4},{1,5},{2,6},{3,7},{4,0},{5,1},{6,2},{7,3},{8,12},{9,13},{10,... | collective-permute-start | bytes 245768 | tf_op jit(solution)/shard_map/ppermute | solution.py:282
  69.4 1.8 %collective-permute-start.8 = (f32[2,20,4,128]{3,2,1,0:T(4,128)S(1)}, f32[2,20,4,128]{3,2,1,0:T(4,128)}, u32[]{:S(2)}, u32[]{:S(2)}) collective-permute-start(f32[2,20,4,128]{3,2,1,0:T(4,128)S(1)} %get-tuple-element.14), channel_id=1, source_target_pairs={{0,6},{1,7},{2,0},{3,1},{4,2},{5,3},{6,4},{7,5},{8,14},{9,15},{10,... | collective-permute-start | bytes 245768 | tf_op jit(solution)/shard_map/ppermute | solution.py:282
  71.2 17.6 %shard_map.77 = (f32[2,20,32,128]{3,2,1,0:T(8,128)}, f32[2,20,32,128]{3,2,1,0:T(8,128)}) custom-call(f32[122,40,256]{2,1,0:T(8,128)} %maximum_maximum_fusion.x_ref, f32[2,20,40,256]{3,2,1,0:T(8,128)S(1)} %get-tuple-element.8.u1_ref, f32[2,20,40,256]{3,2,1,0:T(8,128)S(1)} %get-tuple-element.9.b_ref), custom_call_target="tpu_custom_call" | custom-call | tf_op jit(solution)/shard_map/pallas_call | solution.py:246
  88.8 0.0 collective-permute-done.6
  88.8 0.0 collective-permute-done.7
  88.8 0.0 collective-permute-done.8
  88.8 1.6 %fusion.3 = f32[2,20,4,128]{3,2,1,0:T(4,128)} fusion(f32[2,20,4,128]{3,2,1,0:T(4,128)} %collective-permute-done.8, f32[2,20,4,128]{3,2,1,0:T(4,128)} %collective-permute-done.7, f32[2,20,4,128]{3,2,1,0:T(4,128)S(1)} %collective-permute-done.6, f32[2,20,4,4,128]{4,3,2,1,0:T(4,128)} %copy-done.1, s32[]{:T(128)S(6)} %select_n.47), kind=kLoop, calls=%fused_computation.8 | loop fusion | flops 61440 | bytes 409604 | tf_op jit(solution)/shard_map/add | solution.py:282
  (12 shorter events, 0.2 us)
Async XLA Ops:
  0.6 16.7 %copy-start.4 = (s32[32,128]{1,0:T(8,128)S(1)}, s32[32,128]{1,0:T(8,128)}, u32[]{:S(2)}) copy-start(s32[32,128]{1,0:T(8,128)} %param.7) | copy-start | bytes 49156
  0.6 16.7 %copy-start.5 = (s32[32,128]{1,0:T(8,128)S(1)}, s32[32,128]{1,0:T(8,128)}, u32[]{:S(2)}) copy-start(s32[32,128]{1,0:T(8,128)} %param.8) | copy-start | bytes 49156
  0.7 16.7 %copy-start.2 = (f32[1,2,20,32,128]{4,3,2,1,0:T(8,128)S(1)}, f32[1,2,20,32,128]{4,3,2,1,0:T(8,128)}, u32[]{:S(2)}) copy-start(f32[1,2,20,32,128]{4,3,2,1,0:T(8,128)} %param.5) | copy-start | bytes 1966084
  17.2 1.1 %copy-start.3 = (f32[1,2,20,32,128]{4,3,2,1,0:T(8,128)S(1)}, f32[1,2,20,32,128]{4,3,2,1,0:T(8,128)}, u32[]{:S(2)}) copy-start(f32[1,2,20,32,128]{4,3,2,1,0:T(8,128)} %param.9) | copy-start | bytes 1966084
  19.4 14.8 %collective-permute-start = (f32[2,3904]{1,0:T(2,128)S(1)}, f32[2,3904]{1,0:T(2,128)S(1)}, u32[]{:S(2)}, u32[]{:S(2)}) collective-permute-start(f32[2,3904]{1,0:T(2,128)S(1)} %get-tuple-element.18), channel_id=1, source_target_pairs={{0,24},{8,0},{16,8},{24,16},{1,25},{9,1},{17,9},{25,17},{2,26},{10... | collective-permute-start | bytes 93704 | tf_op jit(solution)/shard_map/ppermute | solution.py:18
  19.9 14.2 %collective-permute-start.1 = (f32[2,3904]{1,0:T(2,128)S(1)}, f32[2,3904]{1,0:T(2,128)S(1)}, u32[]{:S(2)}, u32[]{:S(2)}) collective-permute-start(f32[2,3904]{1,0:T(2,128)S(1)} %get-tuple-element.19), channel_id=1, source_target_pairs={{0,8},{8,16},{16,24},{24,0},{1,9},{9,17},{17,25},{25,1},{2,10},{10... | collective-permute-start | bytes 93704 | tf_op jit(solution)/shard_map/ppermute | solution.py:18
  22.8 4.7 %collective-permute-start.3 = (f32[2,122,2]{2,1,0:T(8,128)S(1)}, f32[2,122,2]{2,1,0:T(8,128)S(1)}, u32[]{:S(2)}, u32[]{:S(2)}) collective-permute-start(f32[2,122,2]{2,1,0:T(8,128)S(1)} %rev.11), channel_id=1, source_target_pairs={{0,16},{8,8},{16,0},{24,24},{1,17},{9,9},{17,1},{25,25},{2,18},{10... | collective-permute-start | bytes 5864 | tf_op jit(solution)/shard_map/ppermute | solution.py:18
  23.6 9.8 %collective-permute-start.4 = (f32[2,122,2]{2,1,0:T(8,128)S(1)}, f32[2,122,2]{2,1,0:T(8,128)S(1)}, u32[]{:S(2)}, u32[]{:S(2)}) collective-permute-start(f32[2,122,2]{2,1,0:T(8,128)S(1)} %rev.12), channel_id=1, source_target_pairs={{0,0},{8,24},{16,16},{24,8},{1,1},{9,25},{17,17},{25,9},{2,2},{10,... | collective-permute-start | bytes 5864 | tf_op jit(solution)/shard_map/ppermute | solution.py:18
  26.6 9.3 %collective-permute-start.2 = (f32[122,2,128]{2,1,0:T(2,128)S(1)}, f32[122,2,128]{2,1,0:T(2,128)S(1)}, u32[]{:S(2)}, u32[]{:S(2)}) collective-permute-start(f32[122,2,128]{2,1,0:T(2,128)S(1)} %rev.10), channel_id=1, source_target_pairs={{0,24},{8,16},{16,8},{24,0},{1,25},{9,17},{17,9},{25,1},{2,26},{10... | collective-permute-start | bytes 374792 | tf_op jit(solution)/shard_map/ppermute | solution.py:18
  60.5 0.8 copy-start
  62.1 2.0 %collective-permute-start.5 = (f32[2,20,4,4,128]{4,3,2,1,0:T(4,128)}, f32[2,20,4,4,128]{4,3,2,1,0:T(4,128)}, u32[]{:S(2)}, u32[]{:S(2)}) collective-permute-start(f32[2,20,4,4,128]{4,3,2,1,0:T(4,128)} %dynamic-slice_bitcast_fusion), channel_id=1, source_target_pairs={{0,1},{1,0},{2,3},{3,2},{4,5},{5,4},{6,7},{7,6},{8,9},{9,8},{10,11... | collective-permute-start | bytes 983048 | tf_op jit(solution)/shard_map/ppermute | solution.py:277
  65.3 0.7 copy-start.1
  66.7 22.1 %collective-permute-start.6 = (f32[2,20,4,128]{3,2,1,0:T(4,128)}, f32[2,20,4,128]{3,2,1,0:T(4,128)S(1)}, u32[]{:S(2)}, u32[]{:S(2)}) collective-permute-start(f32[2,20,4,128]{3,2,1,0:T(4,128)} %get-tuple-element.13), channel_id=1, source_target_pairs={{0,2},{1,3},{2,4},{3,5},{4,6},{5,7},{6,0},{7,1},{8,10},{9,11},{10,... | collective-permute-start | bytes 245768 | tf_op jit(solution)/shard_map/ppermute | solution.py:282
  66.7 22.1 %collective-permute-start.7 = (f32[2,20,4,128]{3,2,1,0:T(4,128)S(1)}, f32[2,20,4,128]{3,2,1,0:T(4,128)}, u32[]{:S(2)}, u32[]{:S(2)}) collective-permute-start(f32[2,20,4,128]{3,2,1,0:T(4,128)S(1)} %get-tuple-element.15), channel_id=1, source_target_pairs={{0,4},{1,5},{2,6},{3,7},{4,0},{5,1},{6,2},{7,3},{8,12},{9,13},{10,... | collective-permute-start | bytes 245768 | tf_op jit(solution)/shard_map/ppermute | solution.py:282
  69.4 19.4 %collective-permute-start.8 = (f32[2,20,4,128]{3,2,1,0:T(4,128)S(1)}, f32[2,20,4,128]{3,2,1,0:T(4,128)}, u32[]{:S(2)}, u32[]{:S(2)}) collective-permute-start(f32[2,20,4,128]{3,2,1,0:T(4,128)S(1)} %get-tuple-element.14), channel_id=1, source_target_pairs={{0,6},{1,7},{2,0},{3,1},{4,2},{5,3},{6,4},{7,5},{8,14},{9,15},{10,... | collective-permute-start | bytes 245768 | tf_op jit(solution)/shard_map/ppermute | solution.py:282

commit v6 on v4

--- a/solution.py
+++ b/solution.py
@@ -37,19 +37,22 @@
     n = lax.axis_size("space")
     count, ny, width = fields.shape
     spare = lanes - width
-    flat = fields.reshape(count * ny, width)
-    edges = contract(picker(width, [width - 2, width - 1, 0, 1]), flat, ((0,), (1,)))
+    mirrored = fields[:, ny - 1:ny - 3:-1, ::-1]
+    ghost = shifted(mirrored, [(q, n - 1 - q) for q in range(n)])
+    pick = picker(width, [width - 2, width - 1, 0, 1])
+    edges = jnp.concatenate(
+        [
+            contract(pick, fields.reshape(count * ny, width), ((0,), (1,))),
+            contract(pick, ghost.reshape(count * 2, width), ((0,), (1,))),
+        ],
+        axis=1,
+    )
     west = shifted(edges[0:2], [(q, (q + 1) % n) for q in range(n)])
     east = shifted(edges[2:4], [(q, (q - 1) % n) for q in range(n)])
-    mirrored = fields[:, ny - 1:ny - 3:-1, ::-1]
-    ghost = shifted(mirrored, [(q, n - 1 - q) for q in range(n)])
-    top_edges = edges.reshape(4, count, ny)[:, :, ny - 1:ny - 3:-1]
-    ghost_east = shifted(top_edges[1::-1], [(q, (n - 2 - q) % n) for q in range(n)])
-    ghost_west = shifted(top_edges[3:1:-1], [(q, (n - q) % n) for q in range(n)])
     place = picker(spare, [0, 1, spare - 2, spare - 1]).T
-    side = contract(jnp.concatenate([east, west]), place, ((0,), (0,))).reshape(count, ny, spare)
-    ghost_halo = jnp.concatenate([ghost_east, ghost_west]).reshape(4, count * 2)
-    ghost_side = contract(ghost_halo, place, ((0,), (0,))).reshape(count, 2, spare)
+    halo = jnp.concatenate([east, west])
+    side = contract(halo[:, :count * ny], place, ((0,), (0,))).reshape(count, ny, spare)
+    ghost_side = contract(halo[:, count * ny:], place, ((0,), (0,))).reshape(count, 2, spare)
     top = jnp.concatenate([fields, side], axis=-1)
     folded = jnp.concatenate([ghost, ghost_side], axis=-1)
     pad = jnp.zeros((count, rows - ny - 2, lanes), fields.dtype)

time: 84.6 us -> 84.2 us (level)
  waiting for transfers between devices: 10.9 us -> 14.3 us
  starting transfers between devices: 12.9 us -> 9.77 us
  local copies, waits for them, and re-layouts: 4.71 us -> 3.74 us
    ppermute x5 -> x3, waiting for transfers between devices: 1.94 us -> 5.35 us  [shifted(): return lax.ppermute(x, 'space', perm)]
    ppermute x5 -> x3, starting transfers between devices: 8.58 us -> 5.45 us  [shifted(): return lax.ppermute(x, 'space', perm)]
    dot_general x3 -> x4, matrix products: 2.96 us -> 3.31 us  [contract(): lax.dot_general(a, b, (dims, ((), ())), precision=lax.Precision.HIGHEST,...]
  transfers between devices with their start and end apart: 9 -> 7, of which waited for: 5 -> 6; matrix products, arithmetic and copies ran while one was open for 4% -> 1% of each run, Pallas kernels for 0% -> 0%
where the time goes in v6:
time: 84.2 us; the launch traced here: 84 us
  Pallas kernels  33.7 us (40%)
  blocking collectives  16.8 us (20%)
  waiting for transfers between devices  14.3 us (17%)
  starting transfers between devices  9.77 us (12%)
  local copies, waits for them, and re-layouts  3.74 us (4%)
  matrix products  3.31 us (4%)
  other arithmetic  1.53 us (2%)
    pallas_call x1, Pallas kernels, on_device(): pl.pallas_call(diffusion_kernel, out_shape=(field, field, jax.ShapeDtypeS...  33.7 us
    all_gather x1, blocking collectives, on_device(): full_kappa = lax.all_gather(diffusivity, 'scen', axis=2, tiled=True)  16.8 us
    ppermute x3, waiting for transfers between devices, summed_over_scen(): lax.ppermute(send, 'scen', [(q, (q // 2 + step) % chips * 2 + q % 2) for...  7.38 us
    ppermute x3, starting transfers between devices, shifted(): return lax.ppermute(x, 'space', perm)  5.45 us
    ppermute x3, waiting for transfers between devices, shifted(): return lax.ppermute(x, 'space', perm)  5.35 us
    ppermute x3, starting transfers between devices, summed_over_scen(): lax.ppermute(send, 'scen', [(q, (q // 2 + step) % chips * 2 + q % 2) for...  4.25 us
    dot_general x4, matrix products, contract(): lax.dot_general(a, b, (dims, ((), ())), precision=lax.Precision.HIGHEST,...  3.31 us
    unnamed x10, local copies, waits for them, and re-layouts  2.71 us
  transfers between devices with their start and end apart: 7, of which 6 were waited for; matrix products, arithmetic and copies ran while one was open for 1% of the time, Pallas kernels for 0%

profile of v6, /device:TPU:0, one launch (start us, length us, event | category | flops | bytes accessed | tf_op | source)
XLA Modules:
  0.0 84.0 jit_solution(11368585884995904730)
XLA Ops:
  0.6 0.0 copy-start
  0.6 1.2 %constant_dynamic-update-slice_fusion.2 = f32[122,32,128]{2,1,0:T(8,128)S(1)} fusion(f32[40,32,128]{2,1,0:T(8,128)} %bitcast.43), kind=kLoop, calls=%fused_computation.21 | loop fusion | bytes 1310720
  1.8 0.9 %copy.14 = f32[2,20,4,128]{3,0,1,2:T(2,128)S(1)} copy(f32[2,20,4,128]{3,2,1,0:T(4,128)} %param.6) | data formatting | bytes 163840 | tf_op args[1]
  2.8 16.8 %all_gather.3 = f32[2,20,32,128]{3,0,1,2:T(2,128)S(1)} all-gather(f32[2,20,4,128]{3,0,1,2:T(2,128)S(1)} %copy.14), channel_id=1, replica_groups=mesh['space'=4,'scen'=8] {'scen'}, dimensions={2}, use_global_device_ids=true | all-gather | bytes 737280 | tf_op jit(solution)/shard_map/all_gather | solution.py:205
  19.6 0.0 copy-start.1
  19.6 0.0 copy-start.2
  19.6 0.1 copy.15
  19.7 0.0 copy-done
  19.9 0.5 copy-done.1
  20.3 0.0 copy-done.2
  20.3 0.1 slice.20
  20.4 0.5 rev.3
  20.9 2.5 %collective-permute-start = (f32[122,2,128]{2,1,0:T(2,128)S(1)}, f32[122,2,128]{2,1,0:T(2,128)S(1)}, u32[]{:S(2)}, u32[]{:S(2)}) collective-permute-start(f32[122,2,128]{2,1,0:T(2,128)S(1)} %rev.3), channel_id=1, source_target_pairs={{0,24},{8,16},{16,8},{24,0},{1,25},{9,17},{17,9},{25,1},{2,26},{10... | collective-permute-start | bytes 374792 | tf_op jit(solution)/shard_map/ppermute | solution.py:18
  23.5 0.1 and_or_fusion.1
  23.5 1.0 %fusion.10 = f32[4,3904]{1,0:T(4,128)S(1)} fusion(pred[128,4]{0,1:T(4,128)(4,1)S(1)} %get-tuple-element.14, f32[3904,128]{1,0:T(8,128)S(1)} %bitcast.40), kind=kOutput, calls=%fused_computation.37 | convolution fusion | flops 23986176 | bytes 2061824 | tf_op jit(solution)/shard_map/dot_general | solution.py:31
  24.5 2.9 %collective-permute-done = f32[122,2,128]{2,1,0:T(2,128)S(1)} collective-permute-done((f32[122,2,128]{2,1,0:T(2,128)S(1)}, f32[122,2,128]{2,1,0:T(2,128)S(1)}, u32[]{:S(2)}, u32[]{:S(2)}) %collective-permute-start) | collective-permute-done | bytes 124960 | tf_op jit(solution)/shard_map/ppermute | solution.py:18
  27.5 0.1 reshape.26
  27.6 0.2 fusion.11
  27.7 0.2 fusion.5
  27.9 1.5 %collective-permute-start.2 = (f32[2,4148]{1,0:T(2,128)S(1)}, f32[2,4148]{1,0:T(2,128)S(1)}, u32[]{:S(2)}, u32[]{:S(2)}) collective-permute-start(f32[2,4148]{1,0:T(2,128)S(1)} %get-tuple-element.13), channel_id=1, source_target_pairs={{0,8},{8,16},{16,24},{24,0},{1,9},{9,17},{17,25},{25,1},{2,10},{10... | collective-permute-start | bytes 99560 | tf_op jit(solution)/shard_map/ppermute | solution.py:18
  29.4 1.4 %collective-permute-start.1 = (f32[2,4148]{1,0:T(2,128)S(1)}, f32[2,4148]{1,0:T(2,128)S(1)}, u32[]{:S(2)}, u32[]{:S(2)}) collective-permute-start(f32[2,4148]{1,0:T(2,128)S(1)} %get-tuple-element.12), channel_id=1, source_target_pairs={{0,24},{8,0},{16,8},{24,16},{1,25},{9,1},{17,9},{25,17},{2,26},{10... | collective-permute-start | bytes 99560 | tf_op jit(solution)/shard_map/ppermute | solution.py:18
  30.9 0.1 pad.4.clone
  30.9 2.0 %collective-permute-done.2 = f32[2,4148]{1,0:T(2,128)S(1)} collective-permute-done((f32[2,4148]{1,0:T(2,128)S(1)}, f32[2,4148]{1,0:T(2,128)S(1)}, u32[]{:S(2)}, u32[]{:S(2)}) %collective-permute-start.2) | collective-permute-done | bytes 33216 | tf_op jit(solution)/shard_map/ppermute | solution.py:18
  33.0 0.4 collective-permute-done.1
  33.3 0.4 fusion.6
  33.7 0.1 reshape.28
  33.8 1.7 %fusion.3 = f32[3904,128]{1,0:T(8,128)S(1)} fusion(pred[128,4]{0,1:T(4,128)(4,1)S(1)} %get-tuple-element.15, f32[2,4148]{1,0:T(2,128)S(1)} %collective-permute-done.1, f32[2,4148]{1,0:T(2,128)S(1)} %collective-permute-done.2), kind=kOutput, calls=%fused_computation.14 | convolution fusion | flops 24001792 | bytes 2065728 | tf_op jit(solution)/shard_map/dot_general | solution.py:31
  35.6 0.5 maximum_maximum_fusion.x_ref
  36.1 33.7 %shard_map.76 = (f32[2,20,32,128]{3,2,1,0:T(8,128)}, f32[2,20,32,128]{3,2,1,0:T(8,128)}, f32[2,20,32,128]{3,2,1,0:T(8,128)S(1)}) custom-call(f32[122,40,256]{2,1,0:T(8,128)S(1)} %maximum_maximum_fusion.x_ref), custom_call_target="tpu_custom_call" | custom-call | tf_op jit(solution)/shard_map/pallas_call | solution.py:219
  69.7 0.1 dynamic-slice_bitcast_fusion
  69.8 0.1 collective-permute-start.3
  70.0 1.5 %collective-permute-done.3 = f32[2,20,4,4,128]{4,3,2,1,0:T(4,128)S(1)} collective-permute-done((f32[2,20,4,4,128]{4,3,2,1,0:T(4,128)S(1)}, f32[2,20,4,4,128]{4,3,2,1,0:T(4,128)S(1)}, u32[]{:S(2)}, u32[]{:S(2)}) %collective-permute-start.3) | collective-permute-done | bytes 327712 | tf_op jit(solution)/shard_map/ppermute | solution.py:254
  71.5 0.1 bitcast_add_fusion
  71.6 0.1 dynamic-slice_bitcast_fusion.3
  71.6 3.6 %collective-permute-start.6 = (f32[2,20,4,128]{3,2,1,0:T(4,128)S(1)}, f32[2,20,4,128]{3,2,1,0:T(4,128)S(1)}, u32[]{:S(2)}, u32[]{:S(2)}) collective-permute-start(f32[2,20,4,128]{3,2,1,0:T(4,128)S(1)} %get-tuple-element.10), channel_id=1, source_target_pairs={{0,6},{1,7},{2,0},{3,1},{4,2},{5,3},{6,4},{7,5},{8,14},{9,15},{10,... | collective-permute-start | bytes 245768 | tf_op jit(solution)/shard_map/ppermute | solution.py:259
  75.3 0.0 collective-permute-start.5
  75.3 0.6 collective-permute-start.4
  75.9 2.2 %collective-permute-done.6 = f32[2,20,4,128]{3,2,1,0:T(4,128)S(1)} collective-permute-done((f32[2,20,4,128]{3,2,1,0:T(4,128)S(1)}, f32[2,20,4,128]{3,2,1,0:T(4,128)S(1)}, u32[]{:S(2)}, u32[]{:S(2)}) %collective-permute-start.6) | collective-permute-done | bytes 81952 | tf_op jit(solution)/shard_map/ppermute | solution.py:259
  78.1 5.2 %collective-permute-done.5 = f32[2,20,4,128]{3,2,1,0:T(4,128)S(1)} collective-permute-done((f32[2,20,4,128]{3,2,1,0:T(4,128)S(1)}, f32[2,20,4,128]{3,2,1,0:T(4,128)S(1)}, u32[]{:S(2)}, u32[]{:S(2)}) %collective-permute-start.5) | collective-permute-done | bytes 81952 | tf_op jit(solution)/shard_map/ppermute | solution.py:259
  83.3 0.0 collective-permute-done.4
  83.3 0.7 fusion.1
  (9 shorter events, 0.1 us)
Async XLA Ops:
  0.6 19.1 %copy-start = (f32[1,2,20,32,128]{4,3,2,1,0:T(8,128)S(1)}, f32[1,2,20,32,128]{4,3,2,1,0:T(8,128)}, u32[]{:S(2)}) copy-start(f32[1,2,20,32,128]{4,3,2,1,0:T(8,128)} %param.9) | copy-start | bytes 1966084
  19.6 0.7 copy-start.1
  19.6 0.7 copy-start.2
  20.9 6.6 %collective-permute-start = (f32[122,2,128]{2,1,0:T(2,128)S(1)}, f32[122,2,128]{2,1,0:T(2,128)S(1)}, u32[]{:S(2)}, u32[]{:S(2)}) collective-permute-start(f32[122,2,128]{2,1,0:T(2,128)S(1)} %rev.3), channel_id=1, source_target_pairs={{0,24},{8,16},{16,8},{24,0},{1,25},{9,17},{17,9},{25,1},{2,26},{10... | collective-permute-start | bytes 374792 | tf_op jit(solution)/shard_map/ppermute | solution.py:18
  27.9 5.0 %collective-permute-start.2 = (f32[2,4148]{1,0:T(2,128)S(1)}, f32[2,4148]{1,0:T(2,128)S(1)}, u32[]{:S(2)}, u32[]{:S(2)}) collective-permute-start(f32[2,4148]{1,0:T(2,128)S(1)} %get-tuple-element.13), channel_id=1, source_target_pairs={{0,8},{8,16},{16,24},{24,0},{1,9},{9,17},{17,25},{25,1},{2,10},{10... | collective-permute-start | bytes 99560 | tf_op jit(solution)/shard_map/ppermute | solution.py:18
  29.4 3.9 %collective-permute-start.1 = (f32[2,4148]{1,0:T(2,128)S(1)}, f32[2,4148]{1,0:T(2,128)S(1)}, u32[]{:S(2)}, u32[]{:S(2)}) collective-permute-start(f32[2,4148]{1,0:T(2,128)S(1)} %get-tuple-element.12), channel_id=1, source_target_pairs={{0,24},{8,0},{16,8},{24,16},{1,25},{9,1},{17,9},{25,17},{2,26},{10... | collective-permute-start | bytes 99560 | tf_op jit(solution)/shard_map/ppermute | solution.py:18
  69.8 1.7 %collective-permute-start.3 = (f32[2,20,4,4,128]{4,3,2,1,0:T(4,128)S(1)}, f32[2,20,4,4,128]{4,3,2,1,0:T(4,128)S(1)}, u32[]{:S(2)}, u32[]{:S(2)}) collective-permute-start(f32[2,20,4,4,128]{4,3,2,1,0:T(4,128)S(1)} %dynamic-slice_bitcast_fusion), channel_id=1, source_target_pairs={{0,1},{1,0},{2,3},{3,2},{4,5},{5,4},{6,7},{7,6},{8,9},{9,8},{10,11... | collective-permute-start | bytes 983048 | tf_op jit(solution)/shard_map/ppermute | solution.py:254
  71.6 6.5 %collective-permute-start.6 = (f32[2,20,4,128]{3,2,1,0:T(4,128)S(1)}, f32[2,20,4,128]{3,2,1,0:T(4,128)S(1)}, u32[]{:S(2)}, u32[]{:S(2)}) collective-permute-start(f32[2,20,4,128]{3,2,1,0:T(4,128)S(1)} %get-tuple-element.10), channel_id=1, source_target_pairs={{0,6},{1,7},{2,0},{3,1},{4,2},{5,3},{6,4},{7,5},{8,14},{9,15},{10,... | collective-permute-start | bytes 245768 | tf_op jit(solution)/shard_map/ppermute | solution.py:259
  75.3 8.0 %collective-permute-start.5 = (f32[2,20,4,128]{3,2,1,0:T(4,128)S(1)}, f32[2,20,4,128]{3,2,1,0:T(4,128)S(1)}, u32[]{:S(2)}, u32[]{:S(2)}) collective-permute-start(f32[2,20,4,128]{3,2,1,0:T(4,128)S(1)} %get-tuple-element.11), channel_id=1, source_target_pairs={{0,4},{1,5},{2,6},{3,7},{4,0},{5,1},{6,2},{7,3},{8,12},{9,13},{10,... | collective-permute-start | bytes 245768 | tf_op jit(solution)/shard_map/ppermute | solution.py:259
  75.3 8.0 %collective-permute-start.4 = (f32[2,20,4,128]{3,2,1,0:T(4,128)S(1)}, f32[2,20,4,128]{3,2,1,0:T(4,128)S(1)}, u32[]{:S(2)}, u32[]{:S(2)}) collective-permute-start(f32[2,20,4,128]{3,2,1,0:T(4,128)S(1)} %get-tuple-element.9), channel_id=1, source_target_pairs={{0,2},{1,3},{2,4},{3,5},{4,6},{5,7},{6,0},{7,1},{8,10},{9,11},{10,... | collective-permute-start | bytes 245768 | tf_op jit(solution)/shard_map/ppermute | solution.py:259

commit v7 on v6

--- a/solution.py
+++ b/solution.py
@@ -78,12 +78,12 @@
     x_ref,
     fin_ref, adj_ref, grad_ref,
     wet_ref, ce_ref, cn_ref, cz_ref, src_ref, gem_ref, gnm_ref, u1_ref, a_ref, b_ref,
+    du0e_ref, du0n_ref, du1e_ref, du1n_ref, dv1e_ref, dv1n_ref, dv2e_ref, dv2n_ref,
 ):
     levels, rows, lanes = wet_ref.shape
     chans, _, ny, width = fin_ref.shape
     row = lax.broadcasted_iota(jnp.int32, (rows, lanes), 0)
     lane = lax.broadcasted_iota(jnp.int32, (rows, lanes), 1)
-    owned = (row < ny) & (lane < width)
     planes = chans * levels
     ue_ref = Planes(x_ref, 0, levels)
     ve_ref = Planes(x_ref, planes, levels)
@@ -115,20 +115,25 @@
         cz_ref[k + 1] = vertical_rate * w * w_next
         src_ref[k] = thaw_rate * shelf * w * (1.0 - w_next)
         wet_ref[k] = w
-        gem_ref[k] = jnp.where(owned, east_mask, 0.0)
-        gnm_ref[k] = jnp.where(
-            owned, jnp.where(row < ny - 1, north_mask, jnp.where(row == ny - 1, 0.5 * north_mask, 0.0)), 0.0
-        )
+        gem_ref[k] = east_mask[:ny, :width]
+        gnm_ref[k] = jnp.where(row < ny - 1, north_mask, 0.5 * north_mask)[:ny, :width]
+        for c in range(chans):
+            a_ref[c, k] = w * ve_ref[c, k]
         return carry
 
     lax.fori_loop(0, levels, setup, 0)
 
-    def operate(x_ref, c, k):
+    def operate(x_ref, c, k, diffs=None):
         x = x_ref[c, k]
         above = x_ref[c, jnp.minimum(k + 1, levels - 1)]
         below = x_ref[c, jnp.maximum(k - 1, 0)]
-        east = ce_ref[k] * (roll(x, -1, 1) - x)
-        north = cn_ref[k] * (roll(x, -1, 0) - x)
+        d_east = roll(x, -1, 1) - x
+        d_north = roll(x, -1, 0) - x
+        if diffs is not None:
+            diffs[0][c, k] = d_east[:ny, :width]
+            diffs[1][c, k] = d_north[:ny, :width]
+        east = ce_ref[k] * d_east
+        north = cn_ref[k] * d_north
         change = (east - roll(east, 1, 1)) + (north - roll(north, 1, 0))
         change = change + (cz_ref[k + 1] * (above - x) - cz_ref[k] * (x - below))
         return x, change
@@ -136,7 +141,7 @@
     def forward_first(ck, carry):
         c = ck // levels
         k = ck % levels
-        x, change = operate(ue_ref, c, k)
+        x, change = operate(ue_ref, c, k, (du0e_ref, du0n_ref))
         heat = jnp.where(c == 0, 1.0, 0.0)
         u1_ref[c, k] = wet_ref[k] * (x + change + heat * src_ref[k])
         return carry
@@ -146,7 +151,7 @@
     def forward_second(ck, carry):
         c = ck // levels
         k = ck % levels
-        x, change = operate(u1_ref, c, k)
+        x, change = operate(u1_ref, c, k, (du1e_ref, du1n_ref))
         heat = jnp.where(c == 0, 1.0, 0.0)
         out = wet_ref[k] * (x + change + heat * src_ref[k])
         fin_ref[c, k] = out[:ny, :width]
@@ -154,18 +159,10 @@
 
     lax.fori_loop(0, planes, forward_second, 0)
 
-    def weigh(ck, carry):
-        c = ck // levels
-        k = ck % levels
-        a_ref[c, k] = wet_ref[k] * ve_ref[c, k]
-        return carry
-
-    lax.fori_loop(0, planes, weigh, 0)
-
     def backward_second(ck, carry):
         c = ck // levels
         k = ck % levels
-        x, change = operate(a_ref, c, k)
+        x, change = operate(a_ref, c, k, (dv2e_ref, dv2n_ref))
         b_ref[c, k] = wet_ref[k] * (x + change)
         return carry
 
@@ -174,25 +171,20 @@
     def backward_first(ck, carry):
         c = ck // levels
         k = ck % levels
-        x, change = operate(b_ref, c, k)
+        x, change = operate(b_ref, c, k, (dv1e_ref, dv1n_ref))
         adj_ref[c, k] = (x + change)[:ny, :width]
         return carry
 
     lax.fori_loop(0, planes, backward_first, 0)
 
     def gradient(k, carry):
-        gem = gem_ref[k]
-        gnm = gnm_ref[k]
-        g_east = jnp.zeros((rows, lanes), jnp.float32)
-        g_north = jnp.zeros((rows, lanes), jnp.float32)
-        for c in range(2):
-            for u_ref, v_ref in ((ue_ref, b_ref), (u1_ref, a_ref)):
-                u = u_ref[c, k]
-                v = v_ref[c, k]
-                g_east = g_east + (roll(u, -1, 1) - u) * (v - roll(v, -1, 1))
-                g_north = g_north + (roll(u, -1, 0) - u) * (v - roll(v, -1, 0))
-        grad_ref[0, k] = (gem * g_east)[:ny, :width]
-        grad_ref[1, k] = (gnm * g_north)[:ny, :width]
+        g_east = jnp.zeros((ny, width), jnp.float32)
+        g_north = jnp.zeros((ny, width), jnp.float32)
+        for c in range(chans):
+            g_east = g_east - du0e_ref[c, k] * dv1e_ref[c, k] - du1e_ref[c, k] * dv2e_ref[c, k]
+            g_north = g_north - du0n_ref[c, k] * dv1n_ref[c, k] - du1n_ref[c, k] * dv2n_ref[c, k]
+        grad_ref[0, k] = gem_ref[k] * g_east
+        grad_ref[1, k] = gnm_ref[k] * g_north
         return carry
 
     lax.fori_loop(0, levels, gradient, 0)
@@ -216,6 +208,8 @@
     field = jax.ShapeDtypeStruct((chans, levels, ny, width), jnp.float32)
     plane = pltpu.VMEM((levels, rows, lanes), jnp.float32)
     planes_c = pltpu.VMEM((chans, levels, rows, lanes), jnp.float32)
+    diff = pltpu.VMEM((chans, levels, ny, width), jnp.float32)
+    mask = pltpu.VMEM((levels, ny, width), jnp.float32)
     final, adjoint, grad = pl.pallas_call(
         diffusion_kernel,
         out_shape=(field, field, jax.ShapeDtypeStruct((2, levels, ny, width), jnp.float32)),
@@ -225,12 +219,13 @@
             plane,
             pltpu.VMEM((levels + 1, rows, lanes), jnp.float32),
             plane,
-            plane,
-            plane,
+            mask,
+            mask,
             planes_c,
             planes_c,
             planes_c,
-        ],
+        ]
+        + [diff] * 8,
         compiler_params=pltpu.CompilerParams(vmem_limit_bytes=48 * 1024 * 1024),
         interpret=INTERPRET,
     )(ext)

time: 84.2 us -> 80.8 us (0.960)
  Pallas kernels: 33.7 us -> 30.2 us
    pallas_call x1, Pallas kernels: 33.7 us -> 30.2 us  [on_device(): pl.pallas_call(diffusion_kernel, out_shape=(field, field, jax.ShapeDtypeS...]
where the time goes in v7:
time: 80.8 us; the launch traced here: 80.5 us
  Pallas kernels  30.2 us (37%)
  blocking collectives  16.8 us (21%)
  waiting for transfers between devices  14.3 us (18%)
  starting transfers between devices  9.77 us (12%)
  local copies, waits for them, and re-layouts  3.74 us (5%)
  matrix products  3.31 us (4%)
  other arithmetic  1.53 us (2%)
  between operations  0.84 us (1%)
    pallas_call x1, Pallas kernels, on_device(): pl.pallas_call(diffusion_kernel, out_shape=(field, field, jax.ShapeDtypeS...  30.2 us
    all_gather x1, blocking collectives, on_device(): full_kappa = lax.all_gather(diffusivity, 'scen', axis=2, tiled=True)  16.8 us
    ppermute x3, waiting for transfers between devices, summed_over_scen(): lax.ppermute(send, 'scen', [(q, (q // 2 + step) % chips * 2 + q % 2) for...  7.38 us
    ppermute x3, starting transfers between devices, shifted(): return lax.ppermute(x, 'space', perm)  5.45 us
    ppermute x3, waiting for transfers between devices, shifted(): return lax.ppermute(x, 'space', perm)  5.35 us
    ppermute x3, starting transfers between devices, summed_over_scen(): lax.ppermute(send, 'scen', [(q, (q // 2 + step) % chips * 2 + q % 2) for...  4.25 us
    dot_general x4, matrix products, contract(): lax.dot_general(a, b, (dims, ((), ())), precision=lax.Precision.HIGHEST,...  3.31 us
    unnamed x10, local copies, waits for them, and re-layouts  2.71 us
  transfers between devices with their start and end apart: 7, of which 6 were waited for; matrix products, arithmetic and copies ran while one was open for 1% of the time, Pallas kernels for 0%

profile of v7, /device:TPU:0, one launch (start us, length us, event | category | flops | bytes accessed | tf_op | source)
XLA Modules:
  0.0 80.5 jit_solution(15185816877619955748)
XLA Ops:
  0.6 0.0 copy-start
  0.6 1.2 %constant_dynamic-update-slice_fusion.2 = f32[122,32,128]{2,1,0:T(8,128)S(1)} fusion(f32[40,32,128]{2,1,0:T(8,128)} %bitcast.43), kind=kLoop, calls=%fused_computation.21 | loop fusion | bytes 1310720
  1.8 0.9 %copy.14 = f32[2,20,4,128]{3,0,1,2:T(2,128)S(1)} copy(f32[2,20,4,128]{3,2,1,0:T(4,128)} %param.6) | data formatting | bytes 163840 | tf_op args[1]
  2.8 16.8 %all_gather.3 = f32[2,20,32,128]{3,0,1,2:T(2,128)S(1)} all-gather(f32[2,20,4,128]{3,0,1,2:T(2,128)S(1)} %copy.14), channel_id=1, replica_groups=mesh['space'=4,'scen'=8] {'scen'}, dimensions={2}, use_global_device_ids=true | all-gather | bytes 737280 | tf_op jit(solution)/shard_map/all_gather | solution.py:197
  19.6 0.0 copy-start.1
  19.6 0.0 copy-start.2
  19.6 0.1 copy.15
  19.7 0.0 copy-done
  19.9 0.5 copy-done.1
  20.3 0.0 copy-done.2
  20.3 0.1 slice.20
  20.4 0.5 rev.3
  20.9 2.5 %collective-permute-start = (f32[122,2,128]{2,1,0:T(2,128)S(1)}, f32[122,2,128]{2,1,0:T(2,128)S(1)}, u32[]{:S(2)}, u32[]{:S(2)}) collective-permute-start(f32[122,2,128]{2,1,0:T(2,128)S(1)} %rev.3), channel_id=1, source_target_pairs={{0,24},{8,16},{16,8},{24,0},{1,25},{9,17},{17,9},{25,1},{2,26},{10... | collective-permute-start | bytes 374792 | tf_op jit(solution)/shard_map/ppermute | solution.py:18
  23.5 0.1 and_or_fusion.1
  23.5 1.0 %fusion.10 = f32[4,3904]{1,0:T(4,128)S(1)} fusion(pred[128,4]{0,1:T(4,128)(4,1)S(1)} %get-tuple-element.14, f32[3904,128]{1,0:T(8,128)S(1)} %bitcast.40), kind=kOutput, calls=%fused_computation.37 | convolution fusion | flops 23986176 | bytes 2061824 | tf_op jit(solution)/shard_map/dot_general | solution.py:31
  24.5 2.9 %collective-permute-done = f32[122,2,128]{2,1,0:T(2,128)S(1)} collective-permute-done((f32[122,2,128]{2,1,0:T(2,128)S(1)}, f32[122,2,128]{2,1,0:T(2,128)S(1)}, u32[]{:S(2)}, u32[]{:S(2)}) %collective-permute-start) | collective-permute-done | bytes 124960 | tf_op jit(solution)/shard_map/ppermute | solution.py:18
  27.5 0.1 reshape.26
  27.6 0.2 fusion.11
  27.7 0.2 fusion.5
  27.9 1.5 %collective-permute-start.2 = (f32[2,4148]{1,0:T(2,128)S(1)}, f32[2,4148]{1,0:T(2,128)S(1)}, u32[]{:S(2)}, u32[]{:S(2)}) collective-permute-start(f32[2,4148]{1,0:T(2,128)S(1)} %get-tuple-element.13), channel_id=1, source_target_pairs={{0,8},{8,16},{16,24},{24,0},{1,9},{9,17},{17,25},{25,1},{2,10},{10... | collective-permute-start | bytes 99560 | tf_op jit(solution)/shard_map/ppermute | solution.py:18
  29.4 1.4 %collective-permute-start.1 = (f32[2,4148]{1,0:T(2,128)S(1)}, f32[2,4148]{1,0:T(2,128)S(1)}, u32[]{:S(2)}, u32[]{:S(2)}) collective-permute-start(f32[2,4148]{1,0:T(2,128)S(1)} %get-tuple-element.12), channel_id=1, source_target_pairs={{0,24},{8,0},{16,8},{24,16},{1,25},{9,1},{17,9},{25,17},{2,26},{10... | collective-permute-start | bytes 99560 | tf_op jit(solution)/shard_map/ppermute | solution.py:18
  30.9 0.1 pad.4.clone
  30.9 2.0 %collective-permute-done.2 = f32[2,4148]{1,0:T(2,128)S(1)} collective-permute-done((f32[2,4148]{1,0:T(2,128)S(1)}, f32[2,4148]{1,0:T(2,128)S(1)}, u32[]{:S(2)}, u32[]{:S(2)}) %collective-permute-start.2) | collective-permute-done | bytes 33216 | tf_op jit(solution)/shard_map/ppermute | solution.py:18
  33.0 0.4 collective-permute-done.1
  33.3 0.4 fusion.6
  33.7 0.1 reshape.28
  33.8 1.7 %fusion.3 = f32[3904,128]{1,0:T(8,128)S(1)} fusion(pred[128,4]{0,1:T(4,128)(4,1)S(1)} %get-tuple-element.15, f32[2,4148]{1,0:T(2,128)S(1)} %collective-permute-done.1, f32[2,4148]{1,0:T(2,128)S(1)} %collective-permute-done.2), kind=kOutput, calls=%fused_computation.14 | convolution fusion | flops 24001792 | bytes 2065728 | tf_op jit(solution)/shard_map/dot_general | solution.py:31
  35.6 0.5 maximum_maximum_fusion.x_ref
  36.1 30.2 %shard_map.76 = (f32[2,20,32,128]{3,2,1,0:T(8,128)}, f32[2,20,32,128]{3,2,1,0:T(8,128)}, f32[2,20,32,128]{3,2,1,0:T(8,128)S(1)}) custom-call(f32[122,40,256]{2,1,0:T(8,128)S(1)} %maximum_maximum_fusion.x_ref), custom_call_target="tpu_custom_call" | custom-call | tf_op jit(solution)/shard_map/pallas_call | solution.py:213
  66.3 0.1 dynamic-slice_bitcast_fusion
  66.4 0.1 collective-permute-start.3
  66.5 1.5 %collective-permute-done.3 = f32[2,20,4,4,128]{4,3,2,1,0:T(4,128)S(1)} collective-permute-done((f32[2,20,4,4,128]{4,3,2,1,0:T(4,128)S(1)}, f32[2,20,4,4,128]{4,3,2,1,0:T(4,128)S(1)}, u32[]{:S(2)}, u32[]{:S(2)}) %collective-permute-start.3) | collective-permute-done | bytes 327712 | tf_op jit(solution)/shard_map/ppermute | solution.py:249
  68.1 0.1 bitcast_add_fusion
  68.2 0.1 dynamic-slice_bitcast_fusion.3
  68.2 3.6 %collective-permute-start.6 = (f32[2,20,4,128]{3,2,1,0:T(4,128)S(1)}, f32[2,20,4,128]{3,2,1,0:T(4,128)S(1)}, u32[]{:S(2)}, u32[]{:S(2)}) collective-permute-start(f32[2,20,4,128]{3,2,1,0:T(4,128)S(1)} %get-tuple-element.10), channel_id=1, source_target_pairs={{0,6},{1,7},{2,0},{3,1},{4,2},{5,3},{6,4},{7,5},{8,14},{9,15},{10,... | collective-permute-start | bytes 245768 | tf_op jit(solution)/shard_map/ppermute | solution.py:254
  71.8 0.0 collective-permute-start.5
  71.8 0.6 collective-permute-start.4
  72.5 2.2 %collective-permute-done.6 = f32[2,20,4,128]{3,2,1,0:T(4,128)S(1)} collective-permute-done((f32[2,20,4,128]{3,2,1,0:T(4,128)S(1)}, f32[2,20,4,128]{3,2,1,0:T(4,128)S(1)}, u32[]{:S(2)}, u32[]{:S(2)}) %collective-permute-start.6) | collective-permute-done | bytes 81952 | tf_op jit(solution)/shard_map/ppermute | solution.py:254
  74.7 5.2 %collective-permute-done.5 = f32[2,20,4,128]{3,2,1,0:T(4,128)S(1)} collective-permute-done((f32[2,20,4,128]{3,2,1,0:T(4,128)S(1)}, f32[2,20,4,128]{3,2,1,0:T(4,128)S(1)}, u32[]{:S(2)}, u32[]{:S(2)}) %collective-permute-start.5) | collective-permute-done | bytes 81952 | tf_op jit(solution)/shard_map/ppermute | solution.py:254
  79.9 0.0 collective-permute-done.4
  79.9 0.7 fusion.1
  (9 shorter events, 0.1 us)
Async XLA Ops:
  0.6 19.1 %copy-start = (f32[1,2,20,32,128]{4,3,2,1,0:T(8,128)S(1)}, f32[1,2,20,32,128]{4,3,2,1,0:T(8,128)}, u32[]{:S(2)}) copy-start(f32[1,2,20,32,128]{4,3,2,1,0:T(8,128)} %param.9) | copy-start | bytes 1966084
  19.6 0.7 copy-start.1
  19.6 0.7 copy-start.2
  20.9 6.6 %collective-permute-start = (f32[122,2,128]{2,1,0:T(2,128)S(1)}, f32[122,2,128]{2,1,0:T(2,128)S(1)}, u32[]{:S(2)}, u32[]{:S(2)}) collective-permute-start(f32[122,2,128]{2,1,0:T(2,128)S(1)} %rev.3), channel_id=1, source_target_pairs={{0,24},{8,16},{16,8},{24,0},{1,25},{9,17},{17,9},{25,1},{2,26},{10... | collective-permute-start | bytes 374792 | tf_op jit(solution)/shard_map/ppermute | solution.py:18
  27.9 5.0 %collective-permute-start.2 = (f32[2,4148]{1,0:T(2,128)S(1)}, f32[2,4148]{1,0:T(2,128)S(1)}, u32[]{:S(2)}, u32[]{:S(2)}) collective-permute-start(f32[2,4148]{1,0:T(2,128)S(1)} %get-tuple-element.13), channel_id=1, source_target_pairs={{0,8},{8,16},{16,24},{24,0},{1,9},{9,17},{17,25},{25,1},{2,10},{10... | collective-permute-start | bytes 99560 | tf_op jit(solution)/shard_map/ppermute | solution.py:18
  29.4 3.9 %collective-permute-start.1 = (f32[2,4148]{1,0:T(2,128)S(1)}, f32[2,4148]{1,0:T(2,128)S(1)}, u32[]{:S(2)}, u32[]{:S(2)}) collective-permute-start(f32[2,4148]{1,0:T(2,128)S(1)} %get-tuple-element.12), channel_id=1, source_target_pairs={{0,24},{8,0},{16,8},{24,16},{1,25},{9,1},{17,9},{25,17},{2,26},{10... | collective-permute-start | bytes 99560 | tf_op jit(solution)/shard_map/ppermute | solution.py:18
  66.4 1.7 %collective-permute-start.3 = (f32[2,20,4,4,128]{4,3,2,1,0:T(4,128)S(1)}, f32[2,20,4,4,128]{4,3,2,1,0:T(4,128)S(1)}, u32[]{:S(2)}, u32[]{:S(2)}) collective-permute-start(f32[2,20,4,4,128]{4,3,2,1,0:T(4,128)S(1)} %dynamic-slice_bitcast_fusion), channel_id=1, source_target_pairs={{0,1},{1,0},{2,3},{3,2},{4,5},{5,4},{6,7},{7,6},{8,9},{9,8},{10,11... | collective-permute-start | bytes 983048 | tf_op jit(solution)/shard_map/ppermute | solution.py:249
  68.2 6.5 %collective-permute-start.6 = (f32[2,20,4,128]{3,2,1,0:T(4,128)S(1)}, f32[2,20,4,128]{3,2,1,0:T(4,128)S(1)}, u32[]{:S(2)}, u32[]{:S(2)}) collective-permute-start(f32[2,20,4,128]{3,2,1,0:T(4,128)S(1)} %get-tuple-element.10), channel_id=1, source_target_pairs={{0,6},{1,7},{2,0},{3,1},{4,2},{5,3},{6,4},{7,5},{8,14},{9,15},{10,... | collective-permute-start | bytes 245768 | tf_op jit(solution)/shard_map/ppermute | solution.py:254
  71.8 8.0 %collective-permute-start.5 = (f32[2,20,4,128]{3,2,1,0:T(4,128)S(1)}, f32[2,20,4,128]{3,2,1,0:T(4,128)S(1)}, u32[]{:S(2)}, u32[]{:S(2)}) collective-permute-start(f32[2,20,4,128]{3,2,1,0:T(4,128)S(1)} %get-tuple-element.11), channel_id=1, source_target_pairs={{0,4},{1,5},{2,6},{3,7},{4,0},{5,1},{6,2},{7,3},{8,12},{9,13},{10,... | collective-permute-start | bytes 245768 | tf_op jit(solution)/shard_map/ppermute | solution.py:254
  71.8 8.0 %collective-permute-start.4 = (f32[2,20,4,128]{3,2,1,0:T(4,128)S(1)}, f32[2,20,4,128]{3,2,1,0:T(4,128)S(1)}, u32[]{:S(2)}, u32[]{:S(2)}) collective-permute-start(f32[2,20,4,128]{3,2,1,0:T(4,128)S(1)} %get-tuple-element.9), channel_id=1, source_target_pairs={{0,2},{1,3},{2,4},{3,5},{4,6},{5,7},{6,0},{7,1},{8,10},{9,11},{10,... | collective-permute-start | bytes 245768 | tf_op jit(solution)/shard_map/ppermute | solution.py:254

commit v8 on v7

--- a/solution.py
+++ b/solution.py
@@ -146,7 +146,7 @@
         u1_ref[c, k] = wet_ref[k] * (x + change + heat * src_ref[k])
         return carry
 
-    lax.fori_loop(0, planes, forward_first, 0)
+    lax.fori_loop(0, planes, forward_first, 0, unroll=2)
 
     def forward_second(ck, carry):
         c = ck // levels
@@ -157,7 +157,7 @@
         fin_ref[c, k] = out[:ny, :width]
         return carry
 
-    lax.fori_loop(0, planes, forward_second, 0)
+    lax.fori_loop(0, planes, forward_second, 0, unroll=2)
 
     def backward_second(ck, carry):
         c = ck // levels
@@ -166,7 +166,7 @@
         b_ref[c, k] = wet_ref[k] * (x + change)
         return carry
 
-    lax.fori_loop(0, planes, backward_second, 0)
+    lax.fori_loop(0, planes, backward_second, 0, unroll=2)
 
     def backward_first(ck, carry):
         c = ck // levels
@@ -175,7 +175,7 @@
         adj_ref[c, k] = (x + change)[:ny, :width]
         return carry
 
-    lax.fori_loop(0, planes, backward_first, 0)
+    lax.fori_loop(0, planes, backward_first, 0, unroll=2)
 
     def gradient(k, carry):
         g_east = jnp.zeros((ny, width), jnp.float32)

time: 80.8 us -> 68.3 us (0.85)
  Pallas kernels: 30.2 us -> 17.8 us
    pallas_call x1, Pallas kernels: 30.2 us -> 17.8 us  [on_device(): pl.pallas_call(diffusion_kernel, out_shape=(field, field, jax.ShapeDtypeS...]
  transfers between devices with their start and end apart: 7 -> 7, of which waited for: 6 -> 6; matrix products, arithmetic and copies ran while one was open for 1% -> 2% of each run, Pallas kernels for 0% -> 0%
where the time goes in v8:
time: 68.3 us; the launch traced here: 68.1 us
  Pallas kernels  17.8 us (26%)
  blocking collectives  16.8 us (25%)
  waiting for transfers between devices  14.3 us (21%)
  starting transfers between devices  9.77 us (14%)
  local copies, waits for them, and re-layouts  3.74 us (5%)
  matrix products  3.31 us (5%)
  other arithmetic  1.53 us (2%)
  between operations  0.84 us (1%)
    pallas_call x1, Pallas kernels, on_device(): pl.pallas_call(diffusion_kernel, out_shape=(field, field, jax.ShapeDtypeS...  17.8 us
    all_gather x1, blocking collectives, on_device(): full_kappa = lax.all_gather(diffusivity, 'scen', axis=2, tiled=True)  16.8 us
    ppermute x3, waiting for transfers between devices, summed_over_scen(): lax.ppermute(send, 'scen', [(q, (q // 2 + step) % chips * 2 + q % 2) for...  7.38 us
    ppermute x3, starting transfers between devices, shifted(): return lax.ppermute(x, 'space', perm)  5.45 us
    ppermute x3, waiting for transfers between devices, shifted(): return lax.ppermute(x, 'space', perm)  5.35 us
    ppermute x3, starting transfers between devices, summed_over_scen(): lax.ppermute(send, 'scen', [(q, (q // 2 + step) % chips * 2 + q % 2) for...  4.25 us
    dot_general x4, matrix products, contract(): lax.dot_general(a, b, (dims, ((), ())), precision=lax.Precision.HIGHEST,...  3.31 us
    unnamed x10, local copies, waits for them, and re-layouts  2.71 us
  transfers between devices with their start and end apart: 7, of which 6 were waited for; matrix products, arithmetic and copies ran while one was open for 2% of the time, Pallas kernels for 0%

profile of v8, /device:TPU:0, one launch (start us, length us, event | category | flops | bytes accessed | tf_op | source)
XLA Modules:
  0.0 68.1 jit_solution(9034885405434932062)
XLA Ops:
  0.6 0.0 copy-start
  0.6 1.2 %constant_dynamic-update-slice_fusion.2 = f32[122,32,128]{2,1,0:T(8,128)S(1)} fusion(f32[40,32,128]{2,1,0:T(8,128)} %bitcast.43), kind=kLoop, calls=%fused_computation.21 | loop fusion | bytes 1310720
  1.8 0.9 %copy.14 = f32[2,20,4,128]{3,0,1,2:T(2,128)S(1)} copy(f32[2,20,4,128]{3,2,1,0:T(4,128)} %param.6) | data formatting | bytes 163840 | tf_op args[1]
  2.8 16.8 %all_gather.3 = f32[2,20,32,128]{3,0,1,2:T(2,128)S(1)} all-gather(f32[2,20,4,128]{3,0,1,2:T(2,128)S(1)} %copy.14), channel_id=1, replica_groups=mesh['space'=4,'scen'=8] {'scen'}, dimensions={2}, use_global_device_ids=true | all-gather | bytes 737280 | tf_op jit(solution)/shard_map/all_gather | solution.py:197
  19.6 0.0 copy-start.1
  19.6 0.0 copy-start.2
  19.6 0.1 copy.15
  19.7 0.0 copy-done
  19.9 0.5 copy-done.1
  20.3 0.0 copy-done.2
  20.3 0.1 slice.20
  20.4 0.5 rev.3
  20.9 2.5 %collective-permute-start = (f32[122,2,128]{2,1,0:T(2,128)S(1)}, f32[122,2,128]{2,1,0:T(2,128)S(1)}, u32[]{:S(2)}, u32[]{:S(2)}) collective-permute-start(f32[122,2,128]{2,1,0:T(2,128)S(1)} %rev.3), channel_id=1, source_target_pairs={{0,24},{8,16},{16,8},{24,0},{1,25},{9,17},{17,9},{25,1},{2,26},{10... | collective-permute-start | bytes 374792 | tf_op jit(solution)/shard_map/ppermute | solution.py:18
  23.5 0.1 and_or_fusion.1
  23.5 1.0 %fusion.10 = f32[4,3904]{1,0:T(4,128)S(1)} fusion(pred[128,4]{0,1:T(4,128)(4,1)S(1)} %get-tuple-element.14, f32[3904,128]{1,0:T(8,128)S(1)} %bitcast.40), kind=kOutput, calls=%fused_computation.37 | convolution fusion | flops 23986176 | bytes 2061824 | tf_op jit(solution)/shard_map/dot_general | solution.py:31
  24.5 2.9 %collective-permute-done = f32[122,2,128]{2,1,0:T(2,128)S(1)} collective-permute-done((f32[122,2,128]{2,1,0:T(2,128)S(1)}, f32[122,2,128]{2,1,0:T(2,128)S(1)}, u32[]{:S(2)}, u32[]{:S(2)}) %collective-permute-start) | collective-permute-done | bytes 124960 | tf_op jit(solution)/shard_map/ppermute | solution.py:18
  27.5 0.1 reshape.26
  27.6 0.2 fusion.11
  27.7 0.2 fusion.5
  27.9 1.5 %collective-permute-start.2 = (f32[2,4148]{1,0:T(2,128)S(1)}, f32[2,4148]{1,0:T(2,128)S(1)}, u32[]{:S(2)}, u32[]{:S(2)}) collective-permute-start(f32[2,4148]{1,0:T(2,128)S(1)} %get-tuple-element.13), channel_id=1, source_target_pairs={{0,8},{8,16},{16,24},{24,0},{1,9},{9,17},{17,25},{25,1},{2,10},{10... | collective-permute-start | bytes 99560 | tf_op jit(solution)/shard_map/ppermute | solution.py:18
  29.4 1.4 %collective-permute-start.1 = (f32[2,4148]{1,0:T(2,128)S(1)}, f32[2,4148]{1,0:T(2,128)S(1)}, u32[]{:S(2)}, u32[]{:S(2)}) collective-permute-start(f32[2,4148]{1,0:T(2,128)S(1)} %get-tuple-element.12), channel_id=1, source_target_pairs={{0,24},{8,0},{16,8},{24,16},{1,25},{9,1},{17,9},{25,17},{2,26},{10... | collective-permute-start | bytes 99560 | tf_op jit(solution)/shard_map/ppermute | solution.py:18
  30.9 0.1 pad.4.clone
  30.9 2.0 %collective-permute-done.2 = f32[2,4148]{1,0:T(2,128)S(1)} collective-permute-done((f32[2,4148]{1,0:T(2,128)S(1)}, f32[2,4148]{1,0:T(2,128)S(1)}, u32[]{:S(2)}, u32[]{:S(2)}) %collective-permute-start.2) | collective-permute-done | bytes 33216 | tf_op jit(solution)/shard_map/ppermute | solution.py:18
  33.0 0.4 collective-permute-done.1
  33.3 0.4 fusion.6
  33.7 0.1 reshape.28
  33.8 1.7 %fusion.3 = f32[3904,128]{1,0:T(8,128)S(1)} fusion(pred[128,4]{0,1:T(4,128)(4,1)S(1)} %get-tuple-element.15, f32[2,4148]{1,0:T(2,128)S(1)} %collective-permute-done.1, f32[2,4148]{1,0:T(2,128)S(1)} %collective-permute-done.2), kind=kOutput, calls=%fused_computation.14 | convolution fusion | flops 24001792 | bytes 2065728 | tf_op jit(solution)/shard_map/dot_general | solution.py:31
  35.6 0.5 maximum_maximum_fusion.x_ref
  36.1 17.8 %shard_map.76 = (f32[2,20,32,128]{3,2,1,0:T(8,128)}, f32[2,20,32,128]{3,2,1,0:T(8,128)}, f32[2,20,32,128]{3,2,1,0:T(8,128)S(1)}) custom-call(f32[122,40,256]{2,1,0:T(8,128)S(1)} %maximum_maximum_fusion.x_ref), custom_call_target="tpu_custom_call" | custom-call | tf_op jit(solution)/shard_map/pallas_call | solution.py:213
  53.9 0.1 dynamic-slice_bitcast_fusion
  53.9 0.1 collective-permute-start.3
  54.1 1.5 %collective-permute-done.3 = f32[2,20,4,4,128]{4,3,2,1,0:T(4,128)S(1)} collective-permute-done((f32[2,20,4,4,128]{4,3,2,1,0:T(4,128)S(1)}, f32[2,20,4,4,128]{4,3,2,1,0:T(4,128)S(1)}, u32[]{:S(2)}, u32[]{:S(2)}) %collective-permute-start.3) | collective-permute-done | bytes 327712 | tf_op jit(solution)/shard_map/ppermute | solution.py:249
  55.6 0.1 bitcast_add_fusion
  55.7 0.1 dynamic-slice_bitcast_fusion.3
  55.8 3.6 %collective-permute-start.6 = (f32[2,20,4,128]{3,2,1,0:T(4,128)S(1)}, f32[2,20,4,128]{3,2,1,0:T(4,128)S(1)}, u32[]{:S(2)}, u32[]{:S(2)}) collective-permute-start(f32[2,20,4,128]{3,2,1,0:T(4,128)S(1)} %get-tuple-element.10), channel_id=1, source_target_pairs={{0,6},{1,7},{2,0},{3,1},{4,2},{5,3},{6,4},{7,5},{8,14},{9,15},{10,... | collective-permute-start | bytes 245768 | tf_op jit(solution)/shard_map/ppermute | solution.py:254
  59.4 0.0 collective-permute-start.5
  59.4 0.6 collective-permute-start.4
  60.0 2.2 %collective-permute-done.6 = f32[2,20,4,128]{3,2,1,0:T(4,128)S(1)} collective-permute-done((f32[2,20,4,128]{3,2,1,0:T(4,128)S(1)}, f32[2,20,4,128]{3,2,1,0:T(4,128)S(1)}, u32[]{:S(2)}, u32[]{:S(2)}) %collective-permute-start.6) | collective-permute-done | bytes 81952 | tf_op jit(solution)/shard_map/ppermute | solution.py:254
  62.2 5.2 %collective-permute-done.5 = f32[2,20,4,128]{3,2,1,0:T(4,128)S(1)} collective-permute-done((f32[2,20,4,128]{3,2,1,0:T(4,128)S(1)}, f32[2,20,4,128]{3,2,1,0:T(4,128)S(1)}, u32[]{:S(2)}, u32[]{:S(2)}) %collective-permute-start.5) | collective-permute-done | bytes 81952 | tf_op jit(solution)/shard_map/ppermute | solution.py:254
  67.4 0.0 collective-permute-done.4
  67.4 0.7 fusion.1
  (9 shorter events, 0.1 us)
Async XLA Ops:
  0.6 19.1 %copy-start = (f32[1,2,20,32,128]{4,3,2,1,0:T(8,128)S(1)}, f32[1,2,20,32,128]{4,3,2,1,0:T(8,128)}, u32[]{:S(2)}) copy-start(f32[1,2,20,32,128]{4,3,2,1,0:T(8,128)} %param.9) | copy-start | bytes 1966084
  19.6 0.7 %copy-start.1 = (s32[32,128]{1,0:T(8,128)S(1)}, s32[32,128]{1,0:T(8,128)}, u32[]{:S(2)}) copy-start(s32[32,128]{1,0:T(8,128)} %param.7) | copy-start | bytes 49156
  19.6 0.7 %copy-start.2 = (s32[32,128]{1,0:T(8,128)S(1)}, s32[32,128]{1,0:T(8,128)}, u32[]{:S(2)}) copy-start(s32[32,128]{1,0:T(8,128)} %param.8) | copy-start | bytes 49156
  20.9 6.6 %collective-permute-start = (f32[122,2,128]{2,1,0:T(2,128)S(1)}, f32[122,2,128]{2,1,0:T(2,128)S(1)}, u32[]{:S(2)}, u32[]{:S(2)}) collective-permute-start(f32[122,2,128]{2,1,0:T(2,128)S(1)} %rev.3), channel_id=1, source_target_pairs={{0,24},{8,16},{16,8},{24,0},{1,25},{9,17},{17,9},{25,1},{2,26},{10... | collective-permute-start | bytes 374792 | tf_op jit(solution)/shard_map/ppermute | solution.py:18
  27.9 5.0 %collective-permute-start.2 = (f32[2,4148]{1,0:T(2,128)S(1)}, f32[2,4148]{1,0:T(2,128)S(1)}, u32[]{:S(2)}, u32[]{:S(2)}) collective-permute-start(f32[2,4148]{1,0:T(2,128)S(1)} %get-tuple-element.13), channel_id=1, source_target_pairs={{0,8},{8,16},{16,24},{24,0},{1,9},{9,17},{17,25},{25,1},{2,10},{10... | collective-permute-start | bytes 99560 | tf_op jit(solution)/shard_map/ppermute | solution.py:18
  29.4 3.9 %collective-permute-start.1 = (f32[2,4148]{1,0:T(2,128)S(1)}, f32[2,4148]{1,0:T(2,128)S(1)}, u32[]{:S(2)}, u32[]{:S(2)}) collective-permute-start(f32[2,4148]{1,0:T(2,128)S(1)} %get-tuple-element.12), channel_id=1, source_target_pairs={{0,24},{8,0},{16,8},{24,16},{1,25},{9,1},{17,9},{25,17},{2,26},{10... | collective-permute-start | bytes 99560 | tf_op jit(solution)/shard_map/ppermute | solution.py:18
  53.9 1.7 %collective-permute-start.3 = (f32[2,20,4,4,128]{4,3,2,1,0:T(4,128)S(1)}, f32[2,20,4,4,128]{4,3,2,1,0:T(4,128)S(1)}, u32[]{:S(2)}, u32[]{:S(2)}) collective-permute-start(f32[2,20,4,4,128]{4,3,2,1,0:T(4,128)S(1)} %dynamic-slice_bitcast_fusion), channel_id=1, source_target_pairs={{0,1},{1,0},{2,3},{3,2},{4,5},{5,4},{6,7},{7,6},{8,9},{9,8},{10,11... | collective-permute-start | bytes 983048 | tf_op jit(solution)/shard_map/ppermute | solution.py:249
  55.8 6.5 %collective-permute-start.6 = (f32[2,20,4,128]{3,2,1,0:T(4,128)S(1)}, f32[2,20,4,128]{3,2,1,0:T(4,128)S(1)}, u32[]{:S(2)}, u32[]{:S(2)}) collective-permute-start(f32[2,20,4,128]{3,2,1,0:T(4,128)S(1)} %get-tuple-element.10), channel_id=1, source_target_pairs={{0,6},{1,7},{2,0},{3,1},{4,2},{5,3},{6,4},{7,5},{8,14},{9,15},{10,... | collective-permute-start | bytes 245768 | tf_op jit(solution)/shard_map/ppermute | solution.py:254
  59.4 8.0 %collective-permute-start.5 = (f32[2,20,4,128]{3,2,1,0:T(4,128)S(1)}, f32[2,20,4,128]{3,2,1,0:T(4,128)S(1)}, u32[]{:S(2)}, u32[]{:S(2)}) collective-permute-start(f32[2,20,4,128]{3,2,1,0:T(4,128)S(1)} %get-tuple-element.11), channel_id=1, source_target_pairs={{0,4},{1,5},{2,6},{3,7},{4,0},{5,1},{6,2},{7,3},{8,12},{9,13},{10,... | collective-permute-start | bytes 245768 | tf_op jit(solution)/shard_map/ppermute | solution.py:254
  59.4 8.0 %collective-permute-start.4 = (f32[2,20,4,128]{3,2,1,0:T(4,128)S(1)}, f32[2,20,4,128]{3,2,1,0:T(4,128)S(1)}, u32[]{:S(2)}, u32[]{:S(2)}) collective-permute-start(f32[2,20,4,128]{3,2,1,0:T(4,128)S(1)} %get-tuple-element.9), channel_id=1, source_target_pairs={{0,2},{1,3},{2,4},{3,5},{4,6},{5,7},{6,0},{7,1},{8,10},{9,11},{10,... | collective-permute-start | bytes 245768 | tf_op jit(solution)/shard_map/ppermute | solution.py:254

commit v9 on v8

--- a/solution.py
+++ b/solution.py
@@ -121,7 +121,7 @@
             a_ref[c, k] = w * ve_ref[c, k]
         return carry
 
-    lax.fori_loop(0, levels, setup, 0)
+    lax.fori_loop(0, levels, setup, 0, unroll=2)
 
     def operate(x_ref, c, k, diffs=None):
         x = x_ref[c, k]
@@ -146,7 +146,7 @@
         u1_ref[c, k] = wet_ref[k] * (x + change + heat * src_ref[k])
         return carry
 
-    lax.fori_loop(0, planes, forward_first, 0, unroll=2)
+    lax.fori_loop(0, planes, forward_first, 0, unroll=4)
 
     def forward_second(ck, carry):
         c = ck // levels
@@ -157,7 +157,7 @@
         fin_ref[c, k] = out[:ny, :width]
         return carry
 
-    lax.fori_loop(0, planes, forward_second, 0, unroll=2)
+    lax.fori_loop(0, planes, forward_second, 0, unroll=4)
 
     def backward_second(ck, carry):
         c = ck // levels
@@ -166,7 +166,7 @@
         b_ref[c, k] = wet_ref[k] * (x + change)
         return carry
 
-    lax.fori_loop(0, planes, backward_second, 0, unroll=2)
+    lax.fori_loop(0, planes, backward_second, 0, unroll=4)
 
     def backward_first(ck, carry):
         c = ck // levels
@@ -175,7 +175,7 @@
         adj_ref[c, k] = (x + change)[:ny, :width]
         return carry
 
-    lax.fori_loop(0, planes, backward_first, 0, unroll=2)
+    lax.fori_loop(0, planes, backward_first, 0, unroll=4)
 
     def gradient(k, carry):
         g_east = jnp.zeros((ny, width), jnp.float32)
@@ -187,7 +187,7 @@
         grad_ref[1, k] = gnm_ref[k] * g_north
         return carry
 
-    lax.fori_loop(0, levels, gradient, 0)
+    lax.fori_loop(0, levels, gradient, 0, unroll=2)
 
 
 def on_device(tracers, diffusivity, level_count, shelf_mask, cotangent):

time: 68.3 us -> 61.5 us (0.900)
  Pallas kernels: 17.8 us -> 11 us
    pallas_call x1, Pallas kernels: 17.8 us -> 11 us  [on_device(): pl.pallas_call(diffusion_kernel, out_shape=(field, field, jax.ShapeDtypeS...]
where the time goes in v9:
time: 61.5 us; the launch traced here: 61.3 us
  blocking collectives  16.8 us (27%)
  waiting for transfers between devices  14.3 us (23%)
  Pallas kernels  11 us (18%)
  starting transfers between devices  9.77 us (16%)
  local copies, waits for them, and re-layouts  3.74 us (6%)
  matrix products  3.31 us (5%)
  other arithmetic  1.53 us (2%)
  between operations  0.84 us (1%)
    all_gather x1, blocking collectives, on_device(): full_kappa = lax.all_gather(diffusivity, 'scen', axis=2, tiled=True)  16.8 us
    pallas_call x1, Pallas kernels, on_device(): pl.pallas_call(diffusion_kernel, out_shape=(field, field, jax.ShapeDtypeS...  11 us
    ppermute x3, waiting for transfers between devices, summed_over_scen(): lax.ppermute(send, 'scen', [(q, (q // 2 + step) % chips * 2 + q % 2) for...  7.38 us
    ppermute x3, starting transfers between devices, shifted(): return lax.ppermute(x, 'space', perm)  5.45 us
    ppermute x3, waiting for transfers between devices, shifted(): return lax.ppermute(x, 'space', perm)  5.35 us
    ppermute x3, starting transfers between devices, summed_over_scen(): lax.ppermute(send, 'scen', [(q, (q // 2 + step) % chips * 2 + q % 2) for...  4.25 us
    dot_general x4, matrix products, contract(): lax.dot_general(a, b, (dims, ((), ())), precision=lax.Precision.HIGHEST,...  3.31 us
    unnamed x10, local copies, waits for them, and re-layouts  2.71 us
  transfers between devices with their start and end apart: 7, of which 6 were waited for; matrix products, arithmetic and copies ran while one was open for 2% of the time, Pallas kernels for 0%

profile of v9, /device:TPU:0, one launch (start us, length us, event | category | flops | bytes accessed | tf_op | source)
XLA Modules:
  0.0 61.3 jit_solution(14539989279490103508)
XLA Ops:
  0.6 0.0 copy-start
  0.6 1.2 %constant_dynamic-update-slice_fusion.2 = f32[122,32,128]{2,1,0:T(8,128)S(1)} fusion(f32[40,32,128]{2,1,0:T(8,128)} %bitcast.43), kind=kLoop, calls=%fused_computation.21 | loop fusion | bytes 1310720
  1.8 0.9 %copy.14 = f32[2,20,4,128]{3,0,1,2:T(2,128)S(1)} copy(f32[2,20,4,128]{3,2,1,0:T(4,128)} %param.6) | data formatting | bytes 163840 | tf_op args[1]
  2.8 16.8 %all_gather.3 = f32[2,20,32,128]{3,0,1,2:T(2,128)S(1)} all-gather(f32[2,20,4,128]{3,0,1,2:T(2,128)S(1)} %copy.14), channel_id=1, replica_groups=mesh['space'=4,'scen'=8] {'scen'}, dimensions={2}, use_global_device_ids=true | all-gather | bytes 737280 | tf_op jit(solution)/shard_map/all_gather | solution.py:197
  19.6 0.0 copy-start.1
  19.6 0.0 copy-start.2
  19.6 0.1 copy.15
  19.7 0.0 copy-done
  19.9 0.5 copy-done.1
  20.3 0.0 copy-done.2
  20.3 0.1 slice.20
  20.4 0.5 rev.3
  20.9 2.5 %collective-permute-start = (f32[122,2,128]{2,1,0:T(2,128)S(1)}, f32[122,2,128]{2,1,0:T(2,128)S(1)}, u32[]{:S(2)}, u32[]{:S(2)}) collective-permute-start(f32[122,2,128]{2,1,0:T(2,128)S(1)} %rev.3), channel_id=1, source_target_pairs={{0,24},{8,16},{16,8},{24,0},{1,25},{9,17},{17,9},{25,1},{2,26},{10... | collective-permute-start | bytes 374792 | tf_op jit(solution)/shard_map/ppermute | solution.py:18
  23.5 0.1 and_or_fusion.1
  23.5 1.0 %fusion.10 = f32[4,3904]{1,0:T(4,128)S(1)} fusion(pred[128,4]{0,1:T(4,128)(4,1)S(1)} %get-tuple-element.14, f32[3904,128]{1,0:T(8,128)S(1)} %bitcast.40), kind=kOutput, calls=%fused_computation.37 | convolution fusion | flops 23986176 | bytes 2061824 | tf_op jit(solution)/shard_map/dot_general | solution.py:31
  24.5 2.9 %collective-permute-done = f32[122,2,128]{2,1,0:T(2,128)S(1)} collective-permute-done((f32[122,2,128]{2,1,0:T(2,128)S(1)}, f32[122,2,128]{2,1,0:T(2,128)S(1)}, u32[]{:S(2)}, u32[]{:S(2)}) %collective-permute-start) | collective-permute-done | bytes 124960 | tf_op jit(solution)/shard_map/ppermute | solution.py:18
  27.5 0.1 reshape.26
  27.6 0.2 fusion.11
  27.7 0.2 fusion.5
  27.9 1.5 %collective-permute-start.2 = (f32[2,4148]{1,0:T(2,128)S(1)}, f32[2,4148]{1,0:T(2,128)S(1)}, u32[]{:S(2)}, u32[]{:S(2)}) collective-permute-start(f32[2,4148]{1,0:T(2,128)S(1)} %get-tuple-element.13), channel_id=1, source_target_pairs={{0,8},{8,16},{16,24},{24,0},{1,9},{9,17},{17,25},{25,1},{2,10},{10... | collective-permute-start | bytes 99560 | tf_op jit(solution)/shard_map/ppermute | solution.py:18
  29.4 1.4 %collective-permute-start.1 = (f32[2,4148]{1,0:T(2,128)S(1)}, f32[2,4148]{1,0:T(2,128)S(1)}, u32[]{:S(2)}, u32[]{:S(2)}) collective-permute-start(f32[2,4148]{1,0:T(2,128)S(1)} %get-tuple-element.12), channel_id=1, source_target_pairs={{0,24},{8,0},{16,8},{24,16},{1,25},{9,1},{17,9},{25,17},{2,26},{10... | collective-permute-start | bytes 99560 | tf_op jit(solution)/shard_map/ppermute | solution.py:18
  30.9 0.1 pad.4.clone
  30.9 2.0 %collective-permute-done.2 = f32[2,4148]{1,0:T(2,128)S(1)} collective-permute-done((f32[2,4148]{1,0:T(2,128)S(1)}, f32[2,4148]{1,0:T(2,128)S(1)}, u32[]{:S(2)}, u32[]{:S(2)}) %collective-permute-start.2) | collective-permute-done | bytes 33216 | tf_op jit(solution)/shard_map/ppermute | solution.py:18
  33.0 0.4 collective-permute-done.1
  33.3 0.4 fusion.6
  33.7 0.1 reshape.28
  33.8 1.7 %fusion.3 = f32[3904,128]{1,0:T(8,128)S(1)} fusion(pred[128,4]{0,1:T(4,128)(4,1)S(1)} %get-tuple-element.15, f32[2,4148]{1,0:T(2,128)S(1)} %collective-permute-done.1, f32[2,4148]{1,0:T(2,128)S(1)} %collective-permute-done.2), kind=kOutput, calls=%fused_computation.14 | convolution fusion | flops 24001792 | bytes 2065728 | tf_op jit(solution)/shard_map/dot_general | solution.py:31
  35.6 0.5 maximum_maximum_fusion.x_ref
  36.1 11.0 %shard_map.76 = (f32[2,20,32,128]{3,2,1,0:T(8,128)}, f32[2,20,32,128]{3,2,1,0:T(8,128)}, f32[2,20,32,128]{3,2,1,0:T(8,128)S(1)}) custom-call(f32[122,40,256]{2,1,0:T(8,128)S(1)} %maximum_maximum_fusion.x_ref), custom_call_target="tpu_custom_call" | custom-call | tf_op jit(solution)/shard_map/pallas_call | solution.py:213
  47.0 0.1 dynamic-slice_bitcast_fusion
  47.1 0.1 collective-permute-start.3
  47.3 1.5 %collective-permute-done.3 = f32[2,20,4,4,128]{4,3,2,1,0:T(4,128)S(1)} collective-permute-done((f32[2,20,4,4,128]{4,3,2,1,0:T(4,128)S(1)}, f32[2,20,4,4,128]{4,3,2,1,0:T(4,128)S(1)}, u32[]{:S(2)}, u32[]{:S(2)}) %collective-permute-start.3) | collective-permute-done | bytes 327712 | tf_op jit(solution)/shard_map/ppermute | solution.py:249
  48.8 0.1 bitcast_add_fusion
  48.9 0.1 dynamic-slice_bitcast_fusion.3
  49.0 3.6 %collective-permute-start.6 = (f32[2,20,4,128]{3,2,1,0:T(4,128)S(1)}, f32[2,20,4,128]{3,2,1,0:T(4,128)S(1)}, u32[]{:S(2)}, u32[]{:S(2)}) collective-permute-start(f32[2,20,4,128]{3,2,1,0:T(4,128)S(1)} %get-tuple-element.10), channel_id=1, source_target_pairs={{0,6},{1,7},{2,0},{3,1},{4,2},{5,3},{6,4},{7,5},{8,14},{9,15},{10,... | collective-permute-start | bytes 245768 | tf_op jit(solution)/shard_map/ppermute | solution.py:254
  52.6 0.0 collective-permute-start.5
  52.6 0.6 %collective-permute-start.4 = (f32[2,20,4,128]{3,2,1,0:T(4,128)S(1)}, f32[2,20,4,128]{3,2,1,0:T(4,128)S(1)}, u32[]{:S(2)}, u32[]{:S(2)}) collective-permute-start(f32[2,20,4,128]{3,2,1,0:T(4,128)S(1)} %get-tuple-element.9), channel_id=1, source_target_pairs={{0,2},{1,3},{2,4},{3,5},{4,6},{5,7},{6,0},{7,1},{8,10},{9,11},{10,... | collective-permute-start | bytes 245768 | tf_op jit(solution)/shard_map/ppermute | solution.py:254
  53.2 2.2 %collective-permute-done.6 = f32[2,20,4,128]{3,2,1,0:T(4,128)S(1)} collective-permute-done((f32[2,20,4,128]{3,2,1,0:T(4,128)S(1)}, f32[2,20,4,128]{3,2,1,0:T(4,128)S(1)}, u32[]{:S(2)}, u32[]{:S(2)}) %collective-permute-start.6) | collective-permute-done | bytes 81952 | tf_op jit(solution)/shard_map/ppermute | solution.py:254
  55.4 5.2 %collective-permute-done.5 = f32[2,20,4,128]{3,2,1,0:T(4,128)S(1)} collective-permute-done((f32[2,20,4,128]{3,2,1,0:T(4,128)S(1)}, f32[2,20,4,128]{3,2,1,0:T(4,128)S(1)}, u32[]{:S(2)}, u32[]{:S(2)}) %collective-permute-start.5) | collective-permute-done | bytes 81952 | tf_op jit(solution)/shard_map/ppermute | solution.py:254
  60.6 0.0 collective-permute-done.4
  60.6 0.7 %fusion.1 = f32[2,20,4,128]{3,2,1,0:T(4,128)} fusion(f32[2,20,4,128]{3,2,1,0:T(4,128)S(1)} %collective-permute-done.6, f32[2,20,4,128]{3,2,1,0:T(4,128)S(1)} %collective-permute-done.5, f32[2,20,4,128]{3,2,1,0:T(4,128)S(1)} %collective-permute-done.4, f32[2,20,4,4,128]{4,3,2,1,0:T(4,128)S(1)} %bitcast_add_fusion, s32[]{:T(128)S(6)} %select_n.47), kind=kLoop, calls=%fused_computation.5 | loop fusion | flops 61440 | bytes 409604 | tf_op jit(solution)/shard_map/add | solution.py:254
  (9 shorter events, 0.1 us)
Async XLA Ops:
  0.6 19.1 %copy-start = (f32[1,2,20,32,128]{4,3,2,1,0:T(8,128)S(1)}, f32[1,2,20,32,128]{4,3,2,1,0:T(8,128)}, u32[]{:S(2)}) copy-start(f32[1,2,20,32,128]{4,3,2,1,0:T(8,128)} %param.9) | copy-start | bytes 1966084
  19.6 0.7 %copy-start.1 = (s32[32,128]{1,0:T(8,128)S(1)}, s32[32,128]{1,0:T(8,128)}, u32[]{:S(2)}) copy-start(s32[32,128]{1,0:T(8,128)} %param.7) | copy-start | bytes 49156
  19.6 0.7 %copy-start.2 = (s32[32,128]{1,0:T(8,128)S(1)}, s32[32,128]{1,0:T(8,128)}, u32[]{:S(2)}) copy-start(s32[32,128]{1,0:T(8,128)} %param.8) | copy-start | bytes 49156
  20.9 6.6 %collective-permute-start = (f32[122,2,128]{2,1,0:T(2,128)S(1)}, f32[122,2,128]{2,1,0:T(2,128)S(1)}, u32[]{:S(2)}, u32[]{:S(2)}) collective-permute-start(f32[122,2,128]{2,1,0:T(2,128)S(1)} %rev.3), channel_id=1, source_target_pairs={{0,24},{8,16},{16,8},{24,0},{1,25},{9,17},{17,9},{25,1},{2,26},{10... | collective-permute-start | bytes 374792 | tf_op jit(solution)/shard_map/ppermute | solution.py:18
  27.9 5.0 %collective-permute-start.2 = (f32[2,4148]{1,0:T(2,128)S(1)}, f32[2,4148]{1,0:T(2,128)S(1)}, u32[]{:S(2)}, u32[]{:S(2)}) collective-permute-start(f32[2,4148]{1,0:T(2,128)S(1)} %get-tuple-element.13), channel_id=1, source_target_pairs={{0,8},{8,16},{16,24},{24,0},{1,9},{9,17},{17,25},{25,1},{2,10},{10... | collective-permute-start | bytes 99560 | tf_op jit(solution)/shard_map/ppermute | solution.py:18
  29.4 3.9 %collective-permute-start.1 = (f32[2,4148]{1,0:T(2,128)S(1)}, f32[2,4148]{1,0:T(2,128)S(1)}, u32[]{:S(2)}, u32[]{:S(2)}) collective-permute-start(f32[2,4148]{1,0:T(2,128)S(1)} %get-tuple-element.12), channel_id=1, source_target_pairs={{0,24},{8,0},{16,8},{24,16},{1,25},{9,1},{17,9},{25,17},{2,26},{10... | collective-permute-start | bytes 99560 | tf_op jit(solution)/shard_map/ppermute | solution.py:18
  47.1 1.7 %collective-permute-start.3 = (f32[2,20,4,4,128]{4,3,2,1,0:T(4,128)S(1)}, f32[2,20,4,4,128]{4,3,2,1,0:T(4,128)S(1)}, u32[]{:S(2)}, u32[]{:S(2)}) collective-permute-start(f32[2,20,4,4,128]{4,3,2,1,0:T(4,128)S(1)} %dynamic-slice_bitcast_fusion), channel_id=1, source_target_pairs={{0,1},{1,0},{2,3},{3,2},{4,5},{5,4},{6,7},{7,6},{8,9},{9,8},{10,11... | collective-permute-start | bytes 983048 | tf_op jit(solution)/shard_map/ppermute | solution.py:249
  49.0 6.5 %collective-permute-start.6 = (f32[2,20,4,128]{3,2,1,0:T(4,128)S(1)}, f32[2,20,4,128]{3,2,1,0:T(4,128)S(1)}, u32[]{:S(2)}, u32[]{:S(2)}) collective-permute-start(f32[2,20,4,128]{3,2,1,0:T(4,128)S(1)} %get-tuple-element.10), channel_id=1, source_target_pairs={{0,6},{1,7},{2,0},{3,1},{4,2},{5,3},{6,4},{7,5},{8,14},{9,15},{10,... | collective-permute-start | bytes 245768 | tf_op jit(solution)/shard_map/ppermute | solution.py:254
  52.6 8.0 %collective-permute-start.5 = (f32[2,20,4,128]{3,2,1,0:T(4,128)S(1)}, f32[2,20,4,128]{3,2,1,0:T(4,128)S(1)}, u32[]{:S(2)}, u32[]{:S(2)}) collective-permute-start(f32[2,20,4,128]{3,2,1,0:T(4,128)S(1)} %get-tuple-element.11), channel_id=1, source_target_pairs={{0,4},{1,5},{2,6},{3,7},{4,0},{5,1},{6,2},{7,3},{8,12},{9,13},{10,... | collective-permute-start | bytes 245768 | tf_op jit(solution)/shard_map/ppermute | solution.py:254
  52.6 8.0 %collective-permute-start.4 = (f32[2,20,4,128]{3,2,1,0:T(4,128)S(1)}, f32[2,20,4,128]{3,2,1,0:T(4,128)S(1)}, u32[]{:S(2)}, u32[]{:S(2)}) collective-permute-start(f32[2,20,4,128]{3,2,1,0:T(4,128)S(1)} %get-tuple-element.9), channel_id=1, source_target_pairs={{0,2},{1,3},{2,4},{3,5},{4,6},{5,7},{6,0},{7,1},{8,10},{9,11},{10,... | collective-permute-start | bytes 245768 | tf_op jit(solution)/shard_map/ppermute | solution.py:254

commit v10 on v9

--- a/solution.py
+++ b/solution.py
@@ -121,7 +121,7 @@
             a_ref[c, k] = w * ve_ref[c, k]
         return carry
 
-    lax.fori_loop(0, levels, setup, 0, unroll=2)
+    lax.fori_loop(0, levels, setup, 0, unroll=4)
 
     def operate(x_ref, c, k, diffs=None):
         x = x_ref[c, k]
@@ -146,7 +146,7 @@
         u1_ref[c, k] = wet_ref[k] * (x + change + heat * src_ref[k])
         return carry
 
-    lax.fori_loop(0, planes, forward_first, 0, unroll=4)
+    lax.fori_loop(0, planes, forward_first, 0, unroll=8)
 
     def forward_second(ck, carry):
         c = ck // levels
@@ -157,7 +157,7 @@
         fin_ref[c, k] = out[:ny, :width]
         return carry
 
-    lax.fori_loop(0, planes, forward_second, 0, unroll=4)
+    lax.fori_loop(0, planes, forward_second, 0, unroll=8)
 
     def backward_second(ck, carry):
         c = ck // levels
@@ -166,7 +166,7 @@
         b_ref[c, k] = wet_ref[k] * (x + change)
         return carry
 
-    lax.fori_loop(0, planes, backward_second, 0, unroll=4)
+    lax.fori_loop(0, planes, backward_second, 0, unroll=8)
 
     def backward_first(ck, carry):
         c = ck // levels
@@ -175,7 +175,7 @@
         adj_ref[c, k] = (x + change)[:ny, :width]
         return carry
 
-    lax.fori_loop(0, planes, backward_first, 0, unroll=4)
+    lax.fori_loop(0, planes, backward_first, 0, unroll=8)
 
     def gradient(k, carry):
         g_east = jnp.zeros((ny, width), jnp.float32)
@@ -187,7 +187,7 @@
         grad_ref[1, k] = gnm_ref[k] * g_north
         return carry
 
-    lax.fori_loop(0, levels, gradient, 0, unroll=2)
+    lax.fori_loop(0, levels, gradient, 0, unroll=4)
 
 
 def on_device(tracers, diffusivity, level_count, shelf_mask, cotangent):

time: 61.5 us -> 59.6 us (0.969)
  Pallas kernels: 11 us -> 9.11 us
    pallas_call x1, Pallas kernels: 11 us -> 9.11 us  [on_device(): pl.pallas_call(diffusion_kernel, out_shape=(field, field, jax.ShapeDtypeS...]
where the time goes in v10:
time: 59.6 us; the launch traced here: 59.4 us
  blocking collectives  16.8 us (28%)
  waiting for transfers between devices  14.3 us (24%)
  starting transfers between devices  9.77 us (16%)
  Pallas kernels  9.11 us (15%)
  local copies, waits for them, and re-layouts  3.74 us (6%)
  matrix products  3.31 us (6%)
  other arithmetic  1.53 us (3%)
  between operations  0.84 us (1%)
    all_gather x1, blocking collectives, on_device(): full_kappa = lax.all_gather(diffusivity, 'scen', axis=2, tiled=True)  16.8 us
    pallas_call x1, Pallas kernels, on_device(): pl.pallas_call(diffusion_kernel, out_shape=(field, field, jax.ShapeDtypeS...  9.11 us
    ppermute x3, waiting for transfers between devices, summed_over_scen(): lax.ppermute(send, 'scen', [(q, (q // 2 + step) % chips * 2 + q % 2) for...  7.38 us
    ppermute x3, starting transfers between devices, shifted(): return lax.ppermute(x, 'space', perm)  5.45 us
    ppermute x3, waiting for transfers between devices, shifted(): return lax.ppermute(x, 'space', perm)  5.35 us
    ppermute x3, starting transfers between devices, summed_over_scen(): lax.ppermute(send, 'scen', [(q, (q // 2 + step) % chips * 2 + q % 2) for...  4.25 us
    dot_general x4, matrix products, contract(): lax.dot_general(a, b, (dims, ((), ())), precision=lax.Precision.HIGHEST,...  3.31 us
    unnamed x10, local copies, waits for them, and re-layouts  2.71 us
  transfers between devices with their start and end apart: 7, of which 6 were waited for; matrix products, arithmetic and copies ran while one was open for 2% of the time, Pallas kernels for 0%

profile of v10, /device:TPU:0, one launch (start us, length us, event | category | flops | bytes accessed | tf_op | source)
XLA Modules:
  0.0 59.4 jit_solution(5552047735063260825)
XLA Ops:
  0.6 0.0 copy-start
  0.6 1.2 %constant_dynamic-update-slice_fusion.2 = f32[122,32,128]{2,1,0:T(8,128)S(1)} fusion(f32[40,32,128]{2,1,0:T(8,128)} %bitcast.43), kind=kLoop, calls=%fused_computation.21 | loop fusion | bytes 1310720
  1.8 0.9 %copy.14 = f32[2,20,4,128]{3,0,1,2:T(2,128)S(1)} copy(f32[2,20,4,128]{3,2,1,0:T(4,128)} %param.6) | data formatting | bytes 163840 | tf_op args[1]
  2.8 16.8 %all_gather.3 = f32[2,20,32,128]{3,0,1,2:T(2,128)S(1)} all-gather(f32[2,20,4,128]{3,0,1,2:T(2,128)S(1)} %copy.14), channel_id=1, replica_groups=mesh['space'=4,'scen'=8] {'scen'}, dimensions={2}, use_global_device_ids=true | all-gather | bytes 737280 | tf_op jit(solution)/shard_map/all_gather | solution.py:197
  19.6 0.0 copy-start.1
  19.6 0.0 copy-start.2
  19.6 0.1 copy.15
  19.7 0.0 copy-done
  19.9 0.5 copy-done.1
  20.3 0.0 copy-done.2
  20.3 0.1 slice.20
  20.4 0.5 rev.3
  20.9 2.5 %collective-permute-start = (f32[122,2,128]{2,1,0:T(2,128)S(1)}, f32[122,2,128]{2,1,0:T(2,128)S(1)}, u32[]{:S(2)}, u32[]{:S(2)}) collective-permute-start(f32[122,2,128]{2,1,0:T(2,128)S(1)} %rev.3), channel_id=1, source_target_pairs={{0,24},{8,16},{16,8},{24,0},{1,25},{9,17},{17,9},{25,1},{2,26},{10... | collective-permute-start | bytes 374792 | tf_op jit(solution)/shard_map/ppermute | solution.py:18
  23.5 0.1 and_or_fusion.1
  23.5 1.0 %fusion.10 = f32[4,3904]{1,0:T(4,128)S(1)} fusion(pred[128,4]{0,1:T(4,128)(4,1)S(1)} %get-tuple-element.14, f32[3904,128]{1,0:T(8,128)S(1)} %bitcast.40), kind=kOutput, calls=%fused_computation.37 | convolution fusion | flops 23986176 | bytes 2061824 | tf_op jit(solution)/shard_map/dot_general | solution.py:31
  24.5 2.9 %collective-permute-done = f32[122,2,128]{2,1,0:T(2,128)S(1)} collective-permute-done((f32[122,2,128]{2,1,0:T(2,128)S(1)}, f32[122,2,128]{2,1,0:T(2,128)S(1)}, u32[]{:S(2)}, u32[]{:S(2)}) %collective-permute-start) | collective-permute-done | bytes 124960 | tf_op jit(solution)/shard_map/ppermute | solution.py:18
  27.5 0.1 reshape.26
  27.6 0.2 fusion.11
  27.7 0.2 fusion.5
  27.9 1.5 %collective-permute-start.2 = (f32[2,4148]{1,0:T(2,128)S(1)}, f32[2,4148]{1,0:T(2,128)S(1)}, u32[]{:S(2)}, u32[]{:S(2)}) collective-permute-start(f32[2,4148]{1,0:T(2,128)S(1)} %get-tuple-element.13), channel_id=1, source_target_pairs={{0,8},{8,16},{16,24},{24,0},{1,9},{9,17},{17,25},{25,1},{2,10},{10... | collective-permute-start | bytes 99560 | tf_op jit(solution)/shard_map/ppermute | solution.py:18
  29.4 1.4 %collective-permute-start.1 = (f32[2,4148]{1,0:T(2,128)S(1)}, f32[2,4148]{1,0:T(2,128)S(1)}, u32[]{:S(2)}, u32[]{:S(2)}) collective-permute-start(f32[2,4148]{1,0:T(2,128)S(1)} %get-tuple-element.12), channel_id=1, source_target_pairs={{0,24},{8,0},{16,8},{24,16},{1,25},{9,1},{17,9},{25,17},{2,26},{10... | collective-permute-start | bytes 99560 | tf_op jit(solution)/shard_map/ppermute | solution.py:18
  30.9 0.1 pad.4.clone
  30.9 2.0 %collective-permute-done.2 = f32[2,4148]{1,0:T(2,128)S(1)} collective-permute-done((f32[2,4148]{1,0:T(2,128)S(1)}, f32[2,4148]{1,0:T(2,128)S(1)}, u32[]{:S(2)}, u32[]{:S(2)}) %collective-permute-start.2) | collective-permute-done | bytes 33216 | tf_op jit(solution)/shard_map/ppermute | solution.py:18
  33.0 0.4 collective-permute-done.1
  33.3 0.4 fusion.6
  33.7 0.1 reshape.28
  33.8 1.7 %fusion.3 = f32[3904,128]{1,0:T(8,128)S(1)} fusion(pred[128,4]{0,1:T(4,128)(4,1)S(1)} %get-tuple-element.15, f32[2,4148]{1,0:T(2,128)S(1)} %collective-permute-done.1, f32[2,4148]{1,0:T(2,128)S(1)} %collective-permute-done.2), kind=kOutput, calls=%fused_computation.14 | convolution fusion | flops 24001792 | bytes 2065728 | tf_op jit(solution)/shard_map/dot_general | solution.py:31
  35.6 0.5 maximum_maximum_fusion.x_ref
  36.1 9.1 %shard_map.76 = (f32[2,20,32,128]{3,2,1,0:T(8,128)}, f32[2,20,32,128]{3,2,1,0:T(8,128)}, f32[2,20,32,128]{3,2,1,0:T(8,128)S(1)}) custom-call(f32[122,40,256]{2,1,0:T(8,128)S(1)} %maximum_maximum_fusion.x_ref), custom_call_target="tpu_custom_call" | custom-call | tf_op jit(solution)/shard_map/pallas_call | solution.py:213
  45.2 0.1 dynamic-slice_bitcast_fusion
  45.2 0.1 collective-permute-start.3
  45.4 1.5 %collective-permute-done.3 = f32[2,20,4,4,128]{4,3,2,1,0:T(4,128)S(1)} collective-permute-done((f32[2,20,4,4,128]{4,3,2,1,0:T(4,128)S(1)}, f32[2,20,4,4,128]{4,3,2,1,0:T(4,128)S(1)}, u32[]{:S(2)}, u32[]{:S(2)}) %collective-permute-start.3) | collective-permute-done | bytes 327712 | tf_op jit(solution)/shard_map/ppermute | solution.py:249
  46.9 0.1 bitcast_add_fusion
  47.0 0.1 dynamic-slice_bitcast_fusion.3
  47.1 3.6 %collective-permute-start.6 = (f32[2,20,4,128]{3,2,1,0:T(4,128)S(1)}, f32[2,20,4,128]{3,2,1,0:T(4,128)S(1)}, u32[]{:S(2)}, u32[]{:S(2)}) collective-permute-start(f32[2,20,4,128]{3,2,1,0:T(4,128)S(1)} %get-tuple-element.10), channel_id=1, source_target_pairs={{0,6},{1,7},{2,0},{3,1},{4,2},{5,3},{6,4},{7,5},{8,14},{9,15},{10,... | collective-permute-start | bytes 245768 | tf_op jit(solution)/shard_map/ppermute | solution.py:254
  50.7 0.0 collective-permute-start.5
  50.7 0.6 %collective-permute-start.4 = (f32[2,20,4,128]{3,2,1,0:T(4,128)S(1)}, f32[2,20,4,128]{3,2,1,0:T(4,128)S(1)}, u32[]{:S(2)}, u32[]{:S(2)}) collective-permute-start(f32[2,20,4,128]{3,2,1,0:T(4,128)S(1)} %get-tuple-element.9), channel_id=1, source_target_pairs={{0,2},{1,3},{2,4},{3,5},{4,6},{5,7},{6,0},{7,1},{8,10},{9,11},{10,... | collective-permute-start | bytes 245768 | tf_op jit(solution)/shard_map/ppermute | solution.py:254
  51.3 2.2 %collective-permute-done.6 = f32[2,20,4,128]{3,2,1,0:T(4,128)S(1)} collective-permute-done((f32[2,20,4,128]{3,2,1,0:T(4,128)S(1)}, f32[2,20,4,128]{3,2,1,0:T(4,128)S(1)}, u32[]{:S(2)}, u32[]{:S(2)}) %collective-permute-start.6) | collective-permute-done | bytes 81952 | tf_op jit(solution)/shard_map/ppermute | solution.py:254
  53.6 5.2 %collective-permute-done.5 = f32[2,20,4,128]{3,2,1,0:T(4,128)S(1)} collective-permute-done((f32[2,20,4,128]{3,2,1,0:T(4,128)S(1)}, f32[2,20,4,128]{3,2,1,0:T(4,128)S(1)}, u32[]{:S(2)}, u32[]{:S(2)}) %collective-permute-start.5) | collective-permute-done | bytes 81952 | tf_op jit(solution)/shard_map/ppermute | solution.py:254
  58.7 0.0 collective-permute-done.4
  58.7 0.7 %fusion.1 = f32[2,20,4,128]{3,2,1,0:T(4,128)} fusion(f32[2,20,4,128]{3,2,1,0:T(4,128)S(1)} %collective-permute-done.6, f32[2,20,4,128]{3,2,1,0:T(4,128)S(1)} %collective-permute-done.5, f32[2,20,4,128]{3,2,1,0:T(4,128)S(1)} %collective-permute-done.4, f32[2,20,4,4,128]{4,3,2,1,0:T(4,128)S(1)} %bitcast_add_fusion, s32[]{:T(128)S(6)} %select_n.47), kind=kLoop, calls=%fused_computation.5 | loop fusion | flops 61440 | bytes 409604 | tf_op jit(solution)/shard_map/add | solution.py:254
  (9 shorter events, 0.1 us)
Async XLA Ops:
  0.6 19.1 %copy-start = (f32[1,2,20,32,128]{4,3,2,1,0:T(8,128)S(1)}, f32[1,2,20,32,128]{4,3,2,1,0:T(8,128)}, u32[]{:S(2)}) copy-start(f32[1,2,20,32,128]{4,3,2,1,0:T(8,128)} %param.9) | copy-start | bytes 1966084
  19.6 0.7 %copy-start.1 = (s32[32,128]{1,0:T(8,128)S(1)}, s32[32,128]{1,0:T(8,128)}, u32[]{:S(2)}) copy-start(s32[32,128]{1,0:T(8,128)} %param.7) | copy-start | bytes 49156
  19.6 0.7 %copy-start.2 = (s32[32,128]{1,0:T(8,128)S(1)}, s32[32,128]{1,0:T(8,128)}, u32[]{:S(2)}) copy-start(s32[32,128]{1,0:T(8,128)} %param.8) | copy-start | bytes 49156
  20.9 6.6 %collective-permute-start = (f32[122,2,128]{2,1,0:T(2,128)S(1)}, f32[122,2,128]{2,1,0:T(2,128)S(1)}, u32[]{:S(2)}, u32[]{:S(2)}) collective-permute-start(f32[122,2,128]{2,1,0:T(2,128)S(1)} %rev.3), channel_id=1, source_target_pairs={{0,24},{8,16},{16,8},{24,0},{1,25},{9,17},{17,9},{25,1},{2,26},{10... | collective-permute-start | bytes 374792 | tf_op jit(solution)/shard_map/ppermute | solution.py:18
  27.9 5.0 %collective-permute-start.2 = (f32[2,4148]{1,0:T(2,128)S(1)}, f32[2,4148]{1,0:T(2,128)S(1)}, u32[]{:S(2)}, u32[]{:S(2)}) collective-permute-start(f32[2,4148]{1,0:T(2,128)S(1)} %get-tuple-element.13), channel_id=1, source_target_pairs={{0,8},{8,16},{16,24},{24,0},{1,9},{9,17},{17,25},{25,1},{2,10},{10... | collective-permute-start | bytes 99560 | tf_op jit(solution)/shard_map/ppermute | solution.py:18
  29.4 3.9 %collective-permute-start.1 = (f32[2,4148]{1,0:T(2,128)S(1)}, f32[2,4148]{1,0:T(2,128)S(1)}, u32[]{:S(2)}, u32[]{:S(2)}) collective-permute-start(f32[2,4148]{1,0:T(2,128)S(1)} %get-tuple-element.12), channel_id=1, source_target_pairs={{0,24},{8,0},{16,8},{24,16},{1,25},{9,1},{17,9},{25,17},{2,26},{10... | collective-permute-start | bytes 99560 | tf_op jit(solution)/shard_map/ppermute | solution.py:18
  45.2 1.7 %collective-permute-start.3 = (f32[2,20,4,4,128]{4,3,2,1,0:T(4,128)S(1)}, f32[2,20,4,4,128]{4,3,2,1,0:T(4,128)S(1)}, u32[]{:S(2)}, u32[]{:S(2)}) collective-permute-start(f32[2,20,4,4,128]{4,3,2,1,0:T(4,128)S(1)} %dynamic-slice_bitcast_fusion), channel_id=1, source_target_pairs={{0,1},{1,0},{2,3},{3,2},{4,5},{5,4},{6,7},{7,6},{8,9},{9,8},{10,11... | collective-permute-start | bytes 983048 | tf_op jit(solution)/shard_map/ppermute | solution.py:249
  47.1 6.5 %collective-permute-start.6 = (f32[2,20,4,128]{3,2,1,0:T(4,128)S(1)}, f32[2,20,4,128]{3,2,1,0:T(4,128)S(1)}, u32[]{:S(2)}, u32[]{:S(2)}) collective-permute-start(f32[2,20,4,128]{3,2,1,0:T(4,128)S(1)} %get-tuple-element.10), channel_id=1, source_target_pairs={{0,6},{1,7},{2,0},{3,1},{4,2},{5,3},{6,4},{7,5},{8,14},{9,15},{10,... | collective-permute-start | bytes 245768 | tf_op jit(solution)/shard_map/ppermute | solution.py:254
  50.7 8.0 %collective-permute-start.5 = (f32[2,20,4,128]{3,2,1,0:T(4,128)S(1)}, f32[2,20,4,128]{3,2,1,0:T(4,128)S(1)}, u32[]{:S(2)}, u32[]{:S(2)}) collective-permute-start(f32[2,20,4,128]{3,2,1,0:T(4,128)S(1)} %get-tuple-element.11), channel_id=1, source_target_pairs={{0,4},{1,5},{2,6},{3,7},{4,0},{5,1},{6,2},{7,3},{8,12},{9,13},{10,... | collective-permute-start | bytes 245768 | tf_op jit(solution)/shard_map/ppermute | solution.py:254
  50.7 8.0 %collective-permute-start.4 = (f32[2,20,4,128]{3,2,1,0:T(4,128)S(1)}, f32[2,20,4,128]{3,2,1,0:T(4,128)S(1)}, u32[]{:S(2)}, u32[]{:S(2)}) collective-permute-start(f32[2,20,4,128]{3,2,1,0:T(4,128)S(1)} %get-tuple-element.9), channel_id=1, source_target_pairs={{0,2},{1,3},{2,4},{3,5},{4,6},{5,7},{6,0},{7,1},{8,10},{9,11},{10,... | collective-permute-start | bytes 245768 | tf_op jit(solution)/shard_map/ppermute | solution.py:254

commit v11 on v10

--- a/solution.py
+++ b/solution.py
@@ -121,7 +121,7 @@
             a_ref[c, k] = w * ve_ref[c, k]
         return carry
 
-    lax.fori_loop(0, levels, setup, 0, unroll=4)
+    lax.fori_loop(0, levels, setup, 0, unroll=True)
 
     def operate(x_ref, c, k, diffs=None):
         x = x_ref[c, k]
@@ -146,7 +146,7 @@
         u1_ref[c, k] = wet_ref[k] * (x + change + heat * src_ref[k])
         return carry
 
-    lax.fori_loop(0, planes, forward_first, 0, unroll=8)
+    lax.fori_loop(0, planes, forward_first, 0, unroll=True)
 
     def forward_second(ck, carry):
         c = ck // levels
@@ -157,7 +157,7 @@
         fin_ref[c, k] = out[:ny, :width]
         return carry
 
-    lax.fori_loop(0, planes, forward_second, 0, unroll=8)
+    lax.fori_loop(0, planes, forward_second, 0, unroll=True)
 
     def backward_second(ck, carry):
         c = ck // levels
@@ -166,7 +166,7 @@
         b_ref[c, k] = wet_ref[k] * (x + change)
         return carry
 
-    lax.fori_loop(0, planes, backward_second, 0, unroll=8)
+    lax.fori_loop(0, planes, backward_second, 0, unroll=True)
 
     def backward_first(ck, carry):
         c = ck // levels
@@ -175,7 +175,7 @@
         adj_ref[c, k] = (x + change)[:ny, :width]
         return carry
 
-    lax.fori_loop(0, planes, backward_first, 0, unroll=8)
+    lax.fori_loop(0, planes, backward_first, 0, unroll=True)
 
     def gradient(k, carry):
         g_east = jnp.zeros((ny, width), jnp.float32)
@@ -187,7 +187,7 @@
         grad_ref[1, k] = gnm_ref[k] * g_north
         return carry
 
-    lax.fori_loop(0, levels, gradient, 0, unroll=4)
+    lax.fori_loop(0, levels, gradient, 0, unroll=True)
 
 
 def on_device(tracers, diffusivity, level_count, shelf_mask, cotangent):

time: 59.6 us -> 64.8 us (1.087)
  Pallas kernels: 9.11 us -> 14.3 us
    pallas_call x1, Pallas kernels: 9.11 us -> 14.3 us  [on_device(): pl.pallas_call(diffusion_kernel, out_shape=(field, field, jax.ShapeDtypeS...]
where the time goes in v11:
time: 64.8 us; the launch traced here: 64.6 us
  blocking collectives  16.8 us (26%)
  waiting for transfers between devices  14.3 us (22%)
  Pallas kernels  14.3 us (22%)
  starting transfers between devices  9.78 us (15%)
  local copies, waits for them, and re-layouts  3.74 us (6%)
  matrix products  3.31 us (5%)
  other arithmetic  1.53 us (2%)
  between operations  0.84 us (1%)
    all_gather x1, blocking collectives, on_device(): full_kappa = lax.all_gather(diffusivity, 'scen', axis=2, tiled=True)  16.8 us
    pallas_call x1, Pallas kernels, on_device(): pl.pallas_call(diffusion_kernel, out_shape=(field, field, jax.ShapeDtypeS...  14.3 us
    ppermute x3, waiting for transfers between devices, summed_over_scen(): lax.ppermute(send, 'scen', [(q, (q // 2 + step) % chips * 2 + q % 2) for...  7.38 us
    ppermute x3, starting transfers between devices, shifted(): return lax.ppermute(x, 'space', perm)  5.45 us
    ppermute x3, waiting for transfers between devices, shifted(): return lax.ppermute(x, 'space', perm)  5.35 us
    ppermute x3, starting transfers between devices, summed_over_scen(): lax.ppermute(send, 'scen', [(q, (q // 2 + step) % chips * 2 + q % 2) for...  4.25 us
    dot_general x4, matrix products, contract(): lax.dot_general(a, b, (dims, ((), ())), precision=lax.Precision.HIGHEST,...  3.31 us
    unnamed x10, local copies, waits for them, and re-layouts  2.71 us
  transfers between devices with their start and end apart: 7, of which 6 were waited for; matrix products, arithmetic and copies ran while one was open for 2% of the time, Pallas kernels for 0%

profile of v11, /device:TPU:0, one launch (start us, length us, event | category | flops | bytes accessed | tf_op | source)
XLA Modules:
  0.0 64.6 jit_solution(1455387791167133426)
XLA Ops:
  0.6 0.0 copy-start
  0.6 1.2 %constant_dynamic-update-slice_fusion.2 = f32[122,32,128]{2,1,0:T(8,128)S(1)} fusion(f32[40,32,128]{2,1,0:T(8,128)} %bitcast.43), kind=kLoop, calls=%fused_computation.21 | loop fusion | bytes 1310720
  1.8 0.9 %copy.14 = f32[2,20,4,128]{3,0,1,2:T(2,128)S(1)} copy(f32[2,20,4,128]{3,2,1,0:T(4,128)} %param.6) | data formatting | bytes 163840 | tf_op args[1]
  2.8 16.8 %all_gather.3 = f32[2,20,32,128]{3,0,1,2:T(2,128)S(1)} all-gather(f32[2,20,4,128]{3,0,1,2:T(2,128)S(1)} %copy.14), channel_id=1, replica_groups=mesh['space'=4,'scen'=8] {'scen'}, dimensions={2}, use_global_device_ids=true | all-gather | bytes 737280 | tf_op jit(solution)/shard_map/all_gather | solution.py:197
  19.6 0.0 copy-start.1
  19.6 0.0 copy-start.2
  19.6 0.1 copy.15
  19.7 0.0 copy-done
  19.9 0.5 copy-done.1
  20.3 0.0 copy-done.2
  20.3 0.1 slice.20
  20.4 0.5 rev.3
  20.9 2.5 %collective-permute-start = (f32[122,2,128]{2,1,0:T(2,128)S(1)}, f32[122,2,128]{2,1,0:T(2,128)S(1)}, u32[]{:S(2)}, u32[]{:S(2)}) collective-permute-start(f32[122,2,128]{2,1,0:T(2,128)S(1)} %rev.3), channel_id=1, source_target_pairs={{0,24},{8,16},{16,8},{24,0},{1,25},{9,17},{17,9},{25,1},{2,26},{10... | collective-permute-start | bytes 374792 | tf_op jit(solution)/shard_map/ppermute | solution.py:18
  23.5 0.1 and_or_fusion.1
  23.5 1.0 %fusion.10 = f32[4,3904]{1,0:T(4,128)S(1)} fusion(pred[128,4]{0,1:T(4,128)(4,1)S(1)} %get-tuple-element.14, f32[3904,128]{1,0:T(8,128)S(1)} %bitcast.40), kind=kOutput, calls=%fused_computation.37 | convolution fusion | flops 23986176 | bytes 2061824 | tf_op jit(solution)/shard_map/dot_general | solution.py:31
  24.5 2.9 %collective-permute-done = f32[122,2,128]{2,1,0:T(2,128)S(1)} collective-permute-done((f32[122,2,128]{2,1,0:T(2,128)S(1)}, f32[122,2,128]{2,1,0:T(2,128)S(1)}, u32[]{:S(2)}, u32[]{:S(2)}) %collective-permute-start) | collective-permute-done | bytes 124960 | tf_op jit(solution)/shard_map/ppermute | solution.py:18
  27.5 0.1 reshape.26
  27.6 0.2 fusion.11
  27.7 0.2 fusion.5
  27.9 1.5 %collective-permute-start.2 = (f32[2,4148]{1,0:T(2,128)S(1)}, f32[2,4148]{1,0:T(2,128)S(1)}, u32[]{:S(2)}, u32[]{:S(2)}) collective-permute-start(f32[2,4148]{1,0:T(2,128)S(1)} %get-tuple-element.13), channel_id=1, source_target_pairs={{0,8},{8,16},{16,24},{24,0},{1,9},{9,17},{17,25},{25,1},{2,10},{10... | collective-permute-start | bytes 99560 | tf_op jit(solution)/shard_map/ppermute | solution.py:18
  29.4 1.4 %collective-permute-start.1 = (f32[2,4148]{1,0:T(2,128)S(1)}, f32[2,4148]{1,0:T(2,128)S(1)}, u32[]{:S(2)}, u32[]{:S(2)}) collective-permute-start(f32[2,4148]{1,0:T(2,128)S(1)} %get-tuple-element.12), channel_id=1, source_target_pairs={{0,24},{8,0},{16,8},{24,16},{1,25},{9,1},{17,9},{25,17},{2,26},{10... | collective-permute-start | bytes 99560 | tf_op jit(solution)/shard_map/ppermute | solution.py:18
  30.9 0.1 pad.4.clone
  30.9 2.0 %collective-permute-done.2 = f32[2,4148]{1,0:T(2,128)S(1)} collective-permute-done((f32[2,4148]{1,0:T(2,128)S(1)}, f32[2,4148]{1,0:T(2,128)S(1)}, u32[]{:S(2)}, u32[]{:S(2)}) %collective-permute-start.2) | collective-permute-done | bytes 33216 | tf_op jit(solution)/shard_map/ppermute | solution.py:18
  33.0 0.4 collective-permute-done.1
  33.3 0.4 fusion.6
  33.7 0.1 reshape.28
  33.8 1.7 %fusion.3 = f32[3904,128]{1,0:T(8,128)S(1)} fusion(pred[128,4]{0,1:T(4,128)(4,1)S(1)} %get-tuple-element.15, f32[2,4148]{1,0:T(2,128)S(1)} %collective-permute-done.1, f32[2,4148]{1,0:T(2,128)S(1)} %collective-permute-done.2), kind=kOutput, calls=%fused_computation.14 | convolution fusion | flops 24001792 | bytes 2065728 | tf_op jit(solution)/shard_map/dot_general | solution.py:31
  35.6 0.5 maximum_maximum_fusion.x_ref
  36.1 14.3 %shard_map.76 = (f32[2,20,32,128]{3,2,1,0:T(8,128)}, f32[2,20,32,128]{3,2,1,0:T(8,128)}, f32[2,20,32,128]{3,2,1,0:T(8,128)S(1)}) custom-call(f32[122,40,256]{2,1,0:T(8,128)S(1)} %maximum_maximum_fusion.x_ref), custom_call_target="tpu_custom_call" | custom-call | tf_op jit(solution)/shard_map/pallas_call | solution.py:213
  50.4 0.1 dynamic-slice_bitcast_fusion
  50.4 0.1 collective-permute-start.3
  50.6 1.5 %collective-permute-done.3 = f32[2,20,4,4,128]{4,3,2,1,0:T(4,128)S(1)} collective-permute-done((f32[2,20,4,4,128]{4,3,2,1,0:T(4,128)S(1)}, f32[2,20,4,4,128]{4,3,2,1,0:T(4,128)S(1)}, u32[]{:S(2)}, u32[]{:S(2)}) %collective-permute-start.3) | collective-permute-done | bytes 327712 | tf_op jit(solution)/shard_map/ppermute | solution.py:249
  52.1 0.1 bitcast_add_fusion
  52.2 0.1 dynamic-slice_bitcast_fusion.3
  52.3 3.6 %collective-permute-start.6 = (f32[2,20,4,128]{3,2,1,0:T(4,128)S(1)}, f32[2,20,4,128]{3,2,1,0:T(4,128)S(1)}, u32[]{:S(2)}, u32[]{:S(2)}) collective-permute-start(f32[2,20,4,128]{3,2,1,0:T(4,128)S(1)} %get-tuple-element.10), channel_id=1, source_target_pairs={{0,6},{1,7},{2,0},{3,1},{4,2},{5,3},{6,4},{7,5},{8,14},{9,15},{10,... | collective-permute-start | bytes 245768 | tf_op jit(solution)/shard_map/ppermute | solution.py:254
  55.9 0.0 collective-permute-start.5
  55.9 0.6 collective-permute-start.4
  56.5 2.2 %collective-permute-done.6 = f32[2,20,4,128]{3,2,1,0:T(4,128)S(1)} collective-permute-done((f32[2,20,4,128]{3,2,1,0:T(4,128)S(1)}, f32[2,20,4,128]{3,2,1,0:T(4,128)S(1)}, u32[]{:S(2)}, u32[]{:S(2)}) %collective-permute-start.6) | collective-permute-done | bytes 81952 | tf_op jit(solution)/shard_map/ppermute | solution.py:254
  58.8 5.2 %collective-permute-done.5 = f32[2,20,4,128]{3,2,1,0:T(4,128)S(1)} collective-permute-done((f32[2,20,4,128]{3,2,1,0:T(4,128)S(1)}, f32[2,20,4,128]{3,2,1,0:T(4,128)S(1)}, u32[]{:S(2)}, u32[]{:S(2)}) %collective-permute-start.5) | collective-permute-done | bytes 81952 | tf_op jit(solution)/shard_map/ppermute | solution.py:254
  63.9 0.0 collective-permute-done.4
  63.9 0.7 %fusion.1 = f32[2,20,4,128]{3,2,1,0:T(4,128)} fusion(f32[2,20,4,128]{3,2,1,0:T(4,128)S(1)} %collective-permute-done.6, f32[2,20,4,128]{3,2,1,0:T(4,128)S(1)} %collective-permute-done.5, f32[2,20,4,128]{3,2,1,0:T(4,128)S(1)} %collective-permute-done.4, f32[2,20,4,4,128]{4,3,2,1,0:T(4,128)S(1)} %bitcast_add_fusion, s32[]{:T(128)S(6)} %select_n.47), kind=kLoop, calls=%fused_computation.5 | loop fusion | flops 61440 | bytes 409604 | tf_op jit(solution)/shard_map/add | solution.py:254
  (9 shorter events, 0.1 us)
Async XLA Ops:
  0.6 19.1 %copy-start = (f32[1,2,20,32,128]{4,3,2,1,0:T(8,128)S(1)}, f32[1,2,20,32,128]{4,3,2,1,0:T(8,128)}, u32[]{:S(2)}) copy-start(f32[1,2,20,32,128]{4,3,2,1,0:T(8,128)} %param.9) | copy-start | bytes 1966084
  19.6 0.7 %copy-start.1 = (s32[32,128]{1,0:T(8,128)S(1)}, s32[32,128]{1,0:T(8,128)}, u32[]{:S(2)}) copy-start(s32[32,128]{1,0:T(8,128)} %param.7) | copy-start | bytes 49156
  19.6 0.7 %copy-start.2 = (s32[32,128]{1,0:T(8,128)S(1)}, s32[32,128]{1,0:T(8,128)}, u32[]{:S(2)}) copy-start(s32[32,128]{1,0:T(8,128)} %param.8) | copy-start | bytes 49156
  20.9 6.6 %collective-permute-start = (f32[122,2,128]{2,1,0:T(2,128)S(1)}, f32[122,2,128]{2,1,0:T(2,128)S(1)}, u32[]{:S(2)}, u32[]{:S(2)}) collective-permute-start(f32[122,2,128]{2,1,0:T(2,128)S(1)} %rev.3), channel_id=1, source_target_pairs={{0,24},{8,16},{16,8},{24,0},{1,25},{9,17},{17,9},{25,1},{2,26},{10... | collective-permute-start | bytes 374792 | tf_op jit(solution)/shard_map/ppermute | solution.py:18
  27.9 5.0 %collective-permute-start.2 = (f32[2,4148]{1,0:T(2,128)S(1)}, f32[2,4148]{1,0:T(2,128)S(1)}, u32[]{:S(2)}, u32[]{:S(2)}) collective-permute-start(f32[2,4148]{1,0:T(2,128)S(1)} %get-tuple-element.13), channel_id=1, source_target_pairs={{0,8},{8,16},{16,24},{24,0},{1,9},{9,17},{17,25},{25,1},{2,10},{10... | collective-permute-start | bytes 99560 | tf_op jit(solution)/shard_map/ppermute | solution.py:18
  29.4 3.9 %collective-permute-start.1 = (f32[2,4148]{1,0:T(2,128)S(1)}, f32[2,4148]{1,0:T(2,128)S(1)}, u32[]{:S(2)}, u32[]{:S(2)}) collective-permute-start(f32[2,4148]{1,0:T(2,128)S(1)} %get-tuple-element.12), channel_id=1, source_target_pairs={{0,24},{8,0},{16,8},{24,16},{1,25},{9,1},{17,9},{25,17},{2,26},{10... | collective-permute-start | bytes 99560 | tf_op jit(solution)/shard_map/ppermute | solution.py:18
  50.4 1.7 %collective-permute-start.3 = (f32[2,20,4,4,128]{4,3,2,1,0:T(4,128)S(1)}, f32[2,20,4,4,128]{4,3,2,1,0:T(4,128)S(1)}, u32[]{:S(2)}, u32[]{:S(2)}) collective-permute-start(f32[2,20,4,4,128]{4,3,2,1,0:T(4,128)S(1)} %dynamic-slice_bitcast_fusion), channel_id=1, source_target_pairs={{0,1},{1,0},{2,3},{3,2},{4,5},{5,4},{6,7},{7,6},{8,9},{9,8},{10,11... | collective-permute-start | bytes 983048 | tf_op jit(solution)/shard_map/ppermute | solution.py:249
  52.3 6.5 %collective-permute-start.6 = (f32[2,20,4,128]{3,2,1,0:T(4,128)S(1)}, f32[2,20,4,128]{3,2,1,0:T(4,128)S(1)}, u32[]{:S(2)}, u32[]{:S(2)}) collective-permute-start(f32[2,20,4,128]{3,2,1,0:T(4,128)S(1)} %get-tuple-element.10), channel_id=1, source_target_pairs={{0,6},{1,7},{2,0},{3,1},{4,2},{5,3},{6,4},{7,5},{8,14},{9,15},{10,... | collective-permute-start | bytes 245768 | tf_op jit(solution)/shard_map/ppermute | solution.py:254
  55.9 8.0 %collective-permute-start.5 = (f32[2,20,4,128]{3,2,1,0:T(4,128)S(1)}, f32[2,20,4,128]{3,2,1,0:T(4,128)S(1)}, u32[]{:S(2)}, u32[]{:S(2)}) collective-permute-start(f32[2,20,4,128]{3,2,1,0:T(4,128)S(1)} %get-tuple-element.11), channel_id=1, source_target_pairs={{0,4},{1,5},{2,6},{3,7},{4,0},{5,1},{6,2},{7,3},{8,12},{9,13},{10,... | collective-permute-start | bytes 245768 | tf_op jit(solution)/shard_map/ppermute | solution.py:254
  55.9 8.0 %collective-permute-start.4 = (f32[2,20,4,128]{3,2,1,0:T(4,128)S(1)}, f32[2,20,4,128]{3,2,1,0:T(4,128)S(1)}, u32[]{:S(2)}, u32[]{:S(2)}) collective-permute-start(f32[2,20,4,128]{3,2,1,0:T(4,128)S(1)} %get-tuple-element.9), channel_id=1, source_target_pairs={{0,2},{1,3},{2,4},{3,5},{4,6},{5,7},{6,0},{7,1},{8,10},{9,11},{10,... | collective-permute-start | bytes 245768 | tf_op jit(solution)/shard_map/ppermute | solution.py:254

commit v12 on v10

--- a/solution.py
+++ b/solution.py
@@ -194,7 +194,7 @@
     _, chans, levels, ny, width = tracers.shape
     lanes = width + 128
     rows = -(-(ny + 2) // 8) * 8
-    full_kappa = lax.all_gather(diffusivity, "scen", axis=2, tiled=True)
+    full_kappa = gathered_over_scen(diffusivity)
     fields = jnp.concatenate(
         [
             tracers[0].reshape(chans * levels, ny, width),
@@ -233,6 +233,28 @@
     return (final[None], adjoint[None], kappa_grad)
 
 
+def gathered_over_scen(block):
+    parts = lax.axis_size("scen")
+    if parts % 2:
+        return lax.all_gather(block, "scen", axis=2, tiled=True)
+    kinds, levels, rows, width = block.shape
+    me = lax.axis_index("scen")
+    core = me % 2
+    chip = me // 2
+    chips = parts // 2
+    got = [block]
+    for step in range(1, chips):
+        got.append(
+            lax.ppermute(block, "scen", [(q, ((q // 2 + step) % chips) * 2 + q % 2) for q in range(parts)])
+        )
+    same = jnp.stack(got)
+    other = lax.ppermute(same, "scen", [(q, q ^ 1) for q in range(parts)])
+    by_core = jnp.where(core == 0, jnp.stack([same, other], axis=1), jnp.stack([other, same], axis=1))
+    order = (chip - jnp.arange(chips)) % chips
+    by_chip = jnp.take(by_core, order, axis=0)
+    return by_chip.transpose(2, 3, 0, 1, 4, 5).reshape(kinds, levels, parts * rows, width)
+
+
 def summed_over_scen(grad):
     parts = lax.axis_size("scen")
     kinds, levels, ny, width = grad.shape

time: 59.6 us -> 57.2 us (0.960)
  blocking collectives: 16.8 us -> 0 us
  waiting for transfers between devices: 14.3 us -> 20.9 us
  starting transfers between devices: 9.77 us -> 16.1 us
  local copies, waits for them, and re-layouts: 3.74 us -> 4.61 us
    all_gather x1 -> x0, blocking collectives: 16.8 us -> none  [on_device(): full_kappa = lax.all_gather(diffusivity, 'scen', axis=2, tiled=True)]
    ppermute x0 -> x4, starting transfers between devices: none -> 7.08 us  [the longest x3 7.01 us: gathered_over_scen(): lax.ppermute(block, 'scen', [(q, (q // 2 + step) % chips * 2 + q % 2) for...]
    ppermute x0 -> x4, waiting for transfers between devices: none -> 3.72 us  [the longest x3 2.2 us: gathered_over_scen(): lax.ppermute(block, 'scen', [(q, (q // 2 + step) % chips * 2 + q % 2) for...]
    ppermute x3, waiting for transfers between devices: 5.35 us -> 7.59 us  [shifted(): return lax.ppermute(x, 'space', perm)]
    gather x0 -> x1, local copies, waits for them, and re-layouts: none -> 0.94 us  [gathered_over_scen(): by_chip = jnp.take(by_core, order, axis=0)]
    ppermute x3, waiting for transfers between devices: 7.38 us -> 8.01 us  [summed_over_scen(): lax.ppermute(send, 'scen', [(q, (q // 2 + step) % chips * 2 + q % 2) for...]
    unnamed x10 -> x9, local copies, waits for them, and re-layouts: 2.71 us -> 2.59 us
  transfers between devices with their start and end apart: 7 -> 11, of which waited for: 6 -> 10; matrix products, arithmetic and copies ran while one was open for 2% -> 6% of each run, Pallas kernels for 0% -> 0%
where the time goes in v12:
time: 57.2 us; the launch traced here: 56.9 us
  waiting for transfers between devices  20.9 us (37%)
  starting transfers between devices  16.1 us (28%)
  Pallas kernels  9.11 us (16%)
  local copies, waits for them, and re-layouts  4.61 us (8%)
  matrix products  3.31 us (6%)
  other arithmetic  2.02 us (4%)
  between operations  0.91 us (2%)
    pallas_call x1, Pallas kernels, on_device(): pl.pallas_call(diffusion_kernel, out_shape=(field, field, jax.ShapeDtypeS...  9.11 us
    ppermute x3, waiting for transfers between devices, summed_over_scen(): lax.ppermute(send, 'scen', [(q, (q // 2 + step) % chips * 2 + q % 2) for...  8.01 us
    ppermute x3, waiting for transfers between devices, shifted(): return lax.ppermute(x, 'space', perm)  7.59 us
    ppermute x3, starting transfers between devices, gathered_over_scen(): lax.ppermute(block, 'scen', [(q, (q // 2 + step) % chips * 2 + q % 2) for...  7.01 us
    ppermute x3, starting transfers between devices, shifted(): return lax.ppermute(x, 'space', perm)  4.98 us
    ppermute x3, starting transfers between devices, summed_over_scen(): lax.ppermute(send, 'scen', [(q, (q // 2 + step) % chips * 2 + q % 2) for...  3.96 us
    dot_general x4, matrix products, contract(): lax.dot_general(a, b, (dims, ((), ())), precision=lax.Precision.HIGHEST,...  3.31 us
    unnamed x9, local copies, waits for them, and re-layouts  2.59 us
  transfers between devices with their start and end apart: 11, of which 10 were waited for; matrix products, arithmetic and copies ran while one was open for 6% of the time, Pallas kernels for 0%

profile of v12, /device:TPU:0, one launch (start us, length us, event | category | flops | bytes accessed | tf_op | source)
XLA Modules:
  0.0 56.9 jit_solution(17513808788520076939)
XLA Ops:
  0.6 0.0 copy-start
  0.6 3.1 %collective-permute-start = (f32[2,20,4,128]{3,2,1,0:T(4,128)}, f32[2,20,4,128]{3,2,1,0:T(4,128)S(1)}, u32[]{:S(2)}, u32[]{:S(2)}) collective-permute-start(f32[2,20,4,128]{3,2,1,0:T(4,128)} %param.6), channel_id=1, source_target_pairs={{0,2},{1,3},{2,4},{3,5},{4,6},{5,7},{6,0},{7,1},{8,10},{9,11},{10,... | collective-permute-start | bytes 245768 | tf_op jit(solution)/shard_map/ppermute | solution.py:248
  3.7 2.6 %collective-permute-start.1 = (f32[2,20,4,128]{3,2,1,0:T(4,128)}, f32[2,20,4,128]{3,2,1,0:T(4,128)S(1)}, u32[]{:S(2)}, u32[]{:S(2)}) collective-permute-start(f32[2,20,4,128]{3,2,1,0:T(4,128)} %param.6), channel_id=1, source_target_pairs={{0,4},{1,5},{2,6},{3,7},{4,0},{5,1},{6,2},{7,3},{8,12},{9,13},{10,... | collective-permute-start | bytes 245768 | tf_op jit(solution)/shard_map/ppermute | solution.py:248
  6.3 1.3 %collective-permute-start.2 = (f32[2,20,4,128]{3,2,1,0:T(4,128)}, f32[2,20,4,128]{3,2,1,0:T(4,128)S(1)}, u32[]{:S(2)}, u32[]{:S(2)}) collective-permute-start(f32[2,20,4,128]{3,2,1,0:T(4,128)} %param.6), channel_id=1, source_target_pairs={{0,6},{1,7},{2,0},{3,1},{4,2},{5,3},{6,4},{7,5},{8,14},{9,15},{10,... | collective-permute-start | bytes 245768 | tf_op jit(solution)/shard_map/ppermute | solution.py:248
  7.7 1.1 %constant_dynamic-update-slice_fusion.2 = f32[122,32,128]{2,1,0:T(8,128)S(1)} fusion(f32[40,32,128]{2,1,0:T(8,128)} %bitcast.54), kind=kLoop, calls=%fused_computation.25 | loop fusion | bytes 1310720
  8.9 1.1 %constant_dynamic-update-slice_fusion.1 = f32[122,32,128]{2,1,0:T(8,128)S(1)} fusion(f32[122,32,128]{2,1,0:T(8,128)S(1)} %constant_dynamic-update-slice_fusion.2, f32[40,32,128]{2,1,0:T(8,128)} %bitcast.55), kind=kLoop, calls=%fused_computation.24 | loop fusion | bytes 1310720
  10.0 0.0 collective-permute-done
  10.0 2.0 %collective-permute-done.1 = f32[2,20,4,128]{3,2,1,0:T(4,128)S(1)} collective-permute-done((f32[2,20,4,128]{3,2,1,0:T(4,128)}, f32[2,20,4,128]{3,2,1,0:T(4,128)S(1)}, u32[]{:S(2)}, u32[]{:S(2)}) %collective-permute-start.1) | collective-permute-done | bytes 81952 | tf_op jit(solution)/shard_map/ppermute | solution.py:248
  12.0 0.2 collective-permute-done.2
  12.2 0.0 copy-done
  12.2 0.1 fusion.13
  12.3 0.1 collective-permute-start.3
  12.4 0.1 and_or_fusion.1
  12.5 1.5 %collective-permute-done.3 = f32[4,2,20,4,128]{4,3,2,1,0:T(4,128)S(1)} collective-permute-done((f32[4,2,20,4,128]{4,3,2,1,0:T(4,128)S(1)}, f32[4,2,20,4,128]{4,3,2,1,0:T(4,128)S(1)}, u32[]{:S(2)}, u32[]{:S(2)}) %collective-permute-start.3) | collective-permute-done | bytes 327712 | tf_op jit(solution)/shard_map/ppermute | solution.py:251
  14.0 0.1 maximum_select_fusion
  14.2 0.9 %gather_fusion = f32[4,2,2,20,4,128]{5,4,3,2,1,0:T(4,128)S(1)} fusion(f32[4,2,2,20,4,128]{5,4,3,2,0,1:T(4,128)S(1)} %maximum_select_fusion, s32[1024]{0:T(1024)S(1)} %pad_clamp_fusion), kind=kCustom, calls=%fused_computation | custom fusion | bytes 1310736 | tf_op jit(solution)/shard_map/jit(_take)/gather | solution.py:254
  15.1 0.0 copy-start.1
  15.1 0.0 copy-start.2
  15.2 0.2 select_bitcast_fusion
  15.4 0.2 copy.12
  15.6 0.3 copy-done.1
  15.9 0.0 copy-done.2
  15.9 0.1 slice.22
  15.9 0.5 rev.3
  16.4 2.5 %collective-permute-start.4 = (f32[122,2,128]{2,1,0:T(2,128)S(1)}, f32[122,2,128]{2,1,0:T(2,128)S(1)}, u32[]{:S(2)}, u32[]{:S(2)}) collective-permute-start(f32[122,2,128]{2,1,0:T(2,128)S(1)} %rev.3), channel_id=1, source_target_pairs={{0,24},{8,16},{16,8},{24,0},{1,25},{9,17},{17,9},{25,1},{2,26},{10... | collective-permute-start | bytes 374792 | tf_op jit(solution)/shard_map/ppermute | solution.py:18
  18.9 1.0 %fusion.14 = f32[4,3904]{1,0:T(4,128)S(1)} fusion(pred[128,4]{0,1:T(4,128)(4,1)S(1)} %get-tuple-element.16, f32[3904,128]{1,0:T(8,128)S(1)} %bitcast.51), kind=kOutput, calls=%fused_computation.55 | convolution fusion | flops 23986176 | bytes 2061824 | tf_op jit(solution)/shard_map/dot_general | solution.py:31
  20.0 2.8 %collective-permute-done.4 = f32[122,2,128]{2,1,0:T(2,128)S(1)} collective-permute-done((f32[122,2,128]{2,1,0:T(2,128)S(1)}, f32[122,2,128]{2,1,0:T(2,128)S(1)}, u32[]{:S(2)}, u32[]{:S(2)}) %collective-permute-start.4) | collective-permute-done | bytes 124960 | tf_op jit(solution)/shard_map/ppermute | solution.py:18
  22.8 0.1 reshape.76
  22.9 0.2 fusion.15
  23.1 0.2 fusion.5
  23.2 2.5 %collective-permute-start.5 = (f32[2,4148]{1,0:T(2,128)S(1)}, f32[2,4148]{1,0:T(2,128)S(1)}, u32[]{:S(2)}, u32[]{:S(2)}) collective-permute-start(f32[2,4148]{1,0:T(2,128)S(1)} %get-tuple-element.14), channel_id=1, source_target_pairs={{0,24},{8,0},{16,8},{24,16},{1,25},{9,1},{17,9},{25,17},{2,26},{10... | collective-permute-start | bytes 99560 | tf_op jit(solution)/shard_map/ppermute | solution.py:18
  25.7 0.0 collective-permute-start.6
  25.7 0.1 pad.4.clone
  25.8 1.5 %collective-permute-done.5 = f32[2,4148]{1,0:T(2,128)S(1)} collective-permute-done((f32[2,4148]{1,0:T(2,128)S(1)}, f32[2,4148]{1,0:T(2,128)S(1)}, u32[]{:S(2)}, u32[]{:S(2)}) %collective-permute-start.5) | collective-permute-done | bytes 33216 | tf_op jit(solution)/shard_map/ppermute | solution.py:18
  27.3 3.2 %collective-permute-done.6 = f32[2,4148]{1,0:T(2,128)S(1)} collective-permute-done((f32[2,4148]{1,0:T(2,128)S(1)}, f32[2,4148]{1,0:T(2,128)S(1)}, u32[]{:S(2)}, u32[]{:S(2)}) %collective-permute-start.6) | collective-permute-done | bytes 33216 | tf_op jit(solution)/shard_map/ppermute | solution.py:18
  30.5 0.4 fusion.6
  30.9 0.1 reshape.78
  31.0 1.7 %fusion.3 = f32[3904,128]{1,0:T(8,128)S(1)} fusion(pred[128,4]{0,1:T(4,128)(4,1)S(1)} %get-tuple-element.17, f32[2,4148]{1,0:T(2,128)S(1)} %collective-permute-done.5, f32[2,4148]{1,0:T(2,128)S(1)} %collective-permute-done.6), kind=kOutput, calls=%fused_computation.18 | convolution fusion | flops 24001792 | bytes 2065728 | tf_op jit(solution)/shard_map/dot_general | solution.py:31
  32.7 0.5 maximum_maximum_fusion.x_ref
  33.2 9.1 %shard_map.76 = (f32[2,20,32,128]{3,2,1,0:T(8,128)}, f32[2,20,32,128]{3,2,1,0:T(8,128)}, f32[2,20,32,128]{3,2,1,0:T(8,128)S(1)}) custom-call(f32[122,40,256]{2,1,0:T(8,128)S(1)} %maximum_maximum_fusion.x_ref), custom_call_target="tpu_custom_call" | custom-call | tf_op jit(solution)/shard_map/pallas_call | solution.py:213
  42.3 0.1 dynamic-slice_bitcast_fusion
  42.4 0.1 collective-permute-start.7
  42.6 1.5 %collective-permute-done.7 = f32[2,20,4,4,128]{4,3,2,1,0:T(4,128)S(1)} collective-permute-done((f32[2,20,4,4,128]{4,3,2,1,0:T(4,128)S(1)}, f32[2,20,4,4,128]{4,3,2,1,0:T(4,128)S(1)}, u32[]{:S(2)}, u32[]{:S(2)}) %collective-permute-start.7) | collective-permute-done | bytes 327712 | tf_op jit(solution)/shard_map/ppermute | solution.py:271
  44.1 0.1 bitcast_add_fusion
  44.2 0.1 dynamic-slice_bitcast_fusion.3
  44.3 3.3 %collective-permute-start.10 = (f32[2,20,4,128]{3,2,1,0:T(4,128)S(1)}, f32[2,20,4,128]{3,2,1,0:T(4,128)S(1)}, u32[]{:S(2)}, u32[]{:S(2)}) collective-permute-start(f32[2,20,4,128]{3,2,1,0:T(4,128)S(1)} %get-tuple-element.10), channel_id=1, source_target_pairs={{0,6},{1,7},{2,0},{3,1},{4,2},{5,3},{6,4},{7,5},{8,14},{9,15},{10,... | collective-permute-start | bytes 245768 | tf_op jit(solution)/shard_map/ppermute | solution.py:276
  47.6 0.0 collective-permute-start.8
  47.6 0.6 %collective-permute-start.9 = (f32[2,20,4,128]{3,2,1,0:T(4,128)S(1)}, f32[2,20,4,128]{3,2,1,0:T(4,128)S(1)}, u32[]{:S(2)}, u32[]{:S(2)}) collective-permute-start(f32[2,20,4,128]{3,2,1,0:T(4,128)S(1)} %get-tuple-element.11), channel_id=1, source_target_pairs={{0,4},{1,5},{2,6},{3,7},{4,0},{5,1},{6,2},{7,3},{8,12},{9,13},{10,... | collective-permute-start | bytes 245768 | tf_op jit(solution)/shard_map/ppermute | solution.py:276
  48.2 2.2 %collective-permute-done.10 = f32[2,20,4,128]{3,2,1,0:T(4,128)S(1)} collective-permute-done((f32[2,20,4,128]{3,2,1,0:T(4,128)S(1)}, f32[2,20,4,128]{3,2,1,0:T(4,128)S(1)}, u32[]{:S(2)}, u32[]{:S(2)}) %collective-permute-start.10) | collective-permute-done | bytes 81952 | tf_op jit(solution)/shard_map/ppermute | solution.py:276
  50.4 4.2 %collective-permute-done.8 = f32[2,20,4,128]{3,2,1,0:T(4,128)S(1)} collective-permute-done((f32[2,20,4,128]{3,2,1,0:T(4,128)S(1)}, f32[2,20,4,128]{3,2,1,0:T(4,128)S(1)}, u32[]{:S(2)}, u32[]{:S(2)}) %collective-permute-start.8) | collective-permute-done | bytes 81952 | tf_op jit(solution)/shard_map/ppermute | solution.py:276
  54.6 1.7 %collective-permute-done.9 = f32[2,20,4,128]{3,2,1,0:T(4,128)S(1)} collective-permute-done((f32[2,20,4,128]{3,2,1,0:T(4,128)S(1)}, f32[2,20,4,128]{3,2,1,0:T(4,128)S(1)}, u32[]{:S(2)}, u32[]{:S(2)}) %collective-permute-start.9) | collective-permute-done | bytes 81952 | tf_op jit(solution)/shard_map/ppermute | solution.py:276
  56.2 0.7 %fusion.1 = f32[2,20,4,128]{3,2,1,0:T(4,128)} fusion(f32[2,20,4,128]{3,2,1,0:T(4,128)S(1)} %collective-permute-done.10, f32[2,20,4,128]{3,2,1,0:T(4,128)S(1)} %collective-permute-done.9, f32[2,20,4,128]{3,2,1,0:T(4,128)S(1)} %collective-permute-done.8, f32[2,20,4,4,128]{4,3,2,1,0:T(4,128)S(1)} %bitcast_add_fusion, s32[]{:T(128)S(6)} %select_n.107), kind=kLoop, calls=%fused_computation.9 | loop fusion | flops 61440 | bytes 409604 | tf_op jit(solution)/shard_map/add | solution.py:276
  (11 shorter events, 0.1 us)
Async XLA Ops:
  0.6 11.6 %copy-start = (f32[2,20,4,128]{3,2,1,0:T(4,128)S(1)}, f32[2,20,4,128]{3,2,1,0:T(4,128)}, u32[]{:S(2)}) copy-start(f32[2,20,4,128]{3,2,1,0:T(4,128)} %param.6) | copy-start | bytes 245764
  0.6 9.4 %collective-permute-start = (f32[2,20,4,128]{3,2,1,0:T(4,128)}, f32[2,20,4,128]{3,2,1,0:T(4,128)S(1)}, u32[]{:S(2)}, u32[]{:S(2)}) collective-permute-start(f32[2,20,4,128]{3,2,1,0:T(4,128)} %param.6), channel_id=1, source_target_pairs={{0,2},{1,3},{2,4},{3,5},{4,6},{5,7},{6,0},{7,1},{8,10},{9,11},{10,... | collective-permute-start | bytes 245768 | tf_op jit(solution)/shard_map/ppermute | solution.py:248
  3.7 8.3 %collective-permute-start.1 = (f32[2,20,4,128]{3,2,1,0:T(4,128)}, f32[2,20,4,128]{3,2,1,0:T(4,128)S(1)}, u32[]{:S(2)}, u32[]{:S(2)}) collective-permute-start(f32[2,20,4,128]{3,2,1,0:T(4,128)} %param.6), channel_id=1, source_target_pairs={{0,4},{1,5},{2,6},{3,7},{4,0},{5,1},{6,2},{7,3},{8,12},{9,13},{10,... | collective-permute-start | bytes 245768 | tf_op jit(solution)/shard_map/ppermute | solution.py:248
  6.3 5.9 %collective-permute-start.2 = (f32[2,20,4,128]{3,2,1,0:T(4,128)}, f32[2,20,4,128]{3,2,1,0:T(4,128)S(1)}, u32[]{:S(2)}, u32[]{:S(2)}) collective-permute-start(f32[2,20,4,128]{3,2,1,0:T(4,128)} %param.6), channel_id=1, source_target_pairs={{0,6},{1,7},{2,0},{3,1},{4,2},{5,3},{6,4},{7,5},{8,14},{9,15},{10,... | collective-permute-start | bytes 245768 | tf_op jit(solution)/shard_map/ppermute | solution.py:248
  12.3 1.7 %collective-permute-start.3 = (f32[4,2,20,4,128]{4,3,2,1,0:T(4,128)S(1)}, f32[4,2,20,4,128]{4,3,2,1,0:T(4,128)S(1)}, u32[]{:S(2)}, u32[]{:S(2)}) collective-permute-start(f32[4,2,20,4,128]{4,3,2,1,0:T(4,128)S(1)} %get-tuple-element.13), channel_id=1, source_target_pairs={{0,1},{1,0},{2,3},{3,2},{4,5},{5,4},{6,7},{7,6},{8,9},{9,8},{10,11... | collective-permute-start | bytes 983048 | tf_op jit(solution)/shard_map/ppermute | solution.py:251
  15.1 0.7 %copy-start.1 = (s32[32,128]{1,0:T(8,128)S(1)}, s32[32,128]{1,0:T(8,128)}, u32[]{:S(2)}) copy-start(s32[32,128]{1,0:T(8,128)} %param.7) | copy-start | bytes 49156
  15.1 0.7 %copy-start.2 = (s32[32,128]{1,0:T(8,128)S(1)}, s32[32,128]{1,0:T(8,128)}, u32[]{:S(2)}) copy-start(s32[32,128]{1,0:T(8,128)} %param.8) | copy-start | bytes 49156
  16.4 6.4 %collective-permute-start.4 = (f32[122,2,128]{2,1,0:T(2,128)S(1)}, f32[122,2,128]{2,1,0:T(2,128)S(1)}, u32[]{:S(2)}, u32[]{:S(2)}) collective-permute-start(f32[122,2,128]{2,1,0:T(2,128)S(1)} %rev.3), channel_id=1, source_target_pairs={{0,24},{8,16},{16,8},{24,0},{1,25},{9,17},{17,9},{25,1},{2,26},{10... | collective-permute-start | bytes 374792 | tf_op jit(solution)/shard_map/ppermute | solution.py:18
  23.2 4.1 %collective-permute-start.5 = (f32[2,4148]{1,0:T(2,128)S(1)}, f32[2,4148]{1,0:T(2,128)S(1)}, u32[]{:S(2)}, u32[]{:S(2)}) collective-permute-start(f32[2,4148]{1,0:T(2,128)S(1)} %get-tuple-element.14), channel_id=1, source_target_pairs={{0,24},{8,0},{16,8},{24,16},{1,25},{9,1},{17,9},{25,17},{2,26},{10... | collective-permute-start | bytes 99560 | tf_op jit(solution)/shard_map/ppermute | solution.py:18
  25.7 4.8 %collective-permute-start.6 = (f32[2,4148]{1,0:T(2,128)S(1)}, f32[2,4148]{1,0:T(2,128)S(1)}, u32[]{:S(2)}, u32[]{:S(2)}) collective-permute-start(f32[2,4148]{1,0:T(2,128)S(1)} %get-tuple-element.15), channel_id=1, source_target_pairs={{0,8},{8,16},{16,24},{24,0},{1,9},{9,17},{17,25},{25,1},{2,10},{10... | collective-permute-start | bytes 99560 | tf_op jit(solution)/shard_map/ppermute | solution.py:18
  42.4 1.7 %collective-permute-start.7 = (f32[2,20,4,4,128]{4,3,2,1,0:T(4,128)S(1)}, f32[2,20,4,4,128]{4,3,2,1,0:T(4,128)S(1)}, u32[]{:S(2)}, u32[]{:S(2)}) collective-permute-start(f32[2,20,4,4,128]{4,3,2,1,0:T(4,128)S(1)} %dynamic-slice_bitcast_fusion), channel_id=1, source_target_pairs={{0,1},{1,0},{2,3},{3,2},{4,5},{5,4},{6,7},{7,6},{8,9},{9,8},{10,11... | collective-permute-start | bytes 983048 | tf_op jit(solution)/shard_map/ppermute | solution.py:271
  44.3 6.1 %collective-permute-start.10 = (f32[2,20,4,128]{3,2,1,0:T(4,128)S(1)}, f32[2,20,4,128]{3,2,1,0:T(4,128)S(1)}, u32[]{:S(2)}, u32[]{:S(2)}) collective-permute-start(f32[2,20,4,128]{3,2,1,0:T(4,128)S(1)} %get-tuple-element.10), channel_id=1, source_target_pairs={{0,6},{1,7},{2,0},{3,1},{4,2},{5,3},{6,4},{7,5},{8,14},{9,15},{10,... | collective-permute-start | bytes 245768 | tf_op jit(solution)/shard_map/ppermute | solution.py:276
  47.6 7.0 %collective-permute-start.8 = (f32[2,20,4,128]{3,2,1,0:T(4,128)S(1)}, f32[2,20,4,128]{3,2,1,0:T(4,128)S(1)}, u32[]{:S(2)}, u32[]{:S(2)}) collective-permute-start(f32[2,20,4,128]{3,2,1,0:T(4,128)S(1)} %get-tuple-element.9), channel_id=1, source_target_pairs={{0,2},{1,3},{2,4},{3,5},{4,6},{5,7},{6,0},{7,1},{8,10},{9,11},{10,... | collective-permute-start | bytes 245768 | tf_op jit(solution)/shard_map/ppermute | solution.py:276
  47.6 8.6 %collective-permute-start.9 = (f32[2,20,4,128]{3,2,1,0:T(4,128)S(1)}, f32[2,20,4,128]{3,2,1,0:T(4,128)S(1)}, u32[]{:S(2)}, u32[]{:S(2)}) collective-permute-start(f32[2,20,4,128]{3,2,1,0:T(4,128)S(1)} %get-tuple-element.11), channel_id=1, source_target_pairs={{0,4},{1,5},{2,6},{3,7},{4,0},{5,1},{6,2},{7,3},{8,12},{9,13},{10,... | collective-permute-start | bytes 245768 | tf_op jit(solution)/shard_map/ppermute | solution.py:276

commit v13 on v12

--- a/solution.py
+++ b/solution.py
@@ -37,22 +37,19 @@
     n = lax.axis_size("space")
     count, ny, width = fields.shape
     spare = lanes - width
+    flat = fields.reshape(count * ny, width)
+    edges = contract(picker(width, [width - 2, width - 1, 0, 1]), flat, ((0,), (1,)))
+    west = shifted(edges[0:2], [(q, (q + 1) % n) for q in range(n)])
+    east = shifted(edges[2:4], [(q, (q - 1) % n) for q in range(n)])
     mirrored = fields[:, ny - 1:ny - 3:-1, ::-1]
     ghost = shifted(mirrored, [(q, n - 1 - q) for q in range(n)])
-    pick = picker(width, [width - 2, width - 1, 0, 1])
-    edges = jnp.concatenate(
-        [
-            contract(pick, fields.reshape(count * ny, width), ((0,), (1,))),
-            contract(pick, ghost.reshape(count * 2, width), ((0,), (1,))),
-        ],
-        axis=1,
-    )
-    west = shifted(edges[0:2], [(q, (q + 1) % n) for q in range(n)])
-    east = shifted(edges[2:4], [(q, (q - 1) % n) for q in range(n)])
+    top_edges = edges.reshape(4, count, ny)[:, :, ny - 1:ny - 3:-1]
+    ghost_east = shifted(top_edges[1::-1], [(q, (n - 2 - q) % n) for q in range(n)])
+    ghost_west = shifted(top_edges[3:1:-1], [(q, (n - q) % n) for q in range(n)])
     place = picker(spare, [0, 1, spare - 2, spare - 1]).T
-    halo = jnp.concatenate([east, west])
-    side = contract(halo[:, :count * ny], place, ((0,), (0,))).reshape(count, ny, spare)
-    ghost_side = contract(halo[:, count * ny:], place, ((0,), (0,))).reshape(count, 2, spare)
+    side = contract(jnp.concatenate([east, west]), place, ((0,), (0,))).reshape(count, ny, spare)
+    ghost_halo = jnp.concatenate([ghost_east, ghost_west]).reshape(4, count * 2)
+    ghost_side = contract(ghost_halo, place, ((0,), (0,))).reshape(count, 2, spare)
     top = jnp.concatenate([fields, side], axis=-1)
     folded = jnp.concatenate([ghost, ghost_side], axis=-1)
     pad = jnp.zeros((count, rows - ny - 2, lanes), fields.dtype)

time: 57.2 us -> 53 us (0.927)
  waiting for transfers between devices: 20.9 us -> 11.8 us
  starting transfers between devices: 16.1 us -> 20.2 us
  local copies, waits for them, and re-layouts: 4.61 us -> 5.59 us
    ppermute x3 -> x5, waiting for transfers between devices: 7.59 us -> 0.99 us  [shifted(): return lax.ppermute(x, 'space', perm)]
    ppermute x3 -> x5, starting transfers between devices: 4.98 us -> 8.58 us  [shifted(): return lax.ppermute(x, 'space', perm)]
    ppermute x3, waiting for transfers between devices: 8.01 us -> 5.59 us  [summed_over_scen(): lax.ppermute(send, 'scen', [(q, (q // 2 + step) % chips * 2 + q % 2) for...]
    dot_general x4 -> x3, matrix products: 3.31 us -> 2.96 us  [contract(): lax.dot_general(a, b, (dims, ((), ())), precision=lax.Precision.HIGHEST,...]
  transfers between devices with their start and end apart: 11 -> 13, of which waited for: 10 -> 9; matrix products, arithmetic and copies ran while one was open for 6% -> 11% of each run, Pallas kernels for 0% -> 0%
where the time goes in v13:
time: 53 us; the launch traced here: 52.5 us
  starting transfers between devices  20.2 us (38%)
  waiting for transfers between devices  11.8 us (22%)
  Pallas kernels  9.11 us (17%)
  local copies, waits for them, and re-layouts  5.59 us (11%)
  matrix products  2.96 us (6%)
  other arithmetic  1.87 us (4%)
  between operations  0.97 us (2%)
    pallas_call x1, Pallas kernels, on_device(): pl.pallas_call(diffusion_kernel, out_shape=(field, field, jax.ShapeDtypeS...  9.11 us
    ppermute x5, starting transfers between devices, shifted(): return lax.ppermute(x, 'space', perm)  8.58 us
    ppermute x3, starting transfers between devices, gathered_over_scen(): lax.ppermute(block, 'scen', [(q, (q // 2 + step) % chips * 2 + q % 2) for...  7.01 us
    ppermute x3, waiting for transfers between devices, summed_over_scen(): lax.ppermute(send, 'scen', [(q, (q // 2 + step) % chips * 2 + q % 2) for...  5.59 us
    ppermute x3, starting transfers between devices, summed_over_scen(): lax.ppermute(send, 'scen', [(q, (q // 2 + step) % chips * 2 + q % 2) for...  4.5 us
    dot_general x3, matrix products, contract(): lax.dot_general(a, b, (dims, ((), ())), precision=lax.Precision.HIGHEST,...  2.96 us
    unnamed x9, local copies, waits for them, and re-layouts  2.59 us
    ppermute x3, waiting for transfers between devices, gathered_over_scen(): lax.ppermute(block, 'scen', [(q, (q // 2 + step) % chips * 2 + q % 2) for...  2.12 us
  transfers between devices with their start and end apart: 13, of which 9 were waited for; matrix products, arithmetic and copies ran while one was open for 11% of the time, Pallas kernels for 0%

profile of v13, /device:TPU:0, one launch (start us, length us, event | category | flops | bytes accessed | tf_op | source)
XLA Modules:
  0.0 52.5 jit_solution(12683552456450103031)
XLA Ops:
  0.6 0.0 copy-start
  0.6 3.1 %collective-permute-start = (f32[2,20,4,128]{3,2,1,0:T(4,128)}, f32[2,20,4,128]{3,2,1,0:T(4,128)S(1)}, u32[]{:S(2)}, u32[]{:S(2)}) collective-permute-start(f32[2,20,4,128]{3,2,1,0:T(4,128)} %param.6), channel_id=1, source_target_pairs={{0,2},{1,3},{2,4},{3,5},{4,6},{5,7},{6,0},{7,1},{8,10},{9,11},{10,... | collective-permute-start | bytes 245768 | tf_op jit(solution)/shard_map/ppermute | solution.py:245
  3.7 2.6 %collective-permute-start.1 = (f32[2,20,4,128]{3,2,1,0:T(4,128)}, f32[2,20,4,128]{3,2,1,0:T(4,128)S(1)}, u32[]{:S(2)}, u32[]{:S(2)}) collective-permute-start(f32[2,20,4,128]{3,2,1,0:T(4,128)} %param.6), channel_id=1, source_target_pairs={{0,4},{1,5},{2,6},{3,7},{4,0},{5,1},{6,2},{7,3},{8,12},{9,13},{10,... | collective-permute-start | bytes 245768 | tf_op jit(solution)/shard_map/ppermute | solution.py:245
  6.3 1.3 %collective-permute-start.2 = (f32[2,20,4,128]{3,2,1,0:T(4,128)}, f32[2,20,4,128]{3,2,1,0:T(4,128)S(1)}, u32[]{:S(2)}, u32[]{:S(2)}) collective-permute-start(f32[2,20,4,128]{3,2,1,0:T(4,128)} %param.6), channel_id=1, source_target_pairs={{0,6},{1,7},{2,0},{3,1},{4,2},{5,3},{6,4},{7,5},{8,14},{9,15},{10,... | collective-permute-start | bytes 245768 | tf_op jit(solution)/shard_map/ppermute | solution.py:245
  7.7 1.1 %constant_dynamic-update-slice_fusion.2 = f32[122,32,128]{2,1,0:T(8,128)S(1)} fusion(f32[40,32,128]{2,1,0:T(8,128)} %bitcast.54), kind=kLoop, calls=%fused_computation.24 | loop fusion | bytes 1310720
  8.9 1.1 %constant_dynamic-update-slice_fusion.1 = f32[122,32,128]{2,1,0:T(8,128)S(1)} fusion(f32[122,32,128]{2,1,0:T(8,128)S(1)} %constant_dynamic-update-slice_fusion.2, f32[40,32,128]{2,1,0:T(8,128)} %bitcast.55), kind=kLoop, calls=%fused_computation.23 | loop fusion | bytes 1310720
  10.0 0.1 pad.4.clone
  10.1 0.0 collective-permute-done
  10.1 1.9 %collective-permute-done.1 = f32[2,20,4,128]{3,2,1,0:T(4,128)S(1)} collective-permute-done((f32[2,20,4,128]{3,2,1,0:T(4,128)}, f32[2,20,4,128]{3,2,1,0:T(4,128)S(1)}, u32[]{:S(2)}, u32[]{:S(2)}) %collective-permute-start.1) | collective-permute-done | bytes 81952 | tf_op jit(solution)/shard_map/ppermute | solution.py:245
  12.0 0.2 collective-permute-done.2
  12.2 0.0 copy-done
  12.2 0.1 fusion.29
  12.3 0.1 collective-permute-start.3
  12.4 0.1 and_or_fusion
  12.5 1.5 %collective-permute-done.3 = f32[4,2,20,4,128]{4,3,2,1,0:T(4,128)S(1)} collective-permute-done((f32[4,2,20,4,128]{4,3,2,1,0:T(4,128)S(1)}, f32[4,2,20,4,128]{4,3,2,1,0:T(4,128)S(1)}, u32[]{:S(2)}, u32[]{:S(2)}) %collective-permute-start.3) | collective-permute-done | bytes 327712 | tf_op jit(solution)/shard_map/ppermute | solution.py:248
  14.0 0.1 maximum_select_fusion
  14.2 0.9 %gather_fusion = f32[4,2,2,20,4,128]{5,4,3,2,1,0:T(4,128)S(1)} fusion(f32[4,2,2,20,4,128]{5,4,3,2,0,1:T(4,128)S(1)} %maximum_select_fusion, s32[1024]{0:T(1024)S(1)} %pad_clamp_fusion), kind=kCustom, calls=%fused_computation | custom fusion | bytes 1310736 | tf_op jit(solution)/shard_map/jit(_take)/gather | solution.py:251
  15.1 0.0 copy-start.1
  15.1 0.0 copy-start.2
  15.2 0.2 select_bitcast_fusion
  15.4 0.2 copy.24
  15.6 0.3 copy-done.1
  15.9 0.0 copy-done.2
  15.9 1.0 %fusion.9 = f32[4,3904]{1,0:T(4,128)S(1)} fusion(f32[3904,128]{1,0:T(8,128)S(1)} %bitcast.51, pred[128]{0:T(512)(128)(4,1)S(1)} %get-tuple-element.20, pred[128]{0:T(512)(128)(4,1)S(1)} %get-tuple-element.21, pred[128]{0:T(512)(128)(4,1)S(1)} %get-tuple-element.22, pred[128]{0:T(512)(128)(4,1)S(1)} %get-tuple-element.23, ...), kind=kOutput, calls=%fused_computation.34 | convolution fusion | flops 23989760 | bytes 2061840 | tf_op jit(solution)/shard_map/dot_general | solution.py:31
  16.9 0.1 reshape.79
  17.0 0.1 fusion.30
  17.2 0.2 rev.11
  17.4 3.4 %collective-permute-start.7 = (f32[2,122,2]{2,1,0:T(8,128)S(1)}, f32[2,122,2]{2,1,0:T(8,128)S(1)}, u32[]{:S(2)}, u32[]{:S(2)}) collective-permute-start(f32[2,122,2]{2,1,0:T(8,128)S(1)} %rev.11), channel_id=1, source_target_pairs={{0,16},{8,8},{16,0},{24,24},{1,17},{9,9},{17,1},{25,25},{2,18},{10... | collective-permute-start | bytes 5864 | tf_op jit(solution)/shard_map/ppermute | solution.py:18
  20.8 0.2 rev.12
  21.0 0.7 %collective-permute-start.8 = (f32[2,122,2]{2,1,0:T(8,128)S(1)}, f32[2,122,2]{2,1,0:T(8,128)S(1)}, u32[]{:S(2)}, u32[]{:S(2)}) collective-permute-start(f32[2,122,2]{2,1,0:T(8,128)S(1)} %rev.12), channel_id=1, source_target_pairs={{0,0},{8,24},{16,16},{24,8},{1,1},{9,25},{17,17},{25,9},{2,2},{10,... | collective-permute-start | bytes 5864 | tf_op jit(solution)/shard_map/ppermute | solution.py:18
  21.7 0.1 slice.29
  21.8 1.5 %collective-permute-start.4 = (f32[2,3904]{1,0:T(2,128)S(1)}, f32[2,3904]{1,0:T(2,128)S(1)}, u32[]{:S(2)}, u32[]{:S(2)}) collective-permute-start(f32[2,3904]{1,0:T(2,128)S(1)} %get-tuple-element.16), channel_id=1, source_target_pairs={{0,24},{8,0},{16,8},{24,16},{1,25},{9,1},{17,9},{25,17},{2,26},{10... | collective-permute-start | bytes 93704 | tf_op jit(solution)/shard_map/ppermute | solution.py:18
  23.3 0.6 %collective-permute-start.5 = (f32[2,3904]{1,0:T(2,128)S(1)}, f32[2,3904]{1,0:T(2,128)S(1)}, u32[]{:S(2)}, u32[]{:S(2)}) collective-permute-start(f32[2,3904]{1,0:T(2,128)S(1)} %get-tuple-element.17), channel_id=1, source_target_pairs={{0,8},{8,16},{16,24},{24,0},{1,9},{9,17},{17,25},{25,1},{2,10},{10... | collective-permute-start | bytes 93704 | tf_op jit(solution)/shard_map/ppermute | solution.py:18
  23.8 0.5 rev.10
  24.3 2.4 %collective-permute-start.6 = (f32[122,2,128]{2,1,0:T(2,128)S(1)}, f32[122,2,128]{2,1,0:T(2,128)S(1)}, u32[]{:S(2)}, u32[]{:S(2)}) collective-permute-start(f32[122,2,128]{2,1,0:T(2,128)S(1)} %rev.10), channel_id=1, source_target_pairs={{0,24},{8,16},{16,8},{24,0},{1,25},{9,17},{17,9},{25,1},{2,26},{10... | collective-permute-start | bytes 374792 | tf_op jit(solution)/shard_map/ppermute | solution.py:18
  26.7 0.0 collective-permute-done.7
  26.7 0.0 collective-permute-done.8
  26.8 0.2 reshape.91
  26.9 0.1 copy.30
  27.1 0.1 dot_general.16
  27.2 0.2 fusion
  27.4 0.1 copy.27
  27.5 0.0 collective-permute-done.4
  27.5 0.8 %collective-permute-done.5 = f32[2,3904]{1,0:T(2,128)S(1)} collective-permute-done((f32[2,3904]{1,0:T(2,128)S(1)}, f32[2,3904]{1,0:T(2,128)S(1)}, u32[]{:S(2)}, u32[]{:S(2)}) %collective-permute-start.5) | collective-permute-done | bytes 31264 | tf_op jit(solution)/shard_map/ppermute | solution.py:18
  28.3 1.7 %fusion.4 = f32[3904,128]{1,0:T(8,128)S(1)} fusion(pred[128,4]{0,1:T(4,128)(4,1)S(1)} %and_or_fusion, f32[2,3904]{1,0:T(2,128)S(1)} %collective-permute-done.5, f32[2,3904]{1,0:T(2,128)S(1)} %collective-permute-done.4), kind=kOutput, calls=%fused_computation.16 | convolution fusion | flops 24001792 | bytes 2061824 | tf_op jit(solution)/shard_map/dot_general | solution.py:31
  30.1 0.1 collective-permute-done.6
  30.2 0.5 maximum_maximum_fusion.x_ref
  30.7 9.1 %shard_map.76 = (f32[2,20,32,128]{3,2,1,0:T(8,128)}, f32[2,20,32,128]{3,2,1,0:T(8,128)}, f32[2,20,32,128]{3,2,1,0:T(8,128)S(1)}) custom-call(f32[122,40,256]{2,1,0:T(8,128)S(1)} %maximum_maximum_fusion.x_ref), custom_call_target="tpu_custom_call" | custom-call | tf_op jit(solution)/shard_map/pallas_call | solution.py:210
  39.8 0.1 dynamic-slice_bitcast_fusion
  39.9 0.1 collective-permute-start.9
  40.0 1.5 %collective-permute-done.9 = f32[2,20,4,4,128]{4,3,2,1,0:T(4,128)S(1)} collective-permute-done((f32[2,20,4,4,128]{4,3,2,1,0:T(4,128)S(1)}, f32[2,20,4,4,128]{4,3,2,1,0:T(4,128)S(1)}, u32[]{:S(2)}, u32[]{:S(2)}) %collective-permute-start.9) | collective-permute-done | bytes 327712 | tf_op jit(solution)/shard_map/ppermute | solution.py:268
  41.6 0.1 bitcast_add_fusion
  41.7 0.1 dynamic-slice_bitcast_fusion.3
  41.7 2.1 %collective-permute-start.10 = (f32[2,20,4,128]{3,2,1,0:T(4,128)S(1)}, f32[2,20,4,128]{3,2,1,0:T(4,128)S(1)}, u32[]{:S(2)}, u32[]{:S(2)}) collective-permute-start(f32[2,20,4,128]{3,2,1,0:T(4,128)S(1)} %get-tuple-element.9), channel_id=1, source_target_pairs={{0,2},{1,3},{2,4},{3,5},{4,6},{5,7},{6,0},{7,1},{8,10},{9,11},{10,... | collective-permute-start | bytes 245768 | tf_op jit(solution)/shard_map/ppermute | solution.py:273
  43.8 1.8 %collective-permute-start.11 = (f32[2,20,4,128]{3,2,1,0:T(4,128)S(1)}, f32[2,20,4,128]{3,2,1,0:T(4,128)S(1)}, u32[]{:S(2)}, u32[]{:S(2)}) collective-permute-start(f32[2,20,4,128]{3,2,1,0:T(4,128)S(1)} %get-tuple-element.11), channel_id=1, source_target_pairs={{0,4},{1,5},{2,6},{3,7},{4,0},{5,1},{6,2},{7,3},{8,12},{9,13},{10,... | collective-permute-start | bytes 245768 | tf_op jit(solution)/shard_map/ppermute | solution.py:273
  45.6 0.6 %collective-permute-start.12 = (f32[2,20,4,128]{3,2,1,0:T(4,128)S(1)}, f32[2,20,4,128]{3,2,1,0:T(4,128)S(1)}, u32[]{:S(2)}, u32[]{:S(2)}) collective-permute-start(f32[2,20,4,128]{3,2,1,0:T(4,128)S(1)} %get-tuple-element.10), channel_id=1, source_target_pairs={{0,6},{1,7},{2,0},{3,1},{4,2},{5,3},{6,4},{7,5},{8,14},{9,15},{10,... | collective-permute-start | bytes 245768 | tf_op jit(solution)/shard_map/ppermute | solution.py:273
  46.2 2.7 %collective-permute-done.10 = f32[2,20,4,128]{3,2,1,0:T(4,128)S(1)} collective-permute-done((f32[2,20,4,128]{3,2,1,0:T(4,128)S(1)}, f32[2,20,4,128]{3,2,1,0:T(4,128)S(1)}, u32[]{:S(2)}, u32[]{:S(2)}) %collective-permute-start.10) | collective-permute-done | bytes 81952 | tf_op jit(solution)/shard_map/ppermute | solution.py:273
  49.0 2.7 %collective-permute-done.11 = f32[2,20,4,128]{3,2,1,0:T(4,128)S(1)} collective-permute-done((f32[2,20,4,128]{3,2,1,0:T(4,128)S(1)}, f32[2,20,4,128]{3,2,1,0:T(4,128)S(1)}, u32[]{:S(2)}, u32[]{:S(2)}) %collective-permute-start.11) | collective-permute-done | bytes 81952 | tf_op jit(solution)/shard_map/ppermute | solution.py:273
  51.7 0.1 collective-permute-done.12
  51.8 0.7 %fusion.3 = f32[2,20,4,128]{3,2,1,0:T(4,128)} fusion(f32[2,20,4,128]{3,2,1,0:T(4,128)S(1)} %collective-permute-done.12, f32[2,20,4,128]{3,2,1,0:T(4,128)S(1)} %collective-permute-done.11, f32[2,20,4,128]{3,2,1,0:T(4,128)S(1)} %collective-permute-done.10, f32[2,20,4,4,128]{4,3,2,1,0:T(4,128)S(1)} %bitcast_add_fusion, s32[]{:T(128)S(6)} %select_n.107), kind=kLoop, calls=%fused_computation.12 | loop fusion | flops 61440 | bytes 409604 | tf_op jit(solution)/shard_map/add | solution.py:273
  (13 shorter events, 0.2 us)
Async XLA Ops:
  0.6 11.6 %copy-start = (f32[2,20,4,128]{3,2,1,0:T(4,128)S(1)}, f32[2,20,4,128]{3,2,1,0:T(4,128)}, u32[]{:S(2)}) copy-start(f32[2,20,4,128]{3,2,1,0:T(4,128)} %param.6) | copy-start | bytes 245764
  0.6 9.5 %collective-permute-start = (f32[2,20,4,128]{3,2,1,0:T(4,128)}, f32[2,20,4,128]{3,2,1,0:T(4,128)S(1)}, u32[]{:S(2)}, u32[]{:S(2)}) collective-permute-start(f32[2,20,4,128]{3,2,1,0:T(4,128)} %param.6), channel_id=1, source_target_pairs={{0,2},{1,3},{2,4},{3,5},{4,6},{5,7},{6,0},{7,1},{8,10},{9,11},{10,... | collective-permute-start | bytes 245768 | tf_op jit(solution)/shard_map/ppermute | solution.py:245
  3.7 8.3 %collective-permute-start.1 = (f32[2,20,4,128]{3,2,1,0:T(4,128)}, f32[2,20,4,128]{3,2,1,0:T(4,128)S(1)}, u32[]{:S(2)}, u32[]{:S(2)}) collective-permute-start(f32[2,20,4,128]{3,2,1,0:T(4,128)} %param.6), channel_id=1, source_target_pairs={{0,4},{1,5},{2,6},{3,7},{4,0},{5,1},{6,2},{7,3},{8,12},{9,13},{10,... | collective-permute-start | bytes 245768 | tf_op jit(solution)/shard_map/ppermute | solution.py:245
  6.3 5.9 %collective-permute-start.2 = (f32[2,20,4,128]{3,2,1,0:T(4,128)}, f32[2,20,4,128]{3,2,1,0:T(4,128)S(1)}, u32[]{:S(2)}, u32[]{:S(2)}) collective-permute-start(f32[2,20,4,128]{3,2,1,0:T(4,128)} %param.6), channel_id=1, source_target_pairs={{0,6},{1,7},{2,0},{3,1},{4,2},{5,3},{6,4},{7,5},{8,14},{9,15},{10,... | collective-permute-start | bytes 245768 | tf_op jit(solution)/shard_map/ppermute | solution.py:245
  12.3 1.7 %collective-permute-start.3 = (f32[4,2,20,4,128]{4,3,2,1,0:T(4,128)S(1)}, f32[4,2,20,4,128]{4,3,2,1,0:T(4,128)S(1)}, u32[]{:S(2)}, u32[]{:S(2)}) collective-permute-start(f32[4,2,20,4,128]{4,3,2,1,0:T(4,128)S(1)} %get-tuple-element.13), channel_id=1, source_target_pairs={{0,1},{1,0},{2,3},{3,2},{4,5},{5,4},{6,7},{7,6},{8,9},{9,8},{10,11... | collective-permute-start | bytes 983048 | tf_op jit(solution)/shard_map/ppermute | solution.py:248
  15.1 0.7 %copy-start.1 = (s32[32,128]{1,0:T(8,128)S(1)}, s32[32,128]{1,0:T(8,128)}, u32[]{:S(2)}) copy-start(s32[32,128]{1,0:T(8,128)} %param.7) | copy-start | bytes 49156
  15.1 0.7 %copy-start.2 = (s32[32,128]{1,0:T(8,128)S(1)}, s32[32,128]{1,0:T(8,128)}, u32[]{:S(2)}) copy-start(s32[32,128]{1,0:T(8,128)} %param.8) | copy-start | bytes 49156
  17.4 9.4 %collective-permute-start.7 = (f32[2,122,2]{2,1,0:T(8,128)S(1)}, f32[2,122,2]{2,1,0:T(8,128)S(1)}, u32[]{:S(2)}, u32[]{:S(2)}) collective-permute-start(f32[2,122,2]{2,1,0:T(8,128)S(1)} %rev.11), channel_id=1, source_target_pairs={{0,16},{8,8},{16,0},{24,24},{1,17},{9,9},{17,1},{25,25},{2,18},{10... | collective-permute-start | bytes 5864 | tf_op jit(solution)/shard_map/ppermute | solution.py:18
  21.0 5.8 %collective-permute-start.8 = (f32[2,122,2]{2,1,0:T(8,128)S(1)}, f32[2,122,2]{2,1,0:T(8,128)S(1)}, u32[]{:S(2)}, u32[]{:S(2)}) collective-permute-start(f32[2,122,2]{2,1,0:T(8,128)S(1)} %rev.12), channel_id=1, source_target_pairs={{0,0},{8,24},{16,16},{24,8},{1,1},{9,25},{17,17},{25,9},{2,2},{10,... | collective-permute-start | bytes 5864 | tf_op jit(solution)/shard_map/ppermute | solution.py:18
  21.8 5.7 %collective-permute-start.4 = (f32[2,3904]{1,0:T(2,128)S(1)}, f32[2,3904]{1,0:T(2,128)S(1)}, u32[]{:S(2)}, u32[]{:S(2)}) collective-permute-start(f32[2,3904]{1,0:T(2,128)S(1)} %get-tuple-element.16), channel_id=1, source_target_pairs={{0,24},{8,0},{16,8},{24,16},{1,25},{9,1},{17,9},{25,17},{2,26},{10... | collective-permute-start | bytes 93704 | tf_op jit(solution)/shard_map/ppermute | solution.py:18
  23.3 5.1 %collective-permute-start.5 = (f32[2,3904]{1,0:T(2,128)S(1)}, f32[2,3904]{1,0:T(2,128)S(1)}, u32[]{:S(2)}, u32[]{:S(2)}) collective-permute-start(f32[2,3904]{1,0:T(2,128)S(1)} %get-tuple-element.17), channel_id=1, source_target_pairs={{0,8},{8,16},{16,24},{24,0},{1,9},{9,17},{17,25},{25,1},{2,10},{10... | collective-permute-start | bytes 93704 | tf_op jit(solution)/shard_map/ppermute | solution.py:18
  24.3 5.9 %collective-permute-start.6 = (f32[122,2,128]{2,1,0:T(2,128)S(1)}, f32[122,2,128]{2,1,0:T(2,128)S(1)}, u32[]{:S(2)}, u32[]{:S(2)}) collective-permute-start(f32[122,2,128]{2,1,0:T(2,128)S(1)} %rev.10), channel_id=1, source_target_pairs={{0,24},{8,16},{16,8},{24,0},{1,25},{9,17},{17,9},{25,1},{2,26},{10... | collective-permute-start | bytes 374792 | tf_op jit(solution)/shard_map/ppermute | solution.py:18
  39.9 1.7 %collective-permute-start.9 = (f32[2,20,4,4,128]{4,3,2,1,0:T(4,128)S(1)}, f32[2,20,4,4,128]{4,3,2,1,0:T(4,128)S(1)}, u32[]{:S(2)}, u32[]{:S(2)}) collective-permute-start(f32[2,20,4,4,128]{4,3,2,1,0:T(4,128)S(1)} %dynamic-slice_bitcast_fusion), channel_id=1, source_target_pairs={{0,1},{1,0},{2,3},{3,2},{4,5},{5,4},{6,7},{7,6},{8,9},{9,8},{10,11... | collective-permute-start | bytes 983048 | tf_op jit(solution)/shard_map/ppermute | solution.py:268
  41.7 7.2 %collective-permute-start.10 = (f32[2,20,4,128]{3,2,1,0:T(4,128)S(1)}, f32[2,20,4,128]{3,2,1,0:T(4,128)S(1)}, u32[]{:S(2)}, u32[]{:S(2)}) collective-permute-start(f32[2,20,4,128]{3,2,1,0:T(4,128)S(1)} %get-tuple-element.9), channel_id=1, source_target_pairs={{0,2},{1,3},{2,4},{3,5},{4,6},{5,7},{6,0},{7,1},{8,10},{9,11},{10,... | collective-permute-start | bytes 245768 | tf_op jit(solution)/shard_map/ppermute | solution.py:273
  43.8 7.9 %collective-permute-start.11 = (f32[2,20,4,128]{3,2,1,0:T(4,128)S(1)}, f32[2,20,4,128]{3,2,1,0:T(4,128)S(1)}, u32[]{:S(2)}, u32[]{:S(2)}) collective-permute-start(f32[2,20,4,128]{3,2,1,0:T(4,128)S(1)} %get-tuple-element.11), channel_id=1, source_target_pairs={{0,4},{1,5},{2,6},{3,7},{4,0},{5,1},{6,2},{7,3},{8,12},{9,13},{10,... | collective-permute-start | bytes 245768 | tf_op jit(solution)/shard_map/ppermute | solution.py:273
  45.6 6.2 %collective-permute-start.12 = (f32[2,20,4,128]{3,2,1,0:T(4,128)S(1)}, f32[2,20,4,128]{3,2,1,0:T(4,128)S(1)}, u32[]{:S(2)}, u32[]{:S(2)}) collective-permute-start(f32[2,20,4,128]{3,2,1,0:T(4,128)S(1)} %get-tuple-element.10), channel_id=1, source_target_pairs={{0,6},{1,7},{2,0},{3,1},{4,2},{5,3},{6,4},{7,5},{8,14},{9,15},{10,... | collective-permute-start | bytes 245768 | tf_op jit(solution)/shard_map/ppermute | solution.py:273

commit v14 on v13

--- a/solution.py
+++ b/solution.py
@@ -267,13 +267,26 @@
     other = lax.dynamic_index_in_dim(split, 1 - core, axis=3, keepdims=False)
     pair = lax.ppermute(other, "scen", [(q, q ^ 1) for q in range(parts)])
     chip_sum = mine + pair
-    total = lax.dynamic_index_in_dim(chip_sum, chip, axis=2, keepdims=False)
-    for step in range(1, chips):
-        send = lax.dynamic_index_in_dim(chip_sum, (chip + step) % chips, axis=2, keepdims=False)
-        total = total + lax.ppermute(
-            send, "scen", [(q, ((q // 2 + step) % chips) * 2 + q % 2) for q in range(parts)]
+    if chips & (chips - 1):
+        total = lax.dynamic_index_in_dim(chip_sum, chip, axis=2, keepdims=False)
+        for step in range(1, chips):
+            send = lax.dynamic_index_in_dim(chip_sum, (chip + step) % chips, axis=2, keepdims=False)
+            total = total + lax.ppermute(
+                send, "scen", [(q, ((q // 2 + step) % chips) * 2 + q % 2) for q in range(parts)]
+            )
+        return total
+    part = chip_sum
+    bit = chips // 2
+    while bit:
+        low, high = part[:, :, :bit], part[:, :, bit:]
+        upper = (chip & bit) != 0
+        keep = jnp.where(upper, high, low)
+        send = jnp.where(upper, low, high)
+        part = keep + lax.ppermute(
+            send, "scen", [(q, ((q // 2) ^ bit) * 2 + q % 2) for q in range(parts)]
         )
-    return total
+        bit //= 2
+    return part[:, :, 0]
 
 
 def solution(mesh):

time: 53 us -> 58.2 us (1.098)
  waiting for transfers between devices: 11.8 us -> 19.8 us
  starting transfers between devices: 20.2 us -> 17.4 us
    ppermute x3 -> x2, waiting for transfers between devices: 5.59 us -> 13.6 us  [summed_over_scen(): lax.ppermute(send, 'scen', [(q, (q // 2 ^ bit) * 2 + q % 2) for q in rang...]
    ppermute x3 -> x2, starting transfers between devices: 4.5 us -> 1.65 us  [summed_over_scen(): lax.ppermute(send, 'scen', [(q, (q // 2 ^ bit) * 2 + q % 2) for q in rang...]
    squeeze x0 -> x1, other arithmetic: none -> 0.67 us  [summed_over_scen(): return part[:, :, 0]]
    add x1, other arithmetic: 0.67 us -> 0.06 us  [summed_over_scen(): keep + lax.ppermute(send, 'scen', [(q, (q // 2 ^ bit) * 2 + q % 2) for q...]
  transfers between devices with their start and end apart: 13 -> 12, of which waited for: 9 -> 8; matrix products, arithmetic and copies ran while one was open for 11% -> 10% of each run, Pallas kernels for 0% -> 0%
where the time goes in v14:
time: 58.2 us; the launch traced here: 57.8 us
  waiting for transfers between devices  19.8 us (34%)
  starting transfers between devices  17.4 us (30%)
  Pallas kernels  9.11 us (16%)
  local copies, waits for them, and re-layouts  5.65 us (10%)
  matrix products  2.96 us (5%)
  other arithmetic  1.99 us (3%)
  between operations  0.93 us (2%)
    ppermute x2, waiting for transfers between devices, summed_over_scen(): lax.ppermute(send, 'scen', [(q, (q // 2 ^ bit) * 2 + q % 2) for q in rang...  13.6 us
    pallas_call x1, Pallas kernels, on_device(): pl.pallas_call(diffusion_kernel, out_shape=(field, field, jax.ShapeDtypeS...  9.11 us
    ppermute x5, starting transfers between devices, shifted(): return lax.ppermute(x, 'space', perm)  8.58 us
    ppermute x3, starting transfers between devices, gathered_over_scen(): lax.ppermute(block, 'scen', [(q, (q // 2 + step) % chips * 2 + q % 2) for...  7.01 us
    dot_general x3, matrix products, contract(): lax.dot_general(a, b, (dims, ((), ())), precision=lax.Precision.HIGHEST,...  2.96 us
    unnamed x9, local copies, waits for them, and re-layouts  2.59 us
    ppermute x3, waiting for transfers between devices, gathered_over_scen(): lax.ppermute(block, 'scen', [(q, (q // 2 + step) % chips * 2 + q % 2) for...  2.12 us
    ppermute x2, starting transfers between devices, summed_over_scen(): lax.ppermute(send, 'scen', [(q, (q // 2 ^ bit) * 2 + q % 2) for q in rang...  1.65 us
  transfers between devices with their start and end apart: 12, of which 8 were waited for; matrix products, arithmetic and copies ran while one was open for 10% of the time, Pallas kernels for 0%

profile of v14, /device:TPU:0, one launch (start us, length us, event | category | flops | bytes accessed | tf_op | source)
XLA Modules:
  0.0 57.8 jit_solution(9213743990760934505)
XLA Ops:
  0.6 0.0 copy-start
  0.6 3.1 %collective-permute-start = (f32[2,20,4,128]{3,2,1,0:T(4,128)}, f32[2,20,4,128]{3,2,1,0:T(4,128)S(1)}, u32[]{:S(2)}, u32[]{:S(2)}) collective-permute-start(f32[2,20,4,128]{3,2,1,0:T(4,128)} %param.6), channel_id=1, source_target_pairs={{0,2},{1,3},{2,4},{3,5},{4,6},{5,7},{6,0},{7,1},{8,10},{9,11},{10,... | collective-permute-start | bytes 245768 | tf_op jit(solution)/shard_map/ppermute | solution.py:245
  3.7 2.6 %collective-permute-start.1 = (f32[2,20,4,128]{3,2,1,0:T(4,128)}, f32[2,20,4,128]{3,2,1,0:T(4,128)S(1)}, u32[]{:S(2)}, u32[]{:S(2)}) collective-permute-start(f32[2,20,4,128]{3,2,1,0:T(4,128)} %param.6), channel_id=1, source_target_pairs={{0,4},{1,5},{2,6},{3,7},{4,0},{5,1},{6,2},{7,3},{8,12},{9,13},{10,... | collective-permute-start | bytes 245768 | tf_op jit(solution)/shard_map/ppermute | solution.py:245
  6.3 1.3 %collective-permute-start.2 = (f32[2,20,4,128]{3,2,1,0:T(4,128)}, f32[2,20,4,128]{3,2,1,0:T(4,128)S(1)}, u32[]{:S(2)}, u32[]{:S(2)}) collective-permute-start(f32[2,20,4,128]{3,2,1,0:T(4,128)} %param.6), channel_id=1, source_target_pairs={{0,6},{1,7},{2,0},{3,1},{4,2},{5,3},{6,4},{7,5},{8,14},{9,15},{10,... | collective-permute-start | bytes 245768 | tf_op jit(solution)/shard_map/ppermute | solution.py:245
  7.7 1.1 %constant_dynamic-update-slice_fusion.2 = f32[122,32,128]{2,1,0:T(8,128)S(1)} fusion(f32[40,32,128]{2,1,0:T(8,128)} %bitcast.40), kind=kLoop, calls=%fused_computation.22 | loop fusion | bytes 1310720
  8.9 1.1 %constant_dynamic-update-slice_fusion.1 = f32[122,32,128]{2,1,0:T(8,128)S(1)} fusion(f32[122,32,128]{2,1,0:T(8,128)S(1)} %constant_dynamic-update-slice_fusion.2, f32[40,32,128]{2,1,0:T(8,128)} %bitcast.41), kind=kLoop, calls=%fused_computation.21 | loop fusion | bytes 1310720
  10.0 0.1 pad.4.clone
  10.1 0.0 collective-permute-done
  10.1 1.9 %collective-permute-done.1 = f32[2,20,4,128]{3,2,1,0:T(4,128)S(1)} collective-permute-done((f32[2,20,4,128]{3,2,1,0:T(4,128)}, f32[2,20,4,128]{3,2,1,0:T(4,128)S(1)}, u32[]{:S(2)}, u32[]{:S(2)}) %collective-permute-start.1) | collective-permute-done | bytes 81952 | tf_op jit(solution)/shard_map/ppermute | solution.py:245
  12.0 0.2 collective-permute-done.2
  12.2 0.0 copy-done
  12.2 0.1 fusion.27
  12.3 0.1 collective-permute-start.3
  12.4 0.1 and_or_fusion
  12.5 1.5 %collective-permute-done.3 = f32[4,2,20,4,128]{4,3,2,1,0:T(4,128)S(1)} collective-permute-done((f32[4,2,20,4,128]{4,3,2,1,0:T(4,128)S(1)}, f32[4,2,20,4,128]{4,3,2,1,0:T(4,128)S(1)}, u32[]{:S(2)}, u32[]{:S(2)}) %collective-permute-start.3) | collective-permute-done | bytes 327712 | tf_op jit(solution)/shard_map/ppermute | solution.py:248
  14.0 0.1 maximum_select_fusion
  14.2 0.9 %gather_fusion = f32[4,2,2,20,4,128]{5,4,3,2,1,0:T(4,128)S(1)} fusion(f32[4,2,2,20,4,128]{5,4,3,2,0,1:T(4,128)S(1)} %maximum_select_fusion, s32[1024]{0:T(1024)S(1)} %pad_clamp_fusion), kind=kCustom, calls=%fused_computation | custom fusion | bytes 1310736 | tf_op jit(solution)/shard_map/jit(_take)/gather | solution.py:251
  15.1 0.0 copy-start.1
  15.1 0.0 copy-start.2
  15.2 0.2 select_bitcast_fusion
  15.4 0.2 copy.26
  15.6 0.3 copy-done.1
  15.9 0.0 copy-done.2
  15.9 1.0 %fusion.7 = f32[4,3904]{1,0:T(4,128)S(1)} fusion(f32[3904,128]{1,0:T(8,128)S(1)} %bitcast.37, pred[128]{0:T(512)(128)(4,1)S(1)} %get-tuple-element.19, pred[128]{0:T(512)(128)(4,1)S(1)} %get-tuple-element.20, pred[128]{0:T(512)(128)(4,1)S(1)} %get-tuple-element.21, pred[128]{0:T(512)(128)(4,1)S(1)} %get-tuple-element.22, ...), kind=kOutput, calls=%fused_computation.32 | convolution fusion | flops 23989760 | bytes 2061840 | tf_op jit(solution)/shard_map/dot_general | solution.py:31
  16.9 0.1 reshape.79
  17.0 0.1 fusion.28
  17.2 0.2 rev.11
  17.4 3.4 %collective-permute-start.7 = (f32[2,122,2]{2,1,0:T(8,128)S(1)}, f32[2,122,2]{2,1,0:T(8,128)S(1)}, u32[]{:S(2)}, u32[]{:S(2)}) collective-permute-start(f32[2,122,2]{2,1,0:T(8,128)S(1)} %rev.11), channel_id=1, source_target_pairs={{0,16},{8,8},{16,0},{24,24},{1,17},{9,9},{17,1},{25,25},{2,18},{10... | collective-permute-start | bytes 5864 | tf_op jit(solution)/shard_map/ppermute | solution.py:18
  20.8 0.2 rev.12
  21.0 0.7 %collective-permute-start.8 = (f32[2,122,2]{2,1,0:T(8,128)S(1)}, f32[2,122,2]{2,1,0:T(8,128)S(1)}, u32[]{:S(2)}, u32[]{:S(2)}) collective-permute-start(f32[2,122,2]{2,1,0:T(8,128)S(1)} %rev.12), channel_id=1, source_target_pairs={{0,0},{8,24},{16,16},{24,8},{1,1},{9,25},{17,17},{25,9},{2,2},{10,... | collective-permute-start | bytes 5864 | tf_op jit(solution)/shard_map/ppermute | solution.py:18
  21.7 0.1 slice.45
  21.8 1.5 %collective-permute-start.4 = (f32[2,3904]{1,0:T(2,128)S(1)}, f32[2,3904]{1,0:T(2,128)S(1)}, u32[]{:S(2)}, u32[]{:S(2)}) collective-permute-start(f32[2,3904]{1,0:T(2,128)S(1)} %get-tuple-element.15), channel_id=1, source_target_pairs={{0,24},{8,0},{16,8},{24,16},{1,25},{9,1},{17,9},{25,17},{2,26},{10... | collective-permute-start | bytes 93704 | tf_op jit(solution)/shard_map/ppermute | solution.py:18
  23.3 0.6 %collective-permute-start.5 = (f32[2,3904]{1,0:T(2,128)S(1)}, f32[2,3904]{1,0:T(2,128)S(1)}, u32[]{:S(2)}, u32[]{:S(2)}) collective-permute-start(f32[2,3904]{1,0:T(2,128)S(1)} %get-tuple-element.16), channel_id=1, source_target_pairs={{0,8},{8,16},{16,24},{24,0},{1,9},{9,17},{17,25},{25,1},{2,10},{10... | collective-permute-start | bytes 93704 | tf_op jit(solution)/shard_map/ppermute | solution.py:18
  23.8 0.5 rev.10
  24.3 2.4 %collective-permute-start.6 = (f32[122,2,128]{2,1,0:T(2,128)S(1)}, f32[122,2,128]{2,1,0:T(2,128)S(1)}, u32[]{:S(2)}, u32[]{:S(2)}) collective-permute-start(f32[122,2,128]{2,1,0:T(2,128)S(1)} %rev.10), channel_id=1, source_target_pairs={{0,24},{8,16},{16,8},{24,0},{1,25},{9,17},{17,9},{25,1},{2,26},{10... | collective-permute-start | bytes 374792 | tf_op jit(solution)/shard_map/ppermute | solution.py:18
  26.7 0.0 collective-permute-done.7
  26.7 0.0 collective-permute-done.8
  26.8 0.2 reshape.91
  26.9 0.1 copy.32
  27.1 0.1 dot_general.16
  27.2 0.2 fusion
  27.4 0.1 copy.29
  27.5 0.0 collective-permute-done.4
  27.5 0.8 %collective-permute-done.5 = f32[2,3904]{1,0:T(2,128)S(1)} collective-permute-done((f32[2,3904]{1,0:T(2,128)S(1)}, f32[2,3904]{1,0:T(2,128)S(1)}, u32[]{:S(2)}, u32[]{:S(2)}) %collective-permute-start.5) | collective-permute-done | bytes 31264 | tf_op jit(solution)/shard_map/ppermute | solution.py:18
  28.3 1.7 %fusion.2 = f32[3904,128]{1,0:T(8,128)S(1)} fusion(pred[128,4]{0,1:T(4,128)(4,1)S(1)} %and_or_fusion, f32[2,3904]{1,0:T(2,128)S(1)} %collective-permute-done.5, f32[2,3904]{1,0:T(2,128)S(1)} %collective-permute-done.4), kind=kOutput, calls=%fused_computation.14 | convolution fusion | flops 24001792 | bytes 2061824 | tf_op jit(solution)/shard_map/dot_general | solution.py:31
  30.1 0.1 collective-permute-done.6
  30.2 0.5 maximum_maximum_fusion.x_ref
  30.7 9.1 %shard_map.76 = (f32[2,20,32,128]{3,2,1,0:T(8,128)}, f32[2,20,32,128]{3,2,1,0:T(8,128)}, f32[2,20,32,128]{3,2,1,0:T(8,128)S(1)}) custom-call(f32[122,40,256]{2,1,0:T(8,128)S(1)} %maximum_maximum_fusion.x_ref), custom_call_target="tpu_custom_call" | custom-call | tf_op jit(solution)/shard_map/pallas_call | solution.py:210
  39.8 0.1 constant_dynamic-slice_fusion.1
  39.9 0.1 copy.37
  40.0 0.1 collective-permute-start.9
  40.1 1.6 %collective-permute-done.9 = f32[2,20,4,4,128]{4,3,1,0,2:T(4,128)S(1)} collective-permute-done((f32[2,20,4,4,128]{4,3,1,0,2:T(4,128)S(1)}, f32[2,20,4,4,128]{4,3,1,0,2:T(4,128)S(1)}, u32[]{:S(2)}, u32[]{:S(2)}) %collective-permute-start.9) | collective-permute-done | bytes 327712 | tf_op jit(solution)/shard_map/ppermute | solution.py:268
  41.7 0.1 bitcast_add_fusion
  41.9 1.6 %collective-permute-start.10 = (f32[2,20,2,4,128]{4,3,1,0,2:T(4,128)S(1)}, f32[2,20,2,4,128]{4,3,1,0,2:T(4,128)S(1)}, u32[]{:S(2)}, u32[]{:S(2)}) collective-permute-start(f32[2,20,2,4,128]{4,3,1,0,2:T(4,128)S(1)} %slice_select_fusion), channel_id=1, source_target_pairs={{0,4},{1,5},{2,6},{3,7},{4,0},{5,1},{6,2},{7,3},{8,12},{9,13},{10,... | collective-permute-start | bytes 491528 | tf_op jit(solution)/shard_map/ppermute | solution.py:285
  43.4 9.1 %collective-permute-done.10 = f32[2,20,2,4,128]{4,3,1,0,2:T(4,128)S(1)} collective-permute-done((f32[2,20,2,4,128]{4,3,1,0,2:T(4,128)S(1)}, f32[2,20,2,4,128]{4,3,1,0,2:T(4,128)S(1)}, u32[]{:S(2)}, u32[]{:S(2)}) %collective-permute-start.10) | collective-permute-done | bytes 163872 | tf_op jit(solution)/shard_map/ppermute | solution.py:285
  52.6 0.1 select_add_fusion
  52.7 0.1 collective-permute-start.11
  52.7 4.4 %collective-permute-done.11 = f32[2,20,1,4,128]{4,3,1,0,2:T(4,128)S(1)} collective-permute-done((f32[2,20,1,4,128]{4,3,1,0,2:T(4,128)S(1)}, f32[2,20,1,4,128]{4,3,1,0,2:T(4,128)S(1)}, u32[]{:S(2)}, u32[]{:S(2)}) %collective-permute-start.11) | collective-permute-done | bytes 81952 | tf_op jit(solution)/shard_map/ppermute | solution.py:285
  57.2 0.7 %add_bitcast_fusion = f32[2,20,4,128]{3,2,1,0:T(4,128)} fusion(f32[2,20,1,4,128]{4,3,1,0,2:T(4,128)S(1)} %collective-permute-done.11, f32[2,20,2,4,128]{4,3,1,0,2:T(4,128)S(1)} %select_add_fusion, pred[]{:T(512)S(6)} %ne.54), kind=kLoop, calls=%fused_computation.12 | loop fusion | flops 40960 | bytes 327681 | tf_op jit(solution)/shard_map/squeeze | solution.py:289
  (15 shorter events, 0.2 us)
Async XLA Ops:
  0.6 11.6 %copy-start = (f32[2,20,4,128]{3,2,1,0:T(4,128)S(1)}, f32[2,20,4,128]{3,2,1,0:T(4,128)}, u32[]{:S(2)}) copy-start(f32[2,20,4,128]{3,2,1,0:T(4,128)} %param.6) | copy-start | bytes 245764
  0.6 9.5 %collective-permute-start = (f32[2,20,4,128]{3,2,1,0:T(4,128)}, f32[2,20,4,128]{3,2,1,0:T(4,128)S(1)}, u32[]{:S(2)}, u32[]{:S(2)}) collective-permute-start(f32[2,20,4,128]{3,2,1,0:T(4,128)} %param.6), channel_id=1, source_target_pairs={{0,2},{1,3},{2,4},{3,5},{4,6},{5,7},{6,0},{7,1},{8,10},{9,11},{10,... | collective-permute-start | bytes 245768 | tf_op jit(solution)/shard_map/ppermute | solution.py:245
  3.7 8.3 %collective-permute-start.1 = (f32[2,20,4,128]{3,2,1,0:T(4,128)}, f32[2,20,4,128]{3,2,1,0:T(4,128)S(1)}, u32[]{:S(2)}, u32[]{:S(2)}) collective-permute-start(f32[2,20,4,128]{3,2,1,0:T(4,128)} %param.6), channel_id=1, source_target_pairs={{0,4},{1,5},{2,6},{3,7},{4,0},{5,1},{6,2},{7,3},{8,12},{9,13},{10,... | collective-permute-start | bytes 245768 | tf_op jit(solution)/shard_map/ppermute | solution.py:245
  6.3 5.9 %collective-permute-start.2 = (f32[2,20,4,128]{3,2,1,0:T(4,128)}, f32[2,20,4,128]{3,2,1,0:T(4,128)S(1)}, u32[]{:S(2)}, u32[]{:S(2)}) collective-permute-start(f32[2,20,4,128]{3,2,1,0:T(4,128)} %param.6), channel_id=1, source_target_pairs={{0,6},{1,7},{2,0},{3,1},{4,2},{5,3},{6,4},{7,5},{8,14},{9,15},{10,... | collective-permute-start | bytes 245768 | tf_op jit(solution)/shard_map/ppermute | solution.py:245
  12.3 1.7 %collective-permute-start.3 = (f32[4,2,20,4,128]{4,3,2,1,0:T(4,128)S(1)}, f32[4,2,20,4,128]{4,3,2,1,0:T(4,128)S(1)}, u32[]{:S(2)}, u32[]{:S(2)}) collective-permute-start(f32[4,2,20,4,128]{4,3,2,1,0:T(4,128)S(1)} %get-tuple-element.12), channel_id=1, source_target_pairs={{0,1},{1,0},{2,3},{3,2},{4,5},{5,4},{6,7},{7,6},{8,9},{9,8},{10,11... | collective-permute-start | bytes 983048 | tf_op jit(solution)/shard_map/ppermute | solution.py:248
  15.1 0.7 %copy-start.1 = (s32[32,128]{1,0:T(8,128)S(1)}, s32[32,128]{1,0:T(8,128)}, u32[]{:S(2)}) copy-start(s32[32,128]{1,0:T(8,128)} %param.7) | copy-start | bytes 49156
  15.1 0.7 %copy-start.2 = (s32[32,128]{1,0:T(8,128)S(1)}, s32[32,128]{1,0:T(8,128)}, u32[]{:S(2)}) copy-start(s32[32,128]{1,0:T(8,128)} %param.8) | copy-start | bytes 49156
  17.4 9.4 %collective-permute-start.7 = (f32[2,122,2]{2,1,0:T(8,128)S(1)}, f32[2,122,2]{2,1,0:T(8,128)S(1)}, u32[]{:S(2)}, u32[]{:S(2)}) collective-permute-start(f32[2,122,2]{2,1,0:T(8,128)S(1)} %rev.11), channel_id=1, source_target_pairs={{0,16},{8,8},{16,0},{24,24},{1,17},{9,9},{17,1},{25,25},{2,18},{10... | collective-permute-start | bytes 5864 | tf_op jit(solution)/shard_map/ppermute | solution.py:18
  21.0 5.8 %collective-permute-start.8 = (f32[2,122,2]{2,1,0:T(8,128)S(1)}, f32[2,122,2]{2,1,0:T(8,128)S(1)}, u32[]{:S(2)}, u32[]{:S(2)}) collective-permute-start(f32[2,122,2]{2,1,0:T(8,128)S(1)} %rev.12), channel_id=1, source_target_pairs={{0,0},{8,24},{16,16},{24,8},{1,1},{9,25},{17,17},{25,9},{2,2},{10,... | collective-permute-start | bytes 5864 | tf_op jit(solution)/shard_map/ppermute | solution.py:18
  21.8 5.7 %collective-permute-start.4 = (f32[2,3904]{1,0:T(2,128)S(1)}, f32[2,3904]{1,0:T(2,128)S(1)}, u32[]{:S(2)}, u32[]{:S(2)}) collective-permute-start(f32[2,3904]{1,0:T(2,128)S(1)} %get-tuple-element.15), channel_id=1, source_target_pairs={{0,24},{8,0},{16,8},{24,16},{1,25},{9,1},{17,9},{25,17},{2,26},{10... | collective-permute-start | bytes 93704 | tf_op jit(solution)/shard_map/ppermute | solution.py:18
  23.3 5.1 %collective-permute-start.5 = (f32[2,3904]{1,0:T(2,128)S(1)}, f32[2,3904]{1,0:T(2,128)S(1)}, u32[]{:S(2)}, u32[]{:S(2)}) collective-permute-start(f32[2,3904]{1,0:T(2,128)S(1)} %get-tuple-element.16), channel_id=1, source_target_pairs={{0,8},{8,16},{16,24},{24,0},{1,9},{9,17},{17,25},{25,1},{2,10},{10... | collective-permute-start | bytes 93704 | tf_op jit(solution)/shard_map/ppermute | solution.py:18
  24.3 5.9 %collective-permute-start.6 = (f32[122,2,128]{2,1,0:T(2,128)S(1)}, f32[122,2,128]{2,1,0:T(2,128)S(1)}, u32[]{:S(2)}, u32[]{:S(2)}) collective-permute-start(f32[122,2,128]{2,1,0:T(2,128)S(1)} %rev.10), channel_id=1, source_target_pairs={{0,24},{8,16},{16,8},{24,0},{1,25},{9,17},{17,9},{25,1},{2,26},{10... | collective-permute-start | bytes 374792 | tf_op jit(solution)/shard_map/ppermute | solution.py:18
  40.0 1.7 %collective-permute-start.9 = (f32[2,20,4,4,128]{4,3,1,0,2:T(4,128)S(1)}, f32[2,20,4,4,128]{4,3,1,0,2:T(4,128)S(1)}, u32[]{:S(2)}, u32[]{:S(2)}) collective-permute-start(f32[2,20,4,4,128]{4,3,1,0,2:T(4,128)S(1)} %bitcast.43), channel_id=1, source_target_pairs={{0,1},{1,0},{2,3},{3,2},{4,5},{5,4},{6,7},{7,6},{8,9},{9,8},{10,11... | collective-permute-start | bytes 983048 | tf_op jit(solution)/shard_map/ppermute | solution.py:268
  41.9 10.7 %collective-permute-start.10 = (f32[2,20,2,4,128]{4,3,1,0,2:T(4,128)S(1)}, f32[2,20,2,4,128]{4,3,1,0,2:T(4,128)S(1)}, u32[]{:S(2)}, u32[]{:S(2)}) collective-permute-start(f32[2,20,2,4,128]{4,3,1,0,2:T(4,128)S(1)} %slice_select_fusion), channel_id=1, source_target_pairs={{0,4},{1,5},{2,6},{3,7},{4,0},{5,1},{6,2},{7,3},{8,12},{9,13},{10,... | collective-permute-start | bytes 491528 | tf_op jit(solution)/shard_map/ppermute | solution.py:285
  52.7 4.5 %collective-permute-start.11 = (f32[2,20,1,4,128]{4,3,1,0,2:T(4,128)S(1)}, f32[2,20,1,4,128]{4,3,1,0,2:T(4,128)S(1)}, u32[]{:S(2)}, u32[]{:S(2)}) collective-permute-start(f32[2,20,1,4,128]{4,3,1,0,2:T(4,128)S(1)} %slice_select_fusion.1), channel_id=1, source_target_pairs={{0,2},{1,3},{2,0},{3,1},{4,6},{5,7},{6,4},{7,5},{8,10},{9,11},{10,... | collective-permute-start | bytes 245768 | tf_op jit(solution)/shard_map/ppermute | solution.py:285

commit v15 on v13

--- a/solution.py
+++ b/solution.py
@@ -118,7 +118,7 @@
             a_ref[c, k] = w * ve_ref[c, k]
         return carry
 
-    lax.fori_loop(0, levels, setup, 0, unroll=4)
+    lax.fori_loop(0, levels, setup, 0, unroll=10)
 
     def operate(x_ref, c, k, diffs=None):
         x = x_ref[c, k]
@@ -143,7 +143,7 @@
         u1_ref[c, k] = wet_ref[k] * (x + change + heat * src_ref[k])
         return carry
 
-    lax.fori_loop(0, planes, forward_first, 0, unroll=8)
+    lax.fori_loop(0, planes, forward_first, 0, unroll=10)
 
     def forward_second(ck, carry):
         c = ck // levels
@@ -154,7 +154,7 @@
         fin_ref[c, k] = out[:ny, :width]
         return carry
 
-    lax.fori_loop(0, planes, forward_second, 0, unroll=8)
+    lax.fori_loop(0, planes, forward_second, 0, unroll=10)
 
     def backward_second(ck, carry):
         c = ck // levels
@@ -163,7 +163,7 @@
         b_ref[c, k] = wet_ref[k] * (x + change)
         return carry
 
-    lax.fori_loop(0, planes, backward_second, 0, unroll=8)
+    lax.fori_loop(0, planes, backward_second, 0, unroll=10)
 
     def backward_first(ck, carry):
         c = ck // levels
@@ -172,7 +172,7 @@
         adj_ref[c, k] = (x + change)[:ny, :width]
         return carry
 
-    lax.fori_loop(0, planes, backward_first, 0, unroll=8)
+    lax.fori_loop(0, planes, backward_first, 0, unroll=10)
 
     def gradient(k, carry):
         g_east = jnp.zeros((ny, width), jnp.float32)
@@ -184,7 +184,7 @@
         grad_ref[1, k] = gnm_ref[k] * g_north
         return carry
 
-    lax.fori_loop(0, levels, gradient, 0, unroll=4)
+    lax.fori_loop(0, levels, gradient, 0, unroll=10)
 
 
 def on_device(tracers, diffusivity, level_count, shelf_mask, cotangent):

time: 53 us -> 53.4 us (level)
  no operation moved by 1% of the time
where the time goes in v15:
time: 53.4 us; the launch traced here: 52.8 us
  starting transfers between devices  20.2 us (38%)
  waiting for transfers between devices  11.8 us (22%)
  Pallas kernels  9.45 us (18%)
  local copies, waits for them, and re-layouts  5.59 us (10%)
  matrix products  2.96 us (6%)
  other arithmetic  1.87 us (4%)
  between operations  0.97 us (2%)
    pallas_call x1, Pallas kernels, on_device(): pl.pallas_call(diffusion_kernel, out_shape=(field, field, jax.ShapeDtypeS...  9.45 us
    ppermute x5, starting transfers between devices, shifted(): return lax.ppermute(x, 'space', perm)  8.58 us
    ppermute x3, starting transfers between devices, gathered_over_scen(): lax.ppermute(block, 'scen', [(q, (q // 2 + step) % chips * 2 + q % 2) for...  7.01 us
    ppermute x3, waiting for transfers between devices, summed_over_scen(): lax.ppermute(send, 'scen', [(q, (q // 2 + step) % chips * 2 + q % 2) for...  5.59 us
    ppermute x3, starting transfers between devices, summed_over_scen(): lax.ppermute(send, 'scen', [(q, (q // 2 + step) % chips * 2 + q % 2) for...  4.5 us
    dot_general x3, matrix products, contract(): lax.dot_general(a, b, (dims, ((), ())), precision=lax.Precision.HIGHEST,...  2.96 us
    unnamed x9, local copies, waits for them, and re-layouts  2.59 us
    ppermute x3, waiting for transfers between devices, gathered_over_scen(): lax.ppermute(block, 'scen', [(q, (q // 2 + step) % chips * 2 + q % 2) for...  2.12 us
  transfers between devices with their start and end apart: 13, of which 9 were waited for; matrix products, arithmetic and copies ran while one was open for 11% of the time, Pallas kernels for 0%

profile of v15, /device:TPU:0, one launch (start us, length us, event | category | flops | bytes accessed | tf_op | source)
XLA Modules:
  0.0 52.8 jit_solution(13715699006520663658)
XLA Ops:
  0.6 0.0 copy-start
  0.6 3.1 %collective-permute-start = (f32[2,20,4,128]{3,2,1,0:T(4,128)}, f32[2,20,4,128]{3,2,1,0:T(4,128)S(1)}, u32[]{:S(2)}, u32[]{:S(2)}) collective-permute-start(f32[2,20,4,128]{3,2,1,0:T(4,128)} %param.6), channel_id=1, source_target_pairs={{0,2},{1,3},{2,4},{3,5},{4,6},{5,7},{6,0},{7,1},{8,10},{9,11},{10,... | collective-permute-start | bytes 245768 | tf_op jit(solution)/shard_map/ppermute | solution.py:245
  3.7 2.6 %collective-permute-start.1 = (f32[2,20,4,128]{3,2,1,0:T(4,128)}, f32[2,20,4,128]{3,2,1,0:T(4,128)S(1)}, u32[]{:S(2)}, u32[]{:S(2)}) collective-permute-start(f32[2,20,4,128]{3,2,1,0:T(4,128)} %param.6), channel_id=1, source_target_pairs={{0,4},{1,5},{2,6},{3,7},{4,0},{5,1},{6,2},{7,3},{8,12},{9,13},{10,... | collective-permute-start | bytes 245768 | tf_op jit(solution)/shard_map/ppermute | solution.py:245
  6.3 1.3 %collective-permute-start.2 = (f32[2,20,4,128]{3,2,1,0:T(4,128)}, f32[2,20,4,128]{3,2,1,0:T(4,128)S(1)}, u32[]{:S(2)}, u32[]{:S(2)}) collective-permute-start(f32[2,20,4,128]{3,2,1,0:T(4,128)} %param.6), channel_id=1, source_target_pairs={{0,6},{1,7},{2,0},{3,1},{4,2},{5,3},{6,4},{7,5},{8,14},{9,15},{10,... | collective-permute-start | bytes 245768 | tf_op jit(solution)/shard_map/ppermute | solution.py:245
  7.7 1.1 %constant_dynamic-update-slice_fusion.2 = f32[122,32,128]{2,1,0:T(8,128)S(1)} fusion(f32[40,32,128]{2,1,0:T(8,128)} %bitcast.54), kind=kLoop, calls=%fused_computation.24 | loop fusion | bytes 1310720
  8.9 1.1 %constant_dynamic-update-slice_fusion.1 = f32[122,32,128]{2,1,0:T(8,128)S(1)} fusion(f32[122,32,128]{2,1,0:T(8,128)S(1)} %constant_dynamic-update-slice_fusion.2, f32[40,32,128]{2,1,0:T(8,128)} %bitcast.55), kind=kLoop, calls=%fused_computation.23 | loop fusion | bytes 1310720
  10.0 0.1 pad.4.clone
  10.1 0.0 collective-permute-done
  10.1 1.9 %collective-permute-done.1 = f32[2,20,4,128]{3,2,1,0:T(4,128)S(1)} collective-permute-done((f32[2,20,4,128]{3,2,1,0:T(4,128)}, f32[2,20,4,128]{3,2,1,0:T(4,128)S(1)}, u32[]{:S(2)}, u32[]{:S(2)}) %collective-permute-start.1) | collective-permute-done | bytes 81952 | tf_op jit(solution)/shard_map/ppermute | solution.py:245
  12.0 0.2 collective-permute-done.2
  12.2 0.0 copy-done
  12.2 0.1 fusion.29
  12.3 0.1 collective-permute-start.3
  12.4 0.1 and_or_fusion
  12.5 1.5 %collective-permute-done.3 = f32[4,2,20,4,128]{4,3,2,1,0:T(4,128)S(1)} collective-permute-done((f32[4,2,20,4,128]{4,3,2,1,0:T(4,128)S(1)}, f32[4,2,20,4,128]{4,3,2,1,0:T(4,128)S(1)}, u32[]{:S(2)}, u32[]{:S(2)}) %collective-permute-start.3) | collective-permute-done | bytes 327712 | tf_op jit(solution)/shard_map/ppermute | solution.py:248
  14.0 0.1 maximum_select_fusion
  14.2 0.9 %gather_fusion = f32[4,2,2,20,4,128]{5,4,3,2,1,0:T(4,128)S(1)} fusion(f32[4,2,2,20,4,128]{5,4,3,2,0,1:T(4,128)S(1)} %maximum_select_fusion, s32[1024]{0:T(1024)S(1)} %pad_clamp_fusion), kind=kCustom, calls=%fused_computation | custom fusion | bytes 1310736 | tf_op jit(solution)/shard_map/jit(_take)/gather | solution.py:251
  15.1 0.0 copy-start.1
  15.1 0.0 copy-start.2
  15.2 0.2 select_bitcast_fusion
  15.4 0.2 copy.24
  15.6 0.3 copy-done.1
  15.9 0.0 copy-done.2
  15.9 1.0 %fusion.9 = f32[4,3904]{1,0:T(4,128)S(1)} fusion(f32[3904,128]{1,0:T(8,128)S(1)} %bitcast.51, pred[128]{0:T(512)(128)(4,1)S(1)} %get-tuple-element.20, pred[128]{0:T(512)(128)(4,1)S(1)} %get-tuple-element.21, pred[128]{0:T(512)(128)(4,1)S(1)} %get-tuple-element.22, pred[128]{0:T(512)(128)(4,1)S(1)} %get-tuple-element.23, ...), kind=kOutput, calls=%fused_computation.34 | convolution fusion | flops 23989760 | bytes 2061840 | tf_op jit(solution)/shard_map/dot_general | solution.py:31
  16.9 0.1 reshape.79
  17.0 0.1 fusion.30
  17.2 0.2 rev.11
  17.4 3.4 %collective-permute-start.7 = (f32[2,122,2]{2,1,0:T(8,128)S(1)}, f32[2,122,2]{2,1,0:T(8,128)S(1)}, u32[]{:S(2)}, u32[]{:S(2)}) collective-permute-start(f32[2,122,2]{2,1,0:T(8,128)S(1)} %rev.11), channel_id=1, source_target_pairs={{0,16},{8,8},{16,0},{24,24},{1,17},{9,9},{17,1},{25,25},{2,18},{10... | collective-permute-start | bytes 5864 | tf_op jit(solution)/shard_map/ppermute | solution.py:18
  20.8 0.2 rev.12
  21.0 0.7 %collective-permute-start.8 = (f32[2,122,2]{2,1,0:T(8,128)S(1)}, f32[2,122,2]{2,1,0:T(8,128)S(1)}, u32[]{:S(2)}, u32[]{:S(2)}) collective-permute-start(f32[2,122,2]{2,1,0:T(8,128)S(1)} %rev.12), channel_id=1, source_target_pairs={{0,0},{8,24},{16,16},{24,8},{1,1},{9,25},{17,17},{25,9},{2,2},{10,... | collective-permute-start | bytes 5864 | tf_op jit(solution)/shard_map/ppermute | solution.py:18
  21.7 0.1 slice.29
  21.8 1.5 %collective-permute-start.4 = (f32[2,3904]{1,0:T(2,128)S(1)}, f32[2,3904]{1,0:T(2,128)S(1)}, u32[]{:S(2)}, u32[]{:S(2)}) collective-permute-start(f32[2,3904]{1,0:T(2,128)S(1)} %get-tuple-element.16), channel_id=1, source_target_pairs={{0,24},{8,0},{16,8},{24,16},{1,25},{9,1},{17,9},{25,17},{2,26},{10... | collective-permute-start | bytes 93704 | tf_op jit(solution)/shard_map/ppermute | solution.py:18
  23.3 0.6 %collective-permute-start.5 = (f32[2,3904]{1,0:T(2,128)S(1)}, f32[2,3904]{1,0:T(2,128)S(1)}, u32[]{:S(2)}, u32[]{:S(2)}) collective-permute-start(f32[2,3904]{1,0:T(2,128)S(1)} %get-tuple-element.17), channel_id=1, source_target_pairs={{0,8},{8,16},{16,24},{24,0},{1,9},{9,17},{17,25},{25,1},{2,10},{10... | collective-permute-start | bytes 93704 | tf_op jit(solution)/shard_map/ppermute | solution.py:18
  23.8 0.5 rev.10
  24.3 2.4 %collective-permute-start.6 = (f32[122,2,128]{2,1,0:T(2,128)S(1)}, f32[122,2,128]{2,1,0:T(2,128)S(1)}, u32[]{:S(2)}, u32[]{:S(2)}) collective-permute-start(f32[122,2,128]{2,1,0:T(2,128)S(1)} %rev.10), channel_id=1, source_target_pairs={{0,24},{8,16},{16,8},{24,0},{1,25},{9,17},{17,9},{25,1},{2,26},{10... | collective-permute-start | bytes 374792 | tf_op jit(solution)/shard_map/ppermute | solution.py:18
  26.7 0.0 collective-permute-done.7
  26.7 0.0 collective-permute-done.8
  26.8 0.2 reshape.91
  26.9 0.1 copy.30
  27.1 0.1 dot_general.16
  27.2 0.2 fusion
  27.4 0.1 copy.27
  27.5 0.0 collective-permute-done.4
  27.5 0.8 %collective-permute-done.5 = f32[2,3904]{1,0:T(2,128)S(1)} collective-permute-done((f32[2,3904]{1,0:T(2,128)S(1)}, f32[2,3904]{1,0:T(2,128)S(1)}, u32[]{:S(2)}, u32[]{:S(2)}) %collective-permute-start.5) | collective-permute-done | bytes 31264 | tf_op jit(solution)/shard_map/ppermute | solution.py:18
  28.3 1.7 %fusion.4 = f32[3904,128]{1,0:T(8,128)S(1)} fusion(pred[128,4]{0,1:T(4,128)(4,1)S(1)} %and_or_fusion, f32[2,3904]{1,0:T(2,128)S(1)} %collective-permute-done.5, f32[2,3904]{1,0:T(2,128)S(1)} %collective-permute-done.4), kind=kOutput, calls=%fused_computation.16 | convolution fusion | flops 24001792 | bytes 2061824 | tf_op jit(solution)/shard_map/dot_general | solution.py:31
  30.1 0.1 collective-permute-done.6
  30.2 0.5 maximum_maximum_fusion.x_ref
  30.7 9.4 %shard_map.76 = (f32[2,20,32,128]{3,2,1,0:T(8,128)}, f32[2,20,32,128]{3,2,1,0:T(8,128)}, f32[2,20,32,128]{3,2,1,0:T(8,128)S(1)}) custom-call(f32[122,40,256]{2,1,0:T(8,128)S(1)} %maximum_maximum_fusion.x_ref), custom_call_target="tpu_custom_call" | custom-call | tf_op jit(solution)/shard_map/pallas_call | solution.py:210
  40.2 0.1 dynamic-slice_bitcast_fusion
  40.2 0.1 collective-permute-start.9
  40.4 1.5 %collective-permute-done.9 = f32[2,20,4,4,128]{4,3,2,1,0:T(4,128)S(1)} collective-permute-done((f32[2,20,4,4,128]{4,3,2,1,0:T(4,128)S(1)}, f32[2,20,4,4,128]{4,3,2,1,0:T(4,128)S(1)}, u32[]{:S(2)}, u32[]{:S(2)}) %collective-permute-start.9) | collective-permute-done | bytes 327712 | tf_op jit(solution)/shard_map/ppermute | solution.py:268
  41.9 0.1 bitcast_add_fusion
  42.0 0.1 dynamic-slice_bitcast_fusion.3
  42.1 2.1 %collective-permute-start.10 = (f32[2,20,4,128]{3,2,1,0:T(4,128)S(1)}, f32[2,20,4,128]{3,2,1,0:T(4,128)S(1)}, u32[]{:S(2)}, u32[]{:S(2)}) collective-permute-start(f32[2,20,4,128]{3,2,1,0:T(4,128)S(1)} %get-tuple-element.9), channel_id=1, source_target_pairs={{0,2},{1,3},{2,4},{3,5},{4,6},{5,7},{6,0},{7,1},{8,10},{9,11},{10,... | collective-permute-start | bytes 245768 | tf_op jit(solution)/shard_map/ppermute | solution.py:273
  44.1 1.8 %collective-permute-start.11 = (f32[2,20,4,128]{3,2,1,0:T(4,128)S(1)}, f32[2,20,4,128]{3,2,1,0:T(4,128)S(1)}, u32[]{:S(2)}, u32[]{:S(2)}) collective-permute-start(f32[2,20,4,128]{3,2,1,0:T(4,128)S(1)} %get-tuple-element.11), channel_id=1, source_target_pairs={{0,4},{1,5},{2,6},{3,7},{4,0},{5,1},{6,2},{7,3},{8,12},{9,13},{10,... | collective-permute-start | bytes 245768 | tf_op jit(solution)/shard_map/ppermute | solution.py:273
  46.0 0.6 %collective-permute-start.12 = (f32[2,20,4,128]{3,2,1,0:T(4,128)S(1)}, f32[2,20,4,128]{3,2,1,0:T(4,128)S(1)}, u32[]{:S(2)}, u32[]{:S(2)}) collective-permute-start(f32[2,20,4,128]{3,2,1,0:T(4,128)S(1)} %get-tuple-element.10), channel_id=1, source_target_pairs={{0,6},{1,7},{2,0},{3,1},{4,2},{5,3},{6,4},{7,5},{8,14},{9,15},{10,... | collective-permute-start | bytes 245768 | tf_op jit(solution)/shard_map/ppermute | solution.py:273
  46.6 2.7 %collective-permute-done.10 = f32[2,20,4,128]{3,2,1,0:T(4,128)S(1)} collective-permute-done((f32[2,20,4,128]{3,2,1,0:T(4,128)S(1)}, f32[2,20,4,128]{3,2,1,0:T(4,128)S(1)}, u32[]{:S(2)}, u32[]{:S(2)}) %collective-permute-start.10) | collective-permute-done | bytes 81952 | tf_op jit(solution)/shard_map/ppermute | solution.py:273
  49.3 2.7 %collective-permute-done.11 = f32[2,20,4,128]{3,2,1,0:T(4,128)S(1)} collective-permute-done((f32[2,20,4,128]{3,2,1,0:T(4,128)S(1)}, f32[2,20,4,128]{3,2,1,0:T(4,128)S(1)}, u32[]{:S(2)}, u32[]{:S(2)}) %collective-permute-start.11) | collective-permute-done | bytes 81952 | tf_op jit(solution)/shard_map/ppermute | solution.py:273
  52.0 0.1 collective-permute-done.12
  52.2 0.7 %fusion.3 = f32[2,20,4,128]{3,2,1,0:T(4,128)} fusion(f32[2,20,4,128]{3,2,1,0:T(4,128)S(1)} %collective-permute-done.12, f32[2,20,4,128]{3,2,1,0:T(4,128)S(1)} %collective-permute-done.11, f32[2,20,4,128]{3,2,1,0:T(4,128)S(1)} %collective-permute-done.10, f32[2,20,4,4,128]{4,3,2,1,0:T(4,128)S(1)} %bitcast_add_fusion, s32[]{:T(128)S(6)} %select_n.107), kind=kLoop, calls=%fused_computation.12 | loop fusion | flops 61440 | bytes 409604 | tf_op jit(solution)/shard_map/add | solution.py:273
  (13 shorter events, 0.2 us)
Async XLA Ops:
  0.6 11.6 %copy-start = (f32[2,20,4,128]{3,2,1,0:T(4,128)S(1)}, f32[2,20,4,128]{3,2,1,0:T(4,128)}, u32[]{:S(2)}) copy-start(f32[2,20,4,128]{3,2,1,0:T(4,128)} %param.6) | copy-start | bytes 245764
  0.6 9.5 %collective-permute-start = (f32[2,20,4,128]{3,2,1,0:T(4,128)}, f32[2,20,4,128]{3,2,1,0:T(4,128)S(1)}, u32[]{:S(2)}, u32[]{:S(2)}) collective-permute-start(f32[2,20,4,128]{3,2,1,0:T(4,128)} %param.6), channel_id=1, source_target_pairs={{0,2},{1,3},{2,4},{3,5},{4,6},{5,7},{6,0},{7,1},{8,10},{9,11},{10,... | collective-permute-start | bytes 245768 | tf_op jit(solution)/shard_map/ppermute | solution.py:245
  3.7 8.3 %collective-permute-start.1 = (f32[2,20,4,128]{3,2,1,0:T(4,128)}, f32[2,20,4,128]{3,2,1,0:T(4,128)S(1)}, u32[]{:S(2)}, u32[]{:S(2)}) collective-permute-start(f32[2,20,4,128]{3,2,1,0:T(4,128)} %param.6), channel_id=1, source_target_pairs={{0,4},{1,5},{2,6},{3,7},{4,0},{5,1},{6,2},{7,3},{8,12},{9,13},{10,... | collective-permute-start | bytes 245768 | tf_op jit(solution)/shard_map/ppermute | solution.py:245
  6.3 5.9 %collective-permute-start.2 = (f32[2,20,4,128]{3,2,1,0:T(4,128)}, f32[2,20,4,128]{3,2,1,0:T(4,128)S(1)}, u32[]{:S(2)}, u32[]{:S(2)}) collective-permute-start(f32[2,20,4,128]{3,2,1,0:T(4,128)} %param.6), channel_id=1, source_target_pairs={{0,6},{1,7},{2,0},{3,1},{4,2},{5,3},{6,4},{7,5},{8,14},{9,15},{10,... | collective-permute-start | bytes 245768 | tf_op jit(solution)/shard_map/ppermute | solution.py:245
  12.3 1.7 %collective-permute-start.3 = (f32[4,2,20,4,128]{4,3,2,1,0:T(4,128)S(1)}, f32[4,2,20,4,128]{4,3,2,1,0:T(4,128)S(1)}, u32[]{:S(2)}, u32[]{:S(2)}) collective-permute-start(f32[4,2,20,4,128]{4,3,2,1,0:T(4,128)S(1)} %get-tuple-element.13), channel_id=1, source_target_pairs={{0,1},{1,0},{2,3},{3,2},{4,5},{5,4},{6,7},{7,6},{8,9},{9,8},{10,11... | collective-permute-start | bytes 983048 | tf_op jit(solution)/shard_map/ppermute | solution.py:248
  15.1 0.7 %copy-start.1 = (s32[32,128]{1,0:T(8,128)S(1)}, s32[32,128]{1,0:T(8,128)}, u32[]{:S(2)}) copy-start(s32[32,128]{1,0:T(8,128)} %param.7) | copy-start | bytes 49156
  15.1 0.7 %copy-start.2 = (s32[32,128]{1,0:T(8,128)S(1)}, s32[32,128]{1,0:T(8,128)}, u32[]{:S(2)}) copy-start(s32[32,128]{1,0:T(8,128)} %param.8) | copy-start | bytes 49156
  17.4 9.4 %collective-permute-start.7 = (f32[2,122,2]{2,1,0:T(8,128)S(1)}, f32[2,122,2]{2,1,0:T(8,128)S(1)}, u32[]{:S(2)}, u32[]{:S(2)}) collective-permute-start(f32[2,122,2]{2,1,0:T(8,128)S(1)} %rev.11), channel_id=1, source_target_pairs={{0,16},{8,8},{16,0},{24,24},{1,17},{9,9},{17,1},{25,25},{2,18},{10... | collective-permute-start | bytes 5864 | tf_op jit(solution)/shard_map/ppermute | solution.py:18
  21.0 5.8 %collective-permute-start.8 = (f32[2,122,2]{2,1,0:T(8,128)S(1)}, f32[2,122,2]{2,1,0:T(8,128)S(1)}, u32[]{:S(2)}, u32[]{:S(2)}) collective-permute-start(f32[2,122,2]{2,1,0:T(8,128)S(1)} %rev.12), channel_id=1, source_target_pairs={{0,0},{8,24},{16,16},{24,8},{1,1},{9,25},{17,17},{25,9},{2,2},{10,... | collective-permute-start | bytes 5864 | tf_op jit(solution)/shard_map/ppermute | solution.py:18
  21.8 5.7 %collective-permute-start.4 = (f32[2,3904]{1,0:T(2,128)S(1)}, f32[2,3904]{1,0:T(2,128)S(1)}, u32[]{:S(2)}, u32[]{:S(2)}) collective-permute-start(f32[2,3904]{1,0:T(2,128)S(1)} %get-tuple-element.16), channel_id=1, source_target_pairs={{0,24},{8,0},{16,8},{24,16},{1,25},{9,1},{17,9},{25,17},{2,26},{10... | collective-permute-start | bytes 93704 | tf_op jit(solution)/shard_map/ppermute | solution.py:18
  23.3 5.1 %collective-permute-start.5 = (f32[2,3904]{1,0:T(2,128)S(1)}, f32[2,3904]{1,0:T(2,128)S(1)}, u32[]{:S(2)}, u32[]{:S(2)}) collective-permute-start(f32[2,3904]{1,0:T(2,128)S(1)} %get-tuple-element.17), channel_id=1, source_target_pairs={{0,8},{8,16},{16,24},{24,0},{1,9},{9,17},{17,25},{25,1},{2,10},{10... | collective-permute-start | bytes 93704 | tf_op jit(solution)/shard_map/ppermute | solution.py:18
  24.3 5.9 %collective-permute-start.6 = (f32[122,2,128]{2,1,0:T(2,128)S(1)}, f32[122,2,128]{2,1,0:T(2,128)S(1)}, u32[]{:S(2)}, u32[]{:S(2)}) collective-permute-start(f32[122,2,128]{2,1,0:T(2,128)S(1)} %rev.10), channel_id=1, source_target_pairs={{0,24},{8,16},{16,8},{24,0},{1,25},{9,17},{17,9},{25,1},{2,26},{10... | collective-permute-start | bytes 374792 | tf_op jit(solution)/shard_map/ppermute | solution.py:18
  40.2 1.7 %collective-permute-start.9 = (f32[2,20,4,4,128]{4,3,2,1,0:T(4,128)S(1)}, f32[2,20,4,4,128]{4,3,2,1,0:T(4,128)S(1)}, u32[]{:S(2)}, u32[]{:S(2)}) collective-permute-start(f32[2,20,4,4,128]{4,3,2,1,0:T(4,128)S(1)} %dynamic-slice_bitcast_fusion), channel_id=1, source_target_pairs={{0,1},{1,0},{2,3},{3,2},{4,5},{5,4},{6,7},{7,6},{8,9},{9,8},{10,11... | collective-permute-start | bytes 983048 | tf_op jit(solution)/shard_map/ppermute | solution.py:268
  42.1 7.2 %collective-permute-start.10 = (f32[2,20,4,128]{3,2,1,0:T(4,128)S(1)}, f32[2,20,4,128]{3,2,1,0:T(4,128)S(1)}, u32[]{:S(2)}, u32[]{:S(2)}) collective-permute-start(f32[2,20,4,128]{3,2,1,0:T(4,128)S(1)} %get-tuple-element.9), channel_id=1, source_target_pairs={{0,2},{1,3},{2,4},{3,5},{4,6},{5,7},{6,0},{7,1},{8,10},{9,11},{10,... | collective-permute-start | bytes 245768 | tf_op jit(solution)/shard_map/ppermute | solution.py:273
  44.1 7.9 %collective-permute-start.11 = (f32[2,20,4,128]{3,2,1,0:T(4,128)S(1)}, f32[2,20,4,128]{3,2,1,0:T(4,128)S(1)}, u32[]{:S(2)}, u32[]{:S(2)}) collective-permute-start(f32[2,20,4,128]{3,2,1,0:T(4,128)S(1)} %get-tuple-element.11), channel_id=1, source_target_pairs={{0,4},{1,5},{2,6},{3,7},{4,0},{5,1},{6,2},{7,3},{8,12},{9,13},{10,... | collective-permute-start | bytes 245768 | tf_op jit(solution)/shard_map/ppermute | solution.py:273
  46.0 6.2 %collective-permute-start.12 = (f32[2,20,4,128]{3,2,1,0:T(4,128)S(1)}, f32[2,20,4,128]{3,2,1,0:T(4,128)S(1)}, u32[]{:S(2)}, u32[]{:S(2)}) collective-permute-start(f32[2,20,4,128]{3,2,1,0:T(4,128)S(1)} %get-tuple-element.10), channel_id=1, source_target_pairs={{0,6},{1,7},{2,0},{3,1},{4,2},{5,3},{6,4},{7,5},{8,14},{9,15},{10,... | collective-permute-start | bytes 245768 | tf_op jit(solution)/shard_map/ppermute | solution.py:273

commit v16 on v13

--- a/solution.py
+++ b/solution.py
@@ -44,8 +44,8 @@
     mirrored = fields[:, ny - 1:ny - 3:-1, ::-1]
     ghost = shifted(mirrored, [(q, n - 1 - q) for q in range(n)])
     top_edges = edges.reshape(4, count, ny)[:, :, ny - 1:ny - 3:-1]
-    ghost_east = shifted(top_edges[1::-1], [(q, (n - 2 - q) % n) for q in range(n)])
-    ghost_west = shifted(top_edges[3:1:-1], [(q, (n - q) % n) for q in range(n)])
+    ghost_east = shifted(top_edges[1::-1].reshape(2, count * 2), [(q, (n - 2 - q) % n) for q in range(n)])
+    ghost_west = shifted(top_edges[3:1:-1].reshape(2, count * 2), [(q, (n - q) % n) for q in range(n)])
     place = picker(spare, [0, 1, spare - 2, spare - 1]).T
     side = contract(jnp.concatenate([east, west]), place, ((0,), (0,))).reshape(count, ny, spare)
     ghost_halo = jnp.concatenate([ghost_east, ghost_west]).reshape(4, count * 2)

time: 53 us -> 53.3 us (level)
  no operation moved by 1% of the time
where the time goes in v16:
time: 53.3 us; the launch traced here: 52.8 us
  starting transfers between devices  20.2 us (38%)
  waiting for transfers between devices  12.1 us (23%)
  Pallas kernels  9.11 us (17%)
  local copies, waits for them, and re-layouts  5.49 us (10%)
  matrix products  3.09 us (6%)
  other arithmetic  1.86 us (3%)
  between operations  0.95 us (2%)
    pallas_call x1, Pallas kernels, on_device(): pl.pallas_call(diffusion_kernel, out_shape=(field, field, jax.ShapeDtypeS...  9.11 us
    ppermute x5, starting transfers between devices, shifted(): return lax.ppermute(x, 'space', perm)  8.57 us
    ppermute x3, starting transfers between devices, gathered_over_scen(): lax.ppermute(block, 'scen', [(q, (q // 2 + step) % chips * 2 + q % 2) for...  7.01 us
    ppermute x3, waiting for transfers between devices, summed_over_scen(): lax.ppermute(send, 'scen', [(q, (q // 2 + step) % chips * 2 + q % 2) for...  5.59 us
    ppermute x3, starting transfers between devices, summed_over_scen(): lax.ppermute(send, 'scen', [(q, (q // 2 + step) % chips * 2 + q % 2) for...  4.5 us
    dot_general x3, matrix products, contract(): lax.dot_general(a, b, (dims, ((), ())), precision=lax.Precision.HIGHEST,...  3.09 us
    unnamed x9, local copies, waits for them, and re-layouts  2.59 us
    ppermute x3, waiting for transfers between devices, gathered_over_scen(): lax.ppermute(block, 'scen', [(q, (q // 2 + step) % chips * 2 + q % 2) for...  2.12 us
  transfers between devices with their start and end apart: 13, of which 9 were waited for; matrix products, arithmetic and copies ran while one was open for 11% of the time, Pallas kernels for 0%

profile of v16, /device:TPU:0, one launch (start us, length us, event | category | flops | bytes accessed | tf_op | source)
XLA Modules:
  0.0 52.8 jit_solution(16790441284333497607)
XLA Ops:
  0.6 0.0 copy-start
  0.6 3.1 %collective-permute-start = (f32[2,20,4,128]{3,2,1,0:T(4,128)}, f32[2,20,4,128]{3,2,1,0:T(4,128)S(1)}, u32[]{:S(2)}, u32[]{:S(2)}) collective-permute-start(f32[2,20,4,128]{3,2,1,0:T(4,128)} %param.6), channel_id=1, source_target_pairs={{0,2},{1,3},{2,4},{3,5},{4,6},{5,7},{6,0},{7,1},{8,10},{9,11},{10,... | collective-permute-start | bytes 245768 | tf_op jit(solution)/shard_map/ppermute | solution.py:245
  3.7 2.6 %collective-permute-start.1 = (f32[2,20,4,128]{3,2,1,0:T(4,128)}, f32[2,20,4,128]{3,2,1,0:T(4,128)S(1)}, u32[]{:S(2)}, u32[]{:S(2)}) collective-permute-start(f32[2,20,4,128]{3,2,1,0:T(4,128)} %param.6), channel_id=1, source_target_pairs={{0,4},{1,5},{2,6},{3,7},{4,0},{5,1},{6,2},{7,3},{8,12},{9,13},{10,... | collective-permute-start | bytes 245768 | tf_op jit(solution)/shard_map/ppermute | solution.py:245
  6.3 1.3 %collective-permute-start.2 = (f32[2,20,4,128]{3,2,1,0:T(4,128)}, f32[2,20,4,128]{3,2,1,0:T(4,128)S(1)}, u32[]{:S(2)}, u32[]{:S(2)}) collective-permute-start(f32[2,20,4,128]{3,2,1,0:T(4,128)} %param.6), channel_id=1, source_target_pairs={{0,6},{1,7},{2,0},{3,1},{4,2},{5,3},{6,4},{7,5},{8,14},{9,15},{10,... | collective-permute-start | bytes 245768 | tf_op jit(solution)/shard_map/ppermute | solution.py:245
  7.7 1.1 %constant_dynamic-update-slice_fusion.2 = f32[122,32,128]{2,1,0:T(8,128)S(1)} fusion(f32[40,32,128]{2,1,0:T(8,128)} %bitcast.51), kind=kLoop, calls=%fused_computation.21 | loop fusion | bytes 1310720
  8.9 1.1 %constant_dynamic-update-slice_fusion.1 = f32[122,32,128]{2,1,0:T(8,128)S(1)} fusion(f32[122,32,128]{2,1,0:T(8,128)S(1)} %constant_dynamic-update-slice_fusion.2, f32[40,32,128]{2,1,0:T(8,128)} %bitcast.52), kind=kLoop, calls=%fused_computation.20 | loop fusion | bytes 1310720
  10.0 0.1 pad.4.clone
  10.1 0.0 collective-permute-done
  10.1 1.9 %collective-permute-done.1 = f32[2,20,4,128]{3,2,1,0:T(4,128)S(1)} collective-permute-done((f32[2,20,4,128]{3,2,1,0:T(4,128)}, f32[2,20,4,128]{3,2,1,0:T(4,128)S(1)}, u32[]{:S(2)}, u32[]{:S(2)}) %collective-permute-start.1) | collective-permute-done | bytes 81952 | tf_op jit(solution)/shard_map/ppermute | solution.py:245
  12.0 0.2 collective-permute-done.2
  12.2 0.0 copy-done
  12.2 0.1 fusion.31
  12.3 0.1 collective-permute-start.3
  12.4 0.1 and_or_fusion
  12.5 1.5 %collective-permute-done.3 = f32[4,2,20,4,128]{4,3,2,1,0:T(4,128)S(1)} collective-permute-done((f32[4,2,20,4,128]{4,3,2,1,0:T(4,128)S(1)}, f32[4,2,20,4,128]{4,3,2,1,0:T(4,128)S(1)}, u32[]{:S(2)}, u32[]{:S(2)}) %collective-permute-start.3) | collective-permute-done | bytes 327712 | tf_op jit(solution)/shard_map/ppermute | solution.py:248
  14.0 0.1 maximum_select_fusion
  14.2 0.9 %gather_fusion = f32[4,2,2,20,4,128]{5,4,3,2,1,0:T(4,128)S(1)} fusion(f32[4,2,2,20,4,128]{5,4,3,2,0,1:T(4,128)S(1)} %maximum_select_fusion, s32[1024]{0:T(1024)S(1)} %pad_clamp_fusion), kind=kCustom, calls=%fused_computation | custom fusion | bytes 1310736 | tf_op jit(solution)/shard_map/jit(_take)/gather | solution.py:251
  15.1 0.0 copy-start.1
  15.1 0.0 copy-start.2
  15.2 0.2 select_bitcast_fusion
  15.4 0.2 copy.12
  15.6 0.3 copy-done.1
  15.9 0.0 copy-done.2
  15.9 1.0 %fusion.10 = f32[4,3904]{1,0:T(4,128)S(1)} fusion(f32[3904,128]{1,0:T(8,128)S(1)} %bitcast.48, pred[128]{0:T(512)(128)(4,1)S(1)} %get-tuple-element.20, pred[128]{0:T(512)(128)(4,1)S(1)} %get-tuple-element.21, pred[128]{0:T(512)(128)(4,1)S(1)} %get-tuple-element.22, pred[128]{0:T(512)(128)(4,1)S(1)} %get-tuple-element.23, ...), kind=kOutput, calls=%fused_computation.34 | convolution fusion | flops 23989760 | bytes 2061840 | tf_op jit(solution)/shard_map/dot_general | solution.py:31
  16.9 0.1 reshape.83
  17.0 0.1 fusion.32
  17.2 0.2 rev.11
  17.4 0.2 reshape.84
  17.5 3.4 %collective-permute-start.7 = (f32[2,244]{1,0:T(2,128)S(1)}, f32[2,244]{1,0:T(2,128)S(1)}, u32[]{:S(2)}, u32[]{:S(2)}) collective-permute-start(f32[2,244]{1,0:T(2,128)S(1)} %reshape.84), channel_id=1, source_target_pairs={{0,16},{8,8},{16,0},{24,24},{1,17},{9,9},{17,1},{25,25},{2,18},{10... | collective-permute-start | bytes 5864 | tf_op jit(solution)/shard_map/ppermute | solution.py:18
  20.9 0.2 rev.12
  21.1 0.2 reshape.85
  21.3 0.7 %collective-permute-start.8 = (f32[2,244]{1,0:T(2,128)S(1)}, f32[2,244]{1,0:T(2,128)S(1)}, u32[]{:S(2)}, u32[]{:S(2)}) collective-permute-start(f32[2,244]{1,0:T(2,128)S(1)} %reshape.85), channel_id=1, source_target_pairs={{0,0},{8,24},{16,16},{24,8},{1,1},{9,25},{17,17},{25,9},{2,2},{10,... | collective-permute-start | bytes 5864 | tf_op jit(solution)/shard_map/ppermute | solution.py:18
  22.0 0.1 slice.29
  22.1 1.5 %collective-permute-start.4 = (f32[2,3904]{1,0:T(2,128)S(1)}, f32[2,3904]{1,0:T(2,128)S(1)}, u32[]{:S(2)}, u32[]{:S(2)}) collective-permute-start(f32[2,3904]{1,0:T(2,128)S(1)} %get-tuple-element.16), channel_id=1, source_target_pairs={{0,24},{8,0},{16,8},{24,16},{1,25},{9,1},{17,9},{25,17},{2,26},{10... | collective-permute-start | bytes 93704 | tf_op jit(solution)/shard_map/ppermute | solution.py:18
  23.5 0.6 %collective-permute-start.5 = (f32[2,3904]{1,0:T(2,128)S(1)}, f32[2,3904]{1,0:T(2,128)S(1)}, u32[]{:S(2)}, u32[]{:S(2)}) collective-permute-start(f32[2,3904]{1,0:T(2,128)S(1)} %get-tuple-element.17), channel_id=1, source_target_pairs={{0,8},{8,16},{16,24},{24,0},{1,9},{9,17},{17,25},{25,1},{2,10},{10... | collective-permute-start | bytes 93704 | tf_op jit(solution)/shard_map/ppermute | solution.py:18
  24.1 0.5 rev.10
  24.6 2.4 %collective-permute-start.6 = (f32[122,2,128]{2,1,0:T(2,128)S(1)}, f32[122,2,128]{2,1,0:T(2,128)S(1)}, u32[]{:S(2)}, u32[]{:S(2)}) collective-permute-start(f32[122,2,128]{2,1,0:T(2,128)S(1)} %rev.10), channel_id=1, source_target_pairs={{0,24},{8,16},{16,8},{24,0},{1,25},{9,17},{17,9},{25,1},{2,26},{10... | collective-permute-start | bytes 374792 | tf_op jit(solution)/shard_map/ppermute | solution.py:18
  27.0 0.0 collective-permute-done.7
  27.0 0.0 collective-permute-done.8
  27.0 0.3 fusion.6
  27.4 0.1 reshape.86
  27.4 0.0 collective-permute-done.4
  27.5 1.2 %collective-permute-done.5 = f32[2,3904]{1,0:T(2,128)S(1)} collective-permute-done((f32[2,3904]{1,0:T(2,128)S(1)}, f32[2,3904]{1,0:T(2,128)S(1)}, u32[]{:S(2)}, u32[]{:S(2)}) %collective-permute-start.5) | collective-permute-done | bytes 31264 | tf_op jit(solution)/shard_map/ppermute | solution.py:18
  28.6 1.7 %fusion.2 = f32[3904,128]{1,0:T(8,128)S(1)} fusion(pred[128,4]{0,1:T(4,128)(4,1)S(1)} %and_or_fusion, f32[2,3904]{1,0:T(2,128)S(1)} %collective-permute-done.5, f32[2,3904]{1,0:T(2,128)S(1)} %collective-permute-done.4), kind=kOutput, calls=%fused_computation.13 | convolution fusion | flops 24001792 | bytes 2061824 | tf_op jit(solution)/shard_map/dot_general | solution.py:31
  30.4 0.1 collective-permute-done.6
  30.5 0.5 maximum_maximum_fusion.x_ref
  31.0 9.1 %shard_map.76 = (f32[2,20,32,128]{3,2,1,0:T(8,128)}, f32[2,20,32,128]{3,2,1,0:T(8,128)}, f32[2,20,32,128]{3,2,1,0:T(8,128)S(1)}) custom-call(f32[122,40,256]{2,1,0:T(8,128)S(1)} %maximum_maximum_fusion.x_ref), custom_call_target="tpu_custom_call" | custom-call | tf_op jit(solution)/shard_map/pallas_call | solution.py:210
  40.1 0.1 dynamic-slice_bitcast_fusion
  40.2 0.1 collective-permute-start.9
  40.3 1.5 %collective-permute-done.9 = f32[2,20,4,4,128]{4,3,2,1,0:T(4,128)S(1)} collective-permute-done((f32[2,20,4,4,128]{4,3,2,1,0:T(4,128)S(1)}, f32[2,20,4,4,128]{4,3,2,1,0:T(4,128)S(1)}, u32[]{:S(2)}, u32[]{:S(2)}) %collective-permute-start.9) | collective-permute-done | bytes 327712 | tf_op jit(solution)/shard_map/ppermute | solution.py:268
  41.9 0.1 bitcast_add_fusion
  42.0 0.1 dynamic-slice_bitcast_fusion.3
  42.0 2.1 %collective-permute-start.10 = (f32[2,20,4,128]{3,2,1,0:T(4,128)S(1)}, f32[2,20,4,128]{3,2,1,0:T(4,128)S(1)}, u32[]{:S(2)}, u32[]{:S(2)}) collective-permute-start(f32[2,20,4,128]{3,2,1,0:T(4,128)S(1)} %get-tuple-element.9), channel_id=1, source_target_pairs={{0,2},{1,3},{2,4},{3,5},{4,6},{5,7},{6,0},{7,1},{8,10},{9,11},{10,... | collective-permute-start | bytes 245768 | tf_op jit(solution)/shard_map/ppermute | solution.py:273
  44.1 1.8 %collective-permute-start.11 = (f32[2,20,4,128]{3,2,1,0:T(4,128)S(1)}, f32[2,20,4,128]{3,2,1,0:T(4,128)S(1)}, u32[]{:S(2)}, u32[]{:S(2)}) collective-permute-start(f32[2,20,4,128]{3,2,1,0:T(4,128)S(1)} %get-tuple-element.11), channel_id=1, source_target_pairs={{0,4},{1,5},{2,6},{3,7},{4,0},{5,1},{6,2},{7,3},{8,12},{9,13},{10,... | collective-permute-start | bytes 245768 | tf_op jit(solution)/shard_map/ppermute | solution.py:273
  45.9 0.6 %collective-permute-start.12 = (f32[2,20,4,128]{3,2,1,0:T(4,128)S(1)}, f32[2,20,4,128]{3,2,1,0:T(4,128)S(1)}, u32[]{:S(2)}, u32[]{:S(2)}) collective-permute-start(f32[2,20,4,128]{3,2,1,0:T(4,128)S(1)} %get-tuple-element.10), channel_id=1, source_target_pairs={{0,6},{1,7},{2,0},{3,1},{4,2},{5,3},{6,4},{7,5},{8,14},{9,15},{10,... | collective-permute-start | bytes 245768 | tf_op jit(solution)/shard_map/ppermute | solution.py:273
  46.5 2.7 %collective-permute-done.10 = f32[2,20,4,128]{3,2,1,0:T(4,128)S(1)} collective-permute-done((f32[2,20,4,128]{3,2,1,0:T(4,128)S(1)}, f32[2,20,4,128]{3,2,1,0:T(4,128)S(1)}, u32[]{:S(2)}, u32[]{:S(2)}) %collective-permute-start.10) | collective-permute-done | bytes 81952 | tf_op jit(solution)/shard_map/ppermute | solution.py:273
  49.3 2.7 %collective-permute-done.11 = f32[2,20,4,128]{3,2,1,0:T(4,128)S(1)} collective-permute-done((f32[2,20,4,128]{3,2,1,0:T(4,128)S(1)}, f32[2,20,4,128]{3,2,1,0:T(4,128)S(1)}, u32[]{:S(2)}, u32[]{:S(2)}) %collective-permute-start.11) | collective-permute-done | bytes 81952 | tf_op jit(solution)/shard_map/ppermute | solution.py:273
  52.0 0.1 collective-permute-done.12
  52.1 0.7 %fusion.1 = f32[2,20,4,128]{3,2,1,0:T(4,128)} fusion(f32[2,20,4,128]{3,2,1,0:T(4,128)S(1)} %collective-permute-done.12, f32[2,20,4,128]{3,2,1,0:T(4,128)S(1)} %collective-permute-done.11, f32[2,20,4,128]{3,2,1,0:T(4,128)S(1)} %collective-permute-done.10, f32[2,20,4,4,128]{4,3,2,1,0:T(4,128)S(1)} %bitcast_add_fusion, s32[]{:T(128)S(6)} %select_n.107), kind=kLoop, calls=%fused_computation.9 | loop fusion | flops 61440 | bytes 409604 | tf_op jit(solution)/shard_map/add | solution.py:273
  (12 shorter events, 0.1 us)
Async XLA Ops:
  0.6 11.6 %copy-start = (f32[2,20,4,128]{3,2,1,0:T(4,128)S(1)}, f32[2,20,4,128]{3,2,1,0:T(4,128)}, u32[]{:S(2)}) copy-start(f32[2,20,4,128]{3,2,1,0:T(4,128)} %param.6) | copy-start | bytes 245764
  0.6 9.5 %collective-permute-start = (f32[2,20,4,128]{3,2,1,0:T(4,128)}, f32[2,20,4,128]{3,2,1,0:T(4,128)S(1)}, u32[]{:S(2)}, u32[]{:S(2)}) collective-permute-start(f32[2,20,4,128]{3,2,1,0:T(4,128)} %param.6), channel_id=1, source_target_pairs={{0,2},{1,3},{2,4},{3,5},{4,6},{5,7},{6,0},{7,1},{8,10},{9,11},{10,... | collective-permute-start | bytes 245768 | tf_op jit(solution)/shard_map/ppermute | solution.py:245
  3.7 8.3 %collective-permute-start.1 = (f32[2,20,4,128]{3,2,1,0:T(4,128)}, f32[2,20,4,128]{3,2,1,0:T(4,128)S(1)}, u32[]{:S(2)}, u32[]{:S(2)}) collective-permute-start(f32[2,20,4,128]{3,2,1,0:T(4,128)} %param.6), channel_id=1, source_target_pairs={{0,4},{1,5},{2,6},{3,7},{4,0},{5,1},{6,2},{7,3},{8,12},{9,13},{10,... | collective-permute-start | bytes 245768 | tf_op jit(solution)/shard_map/ppermute | solution.py:245
  6.3 5.9 %collective-permute-start.2 = (f32[2,20,4,128]{3,2,1,0:T(4,128)}, f32[2,20,4,128]{3,2,1,0:T(4,128)S(1)}, u32[]{:S(2)}, u32[]{:S(2)}) collective-permute-start(f32[2,20,4,128]{3,2,1,0:T(4,128)} %param.6), channel_id=1, source_target_pairs={{0,6},{1,7},{2,0},{3,1},{4,2},{5,3},{6,4},{7,5},{8,14},{9,15},{10,... | collective-permute-start | bytes 245768 | tf_op jit(solution)/shard_map/ppermute | solution.py:245
  12.3 1.7 %collective-permute-start.3 = (f32[4,2,20,4,128]{4,3,2,1,0:T(4,128)S(1)}, f32[4,2,20,4,128]{4,3,2,1,0:T(4,128)S(1)}, u32[]{:S(2)}, u32[]{:S(2)}) collective-permute-start(f32[4,2,20,4,128]{4,3,2,1,0:T(4,128)S(1)} %get-tuple-element.13), channel_id=1, source_target_pairs={{0,1},{1,0},{2,3},{3,2},{4,5},{5,4},{6,7},{7,6},{8,9},{9,8},{10,11... | collective-permute-start | bytes 983048 | tf_op jit(solution)/shard_map/ppermute | solution.py:248
  15.1 0.7 %copy-start.1 = (s32[32,128]{1,0:T(8,128)S(1)}, s32[32,128]{1,0:T(8,128)}, u32[]{:S(2)}) copy-start(s32[32,128]{1,0:T(8,128)} %param.7) | copy-start | bytes 49156
  15.1 0.7 %copy-start.2 = (s32[32,128]{1,0:T(8,128)S(1)}, s32[32,128]{1,0:T(8,128)}, u32[]{:S(2)}) copy-start(s32[32,128]{1,0:T(8,128)} %param.8) | copy-start | bytes 49156
  17.5 9.5 %collective-permute-start.7 = (f32[2,244]{1,0:T(2,128)S(1)}, f32[2,244]{1,0:T(2,128)S(1)}, u32[]{:S(2)}, u32[]{:S(2)}) collective-permute-start(f32[2,244]{1,0:T(2,128)S(1)} %reshape.84), channel_id=1, source_target_pairs={{0,16},{8,8},{16,0},{24,24},{1,17},{9,9},{17,1},{25,25},{2,18},{10... | collective-permute-start | bytes 5864 | tf_op jit(solution)/shard_map/ppermute | solution.py:18
  21.3 5.8 %collective-permute-start.8 = (f32[2,244]{1,0:T(2,128)S(1)}, f32[2,244]{1,0:T(2,128)S(1)}, u32[]{:S(2)}, u32[]{:S(2)}) collective-permute-start(f32[2,244]{1,0:T(2,128)S(1)} %reshape.85), channel_id=1, source_target_pairs={{0,0},{8,24},{16,16},{24,8},{1,1},{9,25},{17,17},{25,9},{2,2},{10,... | collective-permute-start | bytes 5864 | tf_op jit(solution)/shard_map/ppermute | solution.py:18
  22.1 5.4 %collective-permute-start.4 = (f32[2,3904]{1,0:T(2,128)S(1)}, f32[2,3904]{1,0:T(2,128)S(1)}, u32[]{:S(2)}, u32[]{:S(2)}) collective-permute-start(f32[2,3904]{1,0:T(2,128)S(1)} %get-tuple-element.16), channel_id=1, source_target_pairs={{0,24},{8,0},{16,8},{24,16},{1,25},{9,1},{17,9},{25,17},{2,26},{10... | collective-permute-start | bytes 93704 | tf_op jit(solution)/shard_map/ppermute | solution.py:18
  23.5 5.1 %collective-permute-start.5 = (f32[2,3904]{1,0:T(2,128)S(1)}, f32[2,3904]{1,0:T(2,128)S(1)}, u32[]{:S(2)}, u32[]{:S(2)}) collective-permute-start(f32[2,3904]{1,0:T(2,128)S(1)} %get-tuple-element.17), channel_id=1, source_target_pairs={{0,8},{8,16},{16,24},{24,0},{1,9},{9,17},{17,25},{25,1},{2,10},{10... | collective-permute-start | bytes 93704 | tf_op jit(solution)/shard_map/ppermute | solution.py:18
  24.6 5.9 %collective-permute-start.6 = (f32[122,2,128]{2,1,0:T(2,128)S(1)}, f32[122,2,128]{2,1,0:T(2,128)S(1)}, u32[]{:S(2)}, u32[]{:S(2)}) collective-permute-start(f32[122,2,128]{2,1,0:T(2,128)S(1)} %rev.10), channel_id=1, source_target_pairs={{0,24},{8,16},{16,8},{24,0},{1,25},{9,17},{17,9},{25,1},{2,26},{10... | collective-permute-start | bytes 374792 | tf_op jit(solution)/shard_map/ppermute | solution.py:18
  40.2 1.7 %collective-permute-start.9 = (f32[2,20,4,4,128]{4,3,2,1,0:T(4,128)S(1)}, f32[2,20,4,4,128]{4,3,2,1,0:T(4,128)S(1)}, u32[]{:S(2)}, u32[]{:S(2)}) collective-permute-start(f32[2,20,4,4,128]{4,3,2,1,0:T(4,128)S(1)} %dynamic-slice_bitcast_fusion), channel_id=1, source_target_pairs={{0,1},{1,0},{2,3},{3,2},{4,5},{5,4},{6,7},{7,6},{8,9},{9,8},{10,11... | collective-permute-start | bytes 983048 | tf_op jit(solution)/shard_map/ppermute | solution.py:268
  42.0 7.2 %collective-permute-start.10 = (f32[2,20,4,128]{3,2,1,0:T(4,128)S(1)}, f32[2,20,4,128]{3,2,1,0:T(4,128)S(1)}, u32[]{:S(2)}, u32[]{:S(2)}) collective-permute-start(f32[2,20,4,128]{3,2,1,0:T(4,128)S(1)} %get-tuple-element.9), channel_id=1, source_target_pairs={{0,2},{1,3},{2,4},{3,5},{4,6},{5,7},{6,0},{7,1},{8,10},{9,11},{10,... | collective-permute-start | bytes 245768 | tf_op jit(solution)/shard_map/ppermute | solution.py:273
  44.1 7.9 %collective-permute-start.11 = (f32[2,20,4,128]{3,2,1,0:T(4,128)S(1)}, f32[2,20,4,128]{3,2,1,0:T(4,128)S(1)}, u32[]{:S(2)}, u32[]{:S(2)}) collective-permute-start(f32[2,20,4,128]{3,2,1,0:T(4,128)S(1)} %get-tuple-element.11), channel_id=1, source_target_pairs={{0,4},{1,5},{2,6},{3,7},{4,0},{5,1},{6,2},{7,3},{8,12},{9,13},{10,... | collective-permute-start | bytes 245768 | tf_op jit(solution)/shard_map/ppermute | solution.py:273
  45.9 6.2 %collective-permute-start.12 = (f32[2,20,4,128]{3,2,1,0:T(4,128)S(1)}, f32[2,20,4,128]{3,2,1,0:T(4,128)S(1)}, u32[]{:S(2)}, u32[]{:S(2)}) collective-permute-start(f32[2,20,4,128]{3,2,1,0:T(4,128)S(1)} %get-tuple-element.10), channel_id=1, source_target_pairs={{0,6},{1,7},{2,0},{3,1},{4,2},{5,3},{6,4},{7,5},{8,14},{9,15},{10,... | collective-permute-start | bytes 245768 | tf_op jit(solution)/shard_map/ppermute | solution.py:273

commit v17 on v13

--- a/solution.py
+++ b/solution.py
@@ -232,24 +232,14 @@
 
 def gathered_over_scen(block):
     parts = lax.axis_size("scen")
-    if parts % 2:
-        return lax.all_gather(block, "scen", axis=2, tiled=True)
     kinds, levels, rows, width = block.shape
     me = lax.axis_index("scen")
-    core = me % 2
-    chip = me // 2
-    chips = parts // 2
     got = [block]
-    for step in range(1, chips):
-        got.append(
-            lax.ppermute(block, "scen", [(q, ((q // 2 + step) % chips) * 2 + q % 2) for q in range(parts)])
-        )
-    same = jnp.stack(got)
-    other = lax.ppermute(same, "scen", [(q, q ^ 1) for q in range(parts)])
-    by_core = jnp.where(core == 0, jnp.stack([same, other], axis=1), jnp.stack([other, same], axis=1))
-    order = (chip - jnp.arange(chips)) % chips
-    by_chip = jnp.take(by_core, order, axis=0)
-    return by_chip.transpose(2, 3, 0, 1, 4, 5).reshape(kinds, levels, parts * rows, width)
+    for step in range(1, parts):
+        got.append(lax.ppermute(block, "scen", [(q, (q + step) % parts) for q in range(parts)]))
+    order = (me - jnp.arange(parts)) % parts
+    by_owner = jnp.take(jnp.stack(got), order, axis=0)
+    return by_owner.transpose(1, 2, 0, 3, 4).reshape(kinds, levels, parts * rows, width)
 
 
 def summed_over_scen(grad):

time: 53 us -> 60.1 us (1.13)
  waiting for transfers between devices: 11.8 us -> 15.2 us
  starting transfers between devices: 20.2 us -> 23.2 us
  local copies, waits for them, and re-layouts: 5.59 us -> 6.61 us
    ppermute x4 -> x7, starting transfers between devices: 7.08 us -> 10.9 us  [gathered_over_scen(): lax.ppermute(block, 'scen', [(q, (q + step) % parts) for q in range(parts)])]
    ppermute x3, waiting for transfers between devices: 5.59 us -> 7.38 us  [summed_over_scen(): lax.ppermute(send, 'scen', [(q, (q // 2 + step) % chips * 2 + q % 2) for...]
    ppermute x5, waiting for transfers between devices: 0.99 us -> 2.47 us  [shifted(): return lax.ppermute(x, 'space', perm)]
    ppermute x3, starting transfers between devices: 4.5 us -> 3.19 us  [summed_over_scen(): lax.ppermute(send, 'scen', [(q, (q // 2 + step) % chips * 2 + q % 2) for...]
    unnamed x9 -> x16, local copies, waits for them, and re-layouts: 2.59 us -> 3.6 us
    ppermute x4 -> x7, waiting for transfers between devices: 3.64 us -> 3.79 us  [gathered_over_scen(): lax.ppermute(block, 'scen', [(q, (q + step) % parts) for q in range(parts)])]
  transfers between devices with their start and end apart: 13 -> 16, of which waited for: 9 -> 8; matrix products, arithmetic and copies ran while one was open for 11% -> 11% of each run, Pallas kernels for 0% -> 0%
where the time goes in v17:
time: 60.1 us; the launch traced here: 59.7 us
  starting transfers between devices  23.2 us (39%)
  waiting for transfers between devices  15.2 us (25%)
  Pallas kernels  9.11 us (15%)
  local copies, waits for them, and re-layouts  6.61 us (11%)
  matrix products  2.96 us (5%)
  other arithmetic  1.62 us (3%)
  between operations  1.04 us (2%)
    ppermute x7, starting transfers between devices, gathered_over_scen(): lax.ppermute(block, 'scen', [(q, (q + step) % parts) for q in range(parts)])  10.9 us
    pallas_call x1, Pallas kernels, on_device(): pl.pallas_call(diffusion_kernel, out_shape=(field, field, jax.ShapeDtypeS...  9.11 us
    ppermute x5, starting transfers between devices, shifted(): return lax.ppermute(x, 'space', perm)  9.01 us
    ppermute x3, waiting for transfers between devices, summed_over_scen(): lax.ppermute(send, 'scen', [(q, (q // 2 + step) % chips * 2 + q % 2) for...  7.38 us
    ppermute x7, waiting for transfers between devices, gathered_over_scen(): lax.ppermute(block, 'scen', [(q, (q + step) % parts) for q in range(parts)])  3.79 us
    unnamed x16, local copies, waits for them, and re-layouts  3.6 us
    ppermute x3, starting transfers between devices, summed_over_scen(): lax.ppermute(send, 'scen', [(q, (q // 2 + step) % chips * 2 + q % 2) for...  3.19 us
    dot_general x3, matrix products, contract(): lax.dot_general(a, b, (dims, ((), ())), precision=lax.Precision.HIGHEST,...  2.96 us
  transfers between devices with their start and end apart: 16, of which 8 were waited for; matrix products, arithmetic and copies ran while one was open for 11% of the time, Pallas kernels for 0%

profile of v17, /device:TPU:0, one launch (start us, length us, event | category | flops | bytes accessed | tf_op | source)
XLA Modules:
  0.0 59.7 jit_solution(3895148191966517950)
XLA Ops:
  0.6 0.0 copy-start
  0.6 0.5 collective-permute-start
  1.1 2.6 %collective-permute-start.1 = (f32[2,20,4,128]{3,2,1,0:T(4,128)}, f32[2,20,4,128]{3,2,1,0:T(4,128)S(1)}, u32[]{:S(2)}, u32[]{:S(2)}) collective-permute-start(f32[2,20,4,128]{3,2,1,0:T(4,128)} %param.6), channel_id=1, source_target_pairs={{0,2},{1,3},{2,4},{3,5},{4,6},{5,7},{6,0},{7,1},{8,10},{9,11},{10,... | collective-permute-start | bytes 245768 | tf_op jit(solution)/shard_map/ppermute | solution.py:239
  3.8 2.5 %collective-permute-start.2 = (f32[2,20,4,128]{3,2,1,0:T(4,128)}, f32[2,20,4,128]{3,2,1,0:T(4,128)S(1)}, u32[]{:S(2)}, u32[]{:S(2)}) collective-permute-start(f32[2,20,4,128]{3,2,1,0:T(4,128)} %param.6), channel_id=1, source_target_pairs={{0,3},{1,4},{2,5},{3,6},{4,7},{5,0},{6,1},{7,2},{8,11},{9,12},{10,... | collective-permute-start | bytes 245768 | tf_op jit(solution)/shard_map/ppermute | solution.py:239
  6.3 1.2 %collective-permute-start.3 = (f32[2,20,4,128]{3,2,1,0:T(4,128)}, f32[2,20,4,128]{3,2,1,0:T(4,128)S(1)}, u32[]{:S(2)}, u32[]{:S(2)}) collective-permute-start(f32[2,20,4,128]{3,2,1,0:T(4,128)} %param.6), channel_id=1, source_target_pairs={{0,4},{1,5},{2,6},{3,7},{4,0},{5,1},{6,2},{7,3},{8,12},{9,13},{10,... | collective-permute-start | bytes 245768 | tf_op jit(solution)/shard_map/ppermute | solution.py:239
  7.5 1.2 %collective-permute-start.4 = (f32[2,20,4,128]{3,2,1,0:T(4,128)}, f32[2,20,4,128]{3,2,1,0:T(4,128)S(1)}, u32[]{:S(2)}, u32[]{:S(2)}) collective-permute-start(f32[2,20,4,128]{3,2,1,0:T(4,128)} %param.6), channel_id=1, source_target_pairs={{0,5},{1,6},{2,7},{3,0},{4,1},{5,2},{6,3},{7,4},{8,13},{9,14},{10,... | collective-permute-start | bytes 245768 | tf_op jit(solution)/shard_map/ppermute | solution.py:239
  8.7 0.9 %bitcast_dynamic-update-slice_fusion.7 = f32[8,2,20,4,128]{4,3,2,1,0:T(4,128)S(1)} fusion(f32[2,20,4,128]{3,2,1,0:T(4,128)} %param.6), kind=kLoop, calls=%fused_computation.18 | loop fusion | bytes 163840
  9.7 1.1 %constant_dynamic-update-slice_fusion.4 = f32[122,32,128]{2,1,0:T(8,128)S(1)} fusion(f32[40,32,128]{2,1,0:T(8,128)} %bitcast.63), kind=kLoop, calls=%fused_computation.30 | loop fusion | bytes 1310720
  10.9 1.1 %constant_dynamic-update-slice_fusion.3 = f32[122,32,128]{2,1,0:T(8,128)S(1)} fusion(f32[122,32,128]{2,1,0:T(8,128)S(1)} %constant_dynamic-update-slice_fusion.4, f32[40,32,128]{2,1,0:T(8,128)} %bitcast.64), kind=kLoop, calls=%fused_computation.29 | loop fusion | bytes 1310720
  12.0 0.1 pad.4.clone
  12.1 0.1 and_or_fusion
  12.2 0.0 collective-permute-done
  12.2 1.4 %collective-permute-start.5 = (f32[2,20,4,128]{3,2,1,0:T(4,128)S(1)}, f32[2,20,4,128]{3,2,1,0:T(4,128)S(1)}, u32[]{:S(2)}, u32[]{:S(2)}) collective-permute-start(f32[2,20,4,128]{3,2,1,0:T(4,128)S(1)} %copy-done), channel_id=1, source_target_pairs={{0,6},{1,7},{2,0},{3,1},{4,2},{5,3},{6,4},{7,5},{8,14},{9,15},{10,... | collective-permute-start | bytes 245768 | tf_op jit(solution)/shard_map/ppermute | solution.py:239
  13.7 0.0 collective-permute-done.1
  13.7 1.5 %collective-permute-start.6 = (f32[2,20,4,128]{3,2,1,0:T(4,128)S(1)}, f32[2,20,4,128]{3,2,1,0:T(4,128)S(1)}, u32[]{:S(2)}, u32[]{:S(2)}) collective-permute-start(f32[2,20,4,128]{3,2,1,0:T(4,128)S(1)} %copy-done), channel_id=1, source_target_pairs={{0,7},{1,0},{2,1},{3,2},{4,3},{5,4},{6,5},{7,6},{8,15},{9,8},{10,9... | collective-permute-start | bytes 245768 | tf_op jit(solution)/shard_map/ppermute | solution.py:239
  15.1 0.2 collective-permute-done.2
  15.4 0.2 collective-permute-done.3
  15.6 0.0 collective-permute-done.4
  15.6 3.3 %collective-permute-done.5 = f32[2,20,4,128]{3,2,1,0:T(4,128)S(1)} collective-permute-done((f32[2,20,4,128]{3,2,1,0:T(4,128)S(1)}, f32[2,20,4,128]{3,2,1,0:T(4,128)S(1)}, u32[]{:S(2)}, u32[]{:S(2)}) %collective-permute-start.5) | collective-permute-done | bytes 81952 | tf_op jit(solution)/shard_map/ppermute | solution.py:239
  19.0 0.0 collective-permute-done.6
  19.0 0.9 %gather_fusion = f32[8,2,20,4,128]{4,3,2,1,0:T(4,128)S(1)} fusion(f32[8,2,20,4,128]{4,3,2,1,0:T(4,128)S(1)} %bitcast_dynamic-update-slice_fusion, s32[1024]{0:T(1024)S(1)} %pad_clamp_fusion), kind=kCustom, calls=%fused_computation | custom fusion | bytes 1310752 | tf_op jit(solution)/shard_map/jit(_take)/gather | solution.py:241
  20.0 0.0 copy-start.1
  20.0 0.0 copy-start.2
  20.0 0.2 select_bitcast_fusion
  20.2 0.2 copy.24
  20.4 0.2 copy-done.1
  20.7 0.0 copy-done.2
  20.7 1.0 %fusion.9 = f32[4,3904]{1,0:T(4,128)S(1)} fusion(f32[3904,128]{1,0:T(8,128)S(1)} %bitcast.60, pred[128]{0:T(512)(128)(4,1)S(1)} %get-tuple-element.16, pred[128]{0:T(512)(128)(4,1)S(1)} %get-tuple-element.17, pred[128]{0:T(512)(128)(4,1)S(1)} %get-tuple-element.18, pred[128]{0:T(512)(128)(4,1)S(1)} %get-tuple-element.19, ...), kind=kOutput, calls=%fused_computation.40 | convolution fusion | flops 23989760 | bytes 2061840 | tf_op jit(solution)/shard_map/dot_general | solution.py:31
  21.7 0.1 reshape.79
  21.9 0.1 fusion.29
  22.0 0.2 rev.12
  22.2 0.7 %collective-permute-start.11 = (f32[2,122,2]{2,1,0:T(8,128)S(1)}, f32[2,122,2]{2,1,0:T(8,128)S(1)}, u32[]{:S(2)}, u32[]{:S(2)}) collective-permute-start(f32[2,122,2]{2,1,0:T(8,128)S(1)} %rev.12), channel_id=1, source_target_pairs={{0,0},{8,24},{16,16},{24,8},{1,1},{9,25},{17,17},{25,9},{2,2},{10,... | collective-permute-start | bytes 5864 | tf_op jit(solution)/shard_map/ppermute | solution.py:18
  22.9 0.2 rev.11
  23.1 3.9 %collective-permute-start.10 = (f32[2,122,2]{2,1,0:T(8,128)S(1)}, f32[2,122,2]{2,1,0:T(8,128)S(1)}, u32[]{:S(2)}, u32[]{:S(2)}) collective-permute-start(f32[2,122,2]{2,1,0:T(8,128)S(1)} %rev.11), channel_id=1, source_target_pairs={{0,16},{8,8},{16,0},{24,24},{1,17},{9,9},{17,1},{25,25},{2,18},{10... | collective-permute-start | bytes 5864 | tf_op jit(solution)/shard_map/ppermute | solution.py:18
  27.0 0.1 slice.29
  27.1 0.5 rev.10
  27.6 1.5 %collective-permute-start.9 = (f32[122,2,128]{2,1,0:T(2,128)S(1)}, f32[122,2,128]{2,1,0:T(2,128)S(1)}, u32[]{:S(2)}, u32[]{:S(2)}) collective-permute-start(f32[122,2,128]{2,1,0:T(2,128)S(1)} %rev.10), channel_id=1, source_target_pairs={{0,24},{8,16},{16,8},{24,0},{1,25},{9,17},{17,9},{25,1},{2,26},{10... | collective-permute-start | bytes 374792 | tf_op jit(solution)/shard_map/ppermute | solution.py:18
  29.1 0.1 collective-permute-start.8
  29.2 2.8 %collective-permute-start.7 = (f32[2,3904]{1,0:T(2,128)S(1)}, f32[2,3904]{1,0:T(2,128)S(1)}, u32[]{:S(2)}, u32[]{:S(2)}) collective-permute-start(f32[2,3904]{1,0:T(2,128)S(1)} %get-tuple-element.14), channel_id=1, source_target_pairs={{0,24},{8,0},{16,8},{24,16},{1,25},{9,1},{17,9},{25,17},{2,26},{10... | collective-permute-start | bytes 93704 | tf_op jit(solution)/shard_map/ppermute | solution.py:18
  32.0 0.0 collective-permute-done.11
  32.0 1.9 %collective-permute-done.10 = f32[2,122,2]{2,1,0:T(8,128)S(1)} collective-permute-done((f32[2,122,2]{2,1,0:T(8,128)S(1)}, f32[2,122,2]{2,1,0:T(8,128)S(1)}, u32[]{:S(2)}, u32[]{:S(2)}) %collective-permute-start.10) | collective-permute-done | bytes 1984 | tf_op jit(solution)/shard_map/ppermute | solution.py:18
  33.9 0.2 reshape.91
  34.1 0.1 copy.30
  34.2 0.1 dot_general.16
  34.3 0.2 fusion
  34.5 0.1 copy.27
  34.6 0.6 %collective-permute-done.8 = f32[2,3904]{1,0:T(2,128)S(1)} collective-permute-done((f32[2,3904]{1,0:T(2,128)S(1)}, f32[2,3904]{1,0:T(2,128)S(1)}, u32[]{:S(2)}, u32[]{:S(2)}) %collective-permute-start.8) | collective-permute-done | bytes 31264 | tf_op jit(solution)/shard_map/ppermute | solution.py:18
  35.2 0.0 collective-permute-done.7
  35.2 1.7 %fusion.4 = f32[3904,128]{1,0:T(8,128)S(1)} fusion(pred[128,4]{0,1:T(4,128)(4,1)S(1)} %and_or_fusion, f32[2,3904]{1,0:T(2,128)S(1)} %collective-permute-done.8, f32[2,3904]{1,0:T(2,128)S(1)} %collective-permute-done.7), kind=kOutput, calls=%fused_computation.22 | convolution fusion | flops 24001792 | bytes 2061824 | tf_op jit(solution)/shard_map/dot_general | solution.py:31
  37.0 0.0 collective-permute-done.9
  37.0 0.5 maximum_maximum_fusion.x_ref
  37.5 9.1 %shard_map.76 = (f32[2,20,32,128]{3,2,1,0:T(8,128)}, f32[2,20,32,128]{3,2,1,0:T(8,128)}, f32[2,20,32,128]{3,2,1,0:T(8,128)S(1)}) custom-call(f32[122,40,256]{2,1,0:T(8,128)S(1)} %maximum_maximum_fusion.x_ref), custom_call_target="tpu_custom_call" | custom-call | tf_op jit(solution)/shard_map/pallas_call | solution.py:210
  46.6 0.1 dynamic-slice_bitcast_fusion
  46.6 0.1 collective-permute-start.12
  46.8 1.5 %collective-permute-done.12 = f32[2,20,4,4,128]{4,3,2,1,0:T(4,128)S(1)} collective-permute-done((f32[2,20,4,4,128]{4,3,2,1,0:T(4,128)S(1)}, f32[2,20,4,4,128]{4,3,2,1,0:T(4,128)S(1)}, u32[]{:S(2)}, u32[]{:S(2)}) %collective-permute-start.12) | collective-permute-done | bytes 327712 | tf_op jit(solution)/shard_map/ppermute | solution.py:258
  48.3 0.1 bitcast_add_fusion
  48.4 0.1 dynamic-slice_bitcast_fusion.3
  48.5 2.6 %collective-permute-start.15 = (f32[2,20,4,128]{3,2,1,0:T(4,128)S(1)}, f32[2,20,4,128]{3,2,1,0:T(4,128)S(1)}, u32[]{:S(2)}, u32[]{:S(2)}) collective-permute-start(f32[2,20,4,128]{3,2,1,0:T(4,128)S(1)} %get-tuple-element.10), channel_id=1, source_target_pairs={{0,6},{1,7},{2,0},{3,1},{4,2},{5,3},{6,4},{7,5},{8,14},{9,15},{10,... | collective-permute-start | bytes 245768 | tf_op jit(solution)/shard_map/ppermute | solution.py:263
  51.0 0.0 collective-permute-start.14
  51.0 0.6 %collective-permute-start.13 = (f32[2,20,4,128]{3,2,1,0:T(4,128)S(1)}, f32[2,20,4,128]{3,2,1,0:T(4,128)S(1)}, u32[]{:S(2)}, u32[]{:S(2)}) collective-permute-start(f32[2,20,4,128]{3,2,1,0:T(4,128)S(1)} %get-tuple-element.9), channel_id=1, source_target_pairs={{0,2},{1,3},{2,4},{3,5},{4,6},{5,7},{6,0},{7,1},{8,10},{9,11},{10,... | collective-permute-start | bytes 245768 | tf_op jit(solution)/shard_map/ppermute | solution.py:263
  51.7 2.2 %collective-permute-done.15 = f32[2,20,4,128]{3,2,1,0:T(4,128)S(1)} collective-permute-done((f32[2,20,4,128]{3,2,1,0:T(4,128)S(1)}, f32[2,20,4,128]{3,2,1,0:T(4,128)S(1)}, u32[]{:S(2)}, u32[]{:S(2)}) %collective-permute-start.15) | collective-permute-done | bytes 81952 | tf_op jit(solution)/shard_map/ppermute | solution.py:263
  53.9 5.2 %collective-permute-done.14 = f32[2,20,4,128]{3,2,1,0:T(4,128)S(1)} collective-permute-done((f32[2,20,4,128]{3,2,1,0:T(4,128)S(1)}, f32[2,20,4,128]{3,2,1,0:T(4,128)S(1)}, u32[]{:S(2)}, u32[]{:S(2)}) %collective-permute-start.14) | collective-permute-done | bytes 81952 | tf_op jit(solution)/shard_map/ppermute | solution.py:263
  59.1 0.0 collective-permute-done.13
  59.1 0.7 %fusion.3 = f32[2,20,4,128]{3,2,1,0:T(4,128)} fusion(f32[2,20,4,128]{3,2,1,0:T(4,128)S(1)} %collective-permute-done.15, f32[2,20,4,128]{3,2,1,0:T(4,128)S(1)} %collective-permute-done.14, f32[2,20,4,128]{3,2,1,0:T(4,128)S(1)} %collective-permute-done.13, f32[2,20,4,4,128]{4,3,2,1,0:T(4,128)S(1)} %bitcast_add_fusion, s32[]{:T(128)S(6)} %select_n.94), kind=kLoop, calls=%fused_computation.10 | loop fusion | flops 61440 | bytes 409604 | tf_op jit(solution)/shard_map/add | solution.py:263
  (21 shorter events, 0.3 us)
Async XLA Ops:
  0.6 11.6 %copy-start = (f32[2,20,4,128]{3,2,1,0:T(4,128)S(1)}, f32[2,20,4,128]{3,2,1,0:T(4,128)}, u32[]{:S(2)}) copy-start(f32[2,20,4,128]{3,2,1,0:T(4,128)} %param.6) | copy-start | bytes 245764
  0.6 11.6 %collective-permute-start = (f32[2,20,4,128]{3,2,1,0:T(4,128)}, f32[2,20,4,128]{3,2,1,0:T(4,128)S(1)}, u32[]{:S(2)}, u32[]{:S(2)}) collective-permute-start(f32[2,20,4,128]{3,2,1,0:T(4,128)} %param.6), channel_id=1, source_target_pairs={{0,1},{1,2},{2,3},{3,4},{4,5},{5,6},{6,7},{7,0},{8,9},{9,10},{10,1... | collective-permute-start | bytes 245768 | tf_op jit(solution)/shard_map/ppermute | solution.py:239
  1.1 12.5 %collective-permute-start.1 = (f32[2,20,4,128]{3,2,1,0:T(4,128)}, f32[2,20,4,128]{3,2,1,0:T(4,128)S(1)}, u32[]{:S(2)}, u32[]{:S(2)}) collective-permute-start(f32[2,20,4,128]{3,2,1,0:T(4,128)} %param.6), channel_id=1, source_target_pairs={{0,2},{1,3},{2,4},{3,5},{4,6},{5,7},{6,0},{7,1},{8,10},{9,11},{10,... | collective-permute-start | bytes 245768 | tf_op jit(solution)/shard_map/ppermute | solution.py:239
  3.8 11.6 %collective-permute-start.2 = (f32[2,20,4,128]{3,2,1,0:T(4,128)}, f32[2,20,4,128]{3,2,1,0:T(4,128)S(1)}, u32[]{:S(2)}, u32[]{:S(2)}) collective-permute-start(f32[2,20,4,128]{3,2,1,0:T(4,128)} %param.6), channel_id=1, source_target_pairs={{0,3},{1,4},{2,5},{3,6},{4,7},{5,0},{6,1},{7,2},{8,11},{9,12},{10,... | collective-permute-start | bytes 245768 | tf_op jit(solution)/shard_map/ppermute | solution.py:239
  6.3 9.3 %collective-permute-start.3 = (f32[2,20,4,128]{3,2,1,0:T(4,128)}, f32[2,20,4,128]{3,2,1,0:T(4,128)S(1)}, u32[]{:S(2)}, u32[]{:S(2)}) collective-permute-start(f32[2,20,4,128]{3,2,1,0:T(4,128)} %param.6), channel_id=1, source_target_pairs={{0,4},{1,5},{2,6},{3,7},{4,0},{5,1},{6,2},{7,3},{8,12},{9,13},{10,... | collective-permute-start | bytes 245768 | tf_op jit(solution)/shard_map/ppermute | solution.py:239
  7.5 8.1 %collective-permute-start.4 = (f32[2,20,4,128]{3,2,1,0:T(4,128)}, f32[2,20,4,128]{3,2,1,0:T(4,128)S(1)}, u32[]{:S(2)}, u32[]{:S(2)}) collective-permute-start(f32[2,20,4,128]{3,2,1,0:T(4,128)} %param.6), channel_id=1, source_target_pairs={{0,5},{1,6},{2,7},{3,0},{4,1},{5,2},{6,3},{7,4},{8,13},{9,14},{10,... | collective-permute-start | bytes 245768 | tf_op jit(solution)/shard_map/ppermute | solution.py:239
  12.2 6.7 %collective-permute-start.5 = (f32[2,20,4,128]{3,2,1,0:T(4,128)S(1)}, f32[2,20,4,128]{3,2,1,0:T(4,128)S(1)}, u32[]{:S(2)}, u32[]{:S(2)}) collective-permute-start(f32[2,20,4,128]{3,2,1,0:T(4,128)S(1)} %copy-done), channel_id=1, source_target_pairs={{0,6},{1,7},{2,0},{3,1},{4,2},{5,3},{6,4},{7,5},{8,14},{9,15},{10,... | collective-permute-start | bytes 245768 | tf_op jit(solution)/shard_map/ppermute | solution.py:239
  13.7 5.3 %collective-permute-start.6 = (f32[2,20,4,128]{3,2,1,0:T(4,128)S(1)}, f32[2,20,4,128]{3,2,1,0:T(4,128)S(1)}, u32[]{:S(2)}, u32[]{:S(2)}) collective-permute-start(f32[2,20,4,128]{3,2,1,0:T(4,128)S(1)} %copy-done), channel_id=1, source_target_pairs={{0,7},{1,0},{2,1},{3,2},{4,3},{5,4},{6,5},{7,6},{8,15},{9,8},{10,9... | collective-permute-start | bytes 245768 | tf_op jit(solution)/shard_map/ppermute | solution.py:239
  20.0 0.7 %copy-start.1 = (s32[32,128]{1,0:T(8,128)S(1)}, s32[32,128]{1,0:T(8,128)}, u32[]{:S(2)}) copy-start(s32[32,128]{1,0:T(8,128)} %param.7) | copy-start | bytes 49156
  20.0 0.7 %copy-start.2 = (s32[32,128]{1,0:T(8,128)S(1)}, s32[32,128]{1,0:T(8,128)}, u32[]{:S(2)}) copy-start(s32[32,128]{1,0:T(8,128)} %param.8) | copy-start | bytes 49156
  22.2 9.8 %collective-permute-start.11 = (f32[2,122,2]{2,1,0:T(8,128)S(1)}, f32[2,122,2]{2,1,0:T(8,128)S(1)}, u32[]{:S(2)}, u32[]{:S(2)}) collective-permute-start(f32[2,122,2]{2,1,0:T(8,128)S(1)} %rev.12), channel_id=1, source_target_pairs={{0,0},{8,24},{16,16},{24,8},{1,1},{9,25},{17,17},{25,9},{2,2},{10,... | collective-permute-start | bytes 5864 | tf_op jit(solution)/shard_map/ppermute | solution.py:18
  23.1 10.8 %collective-permute-start.10 = (f32[2,122,2]{2,1,0:T(8,128)S(1)}, f32[2,122,2]{2,1,0:T(8,128)S(1)}, u32[]{:S(2)}, u32[]{:S(2)}) collective-permute-start(f32[2,122,2]{2,1,0:T(8,128)S(1)} %rev.11), channel_id=1, source_target_pairs={{0,16},{8,8},{16,0},{24,24},{1,17},{9,9},{17,1},{25,25},{2,18},{10... | collective-permute-start | bytes 5864 | tf_op jit(solution)/shard_map/ppermute | solution.py:18
  27.6 9.4 %collective-permute-start.9 = (f32[122,2,128]{2,1,0:T(2,128)S(1)}, f32[122,2,128]{2,1,0:T(2,128)S(1)}, u32[]{:S(2)}, u32[]{:S(2)}) collective-permute-start(f32[122,2,128]{2,1,0:T(2,128)S(1)} %rev.10), channel_id=1, source_target_pairs={{0,24},{8,16},{16,8},{24,0},{1,25},{9,17},{17,9},{25,1},{2,26},{10... | collective-permute-start | bytes 374792 | tf_op jit(solution)/shard_map/ppermute | solution.py:18
  29.1 6.1 %collective-permute-start.8 = (f32[2,3904]{1,0:T(2,128)S(1)}, f32[2,3904]{1,0:T(2,128)S(1)}, u32[]{:S(2)}, u32[]{:S(2)}) collective-permute-start(f32[2,3904]{1,0:T(2,128)S(1)} %get-tuple-element.15), channel_id=1, source_target_pairs={{0,8},{8,16},{16,24},{24,0},{1,9},{9,17},{17,25},{25,1},{2,10},{10... | collective-permute-start | bytes 93704 | tf_op jit(solution)/shard_map/ppermute | solution.py:18
  29.2 6.0 %collective-permute-start.7 = (f32[2,3904]{1,0:T(2,128)S(1)}, f32[2,3904]{1,0:T(2,128)S(1)}, u32[]{:S(2)}, u32[]{:S(2)}) collective-permute-start(f32[2,3904]{1,0:T(2,128)S(1)} %get-tuple-element.14), channel_id=1, source_target_pairs={{0,24},{8,0},{16,8},{24,16},{1,25},{9,1},{17,9},{25,17},{2,26},{10... | collective-permute-start | bytes 93704 | tf_op jit(solution)/shard_map/ppermute | solution.py:18
  46.6 1.7 %collective-permute-start.12 = (f32[2,20,4,4,128]{4,3,2,1,0:T(4,128)S(1)}, f32[2,20,4,4,128]{4,3,2,1,0:T(4,128)S(1)}, u32[]{:S(2)}, u32[]{:S(2)}) collective-permute-start(f32[2,20,4,4,128]{4,3,2,1,0:T(4,128)S(1)} %dynamic-slice_bitcast_fusion), channel_id=1, source_target_pairs={{0,1},{1,0},{2,3},{3,2},{4,5},{5,4},{6,7},{7,6},{8,9},{9,8},{10,11... | collective-permute-start | bytes 983048 | tf_op jit(solution)/shard_map/ppermute | solution.py:258
  48.5 5.4 %collective-permute-start.15 = (f32[2,20,4,128]{3,2,1,0:T(4,128)S(1)}, f32[2,20,4,128]{3,2,1,0:T(4,128)S(1)}, u32[]{:S(2)}, u32[]{:S(2)}) collective-permute-start(f32[2,20,4,128]{3,2,1,0:T(4,128)S(1)} %get-tuple-element.10), channel_id=1, source_target_pairs={{0,6},{1,7},{2,0},{3,1},{4,2},{5,3},{6,4},{7,5},{8,14},{9,15},{10,... | collective-permute-start | bytes 245768 | tf_op jit(solution)/shard_map/ppermute | solution.py:263
  51.0 8.0 %collective-permute-start.14 = (f32[2,20,4,128]{3,2,1,0:T(4,128)S(1)}, f32[2,20,4,128]{3,2,1,0:T(4,128)S(1)}, u32[]{:S(2)}, u32[]{:S(2)}) collective-permute-start(f32[2,20,4,128]{3,2,1,0:T(4,128)S(1)} %get-tuple-element.11), channel_id=1, source_target_pairs={{0,4},{1,5},{2,6},{3,7},{4,0},{5,1},{6,2},{7,3},{8,12},{9,13},{10,... | collective-permute-start | bytes 245768 | tf_op jit(solution)/shard_map/ppermute | solution.py:263
  51.0 8.0 %collective-permute-start.13 = (f32[2,20,4,128]{3,2,1,0:T(4,128)S(1)}, f32[2,20,4,128]{3,2,1,0:T(4,128)S(1)}, u32[]{:S(2)}, u32[]{:S(2)}) collective-permute-start(f32[2,20,4,128]{3,2,1,0:T(4,128)S(1)} %get-tuple-element.9), channel_id=1, source_target_pairs={{0,2},{1,3},{2,4},{3,5},{4,6},{5,7},{6,0},{7,1},{8,10},{9,11},{10,... | collective-permute-start | bytes 245768 | tf_op jit(solution)/shard_map/ppermute | solution.py:263

commit v18 on v13

--- a/solution.py
+++ b/solution.py
@@ -118,7 +118,7 @@
             a_ref[c, k] = w * ve_ref[c, k]
         return carry
 
-    lax.fori_loop(0, levels, setup, 0, unroll=4)
+    lax.fori_loop(0, levels, setup, 0, unroll=True)
 
     def operate(x_ref, c, k, diffs=None):
         x = x_ref[c, k]
@@ -184,7 +184,7 @@
         grad_ref[1, k] = gnm_ref[k] * g_north
         return carry
 
-    lax.fori_loop(0, levels, gradient, 0, unroll=4)
+    lax.fori_loop(0, levels, gradient, 0, unroll=True)
 
 
 def on_device(tracers, diffusivity, level_count, shelf_mask, cotangent):

time: 53 us -> 52.4 us (0.989)
  Pallas kernels: 9.11 us -> 8.52 us
    pallas_call x1, Pallas kernels: 9.11 us -> 8.52 us  [on_device(): pl.pallas_call(diffusion_kernel, out_shape=(field, field, jax.ShapeDtypeS...]
where the time goes in v18:
time: 52.4 us; the launch traced here: 51.9 us
  starting transfers between devices  20.2 us (39%)
  waiting for transfers between devices  11.8 us (23%)
  Pallas kernels  8.52 us (16%)
  local copies, waits for them, and re-layouts  5.59 us (11%)
  matrix products  2.96 us (6%)
  other arithmetic  1.87 us (4%)
  between operations  0.97 us (2%)
    ppermute x5, starting transfers between devices, shifted(): return lax.ppermute(x, 'space', perm)  8.58 us
    pallas_call x1, Pallas kernels, on_device(): pl.pallas_call(diffusion_kernel, out_shape=(field, field, jax.ShapeDtypeS...  8.52 us
    ppermute x3, starting transfers between devices, gathered_over_scen(): lax.ppermute(block, 'scen', [(q, (q // 2 + step) % chips * 2 + q % 2) for...  7.01 us
    ppermute x3, waiting for transfers between devices, summed_over_scen(): lax.ppermute(send, 'scen', [(q, (q // 2 + step) % chips * 2 + q % 2) for...  5.59 us
    ppermute x3, starting transfers between devices, summed_over_scen(): lax.ppermute(send, 'scen', [(q, (q // 2 + step) % chips * 2 + q % 2) for...  4.5 us
    dot_general x3, matrix products, contract(): lax.dot_general(a, b, (dims, ((), ())), precision=lax.Precision.HIGHEST,...  2.96 us
    unnamed x9, local copies, waits for them, and re-layouts  2.59 us
    ppermute x3, waiting for transfers between devices, gathered_over_scen(): lax.ppermute(block, 'scen', [(q, (q // 2 + step) % chips * 2 + q % 2) for...  2.12 us
  transfers between devices with their start and end apart: 13, of which 9 were waited for; matrix products, arithmetic and copies ran while one was open for 11% of the time, Pallas kernels for 0%

profile of v18, /device:TPU:0, one launch (start us, length us, event | category | flops | bytes accessed | tf_op | source)
XLA Modules:
  0.0 51.9 jit_solution(9991357269029183740)
XLA Ops:
  0.6 0.0 copy-start
  0.6 3.1 %collective-permute-start = (f32[2,20,4,128]{3,2,1,0:T(4,128)}, f32[2,20,4,128]{3,2,1,0:T(4,128)S(1)}, u32[]{:S(2)}, u32[]{:S(2)}) collective-permute-start(f32[2,20,4,128]{3,2,1,0:T(4,128)} %param.6), channel_id=1, source_target_pairs={{0,2},{1,3},{2,4},{3,5},{4,6},{5,7},{6,0},{7,1},{8,10},{9,11},{10,... | collective-permute-start | bytes 245768 | tf_op jit(solution)/shard_map/ppermute | solution.py:245
  3.7 2.6 %collective-permute-start.1 = (f32[2,20,4,128]{3,2,1,0:T(4,128)}, f32[2,20,4,128]{3,2,1,0:T(4,128)S(1)}, u32[]{:S(2)}, u32[]{:S(2)}) collective-permute-start(f32[2,20,4,128]{3,2,1,0:T(4,128)} %param.6), channel_id=1, source_target_pairs={{0,4},{1,5},{2,6},{3,7},{4,0},{5,1},{6,2},{7,3},{8,12},{9,13},{10,... | collective-permute-start | bytes 245768 | tf_op jit(solution)/shard_map/ppermute | solution.py:245
  6.3 1.3 %collective-permute-start.2 = (f32[2,20,4,128]{3,2,1,0:T(4,128)}, f32[2,20,4,128]{3,2,1,0:T(4,128)S(1)}, u32[]{:S(2)}, u32[]{:S(2)}) collective-permute-start(f32[2,20,4,128]{3,2,1,0:T(4,128)} %param.6), channel_id=1, source_target_pairs={{0,6},{1,7},{2,0},{3,1},{4,2},{5,3},{6,4},{7,5},{8,14},{9,15},{10,... | collective-permute-start | bytes 245768 | tf_op jit(solution)/shard_map/ppermute | solution.py:245
  7.7 1.1 %constant_dynamic-update-slice_fusion.2 = f32[122,32,128]{2,1,0:T(8,128)S(1)} fusion(f32[40,32,128]{2,1,0:T(8,128)} %bitcast.54), kind=kLoop, calls=%fused_computation.24 | loop fusion | bytes 1310720
  8.9 1.1 %constant_dynamic-update-slice_fusion.1 = f32[122,32,128]{2,1,0:T(8,128)S(1)} fusion(f32[122,32,128]{2,1,0:T(8,128)S(1)} %constant_dynamic-update-slice_fusion.2, f32[40,32,128]{2,1,0:T(8,128)} %bitcast.55), kind=kLoop, calls=%fused_computation.23 | loop fusion | bytes 1310720
  10.0 0.1 pad.4.clone
  10.1 0.0 collective-permute-done
  10.1 1.9 %collective-permute-done.1 = f32[2,20,4,128]{3,2,1,0:T(4,128)S(1)} collective-permute-done((f32[2,20,4,128]{3,2,1,0:T(4,128)}, f32[2,20,4,128]{3,2,1,0:T(4,128)S(1)}, u32[]{:S(2)}, u32[]{:S(2)}) %collective-permute-start.1) | collective-permute-done | bytes 81952 | tf_op jit(solution)/shard_map/ppermute | solution.py:245
  12.0 0.2 collective-permute-done.2
  12.2 0.0 copy-done
  12.2 0.1 fusion.29
  12.3 0.1 collective-permute-start.3
  12.4 0.1 and_or_fusion
  12.5 1.5 %collective-permute-done.3 = f32[4,2,20,4,128]{4,3,2,1,0:T(4,128)S(1)} collective-permute-done((f32[4,2,20,4,128]{4,3,2,1,0:T(4,128)S(1)}, f32[4,2,20,4,128]{4,3,2,1,0:T(4,128)S(1)}, u32[]{:S(2)}, u32[]{:S(2)}) %collective-permute-start.3) | collective-permute-done | bytes 327712 | tf_op jit(solution)/shard_map/ppermute | solution.py:248
  14.0 0.1 maximum_select_fusion
  14.2 0.9 %gather_fusion = f32[4,2,2,20,4,128]{5,4,3,2,1,0:T(4,128)S(1)} fusion(f32[4,2,2,20,4,128]{5,4,3,2,0,1:T(4,128)S(1)} %maximum_select_fusion, s32[1024]{0:T(1024)S(1)} %pad_clamp_fusion), kind=kCustom, calls=%fused_computation | custom fusion | bytes 1310736 | tf_op jit(solution)/shard_map/jit(_take)/gather | solution.py:251
  15.1 0.0 copy-start.1
  15.1 0.0 copy-start.2
  15.2 0.2 select_bitcast_fusion
  15.4 0.2 copy.24
  15.6 0.3 copy-done.1
  15.9 0.0 copy-done.2
  15.9 1.0 %fusion.9 = f32[4,3904]{1,0:T(4,128)S(1)} fusion(f32[3904,128]{1,0:T(8,128)S(1)} %bitcast.51, pred[128]{0:T(512)(128)(4,1)S(1)} %get-tuple-element.20, pred[128]{0:T(512)(128)(4,1)S(1)} %get-tuple-element.21, pred[128]{0:T(512)(128)(4,1)S(1)} %get-tuple-element.22, pred[128]{0:T(512)(128)(4,1)S(1)} %get-tuple-element.23, ...), kind=kOutput, calls=%fused_computation.34 | convolution fusion | flops 23989760 | bytes 2061840 | tf_op jit(solution)/shard_map/dot_general | solution.py:31
  16.9 0.1 reshape.79
  17.0 0.1 fusion.30
  17.2 0.2 rev.11
  17.4 3.4 %collective-permute-start.7 = (f32[2,122,2]{2,1,0:T(8,128)S(1)}, f32[2,122,2]{2,1,0:T(8,128)S(1)}, u32[]{:S(2)}, u32[]{:S(2)}) collective-permute-start(f32[2,122,2]{2,1,0:T(8,128)S(1)} %rev.11), channel_id=1, source_target_pairs={{0,16},{8,8},{16,0},{24,24},{1,17},{9,9},{17,1},{25,25},{2,18},{10... | collective-permute-start | bytes 5864 | tf_op jit(solution)/shard_map/ppermute | solution.py:18
  20.8 0.2 rev.12
  21.0 0.7 %collective-permute-start.8 = (f32[2,122,2]{2,1,0:T(8,128)S(1)}, f32[2,122,2]{2,1,0:T(8,128)S(1)}, u32[]{:S(2)}, u32[]{:S(2)}) collective-permute-start(f32[2,122,2]{2,1,0:T(8,128)S(1)} %rev.12), channel_id=1, source_target_pairs={{0,0},{8,24},{16,16},{24,8},{1,1},{9,25},{17,17},{25,9},{2,2},{10,... | collective-permute-start | bytes 5864 | tf_op jit(solution)/shard_map/ppermute | solution.py:18
  21.7 0.1 slice.29
  21.8 1.5 %collective-permute-start.4 = (f32[2,3904]{1,0:T(2,128)S(1)}, f32[2,3904]{1,0:T(2,128)S(1)}, u32[]{:S(2)}, u32[]{:S(2)}) collective-permute-start(f32[2,3904]{1,0:T(2,128)S(1)} %get-tuple-element.16), channel_id=1, source_target_pairs={{0,24},{8,0},{16,8},{24,16},{1,25},{9,1},{17,9},{25,17},{2,26},{10... | collective-permute-start | bytes 93704 | tf_op jit(solution)/shard_map/ppermute | solution.py:18
  23.3 0.6 %collective-permute-start.5 = (f32[2,3904]{1,0:T(2,128)S(1)}, f32[2,3904]{1,0:T(2,128)S(1)}, u32[]{:S(2)}, u32[]{:S(2)}) collective-permute-start(f32[2,3904]{1,0:T(2,128)S(1)} %get-tuple-element.17), channel_id=1, source_target_pairs={{0,8},{8,16},{16,24},{24,0},{1,9},{9,17},{17,25},{25,1},{2,10},{10... | collective-permute-start | bytes 93704 | tf_op jit(solution)/shard_map/ppermute | solution.py:18
  23.8 0.5 rev.10
  24.3 2.4 %collective-permute-start.6 = (f32[122,2,128]{2,1,0:T(2,128)S(1)}, f32[122,2,128]{2,1,0:T(2,128)S(1)}, u32[]{:S(2)}, u32[]{:S(2)}) collective-permute-start(f32[122,2,128]{2,1,0:T(2,128)S(1)} %rev.10), channel_id=1, source_target_pairs={{0,24},{8,16},{16,8},{24,0},{1,25},{9,17},{17,9},{25,1},{2,26},{10... | collective-permute-start | bytes 374792 | tf_op jit(solution)/shard_map/ppermute | solution.py:18
  26.7 0.0 collective-permute-done.7
  26.7 0.0 collective-permute-done.8
  26.8 0.2 reshape.91
  26.9 0.1 copy.30
  27.1 0.1 dot_general.16
  27.2 0.2 fusion
  27.4 0.1 copy.27
  27.5 0.0 collective-permute-done.4
  27.5 0.8 %collective-permute-done.5 = f32[2,3904]{1,0:T(2,128)S(1)} collective-permute-done((f32[2,3904]{1,0:T(2,128)S(1)}, f32[2,3904]{1,0:T(2,128)S(1)}, u32[]{:S(2)}, u32[]{:S(2)}) %collective-permute-start.5) | collective-permute-done | bytes 31264 | tf_op jit(solution)/shard_map/ppermute | solution.py:18
  28.3 1.7 %fusion.4 = f32[3904,128]{1,0:T(8,128)S(1)} fusion(pred[128,4]{0,1:T(4,128)(4,1)S(1)} %and_or_fusion, f32[2,3904]{1,0:T(2,128)S(1)} %collective-permute-done.5, f32[2,3904]{1,0:T(2,128)S(1)} %collective-permute-done.4), kind=kOutput, calls=%fused_computation.16 | convolution fusion | flops 24001792 | bytes 2061824 | tf_op jit(solution)/shard_map/dot_general | solution.py:31
  30.1 0.1 collective-permute-done.6
  30.2 0.5 maximum_maximum_fusion.x_ref
  30.7 8.5 %shard_map.76 = (f32[2,20,32,128]{3,2,1,0:T(8,128)}, f32[2,20,32,128]{3,2,1,0:T(8,128)}, f32[2,20,32,128]{3,2,1,0:T(8,128)S(1)}) custom-call(f32[122,40,256]{2,1,0:T(8,128)S(1)} %maximum_maximum_fusion.x_ref), custom_call_target="tpu_custom_call" | custom-call | tf_op jit(solution)/shard_map/pallas_call | solution.py:210
  39.2 0.1 dynamic-slice_bitcast_fusion
  39.3 0.1 collective-permute-start.9
  39.4 1.5 %collective-permute-done.9 = f32[2,20,4,4,128]{4,3,2,1,0:T(4,128)S(1)} collective-permute-done((f32[2,20,4,4,128]{4,3,2,1,0:T(4,128)S(1)}, f32[2,20,4,4,128]{4,3,2,1,0:T(4,128)S(1)}, u32[]{:S(2)}, u32[]{:S(2)}) %collective-permute-start.9) | collective-permute-done | bytes 327712 | tf_op jit(solution)/shard_map/ppermute | solution.py:268
  41.0 0.1 bitcast_add_fusion
  41.1 0.1 dynamic-slice_bitcast_fusion.3
  41.1 2.1 %collective-permute-start.10 = (f32[2,20,4,128]{3,2,1,0:T(4,128)S(1)}, f32[2,20,4,128]{3,2,1,0:T(4,128)S(1)}, u32[]{:S(2)}, u32[]{:S(2)}) collective-permute-start(f32[2,20,4,128]{3,2,1,0:T(4,128)S(1)} %get-tuple-element.9), channel_id=1, source_target_pairs={{0,2},{1,3},{2,4},{3,5},{4,6},{5,7},{6,0},{7,1},{8,10},{9,11},{10,... | collective-permute-start | bytes 245768 | tf_op jit(solution)/shard_map/ppermute | solution.py:273
  43.2 1.8 %collective-permute-start.11 = (f32[2,20,4,128]{3,2,1,0:T(4,128)S(1)}, f32[2,20,4,128]{3,2,1,0:T(4,128)S(1)}, u32[]{:S(2)}, u32[]{:S(2)}) collective-permute-start(f32[2,20,4,128]{3,2,1,0:T(4,128)S(1)} %get-tuple-element.11), channel_id=1, source_target_pairs={{0,4},{1,5},{2,6},{3,7},{4,0},{5,1},{6,2},{7,3},{8,12},{9,13},{10,... | collective-permute-start | bytes 245768 | tf_op jit(solution)/shard_map/ppermute | solution.py:273
  45.0 0.6 %collective-permute-start.12 = (f32[2,20,4,128]{3,2,1,0:T(4,128)S(1)}, f32[2,20,4,128]{3,2,1,0:T(4,128)S(1)}, u32[]{:S(2)}, u32[]{:S(2)}) collective-permute-start(f32[2,20,4,128]{3,2,1,0:T(4,128)S(1)} %get-tuple-element.10), channel_id=1, source_target_pairs={{0,6},{1,7},{2,0},{3,1},{4,2},{5,3},{6,4},{7,5},{8,14},{9,15},{10,... | collective-permute-start | bytes 245768 | tf_op jit(solution)/shard_map/ppermute | solution.py:273
  45.6 2.7 %collective-permute-done.10 = f32[2,20,4,128]{3,2,1,0:T(4,128)S(1)} collective-permute-done((f32[2,20,4,128]{3,2,1,0:T(4,128)S(1)}, f32[2,20,4,128]{3,2,1,0:T(4,128)S(1)}, u32[]{:S(2)}, u32[]{:S(2)}) %collective-permute-start.10) | collective-permute-done | bytes 81952 | tf_op jit(solution)/shard_map/ppermute | solution.py:273
  48.4 2.7 %collective-permute-done.11 = f32[2,20,4,128]{3,2,1,0:T(4,128)S(1)} collective-permute-done((f32[2,20,4,128]{3,2,1,0:T(4,128)S(1)}, f32[2,20,4,128]{3,2,1,0:T(4,128)S(1)}, u32[]{:S(2)}, u32[]{:S(2)}) %collective-permute-start.11) | collective-permute-done | bytes 81952 | tf_op jit(solution)/shard_map/ppermute | solution.py:273
  51.1 0.1 collective-permute-done.12
  51.2 0.7 %fusion.3 = f32[2,20,4,128]{3,2,1,0:T(4,128)} fusion(f32[2,20,4,128]{3,2,1,0:T(4,128)S(1)} %collective-permute-done.12, f32[2,20,4,128]{3,2,1,0:T(4,128)S(1)} %collective-permute-done.11, f32[2,20,4,128]{3,2,1,0:T(4,128)S(1)} %collective-permute-done.10, f32[2,20,4,4,128]{4,3,2,1,0:T(4,128)S(1)} %bitcast_add_fusion, s32[]{:T(128)S(6)} %select_n.107), kind=kLoop, calls=%fused_computation.12 | loop fusion | flops 61440 | bytes 409604 | tf_op jit(solution)/shard_map/add | solution.py:273
  (13 shorter events, 0.2 us)
Async XLA Ops:
  0.6 11.6 %copy-start = (f32[2,20,4,128]{3,2,1,0:T(4,128)S(1)}, f32[2,20,4,128]{3,2,1,0:T(4,128)}, u32[]{:S(2)}) copy-start(f32[2,20,4,128]{3,2,1,0:T(4,128)} %param.6) | copy-start | bytes 245764
  0.6 9.5 %collective-permute-start = (f32[2,20,4,128]{3,2,1,0:T(4,128)}, f32[2,20,4,128]{3,2,1,0:T(4,128)S(1)}, u32[]{:S(2)}, u32[]{:S(2)}) collective-permute-start(f32[2,20,4,128]{3,2,1,0:T(4,128)} %param.6), channel_id=1, source_target_pairs={{0,2},{1,3},{2,4},{3,5},{4,6},{5,7},{6,0},{7,1},{8,10},{9,11},{10,... | collective-permute-start | bytes 245768 | tf_op jit(solution)/shard_map/ppermute | solution.py:245
  3.7 8.3 %collective-permute-start.1 = (f32[2,20,4,128]{3,2,1,0:T(4,128)}, f32[2,20,4,128]{3,2,1,0:T(4,128)S(1)}, u32[]{:S(2)}, u32[]{:S(2)}) collective-permute-start(f32[2,20,4,128]{3,2,1,0:T(4,128)} %param.6), channel_id=1, source_target_pairs={{0,4},{1,5},{2,6},{3,7},{4,0},{5,1},{6,2},{7,3},{8,12},{9,13},{10,... | collective-permute-start | bytes 245768 | tf_op jit(solution)/shard_map/ppermute | solution.py:245
  6.3 5.9 %collective-permute-start.2 = (f32[2,20,4,128]{3,2,1,0:T(4,128)}, f32[2,20,4,128]{3,2,1,0:T(4,128)S(1)}, u32[]{:S(2)}, u32[]{:S(2)}) collective-permute-start(f32[2,20,4,128]{3,2,1,0:T(4,128)} %param.6), channel_id=1, source_target_pairs={{0,6},{1,7},{2,0},{3,1},{4,2},{5,3},{6,4},{7,5},{8,14},{9,15},{10,... | collective-permute-start | bytes 245768 | tf_op jit(solution)/shard_map/ppermute | solution.py:245
  12.3 1.7 %collective-permute-start.3 = (f32[4,2,20,4,128]{4,3,2,1,0:T(4,128)S(1)}, f32[4,2,20,4,128]{4,3,2,1,0:T(4,128)S(1)}, u32[]{:S(2)}, u32[]{:S(2)}) collective-permute-start(f32[4,2,20,4,128]{4,3,2,1,0:T(4,128)S(1)} %get-tuple-element.13), channel_id=1, source_target_pairs={{0,1},{1,0},{2,3},{3,2},{4,5},{5,4},{6,7},{7,6},{8,9},{9,8},{10,11... | collective-permute-start | bytes 983048 | tf_op jit(solution)/shard_map/ppermute | solution.py:248
  15.1 0.7 %copy-start.1 = (s32[32,128]{1,0:T(8,128)S(1)}, s32[32,128]{1,0:T(8,128)}, u32[]{:S(2)}) copy-start(s32[32,128]{1,0:T(8,128)} %param.7) | copy-start | bytes 49156
  15.1 0.7 %copy-start.2 = (s32[32,128]{1,0:T(8,128)S(1)}, s32[32,128]{1,0:T(8,128)}, u32[]{:S(2)}) copy-start(s32[32,128]{1,0:T(8,128)} %param.8) | copy-start | bytes 49156
  17.4 9.4 %collective-permute-start.7 = (f32[2,122,2]{2,1,0:T(8,128)S(1)}, f32[2,122,2]{2,1,0:T(8,128)S(1)}, u32[]{:S(2)}, u32[]{:S(2)}) collective-permute-start(f32[2,122,2]{2,1,0:T(8,128)S(1)} %rev.11), channel_id=1, source_target_pairs={{0,16},{8,8},{16,0},{24,24},{1,17},{9,9},{17,1},{25,25},{2,18},{10... | collective-permute-start | bytes 5864 | tf_op jit(solution)/shard_map/ppermute | solution.py:18
  21.0 5.8 %collective-permute-start.8 = (f32[2,122,2]{2,1,0:T(8,128)S(1)}, f32[2,122,2]{2,1,0:T(8,128)S(1)}, u32[]{:S(2)}, u32[]{:S(2)}) collective-permute-start(f32[2,122,2]{2,1,0:T(8,128)S(1)} %rev.12), channel_id=1, source_target_pairs={{0,0},{8,24},{16,16},{24,8},{1,1},{9,25},{17,17},{25,9},{2,2},{10,... | collective-permute-start | bytes 5864 | tf_op jit(solution)/shard_map/ppermute | solution.py:18
  21.8 5.7 %collective-permute-start.4 = (f32[2,3904]{1,0:T(2,128)S(1)}, f32[2,3904]{1,0:T(2,128)S(1)}, u32[]{:S(2)}, u32[]{:S(2)}) collective-permute-start(f32[2,3904]{1,0:T(2,128)S(1)} %get-tuple-element.16), channel_id=1, source_target_pairs={{0,24},{8,0},{16,8},{24,16},{1,25},{9,1},{17,9},{25,17},{2,26},{10... | collective-permute-start | bytes 93704 | tf_op jit(solution)/shard_map/ppermute | solution.py:18
  23.3 5.1 %collective-permute-start.5 = (f32[2,3904]{1,0:T(2,128)S(1)}, f32[2,3904]{1,0:T(2,128)S(1)}, u32[]{:S(2)}, u32[]{:S(2)}) collective-permute-start(f32[2,3904]{1,0:T(2,128)S(1)} %get-tuple-element.17), channel_id=1, source_target_pairs={{0,8},{8,16},{16,24},{24,0},{1,9},{9,17},{17,25},{25,1},{2,10},{10... | collective-permute-start | bytes 93704 | tf_op jit(solution)/shard_map/ppermute | solution.py:18
  24.3 5.9 %collective-permute-start.6 = (f32[122,2,128]{2,1,0:T(2,128)S(1)}, f32[122,2,128]{2,1,0:T(2,128)S(1)}, u32[]{:S(2)}, u32[]{:S(2)}) collective-permute-start(f32[122,2,128]{2,1,0:T(2,128)S(1)} %rev.10), channel_id=1, source_target_pairs={{0,24},{8,16},{16,8},{24,0},{1,25},{9,17},{17,9},{25,1},{2,26},{10... | collective-permute-start | bytes 374792 | tf_op jit(solution)/shard_map/ppermute | solution.py:18
  39.3 1.7 %collective-permute-start.9 = (f32[2,20,4,4,128]{4,3,2,1,0:T(4,128)S(1)}, f32[2,20,4,4,128]{4,3,2,1,0:T(4,128)S(1)}, u32[]{:S(2)}, u32[]{:S(2)}) collective-permute-start(f32[2,20,4,4,128]{4,3,2,1,0:T(4,128)S(1)} %dynamic-slice_bitcast_fusion), channel_id=1, source_target_pairs={{0,1},{1,0},{2,3},{3,2},{4,5},{5,4},{6,7},{7,6},{8,9},{9,8},{10,11... | collective-permute-start | bytes 983048 | tf_op jit(solution)/shard_map/ppermute | solution.py:268
  41.1 7.2 %collective-permute-start.10 = (f32[2,20,4,128]{3,2,1,0:T(4,128)S(1)}, f32[2,20,4,128]{3,2,1,0:T(4,128)S(1)}, u32[]{:S(2)}, u32[]{:S(2)}) collective-permute-start(f32[2,20,4,128]{3,2,1,0:T(4,128)S(1)} %get-tuple-element.9), channel_id=1, source_target_pairs={{0,2},{1,3},{2,4},{3,5},{4,6},{5,7},{6,0},{7,1},{8,10},{9,11},{10,... | collective-permute-start | bytes 245768 | tf_op jit(solution)/shard_map/ppermute | solution.py:273
  43.2 7.9 %collective-permute-start.11 = (f32[2,20,4,128]{3,2,1,0:T(4,128)S(1)}, f32[2,20,4,128]{3,2,1,0:T(4,128)S(1)}, u32[]{:S(2)}, u32[]{:S(2)}) collective-permute-start(f32[2,20,4,128]{3,2,1,0:T(4,128)S(1)} %get-tuple-element.11), channel_id=1, source_target_pairs={{0,4},{1,5},{2,6},{3,7},{4,0},{5,1},{6,2},{7,3},{8,12},{9,13},{10,... | collective-permute-start | bytes 245768 | tf_op jit(solution)/shard_map/ppermute | solution.py:273
  45.0 6.2 %collective-permute-start.12 = (f32[2,20,4,128]{3,2,1,0:T(4,128)S(1)}, f32[2,20,4,128]{3,2,1,0:T(4,128)S(1)}, u32[]{:S(2)}, u32[]{:S(2)}) collective-permute-start(f32[2,20,4,128]{3,2,1,0:T(4,128)S(1)} %get-tuple-element.10), channel_id=1, source_target_pairs={{0,6},{1,7},{2,0},{3,1},{4,2},{5,3},{6,4},{7,5},{8,14},{9,15},{10,... | collective-permute-start | bytes 245768 | tf_op jit(solution)/shard_map/ppermute | solution.py:273

commit v19 on v18

--- a/solution.py
+++ b/solution.py
@@ -30,6 +30,16 @@
 def contract(a, b, dims):
     return lax.dot_general(
         a, b, (dims, ((), ())), precision=lax.Precision.HIGHEST, preferred_element_type=jnp.float32
+    )
+
+
+def placed(values, place):
+    hi = lax.reduce_precision(values, exponent_bits=8, mantissa_bits=7)
+    rest = values - hi
+    mid = lax.reduce_precision(rest, exponent_bits=8, mantissa_bits=7)
+    parts = jnp.concatenate([hi, mid, rest - mid])
+    return lax.dot_general(
+        parts, jnp.concatenate([place] * 3), (((0,), (0,)), ((), ())), preferred_element_type=jnp.float32
     )
 
 
@@ -47,9 +57,9 @@
     ghost_east = shifted(top_edges[1::-1], [(q, (n - 2 - q) % n) for q in range(n)])
     ghost_west = shifted(top_edges[3:1:-1], [(q, (n - q) % n) for q in range(n)])
     place = picker(spare, [0, 1, spare - 2, spare - 1]).T
-    side = contract(jnp.concatenate([east, west]), place, ((0,), (0,))).reshape(count, ny, spare)
+    side = placed(jnp.concatenate([east, west]), place).reshape(count, ny, spare)
     ghost_halo = jnp.concatenate([ghost_east, ghost_west]).reshape(4, count * 2)
-    ghost_side = contract(ghost_halo, place, ((0,), (0,))).reshape(count, 2, spare)
+    ghost_side = placed(ghost_halo, place).reshape(count, 2, spare)
     top = jnp.concatenate([fields, side], axis=-1)
     folded = jnp.concatenate([ghost, ghost_side], axis=-1)
     pad = jnp.zeros((count, rows - ny - 2, lanes), fields.dtype)

time: 52.4 us -> 52.4 us (level)
  waiting for transfers between devices: 11.8 us -> 13.2 us
  matrix products: 2.96 us -> 1.71 us
    dot_general x3 -> x1, matrix products: 2.96 us -> 1.02 us  [contract(): lax.dot_general(a, b, (dims, ((), ())), precision=lax.Precision.HIGHEST,...]
    ppermute x5, waiting for transfers between devices: 0.99 us -> 2.41 us  [shifted(): return lax.ppermute(x, 'space', perm)]
    dot_general x0 -> x2, matrix products: none -> 0.69 us  [placed(): lax.dot_general(parts, jnp.concatenate([place] * 3), (((0,), (0,)), ((),...]
  transfers between devices with their start and end apart: 13 -> 13, of which waited for: 9 -> 9; matrix products, arithmetic and copies ran while one was open for 11% -> 8% of each run, Pallas kernels for 0% -> 0%
where the time goes in v19:
time: 52.4 us; the launch traced here: 51.9 us
  starting transfers between devices  20.2 us (39%)
  waiting for transfers between devices  13.2 us (25%)
  Pallas kernels  8.52 us (16%)
  local copies, waits for them, and re-layouts  5.35 us (10%)
  other arithmetic  1.94 us (4%)
  matrix products  1.71 us (3%)
  between operations  0.96 us (2%)
    ppermute x5, starting transfers between devices, shifted(): return lax.ppermute(x, 'space', perm)  8.58 us
    pallas_call x1, Pallas kernels, on_device(): pl.pallas_call(diffusion_kernel, out_shape=(field, field, jax.ShapeDtypeS...  8.52 us
    ppermute x3, starting transfers between devices, gathered_over_scen(): lax.ppermute(block, 'scen', [(q, (q // 2 + step) % chips * 2 + q % 2) for...  7.01 us
    ppermute x3, waiting for transfers between devices, summed_over_scen(): lax.ppermute(send, 'scen', [(q, (q // 2 + step) % chips * 2 + q % 2) for...  5.59 us
    ppermute x3, starting transfers between devices, summed_over_scen(): lax.ppermute(send, 'scen', [(q, (q // 2 + step) % chips * 2 + q % 2) for...  4.5 us
    unnamed x9, local copies, waits for them, and re-layouts  2.59 us
    ppermute x5, waiting for transfers between devices, shifted(): return lax.ppermute(x, 'space', perm)  2.41 us
    ppermute x3, waiting for transfers between devices, gathered_over_scen(): lax.ppermute(block, 'scen', [(q, (q // 2 + step) % chips * 2 + q % 2) for...  2.12 us
  transfers between devices with their start and end apart: 13, of which 9 were waited for; matrix products, arithmetic and copies ran while one was open for 8% of the time, Pallas kernels for 0%

profile of v19, /device:TPU:0, one launch (start us, length us, event | category | flops | bytes accessed | tf_op | source)
XLA Modules:
  0.0 51.9 jit_solution(14732959468726727634)
XLA Ops:
  0.6 0.0 copy-start
  0.6 3.1 %collective-permute-start = (f32[2,20,4,128]{3,2,1,0:T(4,128)}, f32[2,20,4,128]{3,2,1,0:T(4,128)S(1)}, u32[]{:S(2)}, u32[]{:S(2)}) collective-permute-start(f32[2,20,4,128]{3,2,1,0:T(4,128)} %param.6), channel_id=1, source_target_pairs={{0,2},{1,3},{2,4},{3,5},{4,6},{5,7},{6,0},{7,1},{8,10},{9,11},{10,... | collective-permute-start | bytes 245768 | tf_op jit(solution)/shard_map/ppermute | solution.py:255
  3.7 2.6 %collective-permute-start.1 = (f32[2,20,4,128]{3,2,1,0:T(4,128)}, f32[2,20,4,128]{3,2,1,0:T(4,128)S(1)}, u32[]{:S(2)}, u32[]{:S(2)}) collective-permute-start(f32[2,20,4,128]{3,2,1,0:T(4,128)} %param.6), channel_id=1, source_target_pairs={{0,4},{1,5},{2,6},{3,7},{4,0},{5,1},{6,2},{7,3},{8,12},{9,13},{10,... | collective-permute-start | bytes 245768 | tf_op jit(solution)/shard_map/ppermute | solution.py:255
  6.3 1.3 %collective-permute-start.2 = (f32[2,20,4,128]{3,2,1,0:T(4,128)}, f32[2,20,4,128]{3,2,1,0:T(4,128)S(1)}, u32[]{:S(2)}, u32[]{:S(2)}) collective-permute-start(f32[2,20,4,128]{3,2,1,0:T(4,128)} %param.6), channel_id=1, source_target_pairs={{0,6},{1,7},{2,0},{3,1},{4,2},{5,3},{6,4},{7,5},{8,14},{9,15},{10,... | collective-permute-start | bytes 245768 | tf_op jit(solution)/shard_map/ppermute | solution.py:255
  7.7 1.1 %constant_dynamic-update-slice_fusion.2 = f32[122,32,128]{2,1,0:T(8,128)S(1)} fusion(f32[40,32,128]{2,1,0:T(8,128)} %bitcast.49), kind=kLoop, calls=%fused_computation.34 | loop fusion | bytes 1310720
  8.9 1.1 %constant_dynamic-update-slice_fusion.1 = f32[122,32,128]{2,1,0:T(8,128)S(1)} fusion(f32[122,32,128]{2,1,0:T(8,128)S(1)} %constant_dynamic-update-slice_fusion.2, f32[40,32,128]{2,1,0:T(8,128)} %bitcast.50), kind=kLoop, calls=%fused_computation.33 | loop fusion | bytes 1310720
  10.0 0.1 pad.4.clone
  10.1 0.0 collective-permute-done
  10.1 1.9 %collective-permute-done.1 = f32[2,20,4,128]{3,2,1,0:T(4,128)S(1)} collective-permute-done((f32[2,20,4,128]{3,2,1,0:T(4,128)}, f32[2,20,4,128]{3,2,1,0:T(4,128)S(1)}, u32[]{:S(2)}, u32[]{:S(2)}) %collective-permute-start.1) | collective-permute-done | bytes 81952 | tf_op jit(solution)/shard_map/ppermute | solution.py:255
  12.0 0.2 collective-permute-done.2
  12.2 0.0 copy-done
  12.2 0.1 fusion.40
  12.3 0.1 collective-permute-start.3
  12.4 0.1 and_or_fusion
  12.5 1.5 %collective-permute-done.3 = f32[4,2,20,4,128]{4,3,2,1,0:T(4,128)S(1)} collective-permute-done((f32[4,2,20,4,128]{4,3,2,1,0:T(4,128)S(1)}, f32[4,2,20,4,128]{4,3,2,1,0:T(4,128)S(1)}, u32[]{:S(2)}, u32[]{:S(2)}) %collective-permute-start.3) | collective-permute-done | bytes 327712 | tf_op jit(solution)/shard_map/ppermute | solution.py:258
  14.0 0.1 maximum_select_fusion
  14.2 0.9 %gather_fusion = f32[4,2,2,20,4,128]{5,4,3,2,1,0:T(4,128)S(1)} fusion(f32[4,2,2,20,4,128]{5,4,3,2,0,1:T(4,128)S(1)} %maximum_select_fusion, s32[1024]{0:T(1024)S(1)} %pad_clamp_fusion), kind=kCustom, calls=%fused_computation | custom fusion | bytes 1310736 | tf_op jit(solution)/shard_map/jit(_take)/gather | solution.py:261
  15.1 0.0 copy-start.1
  15.1 0.0 copy-start.2
  15.2 0.2 select_bitcast_fusion
  15.4 0.2 copy.29
  15.6 0.3 copy-done.1
  15.9 0.0 copy-done.2
  15.9 1.0 %fusion.16 = f32[4,3904]{1,0:T(4,128)S(1)} fusion(f32[3904,128]{1,0:T(8,128)S(1)} %bitcast.46, pred[128]{0:T(512)(128)(4,1)S(1)} %get-tuple-element.26, pred[128]{0:T(512)(128)(4,1)S(1)} %get-tuple-element.27, pred[128]{0:T(512)(128)(4,1)S(1)} %get-tuple-element.28, pred[128]{0:T(512)(128)(4,1)S(1)} %get-tuple-element.29, ...), kind=kOutput, calls=%fused_computation.44 | convolution fusion | flops 23989760 | bytes 2061840 | tf_op jit(solution)/shard_map/dot_general | solution.py:31
  16.9 0.1 reshape.80
  17.0 0.1 fusion.41
  17.2 0.2 rev.11
  17.4 3.4 %collective-permute-start.7 = (f32[2,122,2]{2,1,0:T(8,128)S(1)}, f32[2,122,2]{2,1,0:T(8,128)S(1)}, u32[]{:S(2)}, u32[]{:S(2)}) collective-permute-start(f32[2,122,2]{2,1,0:T(8,128)S(1)} %rev.11), channel_id=1, source_target_pairs={{0,16},{8,8},{16,0},{24,24},{1,17},{9,9},{17,1},{25,25},{2,18},{10... | collective-permute-start | bytes 5864 | tf_op jit(solution)/shard_map/ppermute | solution.py:18
  20.8 0.2 rev.12
  21.0 0.7 %collective-permute-start.8 = (f32[2,122,2]{2,1,0:T(8,128)S(1)}, f32[2,122,2]{2,1,0:T(8,128)S(1)}, u32[]{:S(2)}, u32[]{:S(2)}) collective-permute-start(f32[2,122,2]{2,1,0:T(8,128)S(1)} %rev.12), channel_id=1, source_target_pairs={{0,0},{8,24},{16,16},{24,8},{1,1},{9,25},{17,17},{25,9},{2,2},{10,... | collective-permute-start | bytes 5864 | tf_op jit(solution)/shard_map/ppermute | solution.py:18
  21.7 0.1 slice.29
  21.8 1.5 %collective-permute-start.4 = (f32[2,3904]{1,0:T(2,128)S(1)}, f32[2,3904]{1,0:T(2,128)S(1)}, u32[]{:S(2)}, u32[]{:S(2)}) collective-permute-start(f32[2,3904]{1,0:T(2,128)S(1)} %get-tuple-element.19), channel_id=1, source_target_pairs={{0,24},{8,0},{16,8},{24,16},{1,25},{9,1},{17,9},{25,17},{2,26},{10... | collective-permute-start | bytes 93704 | tf_op jit(solution)/shard_map/ppermute | solution.py:18
  23.3 0.6 %collective-permute-start.5 = (f32[2,3904]{1,0:T(2,128)S(1)}, f32[2,3904]{1,0:T(2,128)S(1)}, u32[]{:S(2)}, u32[]{:S(2)}) collective-permute-start(f32[2,3904]{1,0:T(2,128)S(1)} %get-tuple-element.20), channel_id=1, source_target_pairs={{0,8},{8,16},{16,24},{24,0},{1,9},{9,17},{17,25},{25,1},{2,10},{10... | collective-permute-start | bytes 93704 | tf_op jit(solution)/shard_map/ppermute | solution.py:18
  23.8 0.5 rev.10
  24.3 2.4 %collective-permute-start.6 = (f32[122,2,128]{2,1,0:T(2,128)S(1)}, f32[122,2,128]{2,1,0:T(2,128)S(1)}, u32[]{:S(2)}, u32[]{:S(2)}) collective-permute-start(f32[122,2,128]{2,1,0:T(2,128)S(1)} %rev.10), channel_id=1, source_target_pairs={{0,24},{8,16},{16,8},{24,0},{1,25},{9,17},{17,9},{25,1},{2,26},{10... | collective-permute-start | bytes 374792 | tf_op jit(solution)/shard_map/ppermute | solution.py:18
  26.7 0.0 collective-permute-done.7
  26.7 0.0 collective-permute-done.8
  26.8 0.2 reshape.92
  26.9 0.2 fusion.10
  27.2 0.1 reshape.82
  27.3 0.0 collective-permute-done.4
  27.3 1.1 %collective-permute-done.5 = f32[2,3904]{1,0:T(2,128)S(1)} collective-permute-done((f32[2,3904]{1,0:T(2,128)S(1)}, f32[2,3904]{1,0:T(2,128)S(1)}, u32[]{:S(2)}, u32[]{:S(2)}) %collective-permute-start.5) | collective-permute-done | bytes 31264 | tf_op jit(solution)/shard_map/ppermute | solution.py:18
  28.3 0.1 fusion.9
  28.4 0.5 fusion
  28.9 1.3 %collective-permute-done.6 = f32[122,2,128]{2,1,0:T(2,128)S(1)} collective-permute-done((f32[122,2,128]{2,1,0:T(2,128)S(1)}, f32[122,2,128]{2,1,0:T(2,128)S(1)}, u32[]{:S(2)}, u32[]{:S(2)}) %collective-permute-start.6) | collective-permute-done | bytes 124960 | tf_op jit(solution)/shard_map/ppermute | solution.py:18
  30.2 0.5 maximum_maximum_fusion.x_ref
  30.7 8.5 %shard_map.76 = (f32[2,20,32,128]{3,2,1,0:T(8,128)}, f32[2,20,32,128]{3,2,1,0:T(8,128)}, f32[2,20,32,128]{3,2,1,0:T(8,128)S(1)}) custom-call(f32[122,40,256]{2,1,0:T(8,128)S(1)} %maximum_maximum_fusion.x_ref), custom_call_target="tpu_custom_call" | custom-call | tf_op jit(solution)/shard_map/pallas_call | solution.py:220
  39.2 0.1 dynamic-slice_bitcast_fusion
  39.3 0.1 collective-permute-start.9
  39.4 1.5 %collective-permute-done.9 = f32[2,20,4,4,128]{4,3,2,1,0:T(4,128)S(1)} collective-permute-done((f32[2,20,4,4,128]{4,3,2,1,0:T(4,128)S(1)}, f32[2,20,4,4,128]{4,3,2,1,0:T(4,128)S(1)}, u32[]{:S(2)}, u32[]{:S(2)}) %collective-permute-start.9) | collective-permute-done | bytes 327712 | tf_op jit(solution)/shard_map/ppermute | solution.py:278
  41.0 0.1 bitcast_add_fusion
  41.1 0.1 dynamic-slice_bitcast_fusion.3
  41.1 2.1 %collective-permute-start.10 = (f32[2,20,4,128]{3,2,1,0:T(4,128)S(1)}, f32[2,20,4,128]{3,2,1,0:T(4,128)S(1)}, u32[]{:S(2)}, u32[]{:S(2)}) collective-permute-start(f32[2,20,4,128]{3,2,1,0:T(4,128)S(1)} %get-tuple-element.9), channel_id=1, source_target_pairs={{0,2},{1,3},{2,4},{3,5},{4,6},{5,7},{6,0},{7,1},{8,10},{9,11},{10,... | collective-permute-start | bytes 245768 | tf_op jit(solution)/shard_map/ppermute | solution.py:283
  43.2 1.8 %collective-permute-start.11 = (f32[2,20,4,128]{3,2,1,0:T(4,128)S(1)}, f32[2,20,4,128]{3,2,1,0:T(4,128)S(1)}, u32[]{:S(2)}, u32[]{:S(2)}) collective-permute-start(f32[2,20,4,128]{3,2,1,0:T(4,128)S(1)} %get-tuple-element.11), channel_id=1, source_target_pairs={{0,4},{1,5},{2,6},{3,7},{4,0},{5,1},{6,2},{7,3},{8,12},{9,13},{10,... | collective-permute-start | bytes 245768 | tf_op jit(solution)/shard_map/ppermute | solution.py:283
  45.0 0.6 %collective-permute-start.12 = (f32[2,20,4,128]{3,2,1,0:T(4,128)S(1)}, f32[2,20,4,128]{3,2,1,0:T(4,128)S(1)}, u32[]{:S(2)}, u32[]{:S(2)}) collective-permute-start(f32[2,20,4,128]{3,2,1,0:T(4,128)S(1)} %get-tuple-element.10), channel_id=1, source_target_pairs={{0,6},{1,7},{2,0},{3,1},{4,2},{5,3},{6,4},{7,5},{8,14},{9,15},{10,... | collective-permute-start | bytes 245768 | tf_op jit(solution)/shard_map/ppermute | solution.py:283
  45.7 2.7 %collective-permute-done.10 = f32[2,20,4,128]{3,2,1,0:T(4,128)S(1)} collective-permute-done((f32[2,20,4,128]{3,2,1,0:T(4,128)S(1)}, f32[2,20,4,128]{3,2,1,0:T(4,128)S(1)}, u32[]{:S(2)}, u32[]{:S(2)}) %collective-permute-start.10) | collective-permute-done | bytes 81952 | tf_op jit(solution)/shard_map/ppermute | solution.py:283
  48.4 2.7 %collective-permute-done.11 = f32[2,20,4,128]{3,2,1,0:T(4,128)S(1)} collective-permute-done((f32[2,20,4,128]{3,2,1,0:T(4,128)S(1)}, f32[2,20,4,128]{3,2,1,0:T(4,128)S(1)}, u32[]{:S(2)}, u32[]{:S(2)}) %collective-permute-start.11) | collective-permute-done | bytes 81952 | tf_op jit(solution)/shard_map/ppermute | solution.py:283
  51.1 0.1 collective-permute-done.12
  51.2 0.7 %fusion.7 = f32[2,20,4,128]{3,2,1,0:T(4,128)} fusion(f32[2,20,4,128]{3,2,1,0:T(4,128)S(1)} %collective-permute-done.12, f32[2,20,4,128]{3,2,1,0:T(4,128)S(1)} %collective-permute-done.11, f32[2,20,4,128]{3,2,1,0:T(4,128)S(1)} %collective-permute-done.10, f32[2,20,4,4,128]{4,3,2,1,0:T(4,128)S(1)} %bitcast_add_fusion, s32[]{:T(128)S(6)} %select_n.107), kind=kLoop, calls=%fused_computation.16 | loop fusion | flops 61440 | bytes 409604 | tf_op jit(solution)/shard_map/add | solution.py:283
  (14 shorter events, 0.2 us)
Async XLA Ops:
  0.6 11.6 %copy-start = (f32[2,20,4,128]{3,2,1,0:T(4,128)S(1)}, f32[2,20,4,128]{3,2,1,0:T(4,128)}, u32[]{:S(2)}) copy-start(f32[2,20,4,128]{3,2,1,0:T(4,128)} %param.6) | copy-start | bytes 245764
  0.6 9.5 %collective-permute-start = (f32[2,20,4,128]{3,2,1,0:T(4,128)}, f32[2,20,4,128]{3,2,1,0:T(4,128)S(1)}, u32[]{:S(2)}, u32[]{:S(2)}) collective-permute-start(f32[2,20,4,128]{3,2,1,0:T(4,128)} %param.6), channel_id=1, source_target_pairs={{0,2},{1,3},{2,4},{3,5},{4,6},{5,7},{6,0},{7,1},{8,10},{9,11},{10,... | collective-permute-start | bytes 245768 | tf_op jit(solution)/shard_map/ppermute | solution.py:255
  3.7 8.3 %collective-permute-start.1 = (f32[2,20,4,128]{3,2,1,0:T(4,128)}, f32[2,20,4,128]{3,2,1,0:T(4,128)S(1)}, u32[]{:S(2)}, u32[]{:S(2)}) collective-permute-start(f32[2,20,4,128]{3,2,1,0:T(4,128)} %param.6), channel_id=1, source_target_pairs={{0,4},{1,5},{2,6},{3,7},{4,0},{5,1},{6,2},{7,3},{8,12},{9,13},{10,... | collective-permute-start | bytes 245768 | tf_op jit(solution)/shard_map/ppermute | solution.py:255
  6.3 5.9 %collective-permute-start.2 = (f32[2,20,4,128]{3,2,1,0:T(4,128)}, f32[2,20,4,128]{3,2,1,0:T(4,128)S(1)}, u32[]{:S(2)}, u32[]{:S(2)}) collective-permute-start(f32[2,20,4,128]{3,2,1,0:T(4,128)} %param.6), channel_id=1, source_target_pairs={{0,6},{1,7},{2,0},{3,1},{4,2},{5,3},{6,4},{7,5},{8,14},{9,15},{10,... | collective-permute-start | bytes 245768 | tf_op jit(solution)/shard_map/ppermute | solution.py:255
  12.3 1.7 %collective-permute-start.3 = (f32[4,2,20,4,128]{4,3,2,1,0:T(4,128)S(1)}, f32[4,2,20,4,128]{4,3,2,1,0:T(4,128)S(1)}, u32[]{:S(2)}, u32[]{:S(2)}) collective-permute-start(f32[4,2,20,4,128]{4,3,2,1,0:T(4,128)S(1)} %get-tuple-element.13), channel_id=1, source_target_pairs={{0,1},{1,0},{2,3},{3,2},{4,5},{5,4},{6,7},{7,6},{8,9},{9,8},{10,11... | collective-permute-start | bytes 983048 | tf_op jit(solution)/shard_map/ppermute | solution.py:258
  15.1 0.7 %copy-start.1 = (s32[32,128]{1,0:T(8,128)S(1)}, s32[32,128]{1,0:T(8,128)}, u32[]{:S(2)}) copy-start(s32[32,128]{1,0:T(8,128)} %param.7) | copy-start | bytes 49156
  15.1 0.7 %copy-start.2 = (s32[32,128]{1,0:T(8,128)S(1)}, s32[32,128]{1,0:T(8,128)}, u32[]{:S(2)}) copy-start(s32[32,128]{1,0:T(8,128)} %param.8) | copy-start | bytes 49156
  17.4 9.4 %collective-permute-start.7 = (f32[2,122,2]{2,1,0:T(8,128)S(1)}, f32[2,122,2]{2,1,0:T(8,128)S(1)}, u32[]{:S(2)}, u32[]{:S(2)}) collective-permute-start(f32[2,122,2]{2,1,0:T(8,128)S(1)} %rev.11), channel_id=1, source_target_pairs={{0,16},{8,8},{16,0},{24,24},{1,17},{9,9},{17,1},{25,25},{2,18},{10... | collective-permute-start | bytes 5864 | tf_op jit(solution)/shard_map/ppermute | solution.py:18
  21.0 5.8 %collective-permute-start.8 = (f32[2,122,2]{2,1,0:T(8,128)S(1)}, f32[2,122,2]{2,1,0:T(8,128)S(1)}, u32[]{:S(2)}, u32[]{:S(2)}) collective-permute-start(f32[2,122,2]{2,1,0:T(8,128)S(1)} %rev.12), channel_id=1, source_target_pairs={{0,0},{8,24},{16,16},{24,8},{1,1},{9,25},{17,17},{25,9},{2,2},{10,... | collective-permute-start | bytes 5864 | tf_op jit(solution)/shard_map/ppermute | solution.py:18
  21.8 5.5 %collective-permute-start.4 = (f32[2,3904]{1,0:T(2,128)S(1)}, f32[2,3904]{1,0:T(2,128)S(1)}, u32[]{:S(2)}, u32[]{:S(2)}) collective-permute-start(f32[2,3904]{1,0:T(2,128)S(1)} %get-tuple-element.19), channel_id=1, source_target_pairs={{0,24},{8,0},{16,8},{24,16},{1,25},{9,1},{17,9},{25,17},{2,26},{10... | collective-permute-start | bytes 93704 | tf_op jit(solution)/shard_map/ppermute | solution.py:18
  23.3 5.1 %collective-permute-start.5 = (f32[2,3904]{1,0:T(2,128)S(1)}, f32[2,3904]{1,0:T(2,128)S(1)}, u32[]{:S(2)}, u32[]{:S(2)}) collective-permute-start(f32[2,3904]{1,0:T(2,128)S(1)} %get-tuple-element.20), channel_id=1, source_target_pairs={{0,8},{8,16},{16,24},{24,0},{1,9},{9,17},{17,25},{25,1},{2,10},{10... | collective-permute-start | bytes 93704 | tf_op jit(solution)/shard_map/ppermute | solution.py:18
  24.3 5.9 %collective-permute-start.6 = (f32[122,2,128]{2,1,0:T(2,128)S(1)}, f32[122,2,128]{2,1,0:T(2,128)S(1)}, u32[]{:S(2)}, u32[]{:S(2)}) collective-permute-start(f32[122,2,128]{2,1,0:T(2,128)S(1)} %rev.10), channel_id=1, source_target_pairs={{0,24},{8,16},{16,8},{24,0},{1,25},{9,17},{17,9},{25,1},{2,26},{10... | collective-permute-start | bytes 374792 | tf_op jit(solution)/shard_map/ppermute | solution.py:18
  39.3 1.7 %collective-permute-start.9 = (f32[2,20,4,4,128]{4,3,2,1,0:T(4,128)S(1)}, f32[2,20,4,4,128]{4,3,2,1,0:T(4,128)S(1)}, u32[]{:S(2)}, u32[]{:S(2)}) collective-permute-start(f32[2,20,4,4,128]{4,3,2,1,0:T(4,128)S(1)} %dynamic-slice_bitcast_fusion), channel_id=1, source_target_pairs={{0,1},{1,0},{2,3},{3,2},{4,5},{5,4},{6,7},{7,6},{8,9},{9,8},{10,11... | collective-permute-start | bytes 983048 | tf_op jit(solution)/shard_map/ppermute | solution.py:278
  41.1 7.2 %collective-permute-start.10 = (f32[2,20,4,128]{3,2,1,0:T(4,128)S(1)}, f32[2,20,4,128]{3,2,1,0:T(4,128)S(1)}, u32[]{:S(2)}, u32[]{:S(2)}) collective-permute-start(f32[2,20,4,128]{3,2,1,0:T(4,128)S(1)} %get-tuple-element.9), channel_id=1, source_target_pairs={{0,2},{1,3},{2,4},{3,5},{4,6},{5,7},{6,0},{7,1},{8,10},{9,11},{10,... | collective-permute-start | bytes 245768 | tf_op jit(solution)/shard_map/ppermute | solution.py:283
  43.2 7.9 %collective-permute-start.11 = (f32[2,20,4,128]{3,2,1,0:T(4,128)S(1)}, f32[2,20,4,128]{3,2,1,0:T(4,128)S(1)}, u32[]{:S(2)}, u32[]{:S(2)}) collective-permute-start(f32[2,20,4,128]{3,2,1,0:T(4,128)S(1)} %get-tuple-element.11), channel_id=1, source_target_pairs={{0,4},{1,5},{2,6},{3,7},{4,0},{5,1},{6,2},{7,3},{8,12},{9,13},{10,... | collective-permute-start | bytes 245768 | tf_op jit(solution)/shard_map/ppermute | solution.py:283
  45.0 6.2 %collective-permute-start.12 = (f32[2,20,4,128]{3,2,1,0:T(4,128)S(1)}, f32[2,20,4,128]{3,2,1,0:T(4,128)S(1)}, u32[]{:S(2)}, u32[]{:S(2)}) collective-permute-start(f32[2,20,4,128]{3,2,1,0:T(4,128)S(1)} %get-tuple-element.10), channel_id=1, source_target_pairs={{0,6},{1,7},{2,0},{3,1},{4,2},{5,3},{6,4},{7,5},{8,14},{9,15},{10,... | collective-permute-start | bytes 245768 | tf_op jit(solution)/shard_map/ppermute | solution.py:283

commit v20 on v18

--- a/solution.py
+++ b/solution.py
@@ -33,7 +33,13 @@
     )
 
 
-def extended(fields, lanes, rows):
+def mirrored_rows(fields):
+    ny = fields.shape[1]
+    n = lax.axis_size("space")
+    return shifted(fields[:, ny - 1:ny - 3:-1, ::-1], [(q, n - 1 - q) for q in range(n)])
+
+
+def extended(fields, lanes, rows, ghost):
     n = lax.axis_size("space")
     count, ny, width = fields.shape
     spare = lanes - width
@@ -41,8 +47,6 @@
     edges = contract(picker(width, [width - 2, width - 1, 0, 1]), flat, ((0,), (1,)))
     west = shifted(edges[0:2], [(q, (q + 1) % n) for q in range(n)])
     east = shifted(edges[2:4], [(q, (q - 1) % n) for q in range(n)])
-    mirrored = fields[:, ny - 1:ny - 3:-1, ::-1]
-    ghost = shifted(mirrored, [(q, n - 1 - q) for q in range(n)])
     top_edges = edges.reshape(4, count, ny)[:, :, ny - 1:ny - 3:-1]
     ghost_east = shifted(top_edges[1::-1], [(q, (n - 2 - q) % n) for q in range(n)])
     ghost_west = shifted(top_edges[3:1:-1], [(q, (n - q) % n) for q in range(n)])
@@ -191,17 +195,23 @@
     _, chans, levels, ny, width = tracers.shape
     lanes = width + 128
     rows = -(-(ny + 2) // 8) * 8
-    full_kappa = gathered_over_scen(diffusivity)
-    fields = jnp.concatenate(
+    early = jnp.concatenate(
         [
             tracers[0].reshape(chans * levels, ny, width),
             cotangent[0].reshape(chans * levels, ny, width),
+        ]
+    )
+    early_ghost = mirrored_rows(early)
+    full_kappa = gathered_over_scen(diffusivity)
+    late = jnp.concatenate(
+        [
             full_kappa.reshape(2 * levels, ny, width),
             level_count.astype(jnp.float32)[None],
             shelf_mask.astype(jnp.float32)[None],
         ]
     )
-    ext = extended(fields, lanes, rows)
+    ghost = jnp.concatenate([early_ghost, mirrored_rows(late)])
+    ext = extended(jnp.concatenate([early, late]), lanes, rows, ghost)
     field = jax.ShapeDtypeStruct((chans, levels, ny, width), jnp.float32)
     plane = pltpu.VMEM((levels, rows, lanes), jnp.float32)
     planes_c = pltpu.VMEM((chans, levels, rows, lanes), jnp.float32)

time: 52.4 us -> 56.3 us (1.074)
  other arithmetic: 1.87 us -> 5.56 us
  waiting for transfers between devices: 11.8 us -> 13.6 us
  local copies, waits for them, and re-layouts: 5.59 us -> 3.94 us
    ppermute x5 -> x6, waiting for transfers between devices: 0.99 us -> 5.56 us  [shifted(): return lax.ppermute(x, 'space', perm)]
    unnamed x9 -> x15, local copies, waits for them, and re-layouts: 2.59 us -> 0.42 us
    ppermute x3, waiting for transfers between devices: 2.12 us -> 0.01 us  [gathered_over_scen(): lax.ppermute(block, 'scen', [(q, (q // 2 + step) % chips * 2 + q % 2) for...]
    concatenate x1, other arithmetic: 0.01 us -> 1.07 us  [on_device(): jnp.concatenate([tracers[0].reshape(chans * levels, ny, width), cotangent...]
    another operation x1, other arithmetic: 0.11 us -> 1.07 us  [gathered_over_scen(): jnp.stack([same, other], axis=1)]
    concatenate x1, other arithmetic: 0.49 us -> 1.38 us  [extended(): return jnp.concatenate([top, folded, pad], axis=1)]
    broadcast_in_dim x0 -> x1, other arithmetic: none -> 0.74 us  [on_device(): shelf_mask.astype(jnp.float32)[None]]
    ppermute x1, waiting for transfers between devices: 1.52 us -> 0.86 us  [gathered_over_scen(): other = lax.ppermute(same, 'scen', [(q, q ^ 1) for q in range(parts)])]
  transfers between devices with their start and end apart: 13 -> 14, of which waited for: 9 -> 7; matrix products, arithmetic and copies ran while one was open for 11% -> 18% of each run, Pallas kernels for 0% -> 0%
where the time goes in v20:
time: 56.3 us; the launch traced here: 55.8 us
  starting transfers between devices  20.1 us (36%)
  waiting for transfers between devices  13.6 us (24%)
  Pallas kernels  8.52 us (15%)
  other arithmetic  5.56 us (10%)
  local copies, waits for them, and re-layouts  3.94 us (7%)
  matrix products  2.96 us (5%)
  between operations  1.07 us (2%)
    pallas_call x1, Pallas kernels, on_device(): pl.pallas_call(diffusion_kernel, out_shape=(field, field, jax.ShapeDtypeS...  8.52 us
    ppermute x6, starting transfers between devices, shifted(): return lax.ppermute(x, 'space', perm)  8.48 us
    ppermute x3, starting transfers between devices, gathered_over_scen(): lax.ppermute(block, 'scen', [(q, (q // 2 + step) % chips * 2 + q % 2) for...  7.01 us
    ppermute x3, waiting for transfers between devices, summed_over_scen(): lax.ppermute(send, 'scen', [(q, (q // 2 + step) % chips * 2 + q % 2) for...  5.59 us
    ppermute x6, waiting for transfers between devices, shifted(): return lax.ppermute(x, 'space', perm)  5.56 us
    ppermute x3, starting transfers between devices, summed_over_scen(): lax.ppermute(send, 'scen', [(q, (q // 2 + step) % chips * 2 + q % 2) for...  4.5 us
    dot_general x3, matrix products, contract(): lax.dot_general(a, b, (dims, ((), ())), precision=lax.Precision.HIGHEST,...  2.96 us
    ppermute x1, waiting for transfers between devices, summed_over_scen(): pair = lax.ppermute(other, 'scen', [(q, q ^ 1) for q in range(parts)])  1.55 us
  transfers between devices with their start and end apart: 14, of which 7 were waited for; matrix products, arithmetic and copies ran while one was open for 18% of the time, Pallas kernels for 0%

profile of v20, /device:TPU:0, one launch (start us, length us, event | category | flops | bytes accessed | tf_op | source)
XLA Modules:
  0.0 55.8 jit_solution(12758741604495154103)
XLA Ops:
  0.6 0.0 copy-start
  0.6 0.0 copy-start.1
  0.7 3.1 %collective-permute-start = (f32[2,20,4,128]{3,2,1,0:T(4,128)}, f32[2,20,4,128]{3,2,1,0:T(4,128)}, u32[]{:S(2)}, u32[]{:S(2)}) collective-permute-start(f32[2,20,4,128]{3,2,1,0:T(4,128)} %param.6), channel_id=1, source_target_pairs={{0,2},{1,3},{2,4},{3,5},{4,6},{5,7},{6,0},{7,1},{8,10},{9,11},{10,... | collective-permute-start | bytes 245768 | tf_op jit(solution)/shard_map/ppermute | solution.py:255
  3.7 2.6 %collective-permute-start.1 = (f32[2,20,4,128]{3,2,1,0:T(4,128)}, f32[2,20,4,128]{3,2,1,0:T(4,128)}, u32[]{:S(2)}, u32[]{:S(2)}) collective-permute-start(f32[2,20,4,128]{3,2,1,0:T(4,128)} %param.6), channel_id=1, source_target_pairs={{0,4},{1,5},{2,6},{3,7},{4,0},{5,1},{6,2},{7,3},{8,12},{9,13},{10,... | collective-permute-start | bytes 245768 | tf_op jit(solution)/shard_map/ppermute | solution.py:255
  6.3 1.3 %collective-permute-start.2 = (f32[2,20,4,128]{3,2,1,0:T(4,128)}, f32[2,20,4,128]{3,2,1,0:T(4,128)}, u32[]{:S(2)}, u32[]{:S(2)}) collective-permute-start(f32[2,20,4,128]{3,2,1,0:T(4,128)} %param.6), channel_id=1, source_target_pairs={{0,6},{1,7},{2,0},{3,1},{4,2},{5,3},{6,4},{7,5},{8,14},{9,15},{10,... | collective-permute-start | bytes 245768 | tf_op jit(solution)/shard_map/ppermute | solution.py:255
  7.7 1.1 %pad_maximum_fusion.2 = f32[80,2,128]{2,1,0:T(2,128)S(1)} fusion(f32[40,32,128]{2,1,0:T(8,128)} %bitcast.61, f32[40,32,128]{2,1,0:T(8,128)} %bitcast.59), kind=kLoop, calls=%fused_computation.10 | loop fusion | flops 20480 | bytes 1392640 | tf_op jit(solution)/shard_map/concatenate | solution.py:198
  8.7 0.3 rev.13
  9.1 2.5 %collective-permute-start.6 = (f32[80,2,128]{2,1,0:T(2,128)S(1)}, f32[80,2,128]{2,1,0:T(2,128)S(1)}, u32[]{:S(2)}, u32[]{:S(2)}) collective-permute-start(f32[80,2,128]{2,1,0:T(2,128)S(1)} %rev.13), channel_id=1, source_target_pairs={{0,24},{8,16},{16,8},{24,0},{1,25},{9,17},{17,9},{25,1},{2,26},{10... | collective-permute-start | bytes 245768 | tf_op jit(solution)/shard_map/ppermute | solution.py:18
  11.7 0.0 copy-done.1
  11.8 0.6 %pad.5.clone = f32[40]{0:T(128)} pad(f32[6]{0:T(128)S(1)} %broadcast_in_dim.29, f32[]{:T(128)} %constant.106), padding=34_0 | pad | bytes 188 | tf_op jit(solution)/shard_map/concatenate | solution.py:60
  12.4 0.1 and_or_fusion
  12.5 0.0 collective-permute-done
  12.5 0.0 collective-permute-done.1
  12.5 0.0 collective-permute-done.2
  12.5 1.1 %fusion.29 = (f32[4,1,2,20,4,128]{5,4,3,2,0,1:T(4,128)S(1)}, f32[4,2,20,4,128]{4,3,2,1,0:T(4,128)S(1)}) fusion(f32[1,2,20,4,128]{4,3,2,1,0:T(4,128)} %bitcast.5, f32[1,2,20,4,128]{4,3,2,1,0:T(4,128)} %bitcast.4, f32[1,2,20,4,128]{4,3,2,1,0:T(4,128)} %bitcast.3, f32[1,2,20,4,128]{4,3,2,1,0:T(4,128)S(1)} %bitcast.65), kind=kLoop, calls=%fused_computation.70 | loop fusion | flops 245760 | bytes 983040 | tf_op jit(solution)/shard_map/stack | solution.py:259
  13.6 0.1 collective-permute-start.3
  13.7 0.7 %convert_bitcast_fusion = (f32[1,32,128]{2,1,0:T(8,128)S(1)}, f32[1,32,128]{2,1,0:T(8,128)S(1)}) fusion(s32[32,128]{1,0:T(8,128)} %param.8, s32[32,128]{1,0:T(8,128)} %param.7), kind=kLoop, calls=%fused_computation.23 | loop fusion | flops 8192 | bytes 65536 | tf_op jit(solution)/shard_map/broadcast_in_dim | solution.py:210
  14.5 0.9 %collective-permute-done.3 = f32[4,2,20,4,128]{4,3,2,1,0:T(4,128)S(1)} collective-permute-done((f32[4,2,20,4,128]{4,3,2,1,0:T(4,128)S(1)}, f32[4,2,20,4,128]{4,3,2,1,0:T(4,128)S(1)}, u32[]{:S(2)}, u32[]{:S(2)}) %collective-permute-start.3) | collective-permute-done | bytes 327712 | tf_op jit(solution)/shard_map/ppermute | solution.py:258
  15.3 0.1 maximum_select_fusion
  15.5 0.9 %gather_fusion = f32[4,2,2,20,4,128]{5,4,3,2,1,0:T(4,128)S(1)} fusion(f32[4,2,2,20,4,128]{5,4,3,2,0,1:T(4,128)S(1)} %maximum_select_fusion, s32[1024]{0:T(1024)S(1)} %pad_clamp_fusion), kind=kCustom, calls=%fused_computation | custom fusion | bytes 1310736 | tf_op jit(solution)/shard_map/jit(_take)/gather | solution.py:261
  16.4 0.0 copy-start.3
  16.4 0.0 copy-start.4
  16.4 0.2 select_bitcast_fusion
  16.6 0.2 copy.24
  16.9 0.2 copy-done.3
  17.1 0.0 copy-done.4
  17.1 1.0 %fusion.9 = f32[4,3904]{1,0:T(4,128)S(1)} fusion(f32[3904,128]{1,0:T(8,128)S(1)} %bitcast.55, pred[128]{0:T(512)(128)(4,1)S(1)} %get-tuple-element.20, pred[128]{0:T(512)(128)(4,1)S(1)} %get-tuple-element.21, pred[128]{0:T(512)(128)(4,1)S(1)} %get-tuple-element.22, pred[128]{0:T(512)(128)(4,1)S(1)} %get-tuple-element.23, ...), kind=kOutput, calls=%fused_computation.39 | convolution fusion | flops 23989760 | bytes 2061840 | tf_op jit(solution)/shard_map/dot_general | solution.py:31
  18.2 0.1 reshape.79
  18.3 2.3 %collective-permute-start.4 = (f32[2,3904]{1,0:T(2,128)S(1)}, f32[2,3904]{1,0:T(2,128)S(1)}, u32[]{:S(2)}, u32[]{:S(2)}) collective-permute-start(f32[2,3904]{1,0:T(2,128)S(1)} %get-tuple-element.16), channel_id=1, source_target_pairs={{0,24},{8,0},{16,8},{24,16},{1,25},{9,1},{17,9},{25,17},{2,26},{10... | collective-permute-start | bytes 93704 | tf_op jit(solution)/shard_map/ppermute | solution.py:18
  20.6 0.0 collective-permute-start.5
  20.6 0.1 fusion.30
  20.8 0.2 rev.15
  20.9 3.0 %collective-permute-start.8 = (f32[2,122,2]{2,1,0:T(8,128)S(1)}, f32[2,122,2]{2,1,0:T(8,128)S(1)}, u32[]{:S(2)}, u32[]{:S(2)}) collective-permute-start(f32[2,122,2]{2,1,0:T(8,128)S(1)} %rev.15), channel_id=1, source_target_pairs={{0,16},{8,8},{16,0},{24,24},{1,17},{9,9},{17,1},{25,25},{2,18},{10... | collective-permute-start | bytes 5864 | tf_op jit(solution)/shard_map/ppermute | solution.py:18
  24.0 0.2 rev.16
  24.1 0.7 %collective-permute-start.9 = (f32[2,122,2]{2,1,0:T(8,128)S(1)}, f32[2,122,2]{2,1,0:T(8,128)S(1)}, u32[]{:S(2)}, u32[]{:S(2)}) collective-permute-start(f32[2,122,2]{2,1,0:T(8,128)S(1)} %rev.16), channel_id=1, source_target_pairs={{0,0},{8,24},{16,16},{24,8},{1,1},{9,25},{17,17},{25,9},{2,2},{10,... | collective-permute-start | bytes 5864 | tf_op jit(solution)/shard_map/ppermute | solution.py:18
  24.9 0.0 copy-start.5
  24.9 0.2 rev.14
  25.1 3.1 %collective-permute-done.8 = f32[2,122,2]{2,1,0:T(8,128)S(1)} collective-permute-done((f32[2,122,2]{2,1,0:T(8,128)S(1)}, f32[2,122,2]{2,1,0:T(8,128)S(1)}, u32[]{:S(2)}, u32[]{:S(2)}) %collective-permute-start.8) | collective-permute-done | bytes 1984 | tf_op jit(solution)/shard_map/ppermute | solution.py:18
  28.2 0.0 collective-permute-start.7
  28.2 0.0 collective-permute-done.9
  28.3 0.2 reshape.91
  28.4 0.1 copy.30
  28.6 0.1 dot_general.16
  28.7 0.2 fusion
  28.9 0.1 copy.27
  29.0 0.0 collective-permute-done.4
  29.0 0.0 collective-permute-done.5
  29.0 1.7 %fusion.4 = f32[3904,128]{1,0:T(8,128)S(1)} fusion(pred[128,4]{0,1:T(4,128)(4,1)S(1)} %and_or_fusion, f32[2,3904]{1,0:T(2,128)S(1)} %collective-permute-done.5, f32[2,3904]{1,0:T(2,128)S(1)} %collective-permute-done.4), kind=kOutput, calls=%fused_computation.17 | convolution fusion | flops 24001792 | bytes 2061824 | tf_op jit(solution)/shard_map/dot_general | solution.py:31
  30.7 0.0 collective-permute-done.6
  30.8 2.4 %collective-permute-done.7 = f32[42,2,128]{2,1,0:T(2,128)S(1)} collective-permute-done((f32[42,2,128]{2,1,0:T(2,128)S(1)}, f32[42,2,128]{2,1,0:T(2,128)S(1)}, u32[]{:S(2)}, u32[]{:S(2)}) %collective-permute-start.7) | collective-permute-done | bytes 43040 | tf_op jit(solution)/shard_map/ppermute | solution.py:18
  33.2 1.4 %maximum_maximum_fusion.x_ref = f32[122,40,256]{2,1,0:T(8,128)S(1)} fusion(f32[122,2,128]{2,1,0:T(2,128)S(1)} %copy.27, f32[42,2,128]{2,1,0:T(2,128)S(1)} %collective-permute-done.7, f32[80,2,128]{2,1,0:T(2,128)S(1)} %collective-permute-done.6, f32[122,32,128]{2,1,0:T(8,128)S(1)} %bitcast.56, f32[122,32,128]{2,1,0:T(8,128)S(1)} %constant_dynamic-update-slice_fusion, ...), kind=kLoop, calls=%fused_computation.1 | loop fusion | flops 6246400 | bytes 9244832 | tf_op jit(solution)/shard_map/concatenate | solution.py:60
  34.6 8.5 %shard_map.76 = (f32[2,20,32,128]{3,2,1,0:T(8,128)}, f32[2,20,32,128]{3,2,1,0:T(8,128)}, f32[2,20,32,128]{3,2,1,0:T(8,128)S(1)}) custom-call(f32[122,40,256]{2,1,0:T(8,128)S(1)} %maximum_maximum_fusion.x_ref), custom_call_target="tpu_custom_call" | custom-call | tf_op jit(solution)/shard_map/pallas_call | solution.py:220
  43.1 0.1 dynamic-slice_bitcast_fusion
  43.1 0.1 collective-permute-start.10
  43.3 1.5 %collective-permute-done.10 = f32[2,20,4,4,128]{4,3,2,1,0:T(4,128)S(1)} collective-permute-done((f32[2,20,4,4,128]{4,3,2,1,0:T(4,128)S(1)}, f32[2,20,4,4,128]{4,3,2,1,0:T(4,128)S(1)}, u32[]{:S(2)}, u32[]{:S(2)}) %collective-permute-start.10) | collective-permute-done | bytes 327712 | tf_op jit(solution)/shard_map/ppermute | solution.py:278
  44.8 0.1 bitcast_add_fusion
  44.9 0.1 dynamic-slice_bitcast_fusion.3
  45.0 2.1 %collective-permute-start.11 = (f32[2,20,4,128]{3,2,1,0:T(4,128)S(1)}, f32[2,20,4,128]{3,2,1,0:T(4,128)S(1)}, u32[]{:S(2)}, u32[]{:S(2)}) collective-permute-start(f32[2,20,4,128]{3,2,1,0:T(4,128)S(1)} %get-tuple-element.9), channel_id=1, source_target_pairs={{0,2},{1,3},{2,4},{3,5},{4,6},{5,7},{6,0},{7,1},{8,10},{9,11},{10,... | collective-permute-start | bytes 245768 | tf_op jit(solution)/shard_map/ppermute | solution.py:283
  47.1 1.8 %collective-permute-start.12 = (f32[2,20,4,128]{3,2,1,0:T(4,128)S(1)}, f32[2,20,4,128]{3,2,1,0:T(4,128)S(1)}, u32[]{:S(2)}, u32[]{:S(2)}) collective-permute-start(f32[2,20,4,128]{3,2,1,0:T(4,128)S(1)} %get-tuple-element.11), channel_id=1, source_target_pairs={{0,4},{1,5},{2,6},{3,7},{4,0},{5,1},{6,2},{7,3},{8,12},{9,13},{10,... | collective-permute-start | bytes 245768 | tf_op jit(solution)/shard_map/ppermute | solution.py:283
  48.9 0.6 %collective-permute-start.13 = (f32[2,20,4,128]{3,2,1,0:T(4,128)S(1)}, f32[2,20,4,128]{3,2,1,0:T(4,128)S(1)}, u32[]{:S(2)}, u32[]{:S(2)}) collective-permute-start(f32[2,20,4,128]{3,2,1,0:T(4,128)S(1)} %get-tuple-element.10), channel_id=1, source_target_pairs={{0,6},{1,7},{2,0},{3,1},{4,2},{5,3},{6,4},{7,5},{8,14},{9,15},{10,... | collective-permute-start | bytes 245768 | tf_op jit(solution)/shard_map/ppermute | solution.py:283
  49.5 2.7 %collective-permute-done.11 = f32[2,20,4,128]{3,2,1,0:T(4,128)S(1)} collective-permute-done((f32[2,20,4,128]{3,2,1,0:T(4,128)S(1)}, f32[2,20,4,128]{3,2,1,0:T(4,128)S(1)}, u32[]{:S(2)}, u32[]{:S(2)}) %collective-permute-start.11) | collective-permute-done | bytes 81952 | tf_op jit(solution)/shard_map/ppermute | solution.py:283
  52.2 2.7 %collective-permute-done.12 = f32[2,20,4,128]{3,2,1,0:T(4,128)S(1)} collective-permute-done((f32[2,20,4,128]{3,2,1,0:T(4,128)S(1)}, f32[2,20,4,128]{3,2,1,0:T(4,128)S(1)}, u32[]{:S(2)}, u32[]{:S(2)}) %collective-permute-start.12) | collective-permute-done | bytes 81952 | tf_op jit(solution)/shard_map/ppermute | solution.py:283
  54.9 0.1 collective-permute-done.13
  55.1 0.7 %fusion.3 = f32[2,20,4,128]{3,2,1,0:T(4,128)} fusion(f32[2,20,4,128]{3,2,1,0:T(4,128)S(1)} %collective-permute-done.13, f32[2,20,4,128]{3,2,1,0:T(4,128)S(1)} %collective-permute-done.12, f32[2,20,4,128]{3,2,1,0:T(4,128)S(1)} %collective-permute-done.11, f32[2,20,4,4,128]{4,3,2,1,0:T(4,128)S(1)} %bitcast_add_fusion, s32[]{:T(128)S(6)} %select_n.107), kind=kLoop, calls=%fused_computation.13 | loop fusion | flops 61440 | bytes 409604 | tf_op jit(solution)/shard_map/add | solution.py:283
  (20 shorter events, 0.3 us)
Async XLA Ops:
  0.6 11.0 %copy-start = (f32[1,2,20,32,128]{4,3,2,1,0:T(8,128)S(1)}, f32[1,2,20,32,128]{4,3,2,1,0:T(8,128)}, u32[]{:S(2)}) copy-start(f32[1,2,20,32,128]{4,3,2,1,0:T(8,128)} %param.5) | copy-start | bytes 1966084
  0.6 11.1 %copy-start.1 = (f32[1,2,20,32,128]{4,3,2,1,0:T(8,128)S(1)}, f32[1,2,20,32,128]{4,3,2,1,0:T(8,128)}, u32[]{:S(2)}) copy-start(f32[1,2,20,32,128]{4,3,2,1,0:T(8,128)} %param.9) | copy-start | bytes 1966084
  0.7 11.9 %collective-permute-start = (f32[2,20,4,128]{3,2,1,0:T(4,128)}, f32[2,20,4,128]{3,2,1,0:T(4,128)}, u32[]{:S(2)}, u32[]{:S(2)}) collective-permute-start(f32[2,20,4,128]{3,2,1,0:T(4,128)} %param.6), channel_id=1, source_target_pairs={{0,2},{1,3},{2,4},{3,5},{4,6},{5,7},{6,0},{7,1},{8,10},{9,11},{10,... | collective-permute-start | bytes 245768 | tf_op jit(solution)/shard_map/ppermute | solution.py:255
  3.7 8.8 %collective-permute-start.1 = (f32[2,20,4,128]{3,2,1,0:T(4,128)}, f32[2,20,4,128]{3,2,1,0:T(4,128)}, u32[]{:S(2)}, u32[]{:S(2)}) collective-permute-start(f32[2,20,4,128]{3,2,1,0:T(4,128)} %param.6), channel_id=1, source_target_pairs={{0,4},{1,5},{2,6},{3,7},{4,0},{5,1},{6,2},{7,3},{8,12},{9,13},{10,... | collective-permute-start | bytes 245768 | tf_op jit(solution)/shard_map/ppermute | solution.py:255
  6.3 6.2 %collective-permute-start.2 = (f32[2,20,4,128]{3,2,1,0:T(4,128)}, f32[2,20,4,128]{3,2,1,0:T(4,128)}, u32[]{:S(2)}, u32[]{:S(2)}) collective-permute-start(f32[2,20,4,128]{3,2,1,0:T(4,128)} %param.6), channel_id=1, source_target_pairs={{0,6},{1,7},{2,0},{3,1},{4,2},{5,3},{6,4},{7,5},{8,14},{9,15},{10,... | collective-permute-start | bytes 245768 | tf_op jit(solution)/shard_map/ppermute | solution.py:255
  7.7 4.9 %copy-start.2 = (f32[2,20,4,128]{3,2,1,0:T(4,128)S(1)}, f32[2,20,4,128]{3,2,1,0:T(4,128)}, u32[]{:S(2)}) copy-start(f32[2,20,4,128]{3,2,1,0:T(4,128)} %param.6) | copy-start | bytes 245764
  9.1 21.7 %collective-permute-start.6 = (f32[80,2,128]{2,1,0:T(2,128)S(1)}, f32[80,2,128]{2,1,0:T(2,128)S(1)}, u32[]{:S(2)}, u32[]{:S(2)}) collective-permute-start(f32[80,2,128]{2,1,0:T(2,128)S(1)} %rev.13), channel_id=1, source_target_pairs={{0,24},{8,16},{16,8},{24,0},{1,25},{9,17},{17,9},{25,1},{2,26},{10... | collective-permute-start | bytes 245768 | tf_op jit(solution)/shard_map/ppermute | solution.py:18
  13.6 1.7 %collective-permute-start.3 = (f32[4,2,20,4,128]{4,3,2,1,0:T(4,128)S(1)}, f32[4,2,20,4,128]{4,3,2,1,0:T(4,128)S(1)}, u32[]{:S(2)}, u32[]{:S(2)}) collective-permute-start(f32[4,2,20,4,128]{4,3,2,1,0:T(4,128)S(1)} %get-tuple-element.13), channel_id=1, source_target_pairs={{0,1},{1,0},{2,3},{3,2},{4,5},{5,4},{6,7},{7,6},{8,9},{9,8},{10,11... | collective-permute-start | bytes 983048 | tf_op jit(solution)/shard_map/ppermute | solution.py:258
  16.4 0.7 %copy-start.3 = (s32[32,128]{1,0:T(8,128)S(1)}, s32[32,128]{1,0:T(8,128)}, u32[]{:S(2)}) copy-start(s32[32,128]{1,0:T(8,128)} %param.7) | copy-start | bytes 49156
  16.4 0.7 %copy-start.4 = (s32[32,128]{1,0:T(8,128)S(1)}, s32[32,128]{1,0:T(8,128)}, u32[]{:S(2)}) copy-start(s32[32,128]{1,0:T(8,128)} %param.8) | copy-start | bytes 49156
  18.3 10.6 %collective-permute-start.4 = (f32[2,3904]{1,0:T(2,128)S(1)}, f32[2,3904]{1,0:T(2,128)S(1)}, u32[]{:S(2)}, u32[]{:S(2)}) collective-permute-start(f32[2,3904]{1,0:T(2,128)S(1)} %get-tuple-element.16), channel_id=1, source_target_pairs={{0,24},{8,0},{16,8},{24,16},{1,25},{9,1},{17,9},{25,17},{2,26},{10... | collective-permute-start | bytes 93704 | tf_op jit(solution)/shard_map/ppermute | solution.py:18
  20.6 8.4 %collective-permute-start.5 = (f32[2,3904]{1,0:T(2,128)S(1)}, f32[2,3904]{1,0:T(2,128)S(1)}, u32[]{:S(2)}, u32[]{:S(2)}) collective-permute-start(f32[2,3904]{1,0:T(2,128)S(1)} %get-tuple-element.17), channel_id=1, source_target_pairs={{0,8},{8,16},{16,24},{24,0},{1,9},{9,17},{17,25},{25,1},{2,10},{10... | collective-permute-start | bytes 93704 | tf_op jit(solution)/shard_map/ppermute | solution.py:18
  20.9 7.3 %collective-permute-start.8 = (f32[2,122,2]{2,1,0:T(8,128)S(1)}, f32[2,122,2]{2,1,0:T(8,128)S(1)}, u32[]{:S(2)}, u32[]{:S(2)}) collective-permute-start(f32[2,122,2]{2,1,0:T(8,128)S(1)} %rev.15), channel_id=1, source_target_pairs={{0,16},{8,8},{16,0},{24,24},{1,17},{9,9},{17,1},{25,25},{2,18},{10... | collective-permute-start | bytes 5864 | tf_op jit(solution)/shard_map/ppermute | solution.py:18
  24.1 4.1 %collective-permute-start.9 = (f32[2,122,2]{2,1,0:T(8,128)S(1)}, f32[2,122,2]{2,1,0:T(8,128)S(1)}, u32[]{:S(2)}, u32[]{:S(2)}) collective-permute-start(f32[2,122,2]{2,1,0:T(8,128)S(1)} %rev.16), channel_id=1, source_target_pairs={{0,0},{8,24},{16,16},{24,8},{1,1},{9,25},{17,17},{25,9},{2,2},{10,... | collective-permute-start | bytes 5864 | tf_op jit(solution)/shard_map/ppermute | solution.py:18
  24.9 8.3 %copy-start.5 = (f32[40]{0:T(128)S(1)}, f32[40]{0:T(128)}, u32[]{:S(2)}) copy-start(f32[40]{0:T(128)} %pad.5.clone) | copy-start | bytes 484
  28.2 4.9 %collective-permute-start.7 = (f32[42,2,128]{2,1,0:T(2,128)S(1)}, f32[42,2,128]{2,1,0:T(2,128)S(1)}, u32[]{:S(2)}, u32[]{:S(2)}) collective-permute-start(f32[42,2,128]{2,1,0:T(2,128)S(1)} %rev.14), channel_id=1, source_target_pairs={{0,24},{8,16},{16,8},{24,0},{1,25},{9,17},{17,9},{25,1},{2,26},{10... | collective-permute-start | bytes 129032 | tf_op jit(solution)/shard_map/ppermute | solution.py:18
  43.1 1.7 %collective-permute-start.10 = (f32[2,20,4,4,128]{4,3,2,1,0:T(4,128)S(1)}, f32[2,20,4,4,128]{4,3,2,1,0:T(4,128)S(1)}, u32[]{:S(2)}, u32[]{:S(2)}) collective-permute-start(f32[2,20,4,4,128]{4,3,2,1,0:T(4,128)S(1)} %dynamic-slice_bitcast_fusion), channel_id=1, source_target_pairs={{0,1},{1,0},{2,3},{3,2},{4,5},{5,4},{6,7},{7,6},{8,9},{9,8},{10,11... | collective-permute-start | bytes 983048 | tf_op jit(solution)/shard_map/ppermute | solution.py:278
  45.0 7.2 %collective-permute-start.11 = (f32[2,20,4,128]{3,2,1,0:T(4,128)S(1)}, f32[2,20,4,128]{3,2,1,0:T(4,128)S(1)}, u32[]{:S(2)}, u32[]{:S(2)}) collective-permute-start(f32[2,20,4,128]{3,2,1,0:T(4,128)S(1)} %get-tuple-element.9), channel_id=1, source_target_pairs={{0,2},{1,3},{2,4},{3,5},{4,6},{5,7},{6,0},{7,1},{8,10},{9,11},{10,... | collective-permute-start | bytes 245768 | tf_op jit(solution)/shard_map/ppermute | solution.py:283
  47.1 7.9 %collective-permute-start.12 = (f32[2,20,4,128]{3,2,1,0:T(4,128)S(1)}, f32[2,20,4,128]{3,2,1,0:T(4,128)S(1)}, u32[]{:S(2)}, u32[]{:S(2)}) collective-permute-start(f32[2,20,4,128]{3,2,1,0:T(4,128)S(1)} %get-tuple-element.11), channel_id=1, source_target_pairs={{0,4},{1,5},{2,6},{3,7},{4,0},{5,1},{6,2},{7,3},{8,12},{9,13},{10,... | collective-permute-start | bytes 245768 | tf_op jit(solution)/shard_map/ppermute | solution.py:283
  48.9 6.2 %collective-permute-start.13 = (f32[2,20,4,128]{3,2,1,0:T(4,128)S(1)}, f32[2,20,4,128]{3,2,1,0:T(4,128)S(1)}, u32[]{:S(2)}, u32[]{:S(2)}) collective-permute-start(f32[2,20,4,128]{3,2,1,0:T(4,128)S(1)} %get-tuple-element.10), channel_id=1, source_target_pairs={{0,6},{1,7},{2,0},{3,1},{4,2},{5,3},{6,4},{7,5},{8,14},{9,15},{10,... | collective-permute-start | bytes 245768 | tf_op jit(solution)/shard_map/ppermute | solution.py:283

commit v21 on v18

--- a/solution.py
+++ b/solution.py
@@ -1,3 +1,5 @@
+import functools
+
 import jax
 import jax.numpy as jnp
 from jax import lax
@@ -135,44 +137,42 @@
         change = change + (cz_ref[k + 1] * (above - x) - cz_ref[k] * (x - below))
         return x, change
 
-    def forward_first(ck, carry):
-        c = ck // levels
-        k = ck % levels
+    def forward_first(c, k, carry):
         x, change = operate(ue_ref, c, k, (du0e_ref, du0n_ref))
-        heat = jnp.where(c == 0, 1.0, 0.0)
-        u1_ref[c, k] = wet_ref[k] * (x + change + heat * src_ref[k])
-        return carry
-
-    lax.fori_loop(0, planes, forward_first, 0, unroll=8)
-
-    def forward_second(ck, carry):
-        c = ck // levels
-        k = ck % levels
+        if c == 0:
+            change = change + src_ref[k]
+        u1_ref[c, k] = wet_ref[k] * (x + change)
+        return carry
+
+    for c in range(chans):
+        lax.fori_loop(0, levels, functools.partial(forward_first, c), 0, unroll=10)
+
+    def forward_second(c, k, carry):
         x, change = operate(u1_ref, c, k, (du1e_ref, du1n_ref))
-        heat = jnp.where(c == 0, 1.0, 0.0)
-        out = wet_ref[k] * (x + change + heat * src_ref[k])
+        if c == 0:
+            change = change + src_ref[k]
+        out = wet_ref[k] * (x + change)
         fin_ref[c, k] = out[:ny, :width]
         return carry
 
-    lax.fori_loop(0, planes, forward_second, 0, unroll=8)
-
-    def backward_second(ck, carry):
-        c = ck // levels
-        k = ck % levels
+    for c in range(chans):
+        lax.fori_loop(0, levels, functools.partial(forward_second, c), 0, unroll=10)
+
+    def backward_second(c, k, carry):
         x, change = operate(a_ref, c, k, (dv2e_ref, dv2n_ref))
         b_ref[c, k] = wet_ref[k] * (x + change)
         return carry
 
-    lax.fori_loop(0, planes, backward_second, 0, unroll=8)
-
-    def backward_first(ck, carry):
-        c = ck // levels
-        k = ck % levels
+    for c in range(chans):
+        lax.fori_loop(0, levels, functools.partial(backward_second, c), 0, unroll=10)
+
+    def backward_first(c, k, carry):
         x, change = operate(b_ref, c, k, (dv1e_ref, dv1n_ref))
         adj_ref[c, k] = (x + change)[:ny, :width]
         return carry
 
-    lax.fori_loop(0, planes, backward_first, 0, unroll=8)
+    for c in range(chans):
+        lax.fori_loop(0, levels, functools.partial(backward_first, c), 0, unroll=10)
 
     def gradient(k, carry):
         g_east = jnp.zeros((ny, width), jnp.float32)

time: 52.4 us -> 53.1 us (1.013)
  Pallas kernels: 8.52 us -> 9.13 us
    pallas_call x1, Pallas kernels: 8.52 us -> 9.13 us  [on_device(): pl.pallas_call(diffusion_kernel, out_shape=(field, field, jax.ShapeDtypeS...]
where the time goes in v21:
time: 53.1 us; the launch traced here: 52.5 us
  starting transfers between devices  20.2 us (38%)
  waiting for transfers between devices  11.8 us (22%)
  Pallas kernels  9.13 us (17%)
  local copies, waits for them, and re-layouts  5.59 us (11%)
  matrix products  2.96 us (6%)
  other arithmetic  1.87 us (4%)
  between operations  0.97 us (2%)
    pallas_call x1, Pallas kernels, on_device(): pl.pallas_call(diffusion_kernel, out_shape=(field, field, jax.ShapeDtypeS...  9.13 us
    ppermute x5, starting transfers between devices, shifted(): return lax.ppermute(x, 'space', perm)  8.58 us
    ppermute x3, starting transfers between devices, gathered_over_scen(): lax.ppermute(block, 'scen', [(q, (q // 2 + step) % chips * 2 + q % 2) for...  7.01 us
    ppermute x3, waiting for transfers between devices, summed_over_scen(): lax.ppermute(send, 'scen', [(q, (q // 2 + step) % chips * 2 + q % 2) for...  5.59 us
    ppermute x3, starting transfers between devices, summed_over_scen(): lax.ppermute(send, 'scen', [(q, (q // 2 + step) % chips * 2 + q % 2) for...  4.5 us
    dot_general x3, matrix products, contract(): lax.dot_general(a, b, (dims, ((), ())), precision=lax.Precision.HIGHEST,...  2.96 us
    unnamed x9, local copies, waits for them, and re-layouts  2.59 us
    ppermute x3, waiting for transfers between devices, gathered_over_scen(): lax.ppermute(block, 'scen', [(q, (q // 2 + step) % chips * 2 + q % 2) for...  2.12 us
  transfers between devices with their start and end apart: 13, of which 9 were waited for; matrix products, arithmetic and copies ran while one was open for 11% of the time, Pallas kernels for 0%

profile of v21, /device:TPU:0, one launch (start us, length us, event | category | flops | bytes accessed | tf_op | source)
XLA Modules:
  0.0 52.5 jit_solution(12726278890932108677)
XLA Ops:
  0.6 0.0 copy-start
  0.6 3.1 %collective-permute-start = (f32[2,20,4,128]{3,2,1,0:T(4,128)}, f32[2,20,4,128]{3,2,1,0:T(4,128)S(1)}, u32[]{:S(2)}, u32[]{:S(2)}) collective-permute-start(f32[2,20,4,128]{3,2,1,0:T(4,128)} %param.6), channel_id=1, source_target_pairs={{0,2},{1,3},{2,4},{3,5},{4,6},{5,7},{6,0},{7,1},{8,10},{9,11},{10,... | collective-permute-start | bytes 245768 | tf_op jit(solution)/shard_map/ppermute | solution.py:245
  3.7 2.6 %collective-permute-start.1 = (f32[2,20,4,128]{3,2,1,0:T(4,128)}, f32[2,20,4,128]{3,2,1,0:T(4,128)S(1)}, u32[]{:S(2)}, u32[]{:S(2)}) collective-permute-start(f32[2,20,4,128]{3,2,1,0:T(4,128)} %param.6), channel_id=1, source_target_pairs={{0,4},{1,5},{2,6},{3,7},{4,0},{5,1},{6,2},{7,3},{8,12},{9,13},{10,... | collective-permute-start | bytes 245768 | tf_op jit(solution)/shard_map/ppermute | solution.py:245
  6.3 1.3 %collective-permute-start.2 = (f32[2,20,4,128]{3,2,1,0:T(4,128)}, f32[2,20,4,128]{3,2,1,0:T(4,128)S(1)}, u32[]{:S(2)}, u32[]{:S(2)}) collective-permute-start(f32[2,20,4,128]{3,2,1,0:T(4,128)} %param.6), channel_id=1, source_target_pairs={{0,6},{1,7},{2,0},{3,1},{4,2},{5,3},{6,4},{7,5},{8,14},{9,15},{10,... | collective-permute-start | bytes 245768 | tf_op jit(solution)/shard_map/ppermute | solution.py:245
  7.7 1.1 %constant_dynamic-update-slice_fusion.2 = f32[122,32,128]{2,1,0:T(8,128)S(1)} fusion(f32[40,32,128]{2,1,0:T(8,128)} %bitcast.54), kind=kLoop, calls=%fused_computation.24 | loop fusion | bytes 1310720
  8.9 1.1 %constant_dynamic-update-slice_fusion.1 = f32[122,32,128]{2,1,0:T(8,128)S(1)} fusion(f32[122,32,128]{2,1,0:T(8,128)S(1)} %constant_dynamic-update-slice_fusion.2, f32[40,32,128]{2,1,0:T(8,128)} %bitcast.55), kind=kLoop, calls=%fused_computation.23 | loop fusion | bytes 1310720
  10.0 0.1 pad.4.clone
  10.1 0.0 collective-permute-done
  10.1 1.9 %collective-permute-done.1 = f32[2,20,4,128]{3,2,1,0:T(4,128)S(1)} collective-permute-done((f32[2,20,4,128]{3,2,1,0:T(4,128)}, f32[2,20,4,128]{3,2,1,0:T(4,128)S(1)}, u32[]{:S(2)}, u32[]{:S(2)}) %collective-permute-start.1) | collective-permute-done | bytes 81952 | tf_op jit(solution)/shard_map/ppermute | solution.py:245
  12.0 0.2 collective-permute-done.2
  12.2 0.0 copy-done
  12.2 0.1 fusion.29
  12.3 0.1 collective-permute-start.3
  12.4 0.1 and_or_fusion
  12.5 1.5 %collective-permute-done.3 = f32[4,2,20,4,128]{4,3,2,1,0:T(4,128)S(1)} collective-permute-done((f32[4,2,20,4,128]{4,3,2,1,0:T(4,128)S(1)}, f32[4,2,20,4,128]{4,3,2,1,0:T(4,128)S(1)}, u32[]{:S(2)}, u32[]{:S(2)}) %collective-permute-start.3) | collective-permute-done | bytes 327712 | tf_op jit(solution)/shard_map/ppermute | solution.py:248
  14.0 0.1 maximum_select_fusion
  14.2 0.9 %gather_fusion = f32[4,2,2,20,4,128]{5,4,3,2,1,0:T(4,128)S(1)} fusion(f32[4,2,2,20,4,128]{5,4,3,2,0,1:T(4,128)S(1)} %maximum_select_fusion, s32[1024]{0:T(1024)S(1)} %pad_clamp_fusion), kind=kCustom, calls=%fused_computation | custom fusion | bytes 1310736 | tf_op jit(solution)/shard_map/jit(_take)/gather | solution.py:251
  15.1 0.0 copy-start.1
  15.1 0.0 copy-start.2
  15.2 0.2 select_bitcast_fusion
  15.4 0.2 copy.24
  15.6 0.3 copy-done.1
  15.9 0.0 copy-done.2
  15.9 1.0 %fusion.9 = f32[4,3904]{1,0:T(4,128)S(1)} fusion(f32[3904,128]{1,0:T(8,128)S(1)} %bitcast.51, pred[128]{0:T(512)(128)(4,1)S(1)} %get-tuple-element.20, pred[128]{0:T(512)(128)(4,1)S(1)} %get-tuple-element.21, pred[128]{0:T(512)(128)(4,1)S(1)} %get-tuple-element.22, pred[128]{0:T(512)(128)(4,1)S(1)} %get-tuple-element.23, ...), kind=kOutput, calls=%fused_computation.34 | convolution fusion | flops 23989760 | bytes 2061840 | tf_op jit(solution)/shard_map/dot_general | solution.py:33
  16.9 0.1 reshape.79
  17.0 0.1 fusion.30
  17.2 0.2 rev.11
  17.4 3.4 %collective-permute-start.7 = (f32[2,122,2]{2,1,0:T(8,128)S(1)}, f32[2,122,2]{2,1,0:T(8,128)S(1)}, u32[]{:S(2)}, u32[]{:S(2)}) collective-permute-start(f32[2,122,2]{2,1,0:T(8,128)S(1)} %rev.11), channel_id=1, source_target_pairs={{0,16},{8,8},{16,0},{24,24},{1,17},{9,9},{17,1},{25,25},{2,18},{10... | collective-permute-start | bytes 5864 | tf_op jit(solution)/shard_map/ppermute | solution.py:20
  20.8 0.2 rev.12
  21.0 0.7 %collective-permute-start.8 = (f32[2,122,2]{2,1,0:T(8,128)S(1)}, f32[2,122,2]{2,1,0:T(8,128)S(1)}, u32[]{:S(2)}, u32[]{:S(2)}) collective-permute-start(f32[2,122,2]{2,1,0:T(8,128)S(1)} %rev.12), channel_id=1, source_target_pairs={{0,0},{8,24},{16,16},{24,8},{1,1},{9,25},{17,17},{25,9},{2,2},{10,... | collective-permute-start | bytes 5864 | tf_op jit(solution)/shard_map/ppermute | solution.py:20
  21.7 0.1 slice.29
  21.8 1.5 %collective-permute-start.4 = (f32[2,3904]{1,0:T(2,128)S(1)}, f32[2,3904]{1,0:T(2,128)S(1)}, u32[]{:S(2)}, u32[]{:S(2)}) collective-permute-start(f32[2,3904]{1,0:T(2,128)S(1)} %get-tuple-element.16), channel_id=1, source_target_pairs={{0,24},{8,0},{16,8},{24,16},{1,25},{9,1},{17,9},{25,17},{2,26},{10... | collective-permute-start | bytes 93704 | tf_op jit(solution)/shard_map/ppermute | solution.py:20
  23.3 0.6 %collective-permute-start.5 = (f32[2,3904]{1,0:T(2,128)S(1)}, f32[2,3904]{1,0:T(2,128)S(1)}, u32[]{:S(2)}, u32[]{:S(2)}) collective-permute-start(f32[2,3904]{1,0:T(2,128)S(1)} %get-tuple-element.17), channel_id=1, source_target_pairs={{0,8},{8,16},{16,24},{24,0},{1,9},{9,17},{17,25},{25,1},{2,10},{10... | collective-permute-start | bytes 93704 | tf_op jit(solution)/shard_map/ppermute | solution.py:20
  23.8 0.5 rev.10
  24.3 2.4 %collective-permute-start.6 = (f32[122,2,128]{2,1,0:T(2,128)S(1)}, f32[122,2,128]{2,1,0:T(2,128)S(1)}, u32[]{:S(2)}, u32[]{:S(2)}) collective-permute-start(f32[122,2,128]{2,1,0:T(2,128)S(1)} %rev.10), channel_id=1, source_target_pairs={{0,24},{8,16},{16,8},{24,0},{1,25},{9,17},{17,9},{25,1},{2,26},{10... | collective-permute-start | bytes 374792 | tf_op jit(solution)/shard_map/ppermute | solution.py:20
  26.7 0.0 collective-permute-done.7
  26.7 0.0 collective-permute-done.8
  26.8 0.2 reshape.91
  26.9 0.1 copy.30
  27.1 0.1 dot_general.16
  27.2 0.2 fusion
  27.4 0.1 copy.27
  27.5 0.0 collective-permute-done.4
  27.5 0.8 %collective-permute-done.5 = f32[2,3904]{1,0:T(2,128)S(1)} collective-permute-done((f32[2,3904]{1,0:T(2,128)S(1)}, f32[2,3904]{1,0:T(2,128)S(1)}, u32[]{:S(2)}, u32[]{:S(2)}) %collective-permute-start.5) | collective-permute-done | bytes 31264 | tf_op jit(solution)/shard_map/ppermute | solution.py:20
  28.3 1.7 %fusion.4 = f32[3904,128]{1,0:T(8,128)S(1)} fusion(pred[128,4]{0,1:T(4,128)(4,1)S(1)} %and_or_fusion, f32[2,3904]{1,0:T(2,128)S(1)} %collective-permute-done.5, f32[2,3904]{1,0:T(2,128)S(1)} %collective-permute-done.4), kind=kOutput, calls=%fused_computation.16 | convolution fusion | flops 24001792 | bytes 2061824 | tf_op jit(solution)/shard_map/dot_general | solution.py:33
  30.1 0.1 collective-permute-done.6
  30.2 0.5 maximum_maximum_fusion.x_ref
  30.7 9.1 %shard_map.76 = (f32[2,20,32,128]{3,2,1,0:T(8,128)}, f32[2,20,32,128]{3,2,1,0:T(8,128)}, f32[2,20,32,128]{3,2,1,0:T(8,128)S(1)}) custom-call(f32[122,40,256]{2,1,0:T(8,128)S(1)} %maximum_maximum_fusion.x_ref), custom_call_target="tpu_custom_call" | custom-call | tf_op jit(solution)/shard_map/pallas_call | solution.py:210
  39.8 0.1 dynamic-slice_bitcast_fusion
  39.9 0.1 collective-permute-start.9
  40.1 1.5 %collective-permute-done.9 = f32[2,20,4,4,128]{4,3,2,1,0:T(4,128)S(1)} collective-permute-done((f32[2,20,4,4,128]{4,3,2,1,0:T(4,128)S(1)}, f32[2,20,4,4,128]{4,3,2,1,0:T(4,128)S(1)}, u32[]{:S(2)}, u32[]{:S(2)}) %collective-permute-start.9) | collective-permute-done | bytes 327712 | tf_op jit(solution)/shard_map/ppermute | solution.py:268
  41.6 0.1 bitcast_add_fusion
  41.7 0.1 dynamic-slice_bitcast_fusion.3
  41.8 2.1 %collective-permute-start.10 = (f32[2,20,4,128]{3,2,1,0:T(4,128)S(1)}, f32[2,20,4,128]{3,2,1,0:T(4,128)S(1)}, u32[]{:S(2)}, u32[]{:S(2)}) collective-permute-start(f32[2,20,4,128]{3,2,1,0:T(4,128)S(1)} %get-tuple-element.9), channel_id=1, source_target_pairs={{0,2},{1,3},{2,4},{3,5},{4,6},{5,7},{6,0},{7,1},{8,10},{9,11},{10,... | collective-permute-start | bytes 245768 | tf_op jit(solution)/shard_map/ppermute | solution.py:273
  43.8 1.8 %collective-permute-start.11 = (f32[2,20,4,128]{3,2,1,0:T(4,128)S(1)}, f32[2,20,4,128]{3,2,1,0:T(4,128)S(1)}, u32[]{:S(2)}, u32[]{:S(2)}) collective-permute-start(f32[2,20,4,128]{3,2,1,0:T(4,128)S(1)} %get-tuple-element.11), channel_id=1, source_target_pairs={{0,4},{1,5},{2,6},{3,7},{4,0},{5,1},{6,2},{7,3},{8,12},{9,13},{10,... | collective-permute-start | bytes 245768 | tf_op jit(solution)/shard_map/ppermute | solution.py:273
  45.7 0.6 %collective-permute-start.12 = (f32[2,20,4,128]{3,2,1,0:T(4,128)S(1)}, f32[2,20,4,128]{3,2,1,0:T(4,128)S(1)}, u32[]{:S(2)}, u32[]{:S(2)}) collective-permute-start(f32[2,20,4,128]{3,2,1,0:T(4,128)S(1)} %get-tuple-element.10), channel_id=1, source_target_pairs={{0,6},{1,7},{2,0},{3,1},{4,2},{5,3},{6,4},{7,5},{8,14},{9,15},{10,... | collective-permute-start | bytes 245768 | tf_op jit(solution)/shard_map/ppermute | solution.py:273
  46.3 2.7 %collective-permute-done.10 = f32[2,20,4,128]{3,2,1,0:T(4,128)S(1)} collective-permute-done((f32[2,20,4,128]{3,2,1,0:T(4,128)S(1)}, f32[2,20,4,128]{3,2,1,0:T(4,128)S(1)}, u32[]{:S(2)}, u32[]{:S(2)}) %collective-permute-start.10) | collective-permute-done | bytes 81952 | tf_op jit(solution)/shard_map/ppermute | solution.py:273
  49.0 2.7 %collective-permute-done.11 = f32[2,20,4,128]{3,2,1,0:T(4,128)S(1)} collective-permute-done((f32[2,20,4,128]{3,2,1,0:T(4,128)S(1)}, f32[2,20,4,128]{3,2,1,0:T(4,128)S(1)}, u32[]{:S(2)}, u32[]{:S(2)}) %collective-permute-start.11) | collective-permute-done | bytes 81952 | tf_op jit(solution)/shard_map/ppermute | solution.py:273
  51.7 0.1 collective-permute-done.12
  51.8 0.7 %fusion.3 = f32[2,20,4,128]{3,2,1,0:T(4,128)} fusion(f32[2,20,4,128]{3,2,1,0:T(4,128)S(1)} %collective-permute-done.12, f32[2,20,4,128]{3,2,1,0:T(4,128)S(1)} %collective-permute-done.11, f32[2,20,4,128]{3,2,1,0:T(4,128)S(1)} %collective-permute-done.10, f32[2,20,4,4,128]{4,3,2,1,0:T(4,128)S(1)} %bitcast_add_fusion, s32[]{:T(128)S(6)} %select_n.107), kind=kLoop, calls=%fused_computation.12 | loop fusion | flops 61440 | bytes 409604 | tf_op jit(solution)/shard_map/add | solution.py:273
  (13 shorter events, 0.2 us)
Async XLA Ops:
  0.6 11.6 %copy-start = (f32[2,20,4,128]{3,2,1,0:T(4,128)S(1)}, f32[2,20,4,128]{3,2,1,0:T(4,128)}, u32[]{:S(2)}) copy-start(f32[2,20,4,128]{3,2,1,0:T(4,128)} %param.6) | copy-start | bytes 245764
  0.6 9.5 %collective-permute-start = (f32[2,20,4,128]{3,2,1,0:T(4,128)}, f32[2,20,4,128]{3,2,1,0:T(4,128)S(1)}, u32[]{:S(2)}, u32[]{:S(2)}) collective-permute-start(f32[2,20,4,128]{3,2,1,0:T(4,128)} %param.6), channel_id=1, source_target_pairs={{0,2},{1,3},{2,4},{3,5},{4,6},{5,7},{6,0},{7,1},{8,10},{9,11},{10,... | collective-permute-start | bytes 245768 | tf_op jit(solution)/shard_map/ppermute | solution.py:245
  3.7 8.3 %collective-permute-start.1 = (f32[2,20,4,128]{3,2,1,0:T(4,128)}, f32[2,20,4,128]{3,2,1,0:T(4,128)S(1)}, u32[]{:S(2)}, u32[]{:S(2)}) collective-permute-start(f32[2,20,4,128]{3,2,1,0:T(4,128)} %param.6), channel_id=1, source_target_pairs={{0,4},{1,5},{2,6},{3,7},{4,0},{5,1},{6,2},{7,3},{8,12},{9,13},{10,... | collective-permute-start | bytes 245768 | tf_op jit(solution)/shard_map/ppermute | solution.py:245
  6.3 5.9 %collective-permute-start.2 = (f32[2,20,4,128]{3,2,1,0:T(4,128)}, f32[2,20,4,128]{3,2,1,0:T(4,128)S(1)}, u32[]{:S(2)}, u32[]{:S(2)}) collective-permute-start(f32[2,20,4,128]{3,2,1,0:T(4,128)} %param.6), channel_id=1, source_target_pairs={{0,6},{1,7},{2,0},{3,1},{4,2},{5,3},{6,4},{7,5},{8,14},{9,15},{10,... | collective-permute-start | bytes 245768 | tf_op jit(solution)/shard_map/ppermute | solution.py:245
  12.3 1.7 %collective-permute-start.3 = (f32[4,2,20,4,128]{4,3,2,1,0:T(4,128)S(1)}, f32[4,2,20,4,128]{4,3,2,1,0:T(4,128)S(1)}, u32[]{:S(2)}, u32[]{:S(2)}) collective-permute-start(f32[4,2,20,4,128]{4,3,2,1,0:T(4,128)S(1)} %get-tuple-element.13), channel_id=1, source_target_pairs={{0,1},{1,0},{2,3},{3,2},{4,5},{5,4},{6,7},{7,6},{8,9},{9,8},{10,11... | collective-permute-start | bytes 983048 | tf_op jit(solution)/shard_map/ppermute | solution.py:248
  15.1 0.7 %copy-start.1 = (s32[32,128]{1,0:T(8,128)S(1)}, s32[32,128]{1,0:T(8,128)}, u32[]{:S(2)}) copy-start(s32[32,128]{1,0:T(8,128)} %param.7) | copy-start | bytes 49156
  15.1 0.7 %copy-start.2 = (s32[32,128]{1,0:T(8,128)S(1)}, s32[32,128]{1,0:T(8,128)}, u32[]{:S(2)}) copy-start(s32[32,128]{1,0:T(8,128)} %param.8) | copy-start | bytes 49156
  17.4 9.4 %collective-permute-start.7 = (f32[2,122,2]{2,1,0:T(8,128)S(1)}, f32[2,122,2]{2,1,0:T(8,128)S(1)}, u32[]{:S(2)}, u32[]{:S(2)}) collective-permute-start(f32[2,122,2]{2,1,0:T(8,128)S(1)} %rev.11), channel_id=1, source_target_pairs={{0,16},{8,8},{16,0},{24,24},{1,17},{9,9},{17,1},{25,25},{2,18},{10... | collective-permute-start | bytes 5864 | tf_op jit(solution)/shard_map/ppermute | solution.py:20
  21.0 5.8 %collective-permute-start.8 = (f32[2,122,2]{2,1,0:T(8,128)S(1)}, f32[2,122,2]{2,1,0:T(8,128)S(1)}, u32[]{:S(2)}, u32[]{:S(2)}) collective-permute-start(f32[2,122,2]{2,1,0:T(8,128)S(1)} %rev.12), channel_id=1, source_target_pairs={{0,0},{8,24},{16,16},{24,8},{1,1},{9,25},{17,17},{25,9},{2,2},{10,... | collective-permute-start | bytes 5864 | tf_op jit(solution)/shard_map/ppermute | solution.py:20
  21.8 5.7 %collective-permute-start.4 = (f32[2,3904]{1,0:T(2,128)S(1)}, f32[2,3904]{1,0:T(2,128)S(1)}, u32[]{:S(2)}, u32[]{:S(2)}) collective-permute-start(f32[2,3904]{1,0:T(2,128)S(1)} %get-tuple-element.16), channel_id=1, source_target_pairs={{0,24},{8,0},{16,8},{24,16},{1,25},{9,1},{17,9},{25,17},{2,26},{10... | collective-permute-start | bytes 93704 | tf_op jit(solution)/shard_map/ppermute | solution.py:20
  23.3 5.1 %collective-permute-start.5 = (f32[2,3904]{1,0:T(2,128)S(1)}, f32[2,3904]{1,0:T(2,128)S(1)}, u32[]{:S(2)}, u32[]{:S(2)}) collective-permute-start(f32[2,3904]{1,0:T(2,128)S(1)} %get-tuple-element.17), channel_id=1, source_target_pairs={{0,8},{8,16},{16,24},{24,0},{1,9},{9,17},{17,25},{25,1},{2,10},{10... | collective-permute-start | bytes 93704 | tf_op jit(solution)/shard_map/ppermute | solution.py:20
  24.3 5.9 %collective-permute-start.6 = (f32[122,2,128]{2,1,0:T(2,128)S(1)}, f32[122,2,128]{2,1,0:T(2,128)S(1)}, u32[]{:S(2)}, u32[]{:S(2)}) collective-permute-start(f32[122,2,128]{2,1,0:T(2,128)S(1)} %rev.10), channel_id=1, source_target_pairs={{0,24},{8,16},{16,8},{24,0},{1,25},{9,17},{17,9},{25,1},{2,26},{10... | collective-permute-start | bytes 374792 | tf_op jit(solution)/shard_map/ppermute | solution.py:20
  39.9 1.7 %collective-permute-start.9 = (f32[2,20,4,4,128]{4,3,2,1,0:T(4,128)S(1)}, f32[2,20,4,4,128]{4,3,2,1,0:T(4,128)S(1)}, u32[]{:S(2)}, u32[]{:S(2)}) collective-permute-start(f32[2,20,4,4,128]{4,3,2,1,0:T(4,128)S(1)} %dynamic-slice_bitcast_fusion), channel_id=1, source_target_pairs={{0,1},{1,0},{2,3},{3,2},{4,5},{5,4},{6,7},{7,6},{8,9},{9,8},{10,11... | collective-permute-start | bytes 983048 | tf_op jit(solution)/shard_map/ppermute | solution.py:268
  41.8 7.2 %collective-permute-start.10 = (f32[2,20,4,128]{3,2,1,0:T(4,128)S(1)}, f32[2,20,4,128]{3,2,1,0:T(4,128)S(1)}, u32[]{:S(2)}, u32[]{:S(2)}) collective-permute-start(f32[2,20,4,128]{3,2,1,0:T(4,128)S(1)} %get-tuple-element.9), channel_id=1, source_target_pairs={{0,2},{1,3},{2,4},{3,5},{4,6},{5,7},{6,0},{7,1},{8,10},{9,11},{10,... | collective-permute-start | bytes 245768 | tf_op jit(solution)/shard_map/ppermute | solution.py:273
  43.8 7.9 %collective-permute-start.11 = (f32[2,20,4,128]{3,2,1,0:T(4,128)S(1)}, f32[2,20,4,128]{3,2,1,0:T(4,128)S(1)}, u32[]{:S(2)}, u32[]{:S(2)}) collective-permute-start(f32[2,20,4,128]{3,2,1,0:T(4,128)S(1)} %get-tuple-element.11), channel_id=1, source_target_pairs={{0,4},{1,5},{2,6},{3,7},{4,0},{5,1},{6,2},{7,3},{8,12},{9,13},{10,... | collective-permute-start | bytes 245768 | tf_op jit(solution)/shard_map/ppermute | solution.py:273
  45.7 6.2 %collective-permute-start.12 = (f32[2,20,4,128]{3,2,1,0:T(4,128)S(1)}, f32[2,20,4,128]{3,2,1,0:T(4,128)S(1)}, u32[]{:S(2)}, u32[]{:S(2)}) collective-permute-start(f32[2,20,4,128]{3,2,1,0:T(4,128)S(1)} %get-tuple-element.10), channel_id=1, source_target_pairs={{0,6},{1,7},{2,0},{3,1},{4,2},{5,3},{6,4},{7,5},{8,14},{9,15},{10,... | collective-permute-start | bytes 245768 | tf_op jit(solution)/shard_map/ppermute | solution.py:273

commit v22 on v18

--- a/solution.py
+++ b/solution.py
@@ -143,7 +143,6 @@
         u1_ref[c, k] = wet_ref[k] * (x + change + heat * src_ref[k])
         return carry
 
-    lax.fori_loop(0, planes, forward_first, 0, unroll=8)
 
     def forward_second(ck, carry):
         c = ck // levels
@@ -154,7 +153,6 @@
         fin_ref[c, k] = out[:ny, :width]
         return carry
 
-    lax.fori_loop(0, planes, forward_second, 0, unroll=8)
 
     def backward_second(ck, carry):
         c = ck // levels
@@ -163,7 +161,11 @@
         b_ref[c, k] = wet_ref[k] * (x + change)
         return carry
 
-    lax.fori_loop(0, planes, backward_second, 0, unroll=8)
+    def first_pair(ck, carry):
+        forward_first(ck, carry)
+        return backward_second(ck, carry)
+
+    lax.fori_loop(0, planes, first_pair, 0, unroll=4)
 
     def backward_first(ck, carry):
         c = ck // levels
@@ -172,7 +174,11 @@
         adj_ref[c, k] = (x + change)[:ny, :width]
         return carry
 
-    lax.fori_loop(0, planes, backward_first, 0, unroll=8)
+    def second_pair(ck, carry):
+        forward_second(ck, carry)
+        return backward_first(ck, carry)
+
+    lax.fori_loop(0, planes, second_pair, 0, unroll=4)
 
     def gradient(k, carry):
         g_east = jnp.zeros((ny, width), jnp.float32)

time: 52.4 us -> 52.2 us (level)
  no operation moved by 1% of the time
where the time goes in v22:
time: 52.2 us; the launch traced here: 51.7 us
  starting transfers between devices  20.2 us (39%)
  waiting for transfers between devices  11.8 us (23%)
  Pallas kernels  8.31 us (16%)
  local copies, waits for them, and re-layouts  5.59 us (11%)
  matrix products  2.96 us (6%)
  other arithmetic  1.87 us (4%)
  between operations  0.97 us (2%)
    ppermute x5, starting transfers between devices, shifted(): return lax.ppermute(x, 'space', perm)  8.58 us
    pallas_call x1, Pallas kernels, on_device(): pl.pallas_call(diffusion_kernel, out_shape=(field, field, jax.ShapeDtypeS...  8.31 us
    ppermute x3, starting transfers between devices, gathered_over_scen(): lax.ppermute(block, 'scen', [(q, (q // 2 + step) % chips * 2 + q % 2) for...  7.01 us
    ppermute x3, waiting for transfers between devices, summed_over_scen(): lax.ppermute(send, 'scen', [(q, (q // 2 + step) % chips * 2 + q % 2) for...  5.59 us
    ppermute x3, starting transfers between devices, summed_over_scen(): lax.ppermute(send, 'scen', [(q, (q // 2 + step) % chips * 2 + q % 2) for...  4.5 us
    dot_general x3, matrix products, contract(): lax.dot_general(a, b, (dims, ((), ())), precision=lax.Precision.HIGHEST,...  2.96 us
    unnamed x9, local copies, waits for them, and re-layouts  2.59 us
    ppermute x3, waiting for transfers between devices, gathered_over_scen(): lax.ppermute(block, 'scen', [(q, (q // 2 + step) % chips * 2 + q % 2) for...  2.12 us
  transfers between devices with their start and end apart: 13, of which 9 were waited for; matrix products, arithmetic and copies ran while one was open for 11% of the time, Pallas kernels for 0%

profile of v22, /device:TPU:0, one launch (start us, length us, event | category | flops | bytes accessed | tf_op | source)
XLA Modules:
  0.0 51.7 jit_solution(5465535664459569894)
XLA Ops:
  0.6 0.0 copy-start
  0.6 3.1 %collective-permute-start = (f32[2,20,4,128]{3,2,1,0:T(4,128)}, f32[2,20,4,128]{3,2,1,0:T(4,128)S(1)}, u32[]{:S(2)}, u32[]{:S(2)}) collective-permute-start(f32[2,20,4,128]{3,2,1,0:T(4,128)} %param.6), channel_id=1, source_target_pairs={{0,2},{1,3},{2,4},{3,5},{4,6},{5,7},{6,0},{7,1},{8,10},{9,11},{10,... | collective-permute-start | bytes 245768 | tf_op jit(solution)/shard_map/ppermute | solution.py:251
  3.7 2.6 %collective-permute-start.1 = (f32[2,20,4,128]{3,2,1,0:T(4,128)}, f32[2,20,4,128]{3,2,1,0:T(4,128)S(1)}, u32[]{:S(2)}, u32[]{:S(2)}) collective-permute-start(f32[2,20,4,128]{3,2,1,0:T(4,128)} %param.6), channel_id=1, source_target_pairs={{0,4},{1,5},{2,6},{3,7},{4,0},{5,1},{6,2},{7,3},{8,12},{9,13},{10,... | collective-permute-start | bytes 245768 | tf_op jit(solution)/shard_map/ppermute | solution.py:251
  6.3 1.3 %collective-permute-start.2 = (f32[2,20,4,128]{3,2,1,0:T(4,128)}, f32[2,20,4,128]{3,2,1,0:T(4,128)S(1)}, u32[]{:S(2)}, u32[]{:S(2)}) collective-permute-start(f32[2,20,4,128]{3,2,1,0:T(4,128)} %param.6), channel_id=1, source_target_pairs={{0,6},{1,7},{2,0},{3,1},{4,2},{5,3},{6,4},{7,5},{8,14},{9,15},{10,... | collective-permute-start | bytes 245768 | tf_op jit(solution)/shard_map/ppermute | solution.py:251
  7.7 1.1 %constant_dynamic-update-slice_fusion.2 = f32[122,32,128]{2,1,0:T(8,128)S(1)} fusion(f32[40,32,128]{2,1,0:T(8,128)} %bitcast.54), kind=kLoop, calls=%fused_computation.24 | loop fusion | bytes 1310720
  8.9 1.1 %constant_dynamic-update-slice_fusion.1 = f32[122,32,128]{2,1,0:T(8,128)S(1)} fusion(f32[122,32,128]{2,1,0:T(8,128)S(1)} %constant_dynamic-update-slice_fusion.2, f32[40,32,128]{2,1,0:T(8,128)} %bitcast.55), kind=kLoop, calls=%fused_computation.23 | loop fusion | bytes 1310720
  10.0 0.1 pad.4.clone
  10.1 0.0 collective-permute-done
  10.1 1.9 %collective-permute-done.1 = f32[2,20,4,128]{3,2,1,0:T(4,128)S(1)} collective-permute-done((f32[2,20,4,128]{3,2,1,0:T(4,128)}, f32[2,20,4,128]{3,2,1,0:T(4,128)S(1)}, u32[]{:S(2)}, u32[]{:S(2)}) %collective-permute-start.1) | collective-permute-done | bytes 81952 | tf_op jit(solution)/shard_map/ppermute | solution.py:251
  12.0 0.2 collective-permute-done.2
  12.2 0.0 copy-done
  12.2 0.1 fusion.29
  12.3 0.1 collective-permute-start.3
  12.4 0.1 and_or_fusion
  12.5 1.5 %collective-permute-done.3 = f32[4,2,20,4,128]{4,3,2,1,0:T(4,128)S(1)} collective-permute-done((f32[4,2,20,4,128]{4,3,2,1,0:T(4,128)S(1)}, f32[4,2,20,4,128]{4,3,2,1,0:T(4,128)S(1)}, u32[]{:S(2)}, u32[]{:S(2)}) %collective-permute-start.3) | collective-permute-done | bytes 327712 | tf_op jit(solution)/shard_map/ppermute | solution.py:254
  14.0 0.1 maximum_select_fusion
  14.2 0.9 %gather_fusion = f32[4,2,2,20,4,128]{5,4,3,2,1,0:T(4,128)S(1)} fusion(f32[4,2,2,20,4,128]{5,4,3,2,0,1:T(4,128)S(1)} %maximum_select_fusion, s32[1024]{0:T(1024)S(1)} %pad_clamp_fusion), kind=kCustom, calls=%fused_computation | custom fusion | bytes 1310736 | tf_op jit(solution)/shard_map/jit(_take)/gather | solution.py:257
  15.1 0.0 copy-start.1
  15.1 0.0 copy-start.2
  15.2 0.2 select_bitcast_fusion
  15.4 0.2 copy.24
  15.6 0.3 copy-done.1
  15.9 0.0 copy-done.2
  15.9 1.0 %fusion.9 = f32[4,3904]{1,0:T(4,128)S(1)} fusion(f32[3904,128]{1,0:T(8,128)S(1)} %bitcast.51, pred[128]{0:T(512)(128)(4,1)S(1)} %get-tuple-element.20, pred[128]{0:T(512)(128)(4,1)S(1)} %get-tuple-element.21, pred[128]{0:T(512)(128)(4,1)S(1)} %get-tuple-element.22, pred[128]{0:T(512)(128)(4,1)S(1)} %get-tuple-element.23, ...), kind=kOutput, calls=%fused_computation.34 | convolution fusion | flops 23989760 | bytes 2061840 | tf_op jit(solution)/shard_map/dot_general | solution.py:31
  16.9 0.1 reshape.79
  17.0 0.1 fusion.30
  17.2 0.2 rev.11
  17.4 3.4 %collective-permute-start.7 = (f32[2,122,2]{2,1,0:T(8,128)S(1)}, f32[2,122,2]{2,1,0:T(8,128)S(1)}, u32[]{:S(2)}, u32[]{:S(2)}) collective-permute-start(f32[2,122,2]{2,1,0:T(8,128)S(1)} %rev.11), channel_id=1, source_target_pairs={{0,16},{8,8},{16,0},{24,24},{1,17},{9,9},{17,1},{25,25},{2,18},{10... | collective-permute-start | bytes 5864 | tf_op jit(solution)/shard_map/ppermute | solution.py:18
  20.8 0.2 rev.12
  21.0 0.7 %collective-permute-start.8 = (f32[2,122,2]{2,1,0:T(8,128)S(1)}, f32[2,122,2]{2,1,0:T(8,128)S(1)}, u32[]{:S(2)}, u32[]{:S(2)}) collective-permute-start(f32[2,122,2]{2,1,0:T(8,128)S(1)} %rev.12), channel_id=1, source_target_pairs={{0,0},{8,24},{16,16},{24,8},{1,1},{9,25},{17,17},{25,9},{2,2},{10,... | collective-permute-start | bytes 5864 | tf_op jit(solution)/shard_map/ppermute | solution.py:18
  21.7 0.1 slice.29
  21.8 1.5 %collective-permute-start.4 = (f32[2,3904]{1,0:T(2,128)S(1)}, f32[2,3904]{1,0:T(2,128)S(1)}, u32[]{:S(2)}, u32[]{:S(2)}) collective-permute-start(f32[2,3904]{1,0:T(2,128)S(1)} %get-tuple-element.16), channel_id=1, source_target_pairs={{0,24},{8,0},{16,8},{24,16},{1,25},{9,1},{17,9},{25,17},{2,26},{10... | collective-permute-start | bytes 93704 | tf_op jit(solution)/shard_map/ppermute | solution.py:18
  23.3 0.6 %collective-permute-start.5 = (f32[2,3904]{1,0:T(2,128)S(1)}, f32[2,3904]{1,0:T(2,128)S(1)}, u32[]{:S(2)}, u32[]{:S(2)}) collective-permute-start(f32[2,3904]{1,0:T(2,128)S(1)} %get-tuple-element.17), channel_id=1, source_target_pairs={{0,8},{8,16},{16,24},{24,0},{1,9},{9,17},{17,25},{25,1},{2,10},{10... | collective-permute-start | bytes 93704 | tf_op jit(solution)/shard_map/ppermute | solution.py:18
  23.8 0.5 rev.10
  24.3 2.4 %collective-permute-start.6 = (f32[122,2,128]{2,1,0:T(2,128)S(1)}, f32[122,2,128]{2,1,0:T(2,128)S(1)}, u32[]{:S(2)}, u32[]{:S(2)}) collective-permute-start(f32[122,2,128]{2,1,0:T(2,128)S(1)} %rev.10), channel_id=1, source_target_pairs={{0,24},{8,16},{16,8},{24,0},{1,25},{9,17},{17,9},{25,1},{2,26},{10... | collective-permute-start | bytes 374792 | tf_op jit(solution)/shard_map/ppermute | solution.py:18
  26.7 0.0 collective-permute-done.7
  26.7 0.0 collective-permute-done.8
  26.8 0.2 reshape.91
  26.9 0.1 copy.30
  27.1 0.1 dot_general.16
  27.2 0.2 fusion
  27.4 0.1 copy.27
  27.5 0.0 collective-permute-done.4
  27.5 0.8 %collective-permute-done.5 = f32[2,3904]{1,0:T(2,128)S(1)} collective-permute-done((f32[2,3904]{1,0:T(2,128)S(1)}, f32[2,3904]{1,0:T(2,128)S(1)}, u32[]{:S(2)}, u32[]{:S(2)}) %collective-permute-start.5) | collective-permute-done | bytes 31264 | tf_op jit(solution)/shard_map/ppermute | solution.py:18
  28.3 1.7 %fusion.4 = f32[3904,128]{1,0:T(8,128)S(1)} fusion(pred[128,4]{0,1:T(4,128)(4,1)S(1)} %and_or_fusion, f32[2,3904]{1,0:T(2,128)S(1)} %collective-permute-done.5, f32[2,3904]{1,0:T(2,128)S(1)} %collective-permute-done.4), kind=kOutput, calls=%fused_computation.16 | convolution fusion | flops 24001792 | bytes 2061824 | tf_op jit(solution)/shard_map/dot_general | solution.py:31
  30.1 0.1 collective-permute-done.6
  30.2 0.5 maximum_maximum_fusion.x_ref
  30.7 8.3 %shard_map.76 = (f32[2,20,32,128]{3,2,1,0:T(8,128)}, f32[2,20,32,128]{3,2,1,0:T(8,128)}, f32[2,20,32,128]{3,2,1,0:T(8,128)S(1)}) custom-call(f32[122,40,256]{2,1,0:T(8,128)S(1)} %maximum_maximum_fusion.x_ref), custom_call_target="tpu_custom_call" | custom-call | tf_op jit(solution)/shard_map/pallas_call | solution.py:216
  39.0 0.1 dynamic-slice_bitcast_fusion
  39.1 0.1 collective-permute-start.9
  39.2 1.5 %collective-permute-done.9 = f32[2,20,4,4,128]{4,3,2,1,0:T(4,128)S(1)} collective-permute-done((f32[2,20,4,4,128]{4,3,2,1,0:T(4,128)S(1)}, f32[2,20,4,4,128]{4,3,2,1,0:T(4,128)S(1)}, u32[]{:S(2)}, u32[]{:S(2)}) %collective-permute-start.9) | collective-permute-done | bytes 327712 | tf_op jit(solution)/shard_map/ppermute | solution.py:274
  40.8 0.1 bitcast_add_fusion
  40.9 0.1 dynamic-slice_bitcast_fusion.3
  40.9 2.1 %collective-permute-start.10 = (f32[2,20,4,128]{3,2,1,0:T(4,128)S(1)}, f32[2,20,4,128]{3,2,1,0:T(4,128)S(1)}, u32[]{:S(2)}, u32[]{:S(2)}) collective-permute-start(f32[2,20,4,128]{3,2,1,0:T(4,128)S(1)} %get-tuple-element.9), channel_id=1, source_target_pairs={{0,2},{1,3},{2,4},{3,5},{4,6},{5,7},{6,0},{7,1},{8,10},{9,11},{10,... | collective-permute-start | bytes 245768 | tf_op jit(solution)/shard_map/ppermute | solution.py:279
  43.0 1.8 %collective-permute-start.11 = (f32[2,20,4,128]{3,2,1,0:T(4,128)S(1)}, f32[2,20,4,128]{3,2,1,0:T(4,128)S(1)}, u32[]{:S(2)}, u32[]{:S(2)}) collective-permute-start(f32[2,20,4,128]{3,2,1,0:T(4,128)S(1)} %get-tuple-element.11), channel_id=1, source_target_pairs={{0,4},{1,5},{2,6},{3,7},{4,0},{5,1},{6,2},{7,3},{8,12},{9,13},{10,... | collective-permute-start | bytes 245768 | tf_op jit(solution)/shard_map/ppermute | solution.py:279
  44.8 0.6 %collective-permute-start.12 = (f32[2,20,4,128]{3,2,1,0:T(4,128)S(1)}, f32[2,20,4,128]{3,2,1,0:T(4,128)S(1)}, u32[]{:S(2)}, u32[]{:S(2)}) collective-permute-start(f32[2,20,4,128]{3,2,1,0:T(4,128)S(1)} %get-tuple-element.10), channel_id=1, source_target_pairs={{0,6},{1,7},{2,0},{3,1},{4,2},{5,3},{6,4},{7,5},{8,14},{9,15},{10,... | collective-permute-start | bytes 245768 | tf_op jit(solution)/shard_map/ppermute | solution.py:279
  45.4 2.7 %collective-permute-done.10 = f32[2,20,4,128]{3,2,1,0:T(4,128)S(1)} collective-permute-done((f32[2,20,4,128]{3,2,1,0:T(4,128)S(1)}, f32[2,20,4,128]{3,2,1,0:T(4,128)S(1)}, u32[]{:S(2)}, u32[]{:S(2)}) %collective-permute-start.10) | collective-permute-done | bytes 81952 | tf_op jit(solution)/shard_map/ppermute | solution.py:279
  48.2 2.7 %collective-permute-done.11 = f32[2,20,4,128]{3,2,1,0:T(4,128)S(1)} collective-permute-done((f32[2,20,4,128]{3,2,1,0:T(4,128)S(1)}, f32[2,20,4,128]{3,2,1,0:T(4,128)S(1)}, u32[]{:S(2)}, u32[]{:S(2)}) %collective-permute-start.11) | collective-permute-done | bytes 81952 | tf_op jit(solution)/shard_map/ppermute | solution.py:279
  50.9 0.1 collective-permute-done.12
  51.0 0.7 %fusion.3 = f32[2,20,4,128]{3,2,1,0:T(4,128)} fusion(f32[2,20,4,128]{3,2,1,0:T(4,128)S(1)} %collective-permute-done.12, f32[2,20,4,128]{3,2,1,0:T(4,128)S(1)} %collective-permute-done.11, f32[2,20,4,128]{3,2,1,0:T(4,128)S(1)} %collective-permute-done.10, f32[2,20,4,4,128]{4,3,2,1,0:T(4,128)S(1)} %bitcast_add_fusion, s32[]{:T(128)S(6)} %select_n.107), kind=kLoop, calls=%fused_computation.12 | loop fusion | flops 61440 | bytes 409604 | tf_op jit(solution)/shard_map/add | solution.py:279
  (13 shorter events, 0.2 us)
Async XLA Ops:
  0.6 11.6 %copy-start = (f32[2,20,4,128]{3,2,1,0:T(4,128)S(1)}, f32[2,20,4,128]{3,2,1,0:T(4,128)}, u32[]{:S(2)}) copy-start(f32[2,20,4,128]{3,2,1,0:T(4,128)} %param.6) | copy-start | bytes 245764
  0.6 9.5 %collective-permute-start = (f32[2,20,4,128]{3,2,1,0:T(4,128)}, f32[2,20,4,128]{3,2,1,0:T(4,128)S(1)}, u32[]{:S(2)}, u32[]{:S(2)}) collective-permute-start(f32[2,20,4,128]{3,2,1,0:T(4,128)} %param.6), channel_id=1, source_target_pairs={{0,2},{1,3},{2,4},{3,5},{4,6},{5,7},{6,0},{7,1},{8,10},{9,11},{10,... | collective-permute-start | bytes 245768 | tf_op jit(solution)/shard_map/ppermute | solution.py:251
  3.7 8.3 %collective-permute-start.1 = (f32[2,20,4,128]{3,2,1,0:T(4,128)}, f32[2,20,4,128]{3,2,1,0:T(4,128)S(1)}, u32[]{:S(2)}, u32[]{:S(2)}) collective-permute-start(f32[2,20,4,128]{3,2,1,0:T(4,128)} %param.6), channel_id=1, source_target_pairs={{0,4},{1,5},{2,6},{3,7},{4,0},{5,1},{6,2},{7,3},{8,12},{9,13},{10,... | collective-permute-start | bytes 245768 | tf_op jit(solution)/shard_map/ppermute | solution.py:251
  6.3 5.9 %collective-permute-start.2 = (f32[2,20,4,128]{3,2,1,0:T(4,128)}, f32[2,20,4,128]{3,2,1,0:T(4,128)S(1)}, u32[]{:S(2)}, u32[]{:S(2)}) collective-permute-start(f32[2,20,4,128]{3,2,1,0:T(4,128)} %param.6), channel_id=1, source_target_pairs={{0,6},{1,7},{2,0},{3,1},{4,2},{5,3},{6,4},{7,5},{8,14},{9,15},{10,... | collective-permute-start | bytes 245768 | tf_op jit(solution)/shard_map/ppermute | solution.py:251
  12.3 1.7 %collective-permute-start.3 = (f32[4,2,20,4,128]{4,3,2,1,0:T(4,128)S(1)}, f32[4,2,20,4,128]{4,3,2,1,0:T(4,128)S(1)}, u32[]{:S(2)}, u32[]{:S(2)}) collective-permute-start(f32[4,2,20,4,128]{4,3,2,1,0:T(4,128)S(1)} %get-tuple-element.13), channel_id=1, source_target_pairs={{0,1},{1,0},{2,3},{3,2},{4,5},{5,4},{6,7},{7,6},{8,9},{9,8},{10,11... | collective-permute-start | bytes 983048 | tf_op jit(solution)/shard_map/ppermute | solution.py:254
  15.1 0.7 %copy-start.1 = (s32[32,128]{1,0:T(8,128)S(1)}, s32[32,128]{1,0:T(8,128)}, u32[]{:S(2)}) copy-start(s32[32,128]{1,0:T(8,128)} %param.7) | copy-start | bytes 49156
  15.1 0.7 %copy-start.2 = (s32[32,128]{1,0:T(8,128)S(1)}, s32[32,128]{1,0:T(8,128)}, u32[]{:S(2)}) copy-start(s32[32,128]{1,0:T(8,128)} %param.8) | copy-start | bytes 49156
  17.4 9.4 %collective-permute-start.7 = (f32[2,122,2]{2,1,0:T(8,128)S(1)}, f32[2,122,2]{2,1,0:T(8,128)S(1)}, u32[]{:S(2)}, u32[]{:S(2)}) collective-permute-start(f32[2,122,2]{2,1,0:T(8,128)S(1)} %rev.11), channel_id=1, source_target_pairs={{0,16},{8,8},{16,0},{24,24},{1,17},{9,9},{17,1},{25,25},{2,18},{10... | collective-permute-start | bytes 5864 | tf_op jit(solution)/shard_map/ppermute | solution.py:18
  21.0 5.8 %collective-permute-start.8 = (f32[2,122,2]{2,1,0:T(8,128)S(1)}, f32[2,122,2]{2,1,0:T(8,128)S(1)}, u32[]{:S(2)}, u32[]{:S(2)}) collective-permute-start(f32[2,122,2]{2,1,0:T(8,128)S(1)} %rev.12), channel_id=1, source_target_pairs={{0,0},{8,24},{16,16},{24,8},{1,1},{9,25},{17,17},{25,9},{2,2},{10,... | collective-permute-start | bytes 5864 | tf_op jit(solution)/shard_map/ppermute | solution.py:18
  21.8 5.7 %collective-permute-start.4 = (f32[2,3904]{1,0:T(2,128)S(1)}, f32[2,3904]{1,0:T(2,128)S(1)}, u32[]{:S(2)}, u32[]{:S(2)}) collective-permute-start(f32[2,3904]{1,0:T(2,128)S(1)} %get-tuple-element.16), channel_id=1, source_target_pairs={{0,24},{8,0},{16,8},{24,16},{1,25},{9,1},{17,9},{25,17},{2,26},{10... | collective-permute-start | bytes 93704 | tf_op jit(solution)/shard_map/ppermute | solution.py:18
  23.3 5.1 %collective-permute-start.5 = (f32[2,3904]{1,0:T(2,128)S(1)}, f32[2,3904]{1,0:T(2,128)S(1)}, u32[]{:S(2)}, u32[]{:S(2)}) collective-permute-start(f32[2,3904]{1,0:T(2,128)S(1)} %get-tuple-element.17), channel_id=1, source_target_pairs={{0,8},{8,16},{16,24},{24,0},{1,9},{9,17},{17,25},{25,1},{2,10},{10... | collective-permute-start | bytes 93704 | tf_op jit(solution)/shard_map/ppermute | solution.py:18
  24.3 5.9 %collective-permute-start.6 = (f32[122,2,128]{2,1,0:T(2,128)S(1)}, f32[122,2,128]{2,1,0:T(2,128)S(1)}, u32[]{:S(2)}, u32[]{:S(2)}) collective-permute-start(f32[122,2,128]{2,1,0:T(2,128)S(1)} %rev.10), channel_id=1, source_target_pairs={{0,24},{8,16},{16,8},{24,0},{1,25},{9,17},{17,9},{25,1},{2,26},{10... | collective-permute-start | bytes 374792 | tf_op jit(solution)/shard_map/ppermute | solution.py:18
  39.1 1.7 %collective-permute-start.9 = (f32[2,20,4,4,128]{4,3,2,1,0:T(4,128)S(1)}, f32[2,20,4,4,128]{4,3,2,1,0:T(4,128)S(1)}, u32[]{:S(2)}, u32[]{:S(2)}) collective-permute-start(f32[2,20,4,4,128]{4,3,2,1,0:T(4,128)S(1)} %dynamic-slice_bitcast_fusion), channel_id=1, source_target_pairs={{0,1},{1,0},{2,3},{3,2},{4,5},{5,4},{6,7},{7,6},{8,9},{9,8},{10,11... | collective-permute-start | bytes 983048 | tf_op jit(solution)/shard_map/ppermute | solution.py:274
  40.9 7.2 %collective-permute-start.10 = (f32[2,20,4,128]{3,2,1,0:T(4,128)S(1)}, f32[2,20,4,128]{3,2,1,0:T(4,128)S(1)}, u32[]{:S(2)}, u32[]{:S(2)}) collective-permute-start(f32[2,20,4,128]{3,2,1,0:T(4,128)S(1)} %get-tuple-element.9), channel_id=1, source_target_pairs={{0,2},{1,3},{2,4},{3,5},{4,6},{5,7},{6,0},{7,1},{8,10},{9,11},{10,... | collective-permute-start | bytes 245768 | tf_op jit(solution)/shard_map/ppermute | solution.py:279
  43.0 7.9 %collective-permute-start.11 = (f32[2,20,4,128]{3,2,1,0:T(4,128)S(1)}, f32[2,20,4,128]{3,2,1,0:T(4,128)S(1)}, u32[]{:S(2)}, u32[]{:S(2)}) collective-permute-start(f32[2,20,4,128]{3,2,1,0:T(4,128)S(1)} %get-tuple-element.11), channel_id=1, source_target_pairs={{0,4},{1,5},{2,6},{3,7},{4,0},{5,1},{6,2},{7,3},{8,12},{9,13},{10,... | collective-permute-start | bytes 245768 | tf_op jit(solution)/shard_map/ppermute | solution.py:279
  44.8 6.2 %collective-permute-start.12 = (f32[2,20,4,128]{3,2,1,0:T(4,128)S(1)}, f32[2,20,4,128]{3,2,1,0:T(4,128)S(1)}, u32[]{:S(2)}, u32[]{:S(2)}) collective-permute-start(f32[2,20,4,128]{3,2,1,0:T(4,128)S(1)} %get-tuple-element.10), channel_id=1, source_target_pairs={{0,6},{1,7},{2,0},{3,1},{4,2},{5,3},{6,4},{7,5},{8,14},{9,15},{10,... | collective-permute-start | bytes 245768 | tf_op jit(solution)/shard_map/ppermute | solution.py:279

commit v23 on v22

--- a/solution.py
+++ b/solution.py
@@ -165,7 +165,7 @@
         forward_first(ck, carry)
         return backward_second(ck, carry)
 
-    lax.fori_loop(0, planes, first_pair, 0, unroll=4)
+    lax.fori_loop(0, planes, first_pair, 0, unroll=8)
 
     def backward_first(ck, carry):
         c = ck // levels
@@ -178,7 +178,7 @@
         forward_second(ck, carry)
         return backward_first(ck, carry)
 
-    lax.fori_loop(0, planes, second_pair, 0, unroll=4)
+    lax.fori_loop(0, planes, second_pair, 0, unroll=8)
 
     def gradient(k, carry):
         g_east = jnp.zeros((ny, width), jnp.float32)

time: 52.2 us -> 55.4 us (1.061)
  Pallas kernels: 8.31 us -> 11.5 us
    pallas_call x1, Pallas kernels: 8.31 us -> 11.5 us  [on_device(): pl.pallas_call(diffusion_kernel, out_shape=(field, field, jax.ShapeDtypeS...]
  transfers between devices with their start and end apart: 13 -> 13, of which waited for: 9 -> 9; matrix products, arithmetic and copies ran while one was open for 11% -> 10% of each run, Pallas kernels for 0% -> 0%
where the time goes in v23:
time: 55.4 us; the launch traced here: 54.8 us
  starting transfers between devices  20.2 us (36%)
  waiting for transfers between devices  11.8 us (21%)
  Pallas kernels  11.5 us (21%)
  local copies, waits for them, and re-layouts  5.59 us (10%)
  matrix products  2.96 us (5%)
  other arithmetic  1.87 us (3%)
  between operations  0.97 us (2%)
    pallas_call x1, Pallas kernels, on_device(): pl.pallas_call(diffusion_kernel, out_shape=(field, field, jax.ShapeDtypeS...  11.5 us
    ppermute x5, starting transfers between devices, shifted(): return lax.ppermute(x, 'space', perm)  8.58 us
    ppermute x3, starting transfers between devices, gathered_over_scen(): lax.ppermute(block, 'scen', [(q, (q // 2 + step) % chips * 2 + q % 2) for...  7.01 us
    ppermute x3, waiting for transfers between devices, summed_over_scen(): lax.ppermute(send, 'scen', [(q, (q // 2 + step) % chips * 2 + q % 2) for...  5.59 us
    ppermute x3, starting transfers between devices, summed_over_scen(): lax.ppermute(send, 'scen', [(q, (q // 2 + step) % chips * 2 + q % 2) for...  4.5 us
    dot_general x3, matrix products, contract(): lax.dot_general(a, b, (dims, ((), ())), precision=lax.Precision.HIGHEST,...  2.96 us
    unnamed x9, local copies, waits for them, and re-layouts  2.59 us
    ppermute x3, waiting for transfers between devices, gathered_over_scen(): lax.ppermute(block, 'scen', [(q, (q // 2 + step) % chips * 2 + q % 2) for...  2.12 us
  transfers between devices with their start and end apart: 13, of which 9 were waited for; matrix products, arithmetic and copies ran while one was open for 10% of the time, Pallas kernels for 0%

profile of v23, /device:TPU:0, one launch (start us, length us, event | category | flops | bytes accessed | tf_op | source)
XLA Modules:
  0.0 54.8 jit_solution(8591023159031999013)
XLA Ops:
  0.6 0.0 copy-start
  0.6 3.1 %collective-permute-start = (f32[2,20,4,128]{3,2,1,0:T(4,128)}, f32[2,20,4,128]{3,2,1,0:T(4,128)S(1)}, u32[]{:S(2)}, u32[]{:S(2)}) collective-permute-start(f32[2,20,4,128]{3,2,1,0:T(4,128)} %param.6), channel_id=1, source_target_pairs={{0,2},{1,3},{2,4},{3,5},{4,6},{5,7},{6,0},{7,1},{8,10},{9,11},{10,... | collective-permute-start | bytes 245768 | tf_op jit(solution)/shard_map/ppermute | solution.py:251
  3.7 2.6 %collective-permute-start.1 = (f32[2,20,4,128]{3,2,1,0:T(4,128)}, f32[2,20,4,128]{3,2,1,0:T(4,128)S(1)}, u32[]{:S(2)}, u32[]{:S(2)}) collective-permute-start(f32[2,20,4,128]{3,2,1,0:T(4,128)} %param.6), channel_id=1, source_target_pairs={{0,4},{1,5},{2,6},{3,7},{4,0},{5,1},{6,2},{7,3},{8,12},{9,13},{10,... | collective-permute-start | bytes 245768 | tf_op jit(solution)/shard_map/ppermute | solution.py:251
  6.3 1.3 %collective-permute-start.2 = (f32[2,20,4,128]{3,2,1,0:T(4,128)}, f32[2,20,4,128]{3,2,1,0:T(4,128)S(1)}, u32[]{:S(2)}, u32[]{:S(2)}) collective-permute-start(f32[2,20,4,128]{3,2,1,0:T(4,128)} %param.6), channel_id=1, source_target_pairs={{0,6},{1,7},{2,0},{3,1},{4,2},{5,3},{6,4},{7,5},{8,14},{9,15},{10,... | collective-permute-start | bytes 245768 | tf_op jit(solution)/shard_map/ppermute | solution.py:251
  7.7 1.1 %constant_dynamic-update-slice_fusion.2 = f32[122,32,128]{2,1,0:T(8,128)S(1)} fusion(f32[40,32,128]{2,1,0:T(8,128)} %bitcast.54), kind=kLoop, calls=%fused_computation.24 | loop fusion | bytes 1310720
  8.9 1.1 %constant_dynamic-update-slice_fusion.1 = f32[122,32,128]{2,1,0:T(8,128)S(1)} fusion(f32[122,32,128]{2,1,0:T(8,128)S(1)} %constant_dynamic-update-slice_fusion.2, f32[40,32,128]{2,1,0:T(8,128)} %bitcast.55), kind=kLoop, calls=%fused_computation.23 | loop fusion | bytes 1310720
  10.0 0.1 pad.4.clone
  10.1 0.0 collective-permute-done
  10.1 1.9 %collective-permute-done.1 = f32[2,20,4,128]{3,2,1,0:T(4,128)S(1)} collective-permute-done((f32[2,20,4,128]{3,2,1,0:T(4,128)}, f32[2,20,4,128]{3,2,1,0:T(4,128)S(1)}, u32[]{:S(2)}, u32[]{:S(2)}) %collective-permute-start.1) | collective-permute-done | bytes 81952 | tf_op jit(solution)/shard_map/ppermute | solution.py:251
  12.0 0.2 collective-permute-done.2
  12.2 0.0 copy-done
  12.2 0.1 fusion.29
  12.3 0.1 collective-permute-start.3
  12.4 0.1 and_or_fusion
  12.5 1.5 %collective-permute-done.3 = f32[4,2,20,4,128]{4,3,2,1,0:T(4,128)S(1)} collective-permute-done((f32[4,2,20,4,128]{4,3,2,1,0:T(4,128)S(1)}, f32[4,2,20,4,128]{4,3,2,1,0:T(4,128)S(1)}, u32[]{:S(2)}, u32[]{:S(2)}) %collective-permute-start.3) | collective-permute-done | bytes 327712 | tf_op jit(solution)/shard_map/ppermute | solution.py:254
  14.0 0.1 maximum_select_fusion
  14.2 0.9 %gather_fusion = f32[4,2,2,20,4,128]{5,4,3,2,1,0:T(4,128)S(1)} fusion(f32[4,2,2,20,4,128]{5,4,3,2,0,1:T(4,128)S(1)} %maximum_select_fusion, s32[1024]{0:T(1024)S(1)} %pad_clamp_fusion), kind=kCustom, calls=%fused_computation | custom fusion | bytes 1310736 | tf_op jit(solution)/shard_map/jit(_take)/gather | solution.py:257
  15.1 0.0 copy-start.1
  15.1 0.0 copy-start.2
  15.2 0.2 select_bitcast_fusion
  15.4 0.2 copy.24
  15.6 0.3 copy-done.1
  15.9 0.0 copy-done.2
  15.9 1.0 %fusion.9 = f32[4,3904]{1,0:T(4,128)S(1)} fusion(f32[3904,128]{1,0:T(8,128)S(1)} %bitcast.51, pred[128]{0:T(512)(128)(4,1)S(1)} %get-tuple-element.20, pred[128]{0:T(512)(128)(4,1)S(1)} %get-tuple-element.21, pred[128]{0:T(512)(128)(4,1)S(1)} %get-tuple-element.22, pred[128]{0:T(512)(128)(4,1)S(1)} %get-tuple-element.23, ...), kind=kOutput, calls=%fused_computation.34 | convolution fusion | flops 23989760 | bytes 2061840 | tf_op jit(solution)/shard_map/dot_general | solution.py:31
  16.9 0.1 reshape.79
  17.0 0.1 fusion.30
  17.2 0.2 rev.11
  17.4 3.4 %collective-permute-start.7 = (f32[2,122,2]{2,1,0:T(8,128)S(1)}, f32[2,122,2]{2,1,0:T(8,128)S(1)}, u32[]{:S(2)}, u32[]{:S(2)}) collective-permute-start(f32[2,122,2]{2,1,0:T(8,128)S(1)} %rev.11), channel_id=1, source_target_pairs={{0,16},{8,8},{16,0},{24,24},{1,17},{9,9},{17,1},{25,25},{2,18},{10... | collective-permute-start | bytes 5864 | tf_op jit(solution)/shard_map/ppermute | solution.py:18
  20.8 0.2 rev.12
  21.0 0.7 %collective-permute-start.8 = (f32[2,122,2]{2,1,0:T(8,128)S(1)}, f32[2,122,2]{2,1,0:T(8,128)S(1)}, u32[]{:S(2)}, u32[]{:S(2)}) collective-permute-start(f32[2,122,2]{2,1,0:T(8,128)S(1)} %rev.12), channel_id=1, source_target_pairs={{0,0},{8,24},{16,16},{24,8},{1,1},{9,25},{17,17},{25,9},{2,2},{10,... | collective-permute-start | bytes 5864 | tf_op jit(solution)/shard_map/ppermute | solution.py:18
  21.7 0.1 slice.29
  21.8 1.5 %collective-permute-start.4 = (f32[2,3904]{1,0:T(2,128)S(1)}, f32[2,3904]{1,0:T(2,128)S(1)}, u32[]{:S(2)}, u32[]{:S(2)}) collective-permute-start(f32[2,3904]{1,0:T(2,128)S(1)} %get-tuple-element.16), channel_id=1, source_target_pairs={{0,24},{8,0},{16,8},{24,16},{1,25},{9,1},{17,9},{25,17},{2,26},{10... | collective-permute-start | bytes 93704 | tf_op jit(solution)/shard_map/ppermute | solution.py:18
  23.3 0.6 %collective-permute-start.5 = (f32[2,3904]{1,0:T(2,128)S(1)}, f32[2,3904]{1,0:T(2,128)S(1)}, u32[]{:S(2)}, u32[]{:S(2)}) collective-permute-start(f32[2,3904]{1,0:T(2,128)S(1)} %get-tuple-element.17), channel_id=1, source_target_pairs={{0,8},{8,16},{16,24},{24,0},{1,9},{9,17},{17,25},{25,1},{2,10},{10... | collective-permute-start | bytes 93704 | tf_op jit(solution)/shard_map/ppermute | solution.py:18
  23.8 0.5 rev.10
  24.3 2.4 %collective-permute-start.6 = (f32[122,2,128]{2,1,0:T(2,128)S(1)}, f32[122,2,128]{2,1,0:T(2,128)S(1)}, u32[]{:S(2)}, u32[]{:S(2)}) collective-permute-start(f32[122,2,128]{2,1,0:T(2,128)S(1)} %rev.10), channel_id=1, source_target_pairs={{0,24},{8,16},{16,8},{24,0},{1,25},{9,17},{17,9},{25,1},{2,26},{10... | collective-permute-start | bytes 374792 | tf_op jit(solution)/shard_map/ppermute | solution.py:18
  26.7 0.0 collective-permute-done.7
  26.7 0.0 collective-permute-done.8
  26.8 0.2 reshape.91
  26.9 0.1 copy.30
  27.1 0.1 dot_general.16
  27.2 0.2 fusion
  27.4 0.1 copy.27
  27.5 0.0 collective-permute-done.4
  27.5 0.8 %collective-permute-done.5 = f32[2,3904]{1,0:T(2,128)S(1)} collective-permute-done((f32[2,3904]{1,0:T(2,128)S(1)}, f32[2,3904]{1,0:T(2,128)S(1)}, u32[]{:S(2)}, u32[]{:S(2)}) %collective-permute-start.5) | collective-permute-done | bytes 31264 | tf_op jit(solution)/shard_map/ppermute | solution.py:18
  28.3 1.7 %fusion.4 = f32[3904,128]{1,0:T(8,128)S(1)} fusion(pred[128,4]{0,1:T(4,128)(4,1)S(1)} %and_or_fusion, f32[2,3904]{1,0:T(2,128)S(1)} %collective-permute-done.5, f32[2,3904]{1,0:T(2,128)S(1)} %collective-permute-done.4), kind=kOutput, calls=%fused_computation.16 | convolution fusion | flops 24001792 | bytes 2061824 | tf_op jit(solution)/shard_map/dot_general | solution.py:31
  30.1 0.1 collective-permute-done.6
  30.2 0.5 maximum_maximum_fusion.x_ref
  30.7 11.5 %shard_map.76 = (f32[2,20,32,128]{3,2,1,0:T(8,128)}, f32[2,20,32,128]{3,2,1,0:T(8,128)}, f32[2,20,32,128]{3,2,1,0:T(8,128)S(1)}) custom-call(f32[122,40,256]{2,1,0:T(8,128)S(1)} %maximum_maximum_fusion.x_ref), custom_call_target="tpu_custom_call" | custom-call | tf_op jit(solution)/shard_map/pallas_call | solution.py:216
  42.2 0.1 dynamic-slice_bitcast_fusion
  42.2 0.1 collective-permute-start.9
  42.4 1.5 %collective-permute-done.9 = f32[2,20,4,4,128]{4,3,2,1,0:T(4,128)S(1)} collective-permute-done((f32[2,20,4,4,128]{4,3,2,1,0:T(4,128)S(1)}, f32[2,20,4,4,128]{4,3,2,1,0:T(4,128)S(1)}, u32[]{:S(2)}, u32[]{:S(2)}) %collective-permute-start.9) | collective-permute-done | bytes 327712 | tf_op jit(solution)/shard_map/ppermute | solution.py:274
  43.9 0.1 bitcast_add_fusion
  44.0 0.1 dynamic-slice_bitcast_fusion.3
  44.1 2.1 %collective-permute-start.10 = (f32[2,20,4,128]{3,2,1,0:T(4,128)S(1)}, f32[2,20,4,128]{3,2,1,0:T(4,128)S(1)}, u32[]{:S(2)}, u32[]{:S(2)}) collective-permute-start(f32[2,20,4,128]{3,2,1,0:T(4,128)S(1)} %get-tuple-element.9), channel_id=1, source_target_pairs={{0,2},{1,3},{2,4},{3,5},{4,6},{5,7},{6,0},{7,1},{8,10},{9,11},{10,... | collective-permute-start | bytes 245768 | tf_op jit(solution)/shard_map/ppermute | solution.py:279
  46.1 1.8 %collective-permute-start.11 = (f32[2,20,4,128]{3,2,1,0:T(4,128)S(1)}, f32[2,20,4,128]{3,2,1,0:T(4,128)S(1)}, u32[]{:S(2)}, u32[]{:S(2)}) collective-permute-start(f32[2,20,4,128]{3,2,1,0:T(4,128)S(1)} %get-tuple-element.11), channel_id=1, source_target_pairs={{0,4},{1,5},{2,6},{3,7},{4,0},{5,1},{6,2},{7,3},{8,12},{9,13},{10,... | collective-permute-start | bytes 245768 | tf_op jit(solution)/shard_map/ppermute | solution.py:279
  48.0 0.6 %collective-permute-start.12 = (f32[2,20,4,128]{3,2,1,0:T(4,128)S(1)}, f32[2,20,4,128]{3,2,1,0:T(4,128)S(1)}, u32[]{:S(2)}, u32[]{:S(2)}) collective-permute-start(f32[2,20,4,128]{3,2,1,0:T(4,128)S(1)} %get-tuple-element.10), channel_id=1, source_target_pairs={{0,6},{1,7},{2,0},{3,1},{4,2},{5,3},{6,4},{7,5},{8,14},{9,15},{10,... | collective-permute-start | bytes 245768 | tf_op jit(solution)/shard_map/ppermute | solution.py:279
  48.6 2.7 %collective-permute-done.10 = f32[2,20,4,128]{3,2,1,0:T(4,128)S(1)} collective-permute-done((f32[2,20,4,128]{3,2,1,0:T(4,128)S(1)}, f32[2,20,4,128]{3,2,1,0:T(4,128)S(1)}, u32[]{:S(2)}, u32[]{:S(2)}) %collective-permute-start.10) | collective-permute-done | bytes 81952 | tf_op jit(solution)/shard_map/ppermute | solution.py:279
  51.3 2.7 %collective-permute-done.11 = f32[2,20,4,128]{3,2,1,0:T(4,128)S(1)} collective-permute-done((f32[2,20,4,128]{3,2,1,0:T(4,128)S(1)}, f32[2,20,4,128]{3,2,1,0:T(4,128)S(1)}, u32[]{:S(2)}, u32[]{:S(2)}) %collective-permute-start.11) | collective-permute-done | bytes 81952 | tf_op jit(solution)/shard_map/ppermute | solution.py:279
  54.0 0.1 collective-permute-done.12
  54.2 0.7 %fusion.3 = f32[2,20,4,128]{3,2,1,0:T(4,128)} fusion(f32[2,20,4,128]{3,2,1,0:T(4,128)S(1)} %collective-permute-done.12, f32[2,20,4,128]{3,2,1,0:T(4,128)S(1)} %collective-permute-done.11, f32[2,20,4,128]{3,2,1,0:T(4,128)S(1)} %collective-permute-done.10, f32[2,20,4,4,128]{4,3,2,1,0:T(4,128)S(1)} %bitcast_add_fusion, s32[]{:T(128)S(6)} %select_n.107), kind=kLoop, calls=%fused_computation.12 | loop fusion | flops 61440 | bytes 409604 | tf_op jit(solution)/shard_map/add | solution.py:279
  (13 shorter events, 0.2 us)
Async XLA Ops:
  0.6 11.6 %copy-start = (f32[2,20,4,128]{3,2,1,0:T(4,128)S(1)}, f32[2,20,4,128]{3,2,1,0:T(4,128)}, u32[]{:S(2)}) copy-start(f32[2,20,4,128]{3,2,1,0:T(4,128)} %param.6) | copy-start | bytes 245764
  0.6 9.5 %collective-permute-start = (f32[2,20,4,128]{3,2,1,0:T(4,128)}, f32[2,20,4,128]{3,2,1,0:T(4,128)S(1)}, u32[]{:S(2)}, u32[]{:S(2)}) collective-permute-start(f32[2,20,4,128]{3,2,1,0:T(4,128)} %param.6), channel_id=1, source_target_pairs={{0,2},{1,3},{2,4},{3,5},{4,6},{5,7},{6,0},{7,1},{8,10},{9,11},{10,... | collective-permute-start | bytes 245768 | tf_op jit(solution)/shard_map/ppermute | solution.py:251
  3.7 8.3 %collective-permute-start.1 = (f32[2,20,4,128]{3,2,1,0:T(4,128)}, f32[2,20,4,128]{3,2,1,0:T(4,128)S(1)}, u32[]{:S(2)}, u32[]{:S(2)}) collective-permute-start(f32[2,20,4,128]{3,2,1,0:T(4,128)} %param.6), channel_id=1, source_target_pairs={{0,4},{1,5},{2,6},{3,7},{4,0},{5,1},{6,2},{7,3},{8,12},{9,13},{10,... | collective-permute-start | bytes 245768 | tf_op jit(solution)/shard_map/ppermute | solution.py:251
  6.3 5.9 %collective-permute-start.2 = (f32[2,20,4,128]{3,2,1,0:T(4,128)}, f32[2,20,4,128]{3,2,1,0:T(4,128)S(1)}, u32[]{:S(2)}, u32[]{:S(2)}) collective-permute-start(f32[2,20,4,128]{3,2,1,0:T(4,128)} %param.6), channel_id=1, source_target_pairs={{0,6},{1,7},{2,0},{3,1},{4,2},{5,3},{6,4},{7,5},{8,14},{9,15},{10,... | collective-permute-start | bytes 245768 | tf_op jit(solution)/shard_map/ppermute | solution.py:251
  12.3 1.7 %collective-permute-start.3 = (f32[4,2,20,4,128]{4,3,2,1,0:T(4,128)S(1)}, f32[4,2,20,4,128]{4,3,2,1,0:T(4,128)S(1)}, u32[]{:S(2)}, u32[]{:S(2)}) collective-permute-start(f32[4,2,20,4,128]{4,3,2,1,0:T(4,128)S(1)} %get-tuple-element.13), channel_id=1, source_target_pairs={{0,1},{1,0},{2,3},{3,2},{4,5},{5,4},{6,7},{7,6},{8,9},{9,8},{10,11... | collective-permute-start | bytes 983048 | tf_op jit(solution)/shard_map/ppermute | solution.py:254
  15.1 0.7 %copy-start.1 = (s32[32,128]{1,0:T(8,128)S(1)}, s32[32,128]{1,0:T(8,128)}, u32[]{:S(2)}) copy-start(s32[32,128]{1,0:T(8,128)} %param.7) | copy-start | bytes 49156
  15.1 0.7 %copy-start.2 = (s32[32,128]{1,0:T(8,128)S(1)}, s32[32,128]{1,0:T(8,128)}, u32[]{:S(2)}) copy-start(s32[32,128]{1,0:T(8,128)} %param.8) | copy-start | bytes 49156
  17.4 9.4 %collective-permute-start.7 = (f32[2,122,2]{2,1,0:T(8,128)S(1)}, f32[2,122,2]{2,1,0:T(8,128)S(1)}, u32[]{:S(2)}, u32[]{:S(2)}) collective-permute-start(f32[2,122,2]{2,1,0:T(8,128)S(1)} %rev.11), channel_id=1, source_target_pairs={{0,16},{8,8},{16,0},{24,24},{1,17},{9,9},{17,1},{25,25},{2,18},{10... | collective-permute-start | bytes 5864 | tf_op jit(solution)/shard_map/ppermute | solution.py:18
  21.0 5.8 %collective-permute-start.8 = (f32[2,122,2]{2,1,0:T(8,128)S(1)}, f32[2,122,2]{2,1,0:T(8,128)S(1)}, u32[]{:S(2)}, u32[]{:S(2)}) collective-permute-start(f32[2,122,2]{2,1,0:T(8,128)S(1)} %rev.12), channel_id=1, source_target_pairs={{0,0},{8,24},{16,16},{24,8},{1,1},{9,25},{17,17},{25,9},{2,2},{10,... | collective-permute-start | bytes 5864 | tf_op jit(solution)/shard_map/ppermute | solution.py:18
  21.8 5.7 %collective-permute-start.4 = (f32[2,3904]{1,0:T(2,128)S(1)}, f32[2,3904]{1,0:T(2,128)S(1)}, u32[]{:S(2)}, u32[]{:S(2)}) collective-permute-start(f32[2,3904]{1,0:T(2,128)S(1)} %get-tuple-element.16), channel_id=1, source_target_pairs={{0,24},{8,0},{16,8},{24,16},{1,25},{9,1},{17,9},{25,17},{2,26},{10... | collective-permute-start | bytes 93704 | tf_op jit(solution)/shard_map/ppermute | solution.py:18
  23.3 5.1 %collective-permute-start.5 = (f32[2,3904]{1,0:T(2,128)S(1)}, f32[2,3904]{1,0:T(2,128)S(1)}, u32[]{:S(2)}, u32[]{:S(2)}) collective-permute-start(f32[2,3904]{1,0:T(2,128)S(1)} %get-tuple-element.17), channel_id=1, source_target_pairs={{0,8},{8,16},{16,24},{24,0},{1,9},{9,17},{17,25},{25,1},{2,10},{10... | collective-permute-start | bytes 93704 | tf_op jit(solution)/shard_map/ppermute | solution.py:18
  24.3 5.9 %collective-permute-start.6 = (f32[122,2,128]{2,1,0:T(2,128)S(1)}, f32[122,2,128]{2,1,0:T(2,128)S(1)}, u32[]{:S(2)}, u32[]{:S(2)}) collective-permute-start(f32[122,2,128]{2,1,0:T(2,128)S(1)} %rev.10), channel_id=1, source_target_pairs={{0,24},{8,16},{16,8},{24,0},{1,25},{9,17},{17,9},{25,1},{2,26},{10... | collective-permute-start | bytes 374792 | tf_op jit(solution)/shard_map/ppermute | solution.py:18
  42.2 1.7 %collective-permute-start.9 = (f32[2,20,4,4,128]{4,3,2,1,0:T(4,128)S(1)}, f32[2,20,4,4,128]{4,3,2,1,0:T(4,128)S(1)}, u32[]{:S(2)}, u32[]{:S(2)}) collective-permute-start(f32[2,20,4,4,128]{4,3,2,1,0:T(4,128)S(1)} %dynamic-slice_bitcast_fusion), channel_id=1, source_target_pairs={{0,1},{1,0},{2,3},{3,2},{4,5},{5,4},{6,7},{7,6},{8,9},{9,8},{10,11... | collective-permute-start | bytes 983048 | tf_op jit(solution)/shard_map/ppermute | solution.py:274
  44.1 7.2 %collective-permute-start.10 = (f32[2,20,4,128]{3,2,1,0:T(4,128)S(1)}, f32[2,20,4,128]{3,2,1,0:T(4,128)S(1)}, u32[]{:S(2)}, u32[]{:S(2)}) collective-permute-start(f32[2,20,4,128]{3,2,1,0:T(4,128)S(1)} %get-tuple-element.9), channel_id=1, source_target_pairs={{0,2},{1,3},{2,4},{3,5},{4,6},{5,7},{6,0},{7,1},{8,10},{9,11},{10,... | collective-permute-start | bytes 245768 | tf_op jit(solution)/shard_map/ppermute | solution.py:279
  46.1 7.9 %collective-permute-start.11 = (f32[2,20,4,128]{3,2,1,0:T(4,128)S(1)}, f32[2,20,4,128]{3,2,1,0:T(4,128)S(1)}, u32[]{:S(2)}, u32[]{:S(2)}) collective-permute-start(f32[2,20,4,128]{3,2,1,0:T(4,128)S(1)} %get-tuple-element.11), channel_id=1, source_target_pairs={{0,4},{1,5},{2,6},{3,7},{4,0},{5,1},{6,2},{7,3},{8,12},{9,13},{10,... | collective-permute-start | bytes 245768 | tf_op jit(solution)/shard_map/ppermute | solution.py:279
  48.0 6.2 %collective-permute-start.12 = (f32[2,20,4,128]{3,2,1,0:T(4,128)S(1)}, f32[2,20,4,128]{3,2,1,0:T(4,128)S(1)}, u32[]{:S(2)}, u32[]{:S(2)}) collective-permute-start(f32[2,20,4,128]{3,2,1,0:T(4,128)S(1)} %get-tuple-element.10), channel_id=1, source_target_pairs={{0,6},{1,7},{2,0},{3,1},{4,2},{5,3},{6,4},{7,5},{8,14},{9,15},{10,... | collective-permute-start | bytes 245768 | tf_op jit(solution)/shard_map/ppermute | solution.py:279

commit v24 on v23

--- a/solution.py
+++ b/solution.py
@@ -165,7 +165,7 @@
         forward_first(ck, carry)
         return backward_second(ck, carry)
 
-    lax.fori_loop(0, planes, first_pair, 0, unroll=8)
+    lax.fori_loop(0, planes, first_pair, 0, unroll=5)
 
     def backward_first(ck, carry):
         c = ck // levels
@@ -178,7 +178,7 @@
         forward_second(ck, carry)
         return backward_first(ck, carry)
 
-    lax.fori_loop(0, planes, second_pair, 0, unroll=8)
+    lax.fori_loop(0, planes, second_pair, 0, unroll=5)
 
     def gradient(k, carry):
         g_east = jnp.zeros((ny, width), jnp.float32)

time: 55.4 us -> 52.9 us (0.955)
  Pallas kernels: 11.5 us -> 8.93 us
    pallas_call x1, Pallas kernels: 11.5 us -> 8.93 us  [on_device(): pl.pallas_call(diffusion_kernel, out_shape=(field, field, jax.ShapeDtypeS...]
  transfers between devices with their start and end apart: 13 -> 13, of which waited for: 9 -> 9; matrix products, arithmetic and copies ran while one was open for 10% -> 11% of each run, Pallas kernels for 0% -> 0%
where the time goes in v24:
time: 52.9 us; the launch traced here: 52.3 us
  starting transfers between devices  20.2 us (38%)
  waiting for transfers between devices  11.8 us (22%)
  Pallas kernels  8.93 us (17%)
  local copies, waits for them, and re-layouts  5.59 us (11%)
  matrix products  2.96 us (6%)
  other arithmetic  1.87 us (4%)
  between operations  0.97 us (2%)
    pallas_call x1, Pallas kernels, on_device(): pl.pallas_call(diffusion_kernel, out_shape=(field, field, jax.ShapeDtypeS...  8.93 us
    ppermute x5, starting transfers between devices, shifted(): return lax.ppermute(x, 'space', perm)  8.58 us
    ppermute x3, starting transfers between devices, gathered_over_scen(): lax.ppermute(block, 'scen', [(q, (q // 2 + step) % chips * 2 + q % 2) for...  7.01 us
    ppermute x3, waiting for transfers between devices, summed_over_scen(): lax.ppermute(send, 'scen', [(q, (q // 2 + step) % chips * 2 + q % 2) for...  5.59 us
    ppermute x3, starting transfers between devices, summed_over_scen(): lax.ppermute(send, 'scen', [(q, (q // 2 + step) % chips * 2 + q % 2) for...  4.5 us
    dot_general x3, matrix products, contract(): lax.dot_general(a, b, (dims, ((), ())), precision=lax.Precision.HIGHEST,...  2.96 us
    unnamed x9, local copies, waits for them, and re-layouts  2.59 us
    ppermute x3, waiting for transfers between devices, gathered_over_scen(): lax.ppermute(block, 'scen', [(q, (q // 2 + step) % chips * 2 + q % 2) for...  2.12 us
  transfers between devices with their start and end apart: 13, of which 9 were waited for; matrix products, arithmetic and copies ran while one was open for 11% of the time, Pallas kernels for 0%

profile of v24, /device:TPU:0, one launch (start us, length us, event | category | flops | bytes accessed | tf_op | source)
XLA Modules:
  0.0 52.3 jit_solution(9076828460145413176)
XLA Ops:
  0.6 0.0 copy-start
  0.6 3.1 %collective-permute-start = (f32[2,20,4,128]{3,2,1,0:T(4,128)}, f32[2,20,4,128]{3,2,1,0:T(4,128)S(1)}, u32[]{:S(2)}, u32[]{:S(2)}) collective-permute-start(f32[2,20,4,128]{3,2,1,0:T(4,128)} %param.6), channel_id=1, source_target_pairs={{0,2},{1,3},{2,4},{3,5},{4,6},{5,7},{6,0},{7,1},{8,10},{9,11},{10,... | collective-permute-start | bytes 245768 | tf_op jit(solution)/shard_map/ppermute | solution.py:251
  3.7 2.6 %collective-permute-start.1 = (f32[2,20,4,128]{3,2,1,0:T(4,128)}, f32[2,20,4,128]{3,2,1,0:T(4,128)S(1)}, u32[]{:S(2)}, u32[]{:S(2)}) collective-permute-start(f32[2,20,4,128]{3,2,1,0:T(4,128)} %param.6), channel_id=1, source_target_pairs={{0,4},{1,5},{2,6},{3,7},{4,0},{5,1},{6,2},{7,3},{8,12},{9,13},{10,... | collective-permute-start | bytes 245768 | tf_op jit(solution)/shard_map/ppermute | solution.py:251
  6.3 1.3 %collective-permute-start.2 = (f32[2,20,4,128]{3,2,1,0:T(4,128)}, f32[2,20,4,128]{3,2,1,0:T(4,128)S(1)}, u32[]{:S(2)}, u32[]{:S(2)}) collective-permute-start(f32[2,20,4,128]{3,2,1,0:T(4,128)} %param.6), channel_id=1, source_target_pairs={{0,6},{1,7},{2,0},{3,1},{4,2},{5,3},{6,4},{7,5},{8,14},{9,15},{10,... | collective-permute-start | bytes 245768 | tf_op jit(solution)/shard_map/ppermute | solution.py:251
  7.7 1.1 %constant_dynamic-update-slice_fusion.2 = f32[122,32,128]{2,1,0:T(8,128)S(1)} fusion(f32[40,32,128]{2,1,0:T(8,128)} %bitcast.54), kind=kLoop, calls=%fused_computation.24 | loop fusion | bytes 1310720
  8.9 1.1 %constant_dynamic-update-slice_fusion.1 = f32[122,32,128]{2,1,0:T(8,128)S(1)} fusion(f32[122,32,128]{2,1,0:T(8,128)S(1)} %constant_dynamic-update-slice_fusion.2, f32[40,32,128]{2,1,0:T(8,128)} %bitcast.55), kind=kLoop, calls=%fused_computation.23 | loop fusion | bytes 1310720
  10.0 0.1 pad.4.clone
  10.1 0.0 collective-permute-done
  10.1 1.9 %collective-permute-done.1 = f32[2,20,4,128]{3,2,1,0:T(4,128)S(1)} collective-permute-done((f32[2,20,4,128]{3,2,1,0:T(4,128)}, f32[2,20,4,128]{3,2,1,0:T(4,128)S(1)}, u32[]{:S(2)}, u32[]{:S(2)}) %collective-permute-start.1) | collective-permute-done | bytes 81952 | tf_op jit(solution)/shard_map/ppermute | solution.py:251
  12.0 0.2 collective-permute-done.2
  12.2 0.0 copy-done
  12.2 0.1 fusion.29
  12.3 0.1 collective-permute-start.3
  12.4 0.1 and_or_fusion
  12.5 1.5 %collective-permute-done.3 = f32[4,2,20,4,128]{4,3,2,1,0:T(4,128)S(1)} collective-permute-done((f32[4,2,20,4,128]{4,3,2,1,0:T(4,128)S(1)}, f32[4,2,20,4,128]{4,3,2,1,0:T(4,128)S(1)}, u32[]{:S(2)}, u32[]{:S(2)}) %collective-permute-start.3) | collective-permute-done | bytes 327712 | tf_op jit(solution)/shard_map/ppermute | solution.py:254
  14.0 0.1 maximum_select_fusion
  14.2 0.9 %gather_fusion = f32[4,2,2,20,4,128]{5,4,3,2,1,0:T(4,128)S(1)} fusion(f32[4,2,2,20,4,128]{5,4,3,2,0,1:T(4,128)S(1)} %maximum_select_fusion, s32[1024]{0:T(1024)S(1)} %pad_clamp_fusion), kind=kCustom, calls=%fused_computation | custom fusion | bytes 1310736 | tf_op jit(solution)/shard_map/jit(_take)/gather | solution.py:257
  15.1 0.0 copy-start.1
  15.1 0.0 copy-start.2
  15.2 0.2 select_bitcast_fusion
  15.4 0.2 copy.24
  15.6 0.3 copy-done.1
  15.9 0.0 copy-done.2
  15.9 1.0 %fusion.9 = f32[4,3904]{1,0:T(4,128)S(1)} fusion(f32[3904,128]{1,0:T(8,128)S(1)} %bitcast.51, pred[128]{0:T(512)(128)(4,1)S(1)} %get-tuple-element.20, pred[128]{0:T(512)(128)(4,1)S(1)} %get-tuple-element.21, pred[128]{0:T(512)(128)(4,1)S(1)} %get-tuple-element.22, pred[128]{0:T(512)(128)(4,1)S(1)} %get-tuple-element.23, ...), kind=kOutput, calls=%fused_computation.34 | convolution fusion | flops 23989760 | bytes 2061840 | tf_op jit(solution)/shard_map/dot_general | solution.py:31
  16.9 0.1 reshape.79
  17.0 0.1 fusion.30
  17.2 0.2 rev.11
  17.4 3.4 %collective-permute-start.7 = (f32[2,122,2]{2,1,0:T(8,128)S(1)}, f32[2,122,2]{2,1,0:T(8,128)S(1)}, u32[]{:S(2)}, u32[]{:S(2)}) collective-permute-start(f32[2,122,2]{2,1,0:T(8,128)S(1)} %rev.11), channel_id=1, source_target_pairs={{0,16},{8,8},{16,0},{24,24},{1,17},{9,9},{17,1},{25,25},{2,18},{10... | collective-permute-start | bytes 5864 | tf_op jit(solution)/shard_map/ppermute | solution.py:18
  20.8 0.2 rev.12
  21.0 0.7 %collective-permute-start.8 = (f32[2,122,2]{2,1,0:T(8,128)S(1)}, f32[2,122,2]{2,1,0:T(8,128)S(1)}, u32[]{:S(2)}, u32[]{:S(2)}) collective-permute-start(f32[2,122,2]{2,1,0:T(8,128)S(1)} %rev.12), channel_id=1, source_target_pairs={{0,0},{8,24},{16,16},{24,8},{1,1},{9,25},{17,17},{25,9},{2,2},{10,... | collective-permute-start | bytes 5864 | tf_op jit(solution)/shard_map/ppermute | solution.py:18
  21.7 0.1 slice.29
  21.8 1.5 %collective-permute-start.4 = (f32[2,3904]{1,0:T(2,128)S(1)}, f32[2,3904]{1,0:T(2,128)S(1)}, u32[]{:S(2)}, u32[]{:S(2)}) collective-permute-start(f32[2,3904]{1,0:T(2,128)S(1)} %get-tuple-element.16), channel_id=1, source_target_pairs={{0,24},{8,0},{16,8},{24,16},{1,25},{9,1},{17,9},{25,17},{2,26},{10... | collective-permute-start | bytes 93704 | tf_op jit(solution)/shard_map/ppermute | solution.py:18
  23.3 0.6 %collective-permute-start.5 = (f32[2,3904]{1,0:T(2,128)S(1)}, f32[2,3904]{1,0:T(2,128)S(1)}, u32[]{:S(2)}, u32[]{:S(2)}) collective-permute-start(f32[2,3904]{1,0:T(2,128)S(1)} %get-tuple-element.17), channel_id=1, source_target_pairs={{0,8},{8,16},{16,24},{24,0},{1,9},{9,17},{17,25},{25,1},{2,10},{10... | collective-permute-start | bytes 93704 | tf_op jit(solution)/shard_map/ppermute | solution.py:18
  23.8 0.5 rev.10
  24.3 2.4 %collective-permute-start.6 = (f32[122,2,128]{2,1,0:T(2,128)S(1)}, f32[122,2,128]{2,1,0:T(2,128)S(1)}, u32[]{:S(2)}, u32[]{:S(2)}) collective-permute-start(f32[122,2,128]{2,1,0:T(2,128)S(1)} %rev.10), channel_id=1, source_target_pairs={{0,24},{8,16},{16,8},{24,0},{1,25},{9,17},{17,9},{25,1},{2,26},{10... | collective-permute-start | bytes 374792 | tf_op jit(solution)/shard_map/ppermute | solution.py:18
  26.7 0.0 collective-permute-done.7
  26.7 0.0 collective-permute-done.8
  26.8 0.2 reshape.91
  26.9 0.1 copy.30
  27.1 0.1 dot_general.16
  27.2 0.2 fusion
  27.4 0.1 copy.27
  27.5 0.0 collective-permute-done.4
  27.5 0.8 %collective-permute-done.5 = f32[2,3904]{1,0:T(2,128)S(1)} collective-permute-done((f32[2,3904]{1,0:T(2,128)S(1)}, f32[2,3904]{1,0:T(2,128)S(1)}, u32[]{:S(2)}, u32[]{:S(2)}) %collective-permute-start.5) | collective-permute-done | bytes 31264 | tf_op jit(solution)/shard_map/ppermute | solution.py:18
  28.3 1.7 %fusion.4 = f32[3904,128]{1,0:T(8,128)S(1)} fusion(pred[128,4]{0,1:T(4,128)(4,1)S(1)} %and_or_fusion, f32[2,3904]{1,0:T(2,128)S(1)} %collective-permute-done.5, f32[2,3904]{1,0:T(2,128)S(1)} %collective-permute-done.4), kind=kOutput, calls=%fused_computation.16 | convolution fusion | flops 24001792 | bytes 2061824 | tf_op jit(solution)/shard_map/dot_general | solution.py:31
  30.1 0.1 collective-permute-done.6
  30.2 0.5 maximum_maximum_fusion.x_ref
  30.7 8.9 %shard_map.76 = (f32[2,20,32,128]{3,2,1,0:T(8,128)}, f32[2,20,32,128]{3,2,1,0:T(8,128)}, f32[2,20,32,128]{3,2,1,0:T(8,128)S(1)}) custom-call(f32[122,40,256]{2,1,0:T(8,128)S(1)} %maximum_maximum_fusion.x_ref), custom_call_target="tpu_custom_call" | custom-call | tf_op jit(solution)/shard_map/pallas_call | solution.py:216
  39.6 0.1 dynamic-slice_bitcast_fusion
  39.7 0.1 collective-permute-start.9
  39.9 1.5 %collective-permute-done.9 = f32[2,20,4,4,128]{4,3,2,1,0:T(4,128)S(1)} collective-permute-done((f32[2,20,4,4,128]{4,3,2,1,0:T(4,128)S(1)}, f32[2,20,4,4,128]{4,3,2,1,0:T(4,128)S(1)}, u32[]{:S(2)}, u32[]{:S(2)}) %collective-permute-start.9) | collective-permute-done | bytes 327712 | tf_op jit(solution)/shard_map/ppermute | solution.py:274
  41.4 0.1 bitcast_add_fusion
  41.5 0.1 dynamic-slice_bitcast_fusion.3
  41.6 2.1 %collective-permute-start.10 = (f32[2,20,4,128]{3,2,1,0:T(4,128)S(1)}, f32[2,20,4,128]{3,2,1,0:T(4,128)S(1)}, u32[]{:S(2)}, u32[]{:S(2)}) collective-permute-start(f32[2,20,4,128]{3,2,1,0:T(4,128)S(1)} %get-tuple-element.9), channel_id=1, source_target_pairs={{0,2},{1,3},{2,4},{3,5},{4,6},{5,7},{6,0},{7,1},{8,10},{9,11},{10,... | collective-permute-start | bytes 245768 | tf_op jit(solution)/shard_map/ppermute | solution.py:279
  43.6 1.8 %collective-permute-start.11 = (f32[2,20,4,128]{3,2,1,0:T(4,128)S(1)}, f32[2,20,4,128]{3,2,1,0:T(4,128)S(1)}, u32[]{:S(2)}, u32[]{:S(2)}) collective-permute-start(f32[2,20,4,128]{3,2,1,0:T(4,128)S(1)} %get-tuple-element.11), channel_id=1, source_target_pairs={{0,4},{1,5},{2,6},{3,7},{4,0},{5,1},{6,2},{7,3},{8,12},{9,13},{10,... | collective-permute-start | bytes 245768 | tf_op jit(solution)/shard_map/ppermute | solution.py:279
  45.5 0.6 %collective-permute-start.12 = (f32[2,20,4,128]{3,2,1,0:T(4,128)S(1)}, f32[2,20,4,128]{3,2,1,0:T(4,128)S(1)}, u32[]{:S(2)}, u32[]{:S(2)}) collective-permute-start(f32[2,20,4,128]{3,2,1,0:T(4,128)S(1)} %get-tuple-element.10), channel_id=1, source_target_pairs={{0,6},{1,7},{2,0},{3,1},{4,2},{5,3},{6,4},{7,5},{8,14},{9,15},{10,... | collective-permute-start | bytes 245768 | tf_op jit(solution)/shard_map/ppermute | solution.py:279
  46.1 2.7 %collective-permute-done.10 = f32[2,20,4,128]{3,2,1,0:T(4,128)S(1)} collective-permute-done((f32[2,20,4,128]{3,2,1,0:T(4,128)S(1)}, f32[2,20,4,128]{3,2,1,0:T(4,128)S(1)}, u32[]{:S(2)}, u32[]{:S(2)}) %collective-permute-start.10) | collective-permute-done | bytes 81952 | tf_op jit(solution)/shard_map/ppermute | solution.py:279
  48.8 2.7 %collective-permute-done.11 = f32[2,20,4,128]{3,2,1,0:T(4,128)S(1)} collective-permute-done((f32[2,20,4,128]{3,2,1,0:T(4,128)S(1)}, f32[2,20,4,128]{3,2,1,0:T(4,128)S(1)}, u32[]{:S(2)}, u32[]{:S(2)}) %collective-permute-start.11) | collective-permute-done | bytes 81952 | tf_op jit(solution)/shard_map/ppermute | solution.py:279
  51.5 0.1 collective-permute-done.12
  51.6 0.7 %fusion.3 = f32[2,20,4,128]{3,2,1,0:T(4,128)} fusion(f32[2,20,4,128]{3,2,1,0:T(4,128)S(1)} %collective-permute-done.12, f32[2,20,4,128]{3,2,1,0:T(4,128)S(1)} %collective-permute-done.11, f32[2,20,4,128]{3,2,1,0:T(4,128)S(1)} %collective-permute-done.10, f32[2,20,4,4,128]{4,3,2,1,0:T(4,128)S(1)} %bitcast_add_fusion, s32[]{:T(128)S(6)} %select_n.107), kind=kLoop, calls=%fused_computation.12 | loop fusion | flops 61440 | bytes 409604 | tf_op jit(solution)/shard_map/add | solution.py:279
  (13 shorter events, 0.2 us)
Async XLA Ops:
  0.6 11.6 %copy-start = (f32[2,20,4,128]{3,2,1,0:T(4,128)S(1)}, f32[2,20,4,128]{3,2,1,0:T(4,128)}, u32[]{:S(2)}) copy-start(f32[2,20,4,128]{3,2,1,0:T(4,128)} %param.6) | copy-start | bytes 245764
  0.6 9.5 %collective-permute-start = (f32[2,20,4,128]{3,2,1,0:T(4,128)}, f32[2,20,4,128]{3,2,1,0:T(4,128)S(1)}, u32[]{:S(2)}, u32[]{:S(2)}) collective-permute-start(f32[2,20,4,128]{3,2,1,0:T(4,128)} %param.6), channel_id=1, source_target_pairs={{0,2},{1,3},{2,4},{3,5},{4,6},{5,7},{6,0},{7,1},{8,10},{9,11},{10,... | collective-permute-start | bytes 245768 | tf_op jit(solution)/shard_map/ppermute | solution.py:251
  3.7 8.3 %collective-permute-start.1 = (f32[2,20,4,128]{3,2,1,0:T(4,128)}, f32[2,20,4,128]{3,2,1,0:T(4,128)S(1)}, u32[]{:S(2)}, u32[]{:S(2)}) collective-permute-start(f32[2,20,4,128]{3,2,1,0:T(4,128)} %param.6), channel_id=1, source_target_pairs={{0,4},{1,5},{2,6},{3,7},{4,0},{5,1},{6,2},{7,3},{8,12},{9,13},{10,... | collective-permute-start | bytes 245768 | tf_op jit(solution)/shard_map/ppermute | solution.py:251
  6.3 5.9 %collective-permute-start.2 = (f32[2,20,4,128]{3,2,1,0:T(4,128)}, f32[2,20,4,128]{3,2,1,0:T(4,128)S(1)}, u32[]{:S(2)}, u32[]{:S(2)}) collective-permute-start(f32[2,20,4,128]{3,2,1,0:T(4,128)} %param.6), channel_id=1, source_target_pairs={{0,6},{1,7},{2,0},{3,1},{4,2},{5,3},{6,4},{7,5},{8,14},{9,15},{10,... | collective-permute-start | bytes 245768 | tf_op jit(solution)/shard_map/ppermute | solution.py:251
  12.3 1.7 %collective-permute-start.3 = (f32[4,2,20,4,128]{4,3,2,1,0:T(4,128)S(1)}, f32[4,2,20,4,128]{4,3,2,1,0:T(4,128)S(1)}, u32[]{:S(2)}, u32[]{:S(2)}) collective-permute-start(f32[4,2,20,4,128]{4,3,2,1,0:T(4,128)S(1)} %get-tuple-element.13), channel_id=1, source_target_pairs={{0,1},{1,0},{2,3},{3,2},{4,5},{5,4},{6,7},{7,6},{8,9},{9,8},{10,11... | collective-permute-start | bytes 983048 | tf_op jit(solution)/shard_map/ppermute | solution.py:254
  15.1 0.7 %copy-start.1 = (s32[32,128]{1,0:T(8,128)S(1)}, s32[32,128]{1,0:T(8,128)}, u32[]{:S(2)}) copy-start(s32[32,128]{1,0:T(8,128)} %param.7) | copy-start | bytes 49156
  15.1 0.7 %copy-start.2 = (s32[32,128]{1,0:T(8,128)S(1)}, s32[32,128]{1,0:T(8,128)}, u32[]{:S(2)}) copy-start(s32[32,128]{1,0:T(8,128)} %param.8) | copy-start | bytes 49156
  17.4 9.4 %collective-permute-start.7 = (f32[2,122,2]{2,1,0:T(8,128)S(1)}, f32[2,122,2]{2,1,0:T(8,128)S(1)}, u32[]{:S(2)}, u32[]{:S(2)}) collective-permute-start(f32[2,122,2]{2,1,0:T(8,128)S(1)} %rev.11), channel_id=1, source_target_pairs={{0,16},{8,8},{16,0},{24,24},{1,17},{9,9},{17,1},{25,25},{2,18},{10... | collective-permute-start | bytes 5864 | tf_op jit(solution)/shard_map/ppermute | solution.py:18
  21.0 5.8 %collective-permute-start.8 = (f32[2,122,2]{2,1,0:T(8,128)S(1)}, f32[2,122,2]{2,1,0:T(8,128)S(1)}, u32[]{:S(2)}, u32[]{:S(2)}) collective-permute-start(f32[2,122,2]{2,1,0:T(8,128)S(1)} %rev.12), channel_id=1, source_target_pairs={{0,0},{8,24},{16,16},{24,8},{1,1},{9,25},{17,17},{25,9},{2,2},{10,... | collective-permute-start | bytes 5864 | tf_op jit(solution)/shard_map/ppermute | solution.py:18
  21.8 5.7 %collective-permute-start.4 = (f32[2,3904]{1,0:T(2,128)S(1)}, f32[2,3904]{1,0:T(2,128)S(1)}, u32[]{:S(2)}, u32[]{:S(2)}) collective-permute-start(f32[2,3904]{1,0:T(2,128)S(1)} %get-tuple-element.16), channel_id=1, source_target_pairs={{0,24},{8,0},{16,8},{24,16},{1,25},{9,1},{17,9},{25,17},{2,26},{10... | collective-permute-start | bytes 93704 | tf_op jit(solution)/shard_map/ppermute | solution.py:18
  23.3 5.1 %collective-permute-start.5 = (f32[2,3904]{1,0:T(2,128)S(1)}, f32[2,3904]{1,0:T(2,128)S(1)}, u32[]{:S(2)}, u32[]{:S(2)}) collective-permute-start(f32[2,3904]{1,0:T(2,128)S(1)} %get-tuple-element.17), channel_id=1, source_target_pairs={{0,8},{8,16},{16,24},{24,0},{1,9},{9,17},{17,25},{25,1},{2,10},{10... | collective-permute-start | bytes 93704 | tf_op jit(solution)/shard_map/ppermute | solution.py:18
  24.3 5.9 %collective-permute-start.6 = (f32[122,2,128]{2,1,0:T(2,128)S(1)}, f32[122,2,128]{2,1,0:T(2,128)S(1)}, u32[]{:S(2)}, u32[]{:S(2)}) collective-permute-start(f32[122,2,128]{2,1,0:T(2,128)S(1)} %rev.10), channel_id=1, source_target_pairs={{0,24},{8,16},{16,8},{24,0},{1,25},{9,17},{17,9},{25,1},{2,26},{10... | collective-permute-start | bytes 374792 | tf_op jit(solution)/shard_map/ppermute | solution.py:18
  39.7 1.7 %collective-permute-start.9 = (f32[2,20,4,4,128]{4,3,2,1,0:T(4,128)S(1)}, f32[2,20,4,4,128]{4,3,2,1,0:T(4,128)S(1)}, u32[]{:S(2)}, u32[]{:S(2)}) collective-permute-start(f32[2,20,4,4,128]{4,3,2,1,0:T(4,128)S(1)} %dynamic-slice_bitcast_fusion), channel_id=1, source_target_pairs={{0,1},{1,0},{2,3},{3,2},{4,5},{5,4},{6,7},{7,6},{8,9},{9,8},{10,11... | collective-permute-start | bytes 983048 | tf_op jit(solution)/shard_map/ppermute | solution.py:274
  41.6 7.2 %collective-permute-start.10 = (f32[2,20,4,128]{3,2,1,0:T(4,128)S(1)}, f32[2,20,4,128]{3,2,1,0:T(4,128)S(1)}, u32[]{:S(2)}, u32[]{:S(2)}) collective-permute-start(f32[2,20,4,128]{3,2,1,0:T(4,128)S(1)} %get-tuple-element.9), channel_id=1, source_target_pairs={{0,2},{1,3},{2,4},{3,5},{4,6},{5,7},{6,0},{7,1},{8,10},{9,11},{10,... | collective-permute-start | bytes 245768 | tf_op jit(solution)/shard_map/ppermute | solution.py:279
  43.6 7.9 %collective-permute-start.11 = (f32[2,20,4,128]{3,2,1,0:T(4,128)S(1)}, f32[2,20,4,128]{3,2,1,0:T(4,128)S(1)}, u32[]{:S(2)}, u32[]{:S(2)}) collective-permute-start(f32[2,20,4,128]{3,2,1,0:T(4,128)S(1)} %get-tuple-element.11), channel_id=1, source_target_pairs={{0,4},{1,5},{2,6},{3,7},{4,0},{5,1},{6,2},{7,3},{8,12},{9,13},{10,... | collective-permute-start | bytes 245768 | tf_op jit(solution)/shard_map/ppermute | solution.py:279
  45.5 6.2 %collective-permute-start.12 = (f32[2,20,4,128]{3,2,1,0:T(4,128)S(1)}, f32[2,20,4,128]{3,2,1,0:T(4,128)S(1)}, u32[]{:S(2)}, u32[]{:S(2)}) collective-permute-start(f32[2,20,4,128]{3,2,1,0:T(4,128)S(1)} %get-tuple-element.10), channel_id=1, source_target_pairs={{0,6},{1,7},{2,0},{3,1},{4,2},{5,3},{6,4},{7,5},{8,14},{9,15},{10,... | collective-permute-start | bytes 245768 | tf_op jit(solution)/shard_map/ppermute | solution.py:279

commit v25 on v22

--- a/solution.py
+++ b/solution.py
@@ -118,7 +118,7 @@
             a_ref[c, k] = w * ve_ref[c, k]
         return carry
 
-    lax.fori_loop(0, levels, setup, 0, unroll=True)
+    lax.fori_loop(0, levels, setup, 0, unroll=10)
 
     def operate(x_ref, c, k, diffs=None):
         x = x_ref[c, k]

time: 52.2 us -> 52.3 us (level)
  no operation moved by 1% of the time
where the time goes in v25:
time: 52.3 us; the launch traced here: 51.8 us
  starting transfers between devices  20.2 us (39%)
  waiting for transfers between devices  11.8 us (23%)
  Pallas kernels  8.42 us (16%)
  local copies, waits for them, and re-layouts  5.59 us (11%)
  matrix products  2.96 us (6%)
  other arithmetic  1.87 us (4%)
  between operations  0.97 us (2%)
    ppermute x5, starting transfers between devices, shifted(): return lax.ppermute(x, 'space', perm)  8.58 us
    pallas_call x1, Pallas kernels, on_device(): pl.pallas_call(diffusion_kernel, out_shape=(field, field, jax.ShapeDtypeS...  8.42 us
    ppermute x3, starting transfers between devices, gathered_over_scen(): lax.ppermute(block, 'scen', [(q, (q // 2 + step) % chips * 2 + q % 2) for...  7.01 us
    ppermute x3, waiting for transfers between devices, summed_over_scen(): lax.ppermute(send, 'scen', [(q, (q // 2 + step) % chips * 2 + q % 2) for...  5.59 us
    ppermute x3, starting transfers between devices, summed_over_scen(): lax.ppermute(send, 'scen', [(q, (q // 2 + step) % chips * 2 + q % 2) for...  4.5 us
    dot_general x3, matrix products, contract(): lax.dot_general(a, b, (dims, ((), ())), precision=lax.Precision.HIGHEST,...  2.96 us
    unnamed x9, local copies, waits for them, and re-layouts  2.59 us
    ppermute x3, waiting for transfers between devices, gathered_over_scen(): lax.ppermute(block, 'scen', [(q, (q // 2 + step) % chips * 2 + q % 2) for...  2.12 us
  transfers between devices with their start and end apart: 13, of which 9 were waited for; matrix products, arithmetic and copies ran while one was open for 11% of the time, Pallas kernels for 0%

profile of v25, /device:TPU:0, one launch (start us, length us, event | category | flops | bytes accessed | tf_op | source)
XLA Modules:
  0.0 51.8 jit_solution(7437067877473079805)
XLA Ops:
  0.6 0.0 copy-start
  0.6 3.1 %collective-permute-start = (f32[2,20,4,128]{3,2,1,0:T(4,128)}, f32[2,20,4,128]{3,2,1,0:T(4,128)S(1)}, u32[]{:S(2)}, u32[]{:S(2)}) collective-permute-start(f32[2,20,4,128]{3,2,1,0:T(4,128)} %param.6), channel_id=1, source_target_pairs={{0,2},{1,3},{2,4},{3,5},{4,6},{5,7},{6,0},{7,1},{8,10},{9,11},{10,... | collective-permute-start | bytes 245768 | tf_op jit(solution)/shard_map/ppermute | solution.py:251
  3.7 2.6 %collective-permute-start.1 = (f32[2,20,4,128]{3,2,1,0:T(4,128)}, f32[2,20,4,128]{3,2,1,0:T(4,128)S(1)}, u32[]{:S(2)}, u32[]{:S(2)}) collective-permute-start(f32[2,20,4,128]{3,2,1,0:T(4,128)} %param.6), channel_id=1, source_target_pairs={{0,4},{1,5},{2,6},{3,7},{4,0},{5,1},{6,2},{7,3},{8,12},{9,13},{10,... | collective-permute-start | bytes 245768 | tf_op jit(solution)/shard_map/ppermute | solution.py:251
  6.3 1.3 %collective-permute-start.2 = (f32[2,20,4,128]{3,2,1,0:T(4,128)}, f32[2,20,4,128]{3,2,1,0:T(4,128)S(1)}, u32[]{:S(2)}, u32[]{:S(2)}) collective-permute-start(f32[2,20,4,128]{3,2,1,0:T(4,128)} %param.6), channel_id=1, source_target_pairs={{0,6},{1,7},{2,0},{3,1},{4,2},{5,3},{6,4},{7,5},{8,14},{9,15},{10,... | collective-permute-start | bytes 245768 | tf_op jit(solution)/shard_map/ppermute | solution.py:251
  7.7 1.1 %constant_dynamic-update-slice_fusion.2 = f32[122,32,128]{2,1,0:T(8,128)S(1)} fusion(f32[40,32,128]{2,1,0:T(8,128)} %bitcast.54), kind=kLoop, calls=%fused_computation.24 | loop fusion | bytes 1310720
  8.9 1.1 %constant_dynamic-update-slice_fusion.1 = f32[122,32,128]{2,1,0:T(8,128)S(1)} fusion(f32[122,32,128]{2,1,0:T(8,128)S(1)} %constant_dynamic-update-slice_fusion.2, f32[40,32,128]{2,1,0:T(8,128)} %bitcast.55), kind=kLoop, calls=%fused_computation.23 | loop fusion | bytes 1310720
  10.0 0.1 pad.4.clone
  10.1 0.0 collective-permute-done
  10.1 1.9 %collective-permute-done.1 = f32[2,20,4,128]{3,2,1,0:T(4,128)S(1)} collective-permute-done((f32[2,20,4,128]{3,2,1,0:T(4,128)}, f32[2,20,4,128]{3,2,1,0:T(4,128)S(1)}, u32[]{:S(2)}, u32[]{:S(2)}) %collective-permute-start.1) | collective-permute-done | bytes 81952 | tf_op jit(solution)/shard_map/ppermute | solution.py:251
  12.0 0.2 collective-permute-done.2
  12.2 0.0 copy-done
  12.2 0.1 fusion.29
  12.3 0.1 collective-permute-start.3
  12.4 0.1 and_or_fusion
  12.5 1.5 %collective-permute-done.3 = f32[4,2,20,4,128]{4,3,2,1,0:T(4,128)S(1)} collective-permute-done((f32[4,2,20,4,128]{4,3,2,1,0:T(4,128)S(1)}, f32[4,2,20,4,128]{4,3,2,1,0:T(4,128)S(1)}, u32[]{:S(2)}, u32[]{:S(2)}) %collective-permute-start.3) | collective-permute-done | bytes 327712 | tf_op jit(solution)/shard_map/ppermute | solution.py:254
  14.0 0.1 maximum_select_fusion
  14.2 0.9 %gather_fusion = f32[4,2,2,20,4,128]{5,4,3,2,1,0:T(4,128)S(1)} fusion(f32[4,2,2,20,4,128]{5,4,3,2,0,1:T(4,128)S(1)} %maximum_select_fusion, s32[1024]{0:T(1024)S(1)} %pad_clamp_fusion), kind=kCustom, calls=%fused_computation | custom fusion | bytes 1310736 | tf_op jit(solution)/shard_map/jit(_take)/gather | solution.py:257
  15.1 0.0 copy-start.1
  15.1 0.0 copy-start.2
  15.2 0.2 select_bitcast_fusion
  15.4 0.2 copy.24
  15.6 0.3 copy-done.1
  15.9 0.0 copy-done.2
  15.9 1.0 %fusion.9 = f32[4,3904]{1,0:T(4,128)S(1)} fusion(f32[3904,128]{1,0:T(8,128)S(1)} %bitcast.51, pred[128]{0:T(512)(128)(4,1)S(1)} %get-tuple-element.20, pred[128]{0:T(512)(128)(4,1)S(1)} %get-tuple-element.21, pred[128]{0:T(512)(128)(4,1)S(1)} %get-tuple-element.22, pred[128]{0:T(512)(128)(4,1)S(1)} %get-tuple-element.23, ...), kind=kOutput, calls=%fused_computation.34 | convolution fusion | flops 23989760 | bytes 2061840 | tf_op jit(solution)/shard_map/dot_general | solution.py:31
  16.9 0.1 reshape.79
  17.0 0.1 fusion.30
  17.2 0.2 rev.11
  17.4 3.4 %collective-permute-start.7 = (f32[2,122,2]{2,1,0:T(8,128)S(1)}, f32[2,122,2]{2,1,0:T(8,128)S(1)}, u32[]{:S(2)}, u32[]{:S(2)}) collective-permute-start(f32[2,122,2]{2,1,0:T(8,128)S(1)} %rev.11), channel_id=1, source_target_pairs={{0,16},{8,8},{16,0},{24,24},{1,17},{9,9},{17,1},{25,25},{2,18},{10... | collective-permute-start | bytes 5864 | tf_op jit(solution)/shard_map/ppermute | solution.py:18
  20.8 0.2 rev.12
  21.0 0.7 %collective-permute-start.8 = (f32[2,122,2]{2,1,0:T(8,128)S(1)}, f32[2,122,2]{2,1,0:T(8,128)S(1)}, u32[]{:S(2)}, u32[]{:S(2)}) collective-permute-start(f32[2,122,2]{2,1,0:T(8,128)S(1)} %rev.12), channel_id=1, source_target_pairs={{0,0},{8,24},{16,16},{24,8},{1,1},{9,25},{17,17},{25,9},{2,2},{10,... | collective-permute-start | bytes 5864 | tf_op jit(solution)/shard_map/ppermute | solution.py:18
  21.7 0.1 slice.29
  21.8 1.5 %collective-permute-start.4 = (f32[2,3904]{1,0:T(2,128)S(1)}, f32[2,3904]{1,0:T(2,128)S(1)}, u32[]{:S(2)}, u32[]{:S(2)}) collective-permute-start(f32[2,3904]{1,0:T(2,128)S(1)} %get-tuple-element.16), channel_id=1, source_target_pairs={{0,24},{8,0},{16,8},{24,16},{1,25},{9,1},{17,9},{25,17},{2,26},{10... | collective-permute-start | bytes 93704 | tf_op jit(solution)/shard_map/ppermute | solution.py:18
  23.3 0.6 %collective-permute-start.5 = (f32[2,3904]{1,0:T(2,128)S(1)}, f32[2,3904]{1,0:T(2,128)S(1)}, u32[]{:S(2)}, u32[]{:S(2)}) collective-permute-start(f32[2,3904]{1,0:T(2,128)S(1)} %get-tuple-element.17), channel_id=1, source_target_pairs={{0,8},{8,16},{16,24},{24,0},{1,9},{9,17},{17,25},{25,1},{2,10},{10... | collective-permute-start | bytes 93704 | tf_op jit(solution)/shard_map/ppermute | solution.py:18
  23.8 0.5 rev.10
  24.3 2.4 %collective-permute-start.6 = (f32[122,2,128]{2,1,0:T(2,128)S(1)}, f32[122,2,128]{2,1,0:T(2,128)S(1)}, u32[]{:S(2)}, u32[]{:S(2)}) collective-permute-start(f32[122,2,128]{2,1,0:T(2,128)S(1)} %rev.10), channel_id=1, source_target_pairs={{0,24},{8,16},{16,8},{24,0},{1,25},{9,17},{17,9},{25,1},{2,26},{10... | collective-permute-start | bytes 374792 | tf_op jit(solution)/shard_map/ppermute | solution.py:18
  26.7 0.0 collective-permute-done.7
  26.7 0.0 collective-permute-done.8
  26.8 0.2 reshape.91
  26.9 0.1 copy.30
  27.1 0.1 dot_general.16
  27.2 0.2 fusion
  27.4 0.1 copy.27
  27.5 0.0 collective-permute-done.4
  27.5 0.8 %collective-permute-done.5 = f32[2,3904]{1,0:T(2,128)S(1)} collective-permute-done((f32[2,3904]{1,0:T(2,128)S(1)}, f32[2,3904]{1,0:T(2,128)S(1)}, u32[]{:S(2)}, u32[]{:S(2)}) %collective-permute-start.5) | collective-permute-done | bytes 31264 | tf_op jit(solution)/shard_map/ppermute | solution.py:18
  28.3 1.7 %fusion.4 = f32[3904,128]{1,0:T(8,128)S(1)} fusion(pred[128,4]{0,1:T(4,128)(4,1)S(1)} %and_or_fusion, f32[2,3904]{1,0:T(2,128)S(1)} %collective-permute-done.5, f32[2,3904]{1,0:T(2,128)S(1)} %collective-permute-done.4), kind=kOutput, calls=%fused_computation.16 | convolution fusion | flops 24001792 | bytes 2061824 | tf_op jit(solution)/shard_map/dot_general | solution.py:31
  30.1 0.1 collective-permute-done.6
  30.2 0.5 maximum_maximum_fusion.x_ref
  30.7 8.4 %shard_map.76 = (f32[2,20,32,128]{3,2,1,0:T(8,128)}, f32[2,20,32,128]{3,2,1,0:T(8,128)}, f32[2,20,32,128]{3,2,1,0:T(8,128)S(1)}) custom-call(f32[122,40,256]{2,1,0:T(8,128)S(1)} %maximum_maximum_fusion.x_ref), custom_call_target="tpu_custom_call" | custom-call | tf_op jit(solution)/shard_map/pallas_call | solution.py:216
  39.1 0.1 dynamic-slice_bitcast_fusion
  39.2 0.1 collective-permute-start.9
  39.3 1.5 %collective-permute-done.9 = f32[2,20,4,4,128]{4,3,2,1,0:T(4,128)S(1)} collective-permute-done((f32[2,20,4,4,128]{4,3,2,1,0:T(4,128)S(1)}, f32[2,20,4,4,128]{4,3,2,1,0:T(4,128)S(1)}, u32[]{:S(2)}, u32[]{:S(2)}) %collective-permute-start.9) | collective-permute-done | bytes 327712 | tf_op jit(solution)/shard_map/ppermute | solution.py:274
  40.9 0.1 bitcast_add_fusion
  41.0 0.1 dynamic-slice_bitcast_fusion.3
  41.0 2.1 %collective-permute-start.10 = (f32[2,20,4,128]{3,2,1,0:T(4,128)S(1)}, f32[2,20,4,128]{3,2,1,0:T(4,128)S(1)}, u32[]{:S(2)}, u32[]{:S(2)}) collective-permute-start(f32[2,20,4,128]{3,2,1,0:T(4,128)S(1)} %get-tuple-element.9), channel_id=1, source_target_pairs={{0,2},{1,3},{2,4},{3,5},{4,6},{5,7},{6,0},{7,1},{8,10},{9,11},{10,... | collective-permute-start | bytes 245768 | tf_op jit(solution)/shard_map/ppermute | solution.py:279
  43.1 1.8 %collective-permute-start.11 = (f32[2,20,4,128]{3,2,1,0:T(4,128)S(1)}, f32[2,20,4,128]{3,2,1,0:T(4,128)S(1)}, u32[]{:S(2)}, u32[]{:S(2)}) collective-permute-start(f32[2,20,4,128]{3,2,1,0:T(4,128)S(1)} %get-tuple-element.11), channel_id=1, source_target_pairs={{0,4},{1,5},{2,6},{3,7},{4,0},{5,1},{6,2},{7,3},{8,12},{9,13},{10,... | collective-permute-start | bytes 245768 | tf_op jit(solution)/shard_map/ppermute | solution.py:279
  44.9 0.6 %collective-permute-start.12 = (f32[2,20,4,128]{3,2,1,0:T(4,128)S(1)}, f32[2,20,4,128]{3,2,1,0:T(4,128)S(1)}, u32[]{:S(2)}, u32[]{:S(2)}) collective-permute-start(f32[2,20,4,128]{3,2,1,0:T(4,128)S(1)} %get-tuple-element.10), channel_id=1, source_target_pairs={{0,6},{1,7},{2,0},{3,1},{4,2},{5,3},{6,4},{7,5},{8,14},{9,15},{10,... | collective-permute-start | bytes 245768 | tf_op jit(solution)/shard_map/ppermute | solution.py:279
  45.5 2.7 %collective-permute-done.10 = f32[2,20,4,128]{3,2,1,0:T(4,128)S(1)} collective-permute-done((f32[2,20,4,128]{3,2,1,0:T(4,128)S(1)}, f32[2,20,4,128]{3,2,1,0:T(4,128)S(1)}, u32[]{:S(2)}, u32[]{:S(2)}) %collective-permute-start.10) | collective-permute-done | bytes 81952 | tf_op jit(solution)/shard_map/ppermute | solution.py:279
  48.3 2.7 %collective-permute-done.11 = f32[2,20,4,128]{3,2,1,0:T(4,128)S(1)} collective-permute-done((f32[2,20,4,128]{3,2,1,0:T(4,128)S(1)}, f32[2,20,4,128]{3,2,1,0:T(4,128)S(1)}, u32[]{:S(2)}, u32[]{:S(2)}) %collective-permute-start.11) | collective-permute-done | bytes 81952 | tf_op jit(solution)/shard_map/ppermute | solution.py:279
  51.0 0.1 collective-permute-done.12
  51.1 0.7 %fusion.3 = f32[2,20,4,128]{3,2,1,0:T(4,128)} fusion(f32[2,20,4,128]{3,2,1,0:T(4,128)S(1)} %collective-permute-done.12, f32[2,20,4,128]{3,2,1,0:T(4,128)S(1)} %collective-permute-done.11, f32[2,20,4,128]{3,2,1,0:T(4,128)S(1)} %collective-permute-done.10, f32[2,20,4,4,128]{4,3,2,1,0:T(4,128)S(1)} %bitcast_add_fusion, s32[]{:T(128)S(6)} %select_n.107), kind=kLoop, calls=%fused_computation.12 | loop fusion | flops 61440 | bytes 409604 | tf_op jit(solution)/shard_map/add | solution.py:279
  (13 shorter events, 0.2 us)
Async XLA Ops:
  0.6 11.6 %copy-start = (f32[2,20,4,128]{3,2,1,0:T(4,128)S(1)}, f32[2,20,4,128]{3,2,1,0:T(4,128)}, u32[]{:S(2)}) copy-start(f32[2,20,4,128]{3,2,1,0:T(4,128)} %param.6) | copy-start | bytes 245764
  0.6 9.5 %collective-permute-start = (f32[2,20,4,128]{3,2,1,0:T(4,128)}, f32[2,20,4,128]{3,2,1,0:T(4,128)S(1)}, u32[]{:S(2)}, u32[]{:S(2)}) collective-permute-start(f32[2,20,4,128]{3,2,1,0:T(4,128)} %param.6), channel_id=1, source_target_pairs={{0,2},{1,3},{2,4},{3,5},{4,6},{5,7},{6,0},{7,1},{8,10},{9,11},{10,... | collective-permute-start | bytes 245768 | tf_op jit(solution)/shard_map/ppermute | solution.py:251
  3.7 8.3 %collective-permute-start.1 = (f32[2,20,4,128]{3,2,1,0:T(4,128)}, f32[2,20,4,128]{3,2,1,0:T(4,128)S(1)}, u32[]{:S(2)}, u32[]{:S(2)}) collective-permute-start(f32[2,20,4,128]{3,2,1,0:T(4,128)} %param.6), channel_id=1, source_target_pairs={{0,4},{1,5},{2,6},{3,7},{4,0},{5,1},{6,2},{7,3},{8,12},{9,13},{10,... | collective-permute-start | bytes 245768 | tf_op jit(solution)/shard_map/ppermute | solution.py:251
  6.3 5.9 %collective-permute-start.2 = (f32[2,20,4,128]{3,2,1,0:T(4,128)}, f32[2,20,4,128]{3,2,1,0:T(4,128)S(1)}, u32[]{:S(2)}, u32[]{:S(2)}) collective-permute-start(f32[2,20,4,128]{3,2,1,0:T(4,128)} %param.6), channel_id=1, source_target_pairs={{0,6},{1,7},{2,0},{3,1},{4,2},{5,3},{6,4},{7,5},{8,14},{9,15},{10,... | collective-permute-start | bytes 245768 | tf_op jit(solution)/shard_map/ppermute | solution.py:251
  12.3 1.7 %collective-permute-start.3 = (f32[4,2,20,4,128]{4,3,2,1,0:T(4,128)S(1)}, f32[4,2,20,4,128]{4,3,2,1,0:T(4,128)S(1)}, u32[]{:S(2)}, u32[]{:S(2)}) collective-permute-start(f32[4,2,20,4,128]{4,3,2,1,0:T(4,128)S(1)} %get-tuple-element.13), channel_id=1, source_target_pairs={{0,1},{1,0},{2,3},{3,2},{4,5},{5,4},{6,7},{7,6},{8,9},{9,8},{10,11... | collective-permute-start | bytes 983048 | tf_op jit(solution)/shard_map/ppermute | solution.py:254
  15.1 0.7 %copy-start.1 = (s32[32,128]{1,0:T(8,128)S(1)}, s32[32,128]{1,0:T(8,128)}, u32[]{:S(2)}) copy-start(s32[32,128]{1,0:T(8,128)} %param.7) | copy-start | bytes 49156
  15.1 0.7 %copy-start.2 = (s32[32,128]{1,0:T(8,128)S(1)}, s32[32,128]{1,0:T(8,128)}, u32[]{:S(2)}) copy-start(s32[32,128]{1,0:T(8,128)} %param.8) | copy-start | bytes 49156
  17.4 9.4 %collective-permute-start.7 = (f32[2,122,2]{2,1,0:T(8,128)S(1)}, f32[2,122,2]{2,1,0:T(8,128)S(1)}, u32[]{:S(2)}, u32[]{:S(2)}) collective-permute-start(f32[2,122,2]{2,1,0:T(8,128)S(1)} %rev.11), channel_id=1, source_target_pairs={{0,16},{8,8},{16,0},{24,24},{1,17},{9,9},{17,1},{25,25},{2,18},{10... | collective-permute-start | bytes 5864 | tf_op jit(solution)/shard_map/ppermute | solution.py:18
  21.0 5.8 %collective-permute-start.8 = (f32[2,122,2]{2,1,0:T(8,128)S(1)}, f32[2,122,2]{2,1,0:T(8,128)S(1)}, u32[]{:S(2)}, u32[]{:S(2)}) collective-permute-start(f32[2,122,2]{2,1,0:T(8,128)S(1)} %rev.12), channel_id=1, source_target_pairs={{0,0},{8,24},{16,16},{24,8},{1,1},{9,25},{17,17},{25,9},{2,2},{10,... | collective-permute-start | bytes 5864 | tf_op jit(solution)/shard_map/ppermute | solution.py:18
  21.8 5.7 %collective-permute-start.4 = (f32[2,3904]{1,0:T(2,128)S(1)}, f32[2,3904]{1,0:T(2,128)S(1)}, u32[]{:S(2)}, u32[]{:S(2)}) collective-permute-start(f32[2,3904]{1,0:T(2,128)S(1)} %get-tuple-element.16), channel_id=1, source_target_pairs={{0,24},{8,0},{16,8},{24,16},{1,25},{9,1},{17,9},{25,17},{2,26},{10... | collective-permute-start | bytes 93704 | tf_op jit(solution)/shard_map/ppermute | solution.py:18
  23.3 5.1 %collective-permute-start.5 = (f32[2,3904]{1,0:T(2,128)S(1)}, f32[2,3904]{1,0:T(2,128)S(1)}, u32[]{:S(2)}, u32[]{:S(2)}) collective-permute-start(f32[2,3904]{1,0:T(2,128)S(1)} %get-tuple-element.17), channel_id=1, source_target_pairs={{0,8},{8,16},{16,24},{24,0},{1,9},{9,17},{17,25},{25,1},{2,10},{10... | collective-permute-start | bytes 93704 | tf_op jit(solution)/shard_map/ppermute | solution.py:18
  24.3 5.9 %collective-permute-start.6 = (f32[122,2,128]{2,1,0:T(2,128)S(1)}, f32[122,2,128]{2,1,0:T(2,128)S(1)}, u32[]{:S(2)}, u32[]{:S(2)}) collective-permute-start(f32[122,2,128]{2,1,0:T(2,128)S(1)} %rev.10), channel_id=1, source_target_pairs={{0,24},{8,16},{16,8},{24,0},{1,25},{9,17},{17,9},{25,1},{2,26},{10... | collective-permute-start | bytes 374792 | tf_op jit(solution)/shard_map/ppermute | solution.py:18
  39.2 1.7 %collective-permute-start.9 = (f32[2,20,4,4,128]{4,3,2,1,0:T(4,128)S(1)}, f32[2,20,4,4,128]{4,3,2,1,0:T(4,128)S(1)}, u32[]{:S(2)}, u32[]{:S(2)}) collective-permute-start(f32[2,20,4,4,128]{4,3,2,1,0:T(4,128)S(1)} %dynamic-slice_bitcast_fusion), channel_id=1, source_target_pairs={{0,1},{1,0},{2,3},{3,2},{4,5},{5,4},{6,7},{7,6},{8,9},{9,8},{10,11... | collective-permute-start | bytes 983048 | tf_op jit(solution)/shard_map/ppermute | solution.py:274
  41.0 7.2 %collective-permute-start.10 = (f32[2,20,4,128]{3,2,1,0:T(4,128)S(1)}, f32[2,20,4,128]{3,2,1,0:T(4,128)S(1)}, u32[]{:S(2)}, u32[]{:S(2)}) collective-permute-start(f32[2,20,4,128]{3,2,1,0:T(4,128)S(1)} %get-tuple-element.9), channel_id=1, source_target_pairs={{0,2},{1,3},{2,4},{3,5},{4,6},{5,7},{6,0},{7,1},{8,10},{9,11},{10,... | collective-permute-start | bytes 245768 | tf_op jit(solution)/shard_map/ppermute | solution.py:279
  43.1 7.9 %collective-permute-start.11 = (f32[2,20,4,128]{3,2,1,0:T(4,128)S(1)}, f32[2,20,4,128]{3,2,1,0:T(4,128)S(1)}, u32[]{:S(2)}, u32[]{:S(2)}) collective-permute-start(f32[2,20,4,128]{3,2,1,0:T(4,128)S(1)} %get-tuple-element.11), channel_id=1, source_target_pairs={{0,4},{1,5},{2,6},{3,7},{4,0},{5,1},{6,2},{7,3},{8,12},{9,13},{10,... | collective-permute-start | bytes 245768 | tf_op jit(solution)/shard_map/ppermute | solution.py:279
  44.9 6.2 %collective-permute-start.12 = (f32[2,20,4,128]{3,2,1,0:T(4,128)S(1)}, f32[2,20,4,128]{3,2,1,0:T(4,128)S(1)}, u32[]{:S(2)}, u32[]{:S(2)}) collective-permute-start(f32[2,20,4,128]{3,2,1,0:T(4,128)S(1)} %get-tuple-element.10), channel_id=1, source_target_pairs={{0,6},{1,7},{2,0},{3,1},{4,2},{5,3},{6,4},{7,5},{8,14},{9,15},{10,... | collective-permute-start | bytes 245768 | tf_op jit(solution)/shard_map/ppermute | solution.py:279

commit v26 on v25

--- a/solution.py
+++ b/solution.py
@@ -190,7 +190,7 @@
         grad_ref[1, k] = gnm_ref[k] * g_north
         return carry
 
-    lax.fori_loop(0, levels, gradient, 0, unroll=True)
+    lax.fori_loop(0, levels, gradient, 0, unroll=10)
 
 
 def on_device(tracers, diffusivity, level_count, shelf_mask, cotangent):

time: 52.3 us -> 52.6 us (level)
  no operation moved by 1% of the time
where the time goes in v26:
time: 52.6 us; the launch traced here: 52.1 us
  starting transfers between devices  20.2 us (38%)
  waiting for transfers between devices  11.8 us (22%)
  Pallas kernels  8.68 us (17%)
  local copies, waits for them, and re-layouts  5.59 us (11%)
  matrix products  2.96 us (6%)
  other arithmetic  1.87 us (4%)
  between operations  0.97 us (2%)
    pallas_call x1, Pallas kernels, on_device(): pl.pallas_call(diffusion_kernel, out_shape=(field, field, jax.ShapeDtypeS...  8.68 us
    ppermute x5, starting transfers between devices, shifted(): return lax.ppermute(x, 'space', perm)  8.58 us
    ppermute x3, starting transfers between devices, gathered_over_scen(): lax.ppermute(block, 'scen', [(q, (q // 2 + step) % chips * 2 + q % 2) for...  7.01 us
    ppermute x3, waiting for transfers between devices, summed_over_scen(): lax.ppermute(send, 'scen', [(q, (q // 2 + step) % chips * 2 + q % 2) for...  5.59 us
    ppermute x3, starting transfers between devices, summed_over_scen(): lax.ppermute(send, 'scen', [(q, (q // 2 + step) % chips * 2 + q % 2) for...  4.5 us
    dot_general x3, matrix products, contract(): lax.dot_general(a, b, (dims, ((), ())), precision=lax.Precision.HIGHEST,...  2.96 us
    unnamed x9, local copies, waits for them, and re-layouts  2.59 us
    ppermute x3, waiting for transfers between devices, gathered_over_scen(): lax.ppermute(block, 'scen', [(q, (q // 2 + step) % chips * 2 + q % 2) for...  2.12 us
  transfers between devices with their start and end apart: 13, of which 9 were waited for; matrix products, arithmetic and copies ran while one was open for 11% of the time, Pallas kernels for 0%

profile of v26, /device:TPU:0, one launch (start us, length us, event | category | flops | bytes accessed | tf_op | source)
XLA Modules:
  0.0 52.1 jit_solution(10746809070649041514)
XLA Ops:
  0.6 0.0 copy-start
  0.6 3.1 %collective-permute-start = (f32[2,20,4,128]{3,2,1,0:T(4,128)}, f32[2,20,4,128]{3,2,1,0:T(4,128)S(1)}, u32[]{:S(2)}, u32[]{:S(2)}) collective-permute-start(f32[2,20,4,128]{3,2,1,0:T(4,128)} %param.6), channel_id=1, source_target_pairs={{0,2},{1,3},{2,4},{3,5},{4,6},{5,7},{6,0},{7,1},{8,10},{9,11},{10,... | collective-permute-start | bytes 245768 | tf_op jit(solution)/shard_map/ppermute | solution.py:251
  3.7 2.6 %collective-permute-start.1 = (f32[2,20,4,128]{3,2,1,0:T(4,128)}, f32[2,20,4,128]{3,2,1,0:T(4,128)S(1)}, u32[]{:S(2)}, u32[]{:S(2)}) collective-permute-start(f32[2,20,4,128]{3,2,1,0:T(4,128)} %param.6), channel_id=1, source_target_pairs={{0,4},{1,5},{2,6},{3,7},{4,0},{5,1},{6,2},{7,3},{8,12},{9,13},{10,... | collective-permute-start | bytes 245768 | tf_op jit(solution)/shard_map/ppermute | solution.py:251
  6.3 1.3 %collective-permute-start.2 = (f32[2,20,4,128]{3,2,1,0:T(4,128)}, f32[2,20,4,128]{3,2,1,0:T(4,128)S(1)}, u32[]{:S(2)}, u32[]{:S(2)}) collective-permute-start(f32[2,20,4,128]{3,2,1,0:T(4,128)} %param.6), channel_id=1, source_target_pairs={{0,6},{1,7},{2,0},{3,1},{4,2},{5,3},{6,4},{7,5},{8,14},{9,15},{10,... | collective-permute-start | bytes 245768 | tf_op jit(solution)/shard_map/ppermute | solution.py:251
  7.7 1.1 %constant_dynamic-update-slice_fusion.2 = f32[122,32,128]{2,1,0:T(8,128)S(1)} fusion(f32[40,32,128]{2,1,0:T(8,128)} %bitcast.54), kind=kLoop, calls=%fused_computation.24 | loop fusion | bytes 1310720
  8.9 1.1 %constant_dynamic-update-slice_fusion.1 = f32[122,32,128]{2,1,0:T(8,128)S(1)} fusion(f32[122,32,128]{2,1,0:T(8,128)S(1)} %constant_dynamic-update-slice_fusion.2, f32[40,32,128]{2,1,0:T(8,128)} %bitcast.55), kind=kLoop, calls=%fused_computation.23 | loop fusion | bytes 1310720
  10.0 0.1 pad.4.clone
  10.1 0.0 collective-permute-done
  10.1 1.9 %collective-permute-done.1 = f32[2,20,4,128]{3,2,1,0:T(4,128)S(1)} collective-permute-done((f32[2,20,4,128]{3,2,1,0:T(4,128)}, f32[2,20,4,128]{3,2,1,0:T(4,128)S(1)}, u32[]{:S(2)}, u32[]{:S(2)}) %collective-permute-start.1) | collective-permute-done | bytes 81952 | tf_op jit(solution)/shard_map/ppermute | solution.py:251
  12.0 0.2 collective-permute-done.2
  12.2 0.0 copy-done
  12.2 0.1 fusion.29
  12.3 0.1 collective-permute-start.3
  12.4 0.1 and_or_fusion
  12.5 1.5 %collective-permute-done.3 = f32[4,2,20,4,128]{4,3,2,1,0:T(4,128)S(1)} collective-permute-done((f32[4,2,20,4,128]{4,3,2,1,0:T(4,128)S(1)}, f32[4,2,20,4,128]{4,3,2,1,0:T(4,128)S(1)}, u32[]{:S(2)}, u32[]{:S(2)}) %collective-permute-start.3) | collective-permute-done | bytes 327712 | tf_op jit(solution)/shard_map/ppermute | solution.py:254
  14.0 0.1 maximum_select_fusion
  14.2 0.9 %gather_fusion = f32[4,2,2,20,4,128]{5,4,3,2,1,0:T(4,128)S(1)} fusion(f32[4,2,2,20,4,128]{5,4,3,2,0,1:T(4,128)S(1)} %maximum_select_fusion, s32[1024]{0:T(1024)S(1)} %pad_clamp_fusion), kind=kCustom, calls=%fused_computation | custom fusion | bytes 1310736 | tf_op jit(solution)/shard_map/jit(_take)/gather | solution.py:257
  15.1 0.0 copy-start.1
  15.1 0.0 copy-start.2
  15.2 0.2 select_bitcast_fusion
  15.4 0.2 copy.24
  15.6 0.3 copy-done.1
  15.9 0.0 copy-done.2
  15.9 1.0 %fusion.9 = f32[4,3904]{1,0:T(4,128)S(1)} fusion(f32[3904,128]{1,0:T(8,128)S(1)} %bitcast.51, pred[128]{0:T(512)(128)(4,1)S(1)} %get-tuple-element.20, pred[128]{0:T(512)(128)(4,1)S(1)} %get-tuple-element.21, pred[128]{0:T(512)(128)(4,1)S(1)} %get-tuple-element.22, pred[128]{0:T(512)(128)(4,1)S(1)} %get-tuple-element.23, ...), kind=kOutput, calls=%fused_computation.34 | convolution fusion | flops 23989760 | bytes 2061840 | tf_op jit(solution)/shard_map/dot_general | solution.py:31
  16.9 0.1 reshape.79
  17.0 0.1 fusion.30
  17.2 0.2 rev.11
  17.4 3.4 %collective-permute-start.7 = (f32[2,122,2]{2,1,0:T(8,128)S(1)}, f32[2,122,2]{2,1,0:T(8,128)S(1)}, u32[]{:S(2)}, u32[]{:S(2)}) collective-permute-start(f32[2,122,2]{2,1,0:T(8,128)S(1)} %rev.11), channel_id=1, source_target_pairs={{0,16},{8,8},{16,0},{24,24},{1,17},{9,9},{17,1},{25,25},{2,18},{10... | collective-permute-start | bytes 5864 | tf_op jit(solution)/shard_map/ppermute | solution.py:18
  20.8 0.2 rev.12
  21.0 0.7 %collective-permute-start.8 = (f32[2,122,2]{2,1,0:T(8,128)S(1)}, f32[2,122,2]{2,1,0:T(8,128)S(1)}, u32[]{:S(2)}, u32[]{:S(2)}) collective-permute-start(f32[2,122,2]{2,1,0:T(8,128)S(1)} %rev.12), channel_id=1, source_target_pairs={{0,0},{8,24},{16,16},{24,8},{1,1},{9,25},{17,17},{25,9},{2,2},{10,... | collective-permute-start | bytes 5864 | tf_op jit(solution)/shard_map/ppermute | solution.py:18
  21.7 0.1 slice.29
  21.8 1.5 %collective-permute-start.4 = (f32[2,3904]{1,0:T(2,128)S(1)}, f32[2,3904]{1,0:T(2,128)S(1)}, u32[]{:S(2)}, u32[]{:S(2)}) collective-permute-start(f32[2,3904]{1,0:T(2,128)S(1)} %get-tuple-element.16), channel_id=1, source_target_pairs={{0,24},{8,0},{16,8},{24,16},{1,25},{9,1},{17,9},{25,17},{2,26},{10... | collective-permute-start | bytes 93704 | tf_op jit(solution)/shard_map/ppermute | solution.py:18
  23.3 0.6 %collective-permute-start.5 = (f32[2,3904]{1,0:T(2,128)S(1)}, f32[2,3904]{1,0:T(2,128)S(1)}, u32[]{:S(2)}, u32[]{:S(2)}) collective-permute-start(f32[2,3904]{1,0:T(2,128)S(1)} %get-tuple-element.17), channel_id=1, source_target_pairs={{0,8},{8,16},{16,24},{24,0},{1,9},{9,17},{17,25},{25,1},{2,10},{10... | collective-permute-start | bytes 93704 | tf_op jit(solution)/shard_map/ppermute | solution.py:18
  23.8 0.5 rev.10
  24.3 2.4 %collective-permute-start.6 = (f32[122,2,128]{2,1,0:T(2,128)S(1)}, f32[122,2,128]{2,1,0:T(2,128)S(1)}, u32[]{:S(2)}, u32[]{:S(2)}) collective-permute-start(f32[122,2,128]{2,1,0:T(2,128)S(1)} %rev.10), channel_id=1, source_target_pairs={{0,24},{8,16},{16,8},{24,0},{1,25},{9,17},{17,9},{25,1},{2,26},{10... | collective-permute-start | bytes 374792 | tf_op jit(solution)/shard_map/ppermute | solution.py:18
  26.7 0.0 collective-permute-done.7
  26.7 0.0 collective-permute-done.8
  26.8 0.2 reshape.91
  26.9 0.1 copy.30
  27.1 0.1 dot_general.16
  27.2 0.2 fusion
  27.4 0.1 copy.27
  27.5 0.0 collective-permute-done.4
  27.5 0.8 %collective-permute-done.5 = f32[2,3904]{1,0:T(2,128)S(1)} collective-permute-done((f32[2,3904]{1,0:T(2,128)S(1)}, f32[2,3904]{1,0:T(2,128)S(1)}, u32[]{:S(2)}, u32[]{:S(2)}) %collective-permute-start.5) | collective-permute-done | bytes 31264 | tf_op jit(solution)/shard_map/ppermute | solution.py:18
  28.3 1.7 %fusion.4 = f32[3904,128]{1,0:T(8,128)S(1)} fusion(pred[128,4]{0,1:T(4,128)(4,1)S(1)} %and_or_fusion, f32[2,3904]{1,0:T(2,128)S(1)} %collective-permute-done.5, f32[2,3904]{1,0:T(2,128)S(1)} %collective-permute-done.4), kind=kOutput, calls=%fused_computation.16 | convolution fusion | flops 24001792 | bytes 2061824 | tf_op jit(solution)/shard_map/dot_general | solution.py:31
  30.1 0.1 collective-permute-done.6
  30.2 0.5 maximum_maximum_fusion.x_ref
  30.7 8.7 %shard_map.76 = (f32[2,20,32,128]{3,2,1,0:T(8,128)}, f32[2,20,32,128]{3,2,1,0:T(8,128)}, f32[2,20,32,128]{3,2,1,0:T(8,128)S(1)}) custom-call(f32[122,40,256]{2,1,0:T(8,128)S(1)} %maximum_maximum_fusion.x_ref), custom_call_target="tpu_custom_call" | custom-call | tf_op jit(solution)/shard_map/pallas_call | solution.py:216
  39.4 0.1 dynamic-slice_bitcast_fusion
  39.5 0.1 collective-permute-start.9
  39.6 1.5 %collective-permute-done.9 = f32[2,20,4,4,128]{4,3,2,1,0:T(4,128)S(1)} collective-permute-done((f32[2,20,4,4,128]{4,3,2,1,0:T(4,128)S(1)}, f32[2,20,4,4,128]{4,3,2,1,0:T(4,128)S(1)}, u32[]{:S(2)}, u32[]{:S(2)}) %collective-permute-start.9) | collective-permute-done | bytes 327712 | tf_op jit(solution)/shard_map/ppermute | solution.py:274
  41.1 0.1 bitcast_add_fusion
  41.2 0.1 dynamic-slice_bitcast_fusion.3
  41.3 2.1 %collective-permute-start.10 = (f32[2,20,4,128]{3,2,1,0:T(4,128)S(1)}, f32[2,20,4,128]{3,2,1,0:T(4,128)S(1)}, u32[]{:S(2)}, u32[]{:S(2)}) collective-permute-start(f32[2,20,4,128]{3,2,1,0:T(4,128)S(1)} %get-tuple-element.9), channel_id=1, source_target_pairs={{0,2},{1,3},{2,4},{3,5},{4,6},{5,7},{6,0},{7,1},{8,10},{9,11},{10,... | collective-permute-start | bytes 245768 | tf_op jit(solution)/shard_map/ppermute | solution.py:279
  43.4 1.8 %collective-permute-start.11 = (f32[2,20,4,128]{3,2,1,0:T(4,128)S(1)}, f32[2,20,4,128]{3,2,1,0:T(4,128)S(1)}, u32[]{:S(2)}, u32[]{:S(2)}) collective-permute-start(f32[2,20,4,128]{3,2,1,0:T(4,128)S(1)} %get-tuple-element.11), channel_id=1, source_target_pairs={{0,4},{1,5},{2,6},{3,7},{4,0},{5,1},{6,2},{7,3},{8,12},{9,13},{10,... | collective-permute-start | bytes 245768 | tf_op jit(solution)/shard_map/ppermute | solution.py:279
  45.2 0.6 %collective-permute-start.12 = (f32[2,20,4,128]{3,2,1,0:T(4,128)S(1)}, f32[2,20,4,128]{3,2,1,0:T(4,128)S(1)}, u32[]{:S(2)}, u32[]{:S(2)}) collective-permute-start(f32[2,20,4,128]{3,2,1,0:T(4,128)S(1)} %get-tuple-element.10), channel_id=1, source_target_pairs={{0,6},{1,7},{2,0},{3,1},{4,2},{5,3},{6,4},{7,5},{8,14},{9,15},{10,... | collective-permute-start | bytes 245768 | tf_op jit(solution)/shard_map/ppermute | solution.py:279
  45.8 2.7 %collective-permute-done.10 = f32[2,20,4,128]{3,2,1,0:T(4,128)S(1)} collective-permute-done((f32[2,20,4,128]{3,2,1,0:T(4,128)S(1)}, f32[2,20,4,128]{3,2,1,0:T(4,128)S(1)}, u32[]{:S(2)}, u32[]{:S(2)}) %collective-permute-start.10) | collective-permute-done | bytes 81952 | tf_op jit(solution)/shard_map/ppermute | solution.py:279
  48.5 2.7 %collective-permute-done.11 = f32[2,20,4,128]{3,2,1,0:T(4,128)S(1)} collective-permute-done((f32[2,20,4,128]{3,2,1,0:T(4,128)S(1)}, f32[2,20,4,128]{3,2,1,0:T(4,128)S(1)}, u32[]{:S(2)}, u32[]{:S(2)}) %collective-permute-start.11) | collective-permute-done | bytes 81952 | tf_op jit(solution)/shard_map/ppermute | solution.py:279
  51.3 0.1 collective-permute-done.12
  51.4 0.7 %fusion.3 = f32[2,20,4,128]{3,2,1,0:T(4,128)} fusion(f32[2,20,4,128]{3,2,1,0:T(4,128)S(1)} %collective-permute-done.12, f32[2,20,4,128]{3,2,1,0:T(4,128)S(1)} %collective-permute-done.11, f32[2,20,4,128]{3,2,1,0:T(4,128)S(1)} %collective-permute-done.10, f32[2,20,4,4,128]{4,3,2,1,0:T(4,128)S(1)} %bitcast_add_fusion, s32[]{:T(128)S(6)} %select_n.107), kind=kLoop, calls=%fused_computation.12 | loop fusion | flops 61440 | bytes 409604 | tf_op jit(solution)/shard_map/add | solution.py:279
  (13 shorter events, 0.2 us)
Async XLA Ops:
  0.6 11.6 %copy-start = (f32[2,20,4,128]{3,2,1,0:T(4,128)S(1)}, f32[2,20,4,128]{3,2,1,0:T(4,128)}, u32[]{:S(2)}) copy-start(f32[2,20,4,128]{3,2,1,0:T(4,128)} %param.6) | copy-start | bytes 245764
  0.6 9.5 %collective-permute-start = (f32[2,20,4,128]{3,2,1,0:T(4,128)}, f32[2,20,4,128]{3,2,1,0:T(4,128)S(1)}, u32[]{:S(2)}, u32[]{:S(2)}) collective-permute-start(f32[2,20,4,128]{3,2,1,0:T(4,128)} %param.6), channel_id=1, source_target_pairs={{0,2},{1,3},{2,4},{3,5},{4,6},{5,7},{6,0},{7,1},{8,10},{9,11},{10,... | collective-permute-start | bytes 245768 | tf_op jit(solution)/shard_map/ppermute | solution.py:251
  3.7 8.3 %collective-permute-start.1 = (f32[2,20,4,128]{3,2,1,0:T(4,128)}, f32[2,20,4,128]{3,2,1,0:T(4,128)S(1)}, u32[]{:S(2)}, u32[]{:S(2)}) collective-permute-start(f32[2,20,4,128]{3,2,1,0:T(4,128)} %param.6), channel_id=1, source_target_pairs={{0,4},{1,5},{2,6},{3,7},{4,0},{5,1},{6,2},{7,3},{8,12},{9,13},{10,... | collective-permute-start | bytes 245768 | tf_op jit(solution)/shard_map/ppermute | solution.py:251
  6.3 5.9 %collective-permute-start.2 = (f32[2,20,4,128]{3,2,1,0:T(4,128)}, f32[2,20,4,128]{3,2,1,0:T(4,128)S(1)}, u32[]{:S(2)}, u32[]{:S(2)}) collective-permute-start(f32[2,20,4,128]{3,2,1,0:T(4,128)} %param.6), channel_id=1, source_target_pairs={{0,6},{1,7},{2,0},{3,1},{4,2},{5,3},{6,4},{7,5},{8,14},{9,15},{10,... | collective-permute-start | bytes 245768 | tf_op jit(solution)/shard_map/ppermute | solution.py:251
  12.3 1.7 %collective-permute-start.3 = (f32[4,2,20,4,128]{4,3,2,1,0:T(4,128)S(1)}, f32[4,2,20,4,128]{4,3,2,1,0:T(4,128)S(1)}, u32[]{:S(2)}, u32[]{:S(2)}) collective-permute-start(f32[4,2,20,4,128]{4,3,2,1,0:T(4,128)S(1)} %get-tuple-element.13), channel_id=1, source_target_pairs={{0,1},{1,0},{2,3},{3,2},{4,5},{5,4},{6,7},{7,6},{8,9},{9,8},{10,11... | collective-permute-start | bytes 983048 | tf_op jit(solution)/shard_map/ppermute | solution.py:254
  15.1 0.7 %copy-start.1 = (s32[32,128]{1,0:T(8,128)S(1)}, s32[32,128]{1,0:T(8,128)}, u32[]{:S(2)}) copy-start(s32[32,128]{1,0:T(8,128)} %param.7) | copy-start | bytes 49156
  15.1 0.7 %copy-start.2 = (s32[32,128]{1,0:T(8,128)S(1)}, s32[32,128]{1,0:T(8,128)}, u32[]{:S(2)}) copy-start(s32[32,128]{1,0:T(8,128)} %param.8) | copy-start | bytes 49156
  17.4 9.4 %collective-permute-start.7 = (f32[2,122,2]{2,1,0:T(8,128)S(1)}, f32[2,122,2]{2,1,0:T(8,128)S(1)}, u32[]{:S(2)}, u32[]{:S(2)}) collective-permute-start(f32[2,122,2]{2,1,0:T(8,128)S(1)} %rev.11), channel_id=1, source_target_pairs={{0,16},{8,8},{16,0},{24,24},{1,17},{9,9},{17,1},{25,25},{2,18},{10... | collective-permute-start | bytes 5864 | tf_op jit(solution)/shard_map/ppermute | solution.py:18
  21.0 5.8 %collective-permute-start.8 = (f32[2,122,2]{2,1,0:T(8,128)S(1)}, f32[2,122,2]{2,1,0:T(8,128)S(1)}, u32[]{:S(2)}, u32[]{:S(2)}) collective-permute-start(f32[2,122,2]{2,1,0:T(8,128)S(1)} %rev.12), channel_id=1, source_target_pairs={{0,0},{8,24},{16,16},{24,8},{1,1},{9,25},{17,17},{25,9},{2,2},{10,... | collective-permute-start | bytes 5864 | tf_op jit(solution)/shard_map/ppermute | solution.py:18
  21.8 5.7 %collective-permute-start.4 = (f32[2,3904]{1,0:T(2,128)S(1)}, f32[2,3904]{1,0:T(2,128)S(1)}, u32[]{:S(2)}, u32[]{:S(2)}) collective-permute-start(f32[2,3904]{1,0:T(2,128)S(1)} %get-tuple-element.16), channel_id=1, source_target_pairs={{0,24},{8,0},{16,8},{24,16},{1,25},{9,1},{17,9},{25,17},{2,26},{10... | collective-permute-start | bytes 93704 | tf_op jit(solution)/shard_map/ppermute | solution.py:18
  23.3 5.1 %collective-permute-start.5 = (f32[2,3904]{1,0:T(2,128)S(1)}, f32[2,3904]{1,0:T(2,128)S(1)}, u32[]{:S(2)}, u32[]{:S(2)}) collective-permute-start(f32[2,3904]{1,0:T(2,128)S(1)} %get-tuple-element.17), channel_id=1, source_target_pairs={{0,8},{8,16},{16,24},{24,0},{1,9},{9,17},{17,25},{25,1},{2,10},{10... | collective-permute-start | bytes 93704 | tf_op jit(solution)/shard_map/ppermute | solution.py:18
  24.3 5.9 %collective-permute-start.6 = (f32[122,2,128]{2,1,0:T(2,128)S(1)}, f32[122,2,128]{2,1,0:T(2,128)S(1)}, u32[]{:S(2)}, u32[]{:S(2)}) collective-permute-start(f32[122,2,128]{2,1,0:T(2,128)S(1)} %rev.10), channel_id=1, source_target_pairs={{0,24},{8,16},{16,8},{24,0},{1,25},{9,17},{17,9},{25,1},{2,26},{10... | collective-permute-start | bytes 374792 | tf_op jit(solution)/shard_map/ppermute | solution.py:18
  39.5 1.7 %collective-permute-start.9 = (f32[2,20,4,4,128]{4,3,2,1,0:T(4,128)S(1)}, f32[2,20,4,4,128]{4,3,2,1,0:T(4,128)S(1)}, u32[]{:S(2)}, u32[]{:S(2)}) collective-permute-start(f32[2,20,4,4,128]{4,3,2,1,0:T(4,128)S(1)} %dynamic-slice_bitcast_fusion), channel_id=1, source_target_pairs={{0,1},{1,0},{2,3},{3,2},{4,5},{5,4},{6,7},{7,6},{8,9},{9,8},{10,11... | collective-permute-start | bytes 983048 | tf_op jit(solution)/shard_map/ppermute | solution.py:274
  41.3 7.2 %collective-permute-start.10 = (f32[2,20,4,128]{3,2,1,0:T(4,128)S(1)}, f32[2,20,4,128]{3,2,1,0:T(4,128)S(1)}, u32[]{:S(2)}, u32[]{:S(2)}) collective-permute-start(f32[2,20,4,128]{3,2,1,0:T(4,128)S(1)} %get-tuple-element.9), channel_id=1, source_target_pairs={{0,2},{1,3},{2,4},{3,5},{4,6},{5,7},{6,0},{7,1},{8,10},{9,11},{10,... | collective-permute-start | bytes 245768 | tf_op jit(solution)/shard_map/ppermute | solution.py:279
  43.4 7.9 %collective-permute-start.11 = (f32[2,20,4,128]{3,2,1,0:T(4,128)S(1)}, f32[2,20,4,128]{3,2,1,0:T(4,128)S(1)}, u32[]{:S(2)}, u32[]{:S(2)}) collective-permute-start(f32[2,20,4,128]{3,2,1,0:T(4,128)S(1)} %get-tuple-element.11), channel_id=1, source_target_pairs={{0,4},{1,5},{2,6},{3,7},{4,0},{5,1},{6,2},{7,3},{8,12},{9,13},{10,... | collective-permute-start | bytes 245768 | tf_op jit(solution)/shard_map/ppermute | solution.py:279
  45.2 6.2 %collective-permute-start.12 = (f32[2,20,4,128]{3,2,1,0:T(4,128)S(1)}, f32[2,20,4,128]{3,2,1,0:T(4,128)S(1)}, u32[]{:S(2)}, u32[]{:S(2)}) collective-permute-start(f32[2,20,4,128]{3,2,1,0:T(4,128)S(1)} %get-tuple-element.10), channel_id=1, source_target_pairs={{0,6},{1,7},{2,0},{3,1},{4,2},{5,3},{6,4},{7,5},{8,14},{9,15},{10,... | collective-permute-start | bytes 245768 | tf_op jit(solution)/shard_map/ppermute | solution.py:279

commit v27 on v25

--- a/solution.py
+++ b/solution.py
@@ -178,7 +178,7 @@
         forward_second(ck, carry)
         return backward_first(ck, carry)
 
-    lax.fori_loop(0, planes, second_pair, 0, unroll=4)
+    lax.fori_loop(0, planes, second_pair, 0, unroll=8)
 
     def gradient(k, carry):
         g_east = jnp.zeros((ny, width), jnp.float32)

time: 52.3 us -> 53.8 us (1.029)
  Pallas kernels: 8.42 us -> 9.91 us
    pallas_call x1, Pallas kernels: 8.42 us -> 9.91 us  [on_device(): pl.pallas_call(diffusion_kernel, out_shape=(field, field, jax.ShapeDtypeS...]
where the time goes in v27:
time: 53.8 us; the launch traced here: 53.3 us
  starting transfers between devices  20.2 us (38%)
  waiting for transfers between devices  11.8 us (22%)
  Pallas kernels  9.91 us (18%)
  local copies, waits for them, and re-layouts  5.59 us (10%)
  matrix products  2.96 us (6%)
  other arithmetic  1.87 us (3%)
  between operations  0.97 us (2%)
    pallas_call x1, Pallas kernels, on_device(): pl.pallas_call(diffusion_kernel, out_shape=(field, field, jax.ShapeDtypeS...  9.91 us
    ppermute x5, starting transfers between devices, shifted(): return lax.ppermute(x, 'space', perm)  8.58 us
    ppermute x3, starting transfers between devices, gathered_over_scen(): lax.ppermute(block, 'scen', [(q, (q // 2 + step) % chips * 2 + q % 2) for...  7.01 us
    ppermute x3, waiting for transfers between devices, summed_over_scen(): lax.ppermute(send, 'scen', [(q, (q // 2 + step) % chips * 2 + q % 2) for...  5.59 us
    ppermute x3, starting transfers between devices, summed_over_scen(): lax.ppermute(send, 'scen', [(q, (q // 2 + step) % chips * 2 + q % 2) for...  4.5 us
    dot_general x3, matrix products, contract(): lax.dot_general(a, b, (dims, ((), ())), precision=lax.Precision.HIGHEST,...  2.96 us
    unnamed x9, local copies, waits for them, and re-layouts  2.59 us
    ppermute x3, waiting for transfers between devices, gathered_over_scen(): lax.ppermute(block, 'scen', [(q, (q // 2 + step) % chips * 2 + q % 2) for...  2.12 us
  transfers between devices with their start and end apart: 13, of which 9 were waited for; matrix products, arithmetic and copies ran while one was open for 11% of the time, Pallas kernels for 0%

profile of v27, /device:TPU:0, one launch (start us, length us, event | category | flops | bytes accessed | tf_op | source)
XLA Modules:
  0.0 53.3 jit_solution(15266060441400507717)
XLA Ops:
  0.6 0.0 copy-start
  0.6 3.1 %collective-permute-start = (f32[2,20,4,128]{3,2,1,0:T(4,128)}, f32[2,20,4,128]{3,2,1,0:T(4,128)S(1)}, u32[]{:S(2)}, u32[]{:S(2)}) collective-permute-start(f32[2,20,4,128]{3,2,1,0:T(4,128)} %param.6), channel_id=1, source_target_pairs={{0,2},{1,3},{2,4},{3,5},{4,6},{5,7},{6,0},{7,1},{8,10},{9,11},{10,... | collective-permute-start | bytes 245768 | tf_op jit(solution)/shard_map/ppermute | solution.py:251
  3.7 2.6 %collective-permute-start.1 = (f32[2,20,4,128]{3,2,1,0:T(4,128)}, f32[2,20,4,128]{3,2,1,0:T(4,128)S(1)}, u32[]{:S(2)}, u32[]{:S(2)}) collective-permute-start(f32[2,20,4,128]{3,2,1,0:T(4,128)} %param.6), channel_id=1, source_target_pairs={{0,4},{1,5},{2,6},{3,7},{4,0},{5,1},{6,2},{7,3},{8,12},{9,13},{10,... | collective-permute-start | bytes 245768 | tf_op jit(solution)/shard_map/ppermute | solution.py:251
  6.3 1.3 %collective-permute-start.2 = (f32[2,20,4,128]{3,2,1,0:T(4,128)}, f32[2,20,4,128]{3,2,1,0:T(4,128)S(1)}, u32[]{:S(2)}, u32[]{:S(2)}) collective-permute-start(f32[2,20,4,128]{3,2,1,0:T(4,128)} %param.6), channel_id=1, source_target_pairs={{0,6},{1,7},{2,0},{3,1},{4,2},{5,3},{6,4},{7,5},{8,14},{9,15},{10,... | collective-permute-start | bytes 245768 | tf_op jit(solution)/shard_map/ppermute | solution.py:251
  7.7 1.1 %constant_dynamic-update-slice_fusion.2 = f32[122,32,128]{2,1,0:T(8,128)S(1)} fusion(f32[40,32,128]{2,1,0:T(8,128)} %bitcast.54), kind=kLoop, calls=%fused_computation.24 | loop fusion | bytes 1310720
  8.9 1.1 %constant_dynamic-update-slice_fusion.1 = f32[122,32,128]{2,1,0:T(8,128)S(1)} fusion(f32[122,32,128]{2,1,0:T(8,128)S(1)} %constant_dynamic-update-slice_fusion.2, f32[40,32,128]{2,1,0:T(8,128)} %bitcast.55), kind=kLoop, calls=%fused_computation.23 | loop fusion | bytes 1310720
  10.0 0.1 pad.4.clone
  10.1 0.0 collective-permute-done
  10.1 1.9 %collective-permute-done.1 = f32[2,20,4,128]{3,2,1,0:T(4,128)S(1)} collective-permute-done((f32[2,20,4,128]{3,2,1,0:T(4,128)}, f32[2,20,4,128]{3,2,1,0:T(4,128)S(1)}, u32[]{:S(2)}, u32[]{:S(2)}) %collective-permute-start.1) | collective-permute-done | bytes 81952 | tf_op jit(solution)/shard_map/ppermute | solution.py:251
  12.0 0.2 collective-permute-done.2
  12.2 0.0 copy-done
  12.2 0.1 fusion.29
  12.3 0.1 collective-permute-start.3
  12.4 0.1 and_or_fusion
  12.5 1.5 %collective-permute-done.3 = f32[4,2,20,4,128]{4,3,2,1,0:T(4,128)S(1)} collective-permute-done((f32[4,2,20,4,128]{4,3,2,1,0:T(4,128)S(1)}, f32[4,2,20,4,128]{4,3,2,1,0:T(4,128)S(1)}, u32[]{:S(2)}, u32[]{:S(2)}) %collective-permute-start.3) | collective-permute-done | bytes 327712 | tf_op jit(solution)/shard_map/ppermute | solution.py:254
  14.0 0.1 maximum_select_fusion
  14.2 0.9 %gather_fusion = f32[4,2,2,20,4,128]{5,4,3,2,1,0:T(4,128)S(1)} fusion(f32[4,2,2,20,4,128]{5,4,3,2,0,1:T(4,128)S(1)} %maximum_select_fusion, s32[1024]{0:T(1024)S(1)} %pad_clamp_fusion), kind=kCustom, calls=%fused_computation | custom fusion | bytes 1310736 | tf_op jit(solution)/shard_map/jit(_take)/gather | solution.py:257
  15.1 0.0 copy-start.1
  15.1 0.0 copy-start.2
  15.2 0.2 select_bitcast_fusion
  15.4 0.2 copy.24
  15.6 0.3 copy-done.1
  15.9 0.0 copy-done.2
  15.9 1.0 %fusion.9 = f32[4,3904]{1,0:T(4,128)S(1)} fusion(f32[3904,128]{1,0:T(8,128)S(1)} %bitcast.51, pred[128]{0:T(512)(128)(4,1)S(1)} %get-tuple-element.20, pred[128]{0:T(512)(128)(4,1)S(1)} %get-tuple-element.21, pred[128]{0:T(512)(128)(4,1)S(1)} %get-tuple-element.22, pred[128]{0:T(512)(128)(4,1)S(1)} %get-tuple-element.23, ...), kind=kOutput, calls=%fused_computation.34 | convolution fusion | flops 23989760 | bytes 2061840 | tf_op jit(solution)/shard_map/dot_general | solution.py:31
  16.9 0.1 reshape.79
  17.0 0.1 fusion.30
  17.2 0.2 rev.11
  17.4 3.4 %collective-permute-start.7 = (f32[2,122,2]{2,1,0:T(8,128)S(1)}, f32[2,122,2]{2,1,0:T(8,128)S(1)}, u32[]{:S(2)}, u32[]{:S(2)}) collective-permute-start(f32[2,122,2]{2,1,0:T(8,128)S(1)} %rev.11), channel_id=1, source_target_pairs={{0,16},{8,8},{16,0},{24,24},{1,17},{9,9},{17,1},{25,25},{2,18},{10... | collective-permute-start | bytes 5864 | tf_op jit(solution)/shard_map/ppermute | solution.py:18
  20.8 0.2 rev.12
  21.0 0.7 %collective-permute-start.8 = (f32[2,122,2]{2,1,0:T(8,128)S(1)}, f32[2,122,2]{2,1,0:T(8,128)S(1)}, u32[]{:S(2)}, u32[]{:S(2)}) collective-permute-start(f32[2,122,2]{2,1,0:T(8,128)S(1)} %rev.12), channel_id=1, source_target_pairs={{0,0},{8,24},{16,16},{24,8},{1,1},{9,25},{17,17},{25,9},{2,2},{10,... | collective-permute-start | bytes 5864 | tf_op jit(solution)/shard_map/ppermute | solution.py:18
  21.7 0.1 slice.29
  21.8 1.5 %collective-permute-start.4 = (f32[2,3904]{1,0:T(2,128)S(1)}, f32[2,3904]{1,0:T(2,128)S(1)}, u32[]{:S(2)}, u32[]{:S(2)}) collective-permute-start(f32[2,3904]{1,0:T(2,128)S(1)} %get-tuple-element.16), channel_id=1, source_target_pairs={{0,24},{8,0},{16,8},{24,16},{1,25},{9,1},{17,9},{25,17},{2,26},{10... | collective-permute-start | bytes 93704 | tf_op jit(solution)/shard_map/ppermute | solution.py:18
  23.3 0.6 %collective-permute-start.5 = (f32[2,3904]{1,0:T(2,128)S(1)}, f32[2,3904]{1,0:T(2,128)S(1)}, u32[]{:S(2)}, u32[]{:S(2)}) collective-permute-start(f32[2,3904]{1,0:T(2,128)S(1)} %get-tuple-element.17), channel_id=1, source_target_pairs={{0,8},{8,16},{16,24},{24,0},{1,9},{9,17},{17,25},{25,1},{2,10},{10... | collective-permute-start | bytes 93704 | tf_op jit(solution)/shard_map/ppermute | solution.py:18
  23.8 0.5 rev.10
  24.3 2.4 %collective-permute-start.6 = (f32[122,2,128]{2,1,0:T(2,128)S(1)}, f32[122,2,128]{2,1,0:T(2,128)S(1)}, u32[]{:S(2)}, u32[]{:S(2)}) collective-permute-start(f32[122,2,128]{2,1,0:T(2,128)S(1)} %rev.10), channel_id=1, source_target_pairs={{0,24},{8,16},{16,8},{24,0},{1,25},{9,17},{17,9},{25,1},{2,26},{10... | collective-permute-start | bytes 374792 | tf_op jit(solution)/shard_map/ppermute | solution.py:18
  26.7 0.0 collective-permute-done.7
  26.7 0.0 collective-permute-done.8
  26.8 0.2 reshape.91
  26.9 0.1 copy.30
  27.1 0.1 dot_general.16
  27.2 0.2 fusion
  27.4 0.1 copy.27
  27.5 0.0 collective-permute-done.4
  27.5 0.8 %collective-permute-done.5 = f32[2,3904]{1,0:T(2,128)S(1)} collective-permute-done((f32[2,3904]{1,0:T(2,128)S(1)}, f32[2,3904]{1,0:T(2,128)S(1)}, u32[]{:S(2)}, u32[]{:S(2)}) %collective-permute-start.5) | collective-permute-done | bytes 31264 | tf_op jit(solution)/shard_map/ppermute | solution.py:18
  28.3 1.7 %fusion.4 = f32[3904,128]{1,0:T(8,128)S(1)} fusion(pred[128,4]{0,1:T(4,128)(4,1)S(1)} %and_or_fusion, f32[2,3904]{1,0:T(2,128)S(1)} %collective-permute-done.5, f32[2,3904]{1,0:T(2,128)S(1)} %collective-permute-done.4), kind=kOutput, calls=%fused_computation.16 | convolution fusion | flops 24001792 | bytes 2061824 | tf_op jit(solution)/shard_map/dot_general | solution.py:31
  30.1 0.1 collective-permute-done.6
  30.2 0.5 maximum_maximum_fusion.x_ref
  30.7 9.9 %shard_map.76 = (f32[2,20,32,128]{3,2,1,0:T(8,128)}, f32[2,20,32,128]{3,2,1,0:T(8,128)}, f32[2,20,32,128]{3,2,1,0:T(8,128)S(1)}) custom-call(f32[122,40,256]{2,1,0:T(8,128)S(1)} %maximum_maximum_fusion.x_ref), custom_call_target="tpu_custom_call" | custom-call | tf_op jit(solution)/shard_map/pallas_call | solution.py:216
  40.6 0.1 dynamic-slice_bitcast_fusion
  40.7 0.1 collective-permute-start.9
  40.8 1.5 %collective-permute-done.9 = f32[2,20,4,4,128]{4,3,2,1,0:T(4,128)S(1)} collective-permute-done((f32[2,20,4,4,128]{4,3,2,1,0:T(4,128)S(1)}, f32[2,20,4,4,128]{4,3,2,1,0:T(4,128)S(1)}, u32[]{:S(2)}, u32[]{:S(2)}) %collective-permute-start.9) | collective-permute-done | bytes 327712 | tf_op jit(solution)/shard_map/ppermute | solution.py:274
  42.4 0.1 bitcast_add_fusion
  42.5 0.1 dynamic-slice_bitcast_fusion.3
  42.5 2.1 %collective-permute-start.10 = (f32[2,20,4,128]{3,2,1,0:T(4,128)S(1)}, f32[2,20,4,128]{3,2,1,0:T(4,128)S(1)}, u32[]{:S(2)}, u32[]{:S(2)}) collective-permute-start(f32[2,20,4,128]{3,2,1,0:T(4,128)S(1)} %get-tuple-element.9), channel_id=1, source_target_pairs={{0,2},{1,3},{2,4},{3,5},{4,6},{5,7},{6,0},{7,1},{8,10},{9,11},{10,... | collective-permute-start | bytes 245768 | tf_op jit(solution)/shard_map/ppermute | solution.py:279
  44.6 1.8 %collective-permute-start.11 = (f32[2,20,4,128]{3,2,1,0:T(4,128)S(1)}, f32[2,20,4,128]{3,2,1,0:T(4,128)S(1)}, u32[]{:S(2)}, u32[]{:S(2)}) collective-permute-start(f32[2,20,4,128]{3,2,1,0:T(4,128)S(1)} %get-tuple-element.11), channel_id=1, source_target_pairs={{0,4},{1,5},{2,6},{3,7},{4,0},{5,1},{6,2},{7,3},{8,12},{9,13},{10,... | collective-permute-start | bytes 245768 | tf_op jit(solution)/shard_map/ppermute | solution.py:279
  46.4 0.6 %collective-permute-start.12 = (f32[2,20,4,128]{3,2,1,0:T(4,128)S(1)}, f32[2,20,4,128]{3,2,1,0:T(4,128)S(1)}, u32[]{:S(2)}, u32[]{:S(2)}) collective-permute-start(f32[2,20,4,128]{3,2,1,0:T(4,128)S(1)} %get-tuple-element.10), channel_id=1, source_target_pairs={{0,6},{1,7},{2,0},{3,1},{4,2},{5,3},{6,4},{7,5},{8,14},{9,15},{10,... | collective-permute-start | bytes 245768 | tf_op jit(solution)/shard_map/ppermute | solution.py:279
  47.0 2.7 %collective-permute-done.10 = f32[2,20,4,128]{3,2,1,0:T(4,128)S(1)} collective-permute-done((f32[2,20,4,128]{3,2,1,0:T(4,128)S(1)}, f32[2,20,4,128]{3,2,1,0:T(4,128)S(1)}, u32[]{:S(2)}, u32[]{:S(2)}) %collective-permute-start.10) | collective-permute-done | bytes 81952 | tf_op jit(solution)/shard_map/ppermute | solution.py:279
  49.8 2.7 %collective-permute-done.11 = f32[2,20,4,128]{3,2,1,0:T(4,128)S(1)} collective-permute-done((f32[2,20,4,128]{3,2,1,0:T(4,128)S(1)}, f32[2,20,4,128]{3,2,1,0:T(4,128)S(1)}, u32[]{:S(2)}, u32[]{:S(2)}) %collective-permute-start.11) | collective-permute-done | bytes 81952 | tf_op jit(solution)/shard_map/ppermute | solution.py:279
  52.5 0.1 collective-permute-done.12
  52.6 0.7 %fusion.3 = f32[2,20,4,128]{3,2,1,0:T(4,128)} fusion(f32[2,20,4,128]{3,2,1,0:T(4,128)S(1)} %collective-permute-done.12, f32[2,20,4,128]{3,2,1,0:T(4,128)S(1)} %collective-permute-done.11, f32[2,20,4,128]{3,2,1,0:T(4,128)S(1)} %collective-permute-done.10, f32[2,20,4,4,128]{4,3,2,1,0:T(4,128)S(1)} %bitcast_add_fusion, s32[]{:T(128)S(6)} %select_n.107), kind=kLoop, calls=%fused_computation.12 | loop fusion | flops 61440 | bytes 409604 | tf_op jit(solution)/shard_map/add | solution.py:279
  (13 shorter events, 0.2 us)
Async XLA Ops:
  0.6 11.6 %copy-start = (f32[2,20,4,128]{3,2,1,0:T(4,128)S(1)}, f32[2,20,4,128]{3,2,1,0:T(4,128)}, u32[]{:S(2)}) copy-start(f32[2,20,4,128]{3,2,1,0:T(4,128)} %param.6) | copy-start | bytes 245764
  0.6 9.5 %collective-permute-start = (f32[2,20,4,128]{3,2,1,0:T(4,128)}, f32[2,20,4,128]{3,2,1,0:T(4,128)S(1)}, u32[]{:S(2)}, u32[]{:S(2)}) collective-permute-start(f32[2,20,4,128]{3,2,1,0:T(4,128)} %param.6), channel_id=1, source_target_pairs={{0,2},{1,3},{2,4},{3,5},{4,6},{5,7},{6,0},{7,1},{8,10},{9,11},{10,... | collective-permute-start | bytes 245768 | tf_op jit(solution)/shard_map/ppermute | solution.py:251
  3.7 8.3 %collective-permute-start.1 = (f32[2,20,4,128]{3,2,1,0:T(4,128)}, f32[2,20,4,128]{3,2,1,0:T(4,128)S(1)}, u32[]{:S(2)}, u32[]{:S(2)}) collective-permute-start(f32[2,20,4,128]{3,2,1,0:T(4,128)} %param.6), channel_id=1, source_target_pairs={{0,4},{1,5},{2,6},{3,7},{4,0},{5,1},{6,2},{7,3},{8,12},{9,13},{10,... | collective-permute-start | bytes 245768 | tf_op jit(solution)/shard_map/ppermute | solution.py:251
  6.3 5.9 %collective-permute-start.2 = (f32[2,20,4,128]{3,2,1,0:T(4,128)}, f32[2,20,4,128]{3,2,1,0:T(4,128)S(1)}, u32[]{:S(2)}, u32[]{:S(2)}) collective-permute-start(f32[2,20,4,128]{3,2,1,0:T(4,128)} %param.6), channel_id=1, source_target_pairs={{0,6},{1,7},{2,0},{3,1},{4,2},{5,3},{6,4},{7,5},{8,14},{9,15},{10,... | collective-permute-start | bytes 245768 | tf_op jit(solution)/shard_map/ppermute | solution.py:251
  12.3 1.7 %collective-permute-start.3 = (f32[4,2,20,4,128]{4,3,2,1,0:T(4,128)S(1)}, f32[4,2,20,4,128]{4,3,2,1,0:T(4,128)S(1)}, u32[]{:S(2)}, u32[]{:S(2)}) collective-permute-start(f32[4,2,20,4,128]{4,3,2,1,0:T(4,128)S(1)} %get-tuple-element.13), channel_id=1, source_target_pairs={{0,1},{1,0},{2,3},{3,2},{4,5},{5,4},{6,7},{7,6},{8,9},{9,8},{10,11... | collective-permute-start | bytes 983048 | tf_op jit(solution)/shard_map/ppermute | solution.py:254
  15.1 0.7 %copy-start.1 = (s32[32,128]{1,0:T(8,128)S(1)}, s32[32,128]{1,0:T(8,128)}, u32[]{:S(2)}) copy-start(s32[32,128]{1,0:T(8,128)} %param.7) | copy-start | bytes 49156
  15.1 0.7 %copy-start.2 = (s32[32,128]{1,0:T(8,128)S(1)}, s32[32,128]{1,0:T(8,128)}, u32[]{:S(2)}) copy-start(s32[32,128]{1,0:T(8,128)} %param.8) | copy-start | bytes 49156
  17.4 9.4 %collective-permute-start.7 = (f32[2,122,2]{2,1,0:T(8,128)S(1)}, f32[2,122,2]{2,1,0:T(8,128)S(1)}, u32[]{:S(2)}, u32[]{:S(2)}) collective-permute-start(f32[2,122,2]{2,1,0:T(8,128)S(1)} %rev.11), channel_id=1, source_target_pairs={{0,16},{8,8},{16,0},{24,24},{1,17},{9,9},{17,1},{25,25},{2,18},{10... | collective-permute-start | bytes 5864 | tf_op jit(solution)/shard_map/ppermute | solution.py:18
  21.0 5.8 %collective-permute-start.8 = (f32[2,122,2]{2,1,0:T(8,128)S(1)}, f32[2,122,2]{2,1,0:T(8,128)S(1)}, u32[]{:S(2)}, u32[]{:S(2)}) collective-permute-start(f32[2,122,2]{2,1,0:T(8,128)S(1)} %rev.12), channel_id=1, source_target_pairs={{0,0},{8,24},{16,16},{24,8},{1,1},{9,25},{17,17},{25,9},{2,2},{10,... | collective-permute-start | bytes 5864 | tf_op jit(solution)/shard_map/ppermute | solution.py:18
  21.8 5.7 %collective-permute-start.4 = (f32[2,3904]{1,0:T(2,128)S(1)}, f32[2,3904]{1,0:T(2,128)S(1)}, u32[]{:S(2)}, u32[]{:S(2)}) collective-permute-start(f32[2,3904]{1,0:T(2,128)S(1)} %get-tuple-element.16), channel_id=1, source_target_pairs={{0,24},{8,0},{16,8},{24,16},{1,25},{9,1},{17,9},{25,17},{2,26},{10... | collective-permute-start | bytes 93704 | tf_op jit(solution)/shard_map/ppermute | solution.py:18
  23.3 5.1 %collective-permute-start.5 = (f32[2,3904]{1,0:T(2,128)S(1)}, f32[2,3904]{1,0:T(2,128)S(1)}, u32[]{:S(2)}, u32[]{:S(2)}) collective-permute-start(f32[2,3904]{1,0:T(2,128)S(1)} %get-tuple-element.17), channel_id=1, source_target_pairs={{0,8},{8,16},{16,24},{24,0},{1,9},{9,17},{17,25},{25,1},{2,10},{10... | collective-permute-start | bytes 93704 | tf_op jit(solution)/shard_map/ppermute | solution.py:18
  24.3 5.9 %collective-permute-start.6 = (f32[122,2,128]{2,1,0:T(2,128)S(1)}, f32[122,2,128]{2,1,0:T(2,128)S(1)}, u32[]{:S(2)}, u32[]{:S(2)}) collective-permute-start(f32[122,2,128]{2,1,0:T(2,128)S(1)} %rev.10), channel_id=1, source_target_pairs={{0,24},{8,16},{16,8},{24,0},{1,25},{9,17},{17,9},{25,1},{2,26},{10... | collective-permute-start | bytes 374792 | tf_op jit(solution)/shard_map/ppermute | solution.py:18
  40.7 1.7 %collective-permute-start.9 = (f32[2,20,4,4,128]{4,3,2,1,0:T(4,128)S(1)}, f32[2,20,4,4,128]{4,3,2,1,0:T(4,128)S(1)}, u32[]{:S(2)}, u32[]{:S(2)}) collective-permute-start(f32[2,20,4,4,128]{4,3,2,1,0:T(4,128)S(1)} %dynamic-slice_bitcast_fusion), channel_id=1, source_target_pairs={{0,1},{1,0},{2,3},{3,2},{4,5},{5,4},{6,7},{7,6},{8,9},{9,8},{10,11... | collective-permute-start | bytes 983048 | tf_op jit(solution)/shard_map/ppermute | solution.py:274
  42.5 7.2 %collective-permute-start.10 = (f32[2,20,4,128]{3,2,1,0:T(4,128)S(1)}, f32[2,20,4,128]{3,2,1,0:T(4,128)S(1)}, u32[]{:S(2)}, u32[]{:S(2)}) collective-permute-start(f32[2,20,4,128]{3,2,1,0:T(4,128)S(1)} %get-tuple-element.9), channel_id=1, source_target_pairs={{0,2},{1,3},{2,4},{3,5},{4,6},{5,7},{6,0},{7,1},{8,10},{9,11},{10,... | collective-permute-start | bytes 245768 | tf_op jit(solution)/shard_map/ppermute | solution.py:279
  44.6 7.9 %collective-permute-start.11 = (f32[2,20,4,128]{3,2,1,0:T(4,128)S(1)}, f32[2,20,4,128]{3,2,1,0:T(4,128)S(1)}, u32[]{:S(2)}, u32[]{:S(2)}) collective-permute-start(f32[2,20,4,128]{3,2,1,0:T(4,128)S(1)} %get-tuple-element.11), channel_id=1, source_target_pairs={{0,4},{1,5},{2,6},{3,7},{4,0},{5,1},{6,2},{7,3},{8,12},{9,13},{10,... | collective-permute-start | bytes 245768 | tf_op jit(solution)/shard_map/ppermute | solution.py:279
  46.4 6.2 %collective-permute-start.12 = (f32[2,20,4,128]{3,2,1,0:T(4,128)S(1)}, f32[2,20,4,128]{3,2,1,0:T(4,128)S(1)}, u32[]{:S(2)}, u32[]{:S(2)}) collective-permute-start(f32[2,20,4,128]{3,2,1,0:T(4,128)S(1)} %get-tuple-element.10), channel_id=1, source_target_pairs={{0,6},{1,7},{2,0},{3,1},{4,2},{5,3},{6,4},{7,5},{8,14},{9,15},{10,... | collective-permute-start | bytes 245768 | tf_op jit(solution)/shard_map/ppermute | solution.py:279
